TPU v7x, 32 devices: a whole 2x2x4 slice. The times are simulated.
32 devices in a mesh: groups: 2 (over y), seq: 8 (over z, x), batch: 2 (over core).
Axes of the slice: x: 2, y: 2, z: 4, core: 2. Of those that a mesh axis runs over, the one named last changes fastest.
Arguments:
- tokens: int32 [4, 4096], P(('groups', 'batch'), 'seq'), parts along dimension 0, may hold values from 0 to 3
- hidden: bfloat16 [4, 4096, 1024], P(('groups', 'batch'), 'seq'), parts along dimension 0, may hold values from -6 to 6
- base_table: bfloat16 [4, 1024], replicated, may hold values from -6 to 6
- w_in: bfloat16 [1024, 2304], replicated, may hold values from -0.1875 to 0.1875
- w_dt: bfloat16 [1024, 16], replicated, may hold values from -0.1875 to 0.1875
- conv_w: float32 [4, 1280], replicated, may hold values from -3 to 3
- conv_b: float32 [1280], replicated, may hold values from -3 to 3
- dt_bias: float32 [16], replicated, as said below
- a_log: float32 [16], replicated, as said below
- d_skip: float32 [16], replicated, may hold values from 0.5 to 1.5
- norm_gain: float32 [1024], replicated, may hold values from 0.1 to 1.9
- w_out: bfloat16 [1024, 1024], replicated, may hold values from -0.1875 to 0.1875
Outputs:
- mixed: bfloat16 [4, 4096, 1024], P(('groups', 'batch'), 'seq'), parts along dimension 0
There are 2 independent parts, one for each index of `groups`. A program takes and returns all parts, laid end to end along the dimension named above; an argument that names none is the same for every part. Nothing has to cross between parts.
Inputs may be any that keep to these rules, and one draw needn't show every extreme that they name: `a_log`: real numbers, one for each head. `dt_bias`: real numbers, one for each head.
All inputs are finite; a program needn't handle non-finite values.
Results may differ from a plain program's by a relative error of at most 0.0017.
The roundings to bfloat16 on the way count: a program that leaves them out, or rounds other values in their place, can miss the bound.
Values may be sent and summed in bfloat16 or wider, within the bound.
No kernel may reach another device: no remote copies, remote signals or barrier semaphores. Data moves between devices by JAX's collectives and lax.ppermute only.
A program may use at most 192 MiB of HBM per device.

v0:
```python
from functools import partial

import jax
import jax.numpy as jnp
from jax import lax
from jax.sharding import PartitionSpec as P

H = 16
P_SIZE = 64
N = 128
Q = 256
KCONV = 4


norm_epsilon = 1e-05


def padded(block, sides, width):
    for axis, dim in sides:
        count = lax.axis_size(axis)
        forward = [(i, i + 1) for i in range(count - 1)]
        backward = [(target, source) for source, target in forward]
        low = lax.ppermute(
            lax.slice_in_dim(block, block.shape[dim] - width, None, axis=dim), axis, forward
        )
        high = lax.ppermute(lax.slice_in_dim(block, 0, width, axis=dim), axis, backward)
        block = jnp.concatenate([low, block, high], axis=dim)
    return block


def prefix(part, axis, combine, identity, reverse):
    count = lax.axis_size(axis)
    place = lax.axis_index(axis)
    ahead = count - 1 - place if reverse else place
    gathered = jax.tree.map(lambda a: lax.all_gather(a, axis), part)
    state = jax.tree.map(lambda a, e: jnp.zeros_like(a) + jnp.asarray(e, a.dtype), part, identity)

    def one(hop, state):
        source = count - 1 - hop if reverse else hop
        return combine(
            state, jax.tree.map(lambda a: lax.dynamic_index_in_dim(a, source, 0, False), gathered)
        )

    return lax.fori_loop(0, ahead, one, state)


def span_terms(heads_x, b_rows, c_rows, step_size, rates):
    log_decay = jnp.cumsum(step_size * rates[None, :], axis=0)
    across = jnp.transpose(log_decay)
    width = across.shape[1]
    lower = (jnp.arange(width)[:, None] >= jnp.arange(width)[None, :])[None]
    gaps = across[:, :, None] - across[:, None, :]
    decays = jnp.where(lower, jnp.exp(jnp.where(lower, gaps, 0.0)), 0.0)
    scores = jnp.dot(c_rows, jnp.transpose(b_rows), preferred_element_type=jnp.float32)
    weights = (decays * scores[None] * jnp.transpose(step_size)[:, None, :]).astype(jnp.bfloat16)
    inside = jnp.einsum("hts,shp->thp", weights, heads_x, preferred_element_type=jnp.float32)
    to_end = jnp.exp(log_decay[-1][None, :] - log_decay) * step_size
    state_weights = (b_rows.astype(jnp.float32)[:, None, :] * to_end[:, :, None]).astype(
        jnp.bfloat16
    )
    state = jnp.einsum("shp,shn->hpn", heads_x, state_weights, preferred_element_type=jnp.float32)
    return (inside, state, jnp.exp(log_decay[-1]), jnp.exp(log_decay))


def local_terms(extended, w_in, w_dt, conv_w, conv_b, dt_bias, a_log):
    inner = H * P_SIZE
    margin = KCONV - 1
    rows_here = extended.shape[1] - margin
    count = extended.shape[0]
    projected = jnp.einsum("grd,de->gre", extended, w_in, preferred_element_type=jnp.float32)
    source = projected[:, :, inner:]
    summed = jnp.broadcast_to(conv_b, (count, rows_here, conv_b.shape[0]))
    for tap in range(KCONV):
        summed = summed + conv_w[tap] * source[:, tap : tap + rows_here]
    activated = jax.nn.silu(summed).astype(jnp.bfloat16)
    step_size = jax.nn.softplus(
        jnp.einsum("grd,dh->grh", extended[:, margin:], w_dt, preferred_element_type=jnp.float32)
        + dt_bias
    )
    spans = rows_here // Q
    heads_x = activated[:, :, :inner].reshape(count, spans, Q, H, P_SIZE)
    b_rows = activated[:, :, inner : inner + N].reshape(count, spans, Q, N)
    c_rows = activated[:, :, inner + N :].reshape(count, spans, Q, N)
    steps_cut = step_size.reshape(count, spans, Q, H)
    rates = -jnp.exp(a_log)
    per_span = jax.vmap(jax.vmap(partial(span_terms, rates=rates)))
    inside, state, total, from_start = per_span(heads_x, b_rows, c_rows, steps_cut)

    def advance(carry, pieces):
        decay_sofar, state_sofar = carry
        total_here, state_here = pieces
        updated = (
            decay_sofar * total_here,
            total_here[:, :, None, None] * state_sofar + state_here,
        )
        return (updated, (decay_sofar, state_sofar))

    start = (jnp.ones((count, H), jnp.float32), jnp.zeros((count, H, P_SIZE, N), jnp.float32))
    summary, before = lax.scan(
        advance, start, (jnp.moveaxis(total, 1, 0), jnp.moveaxis(state, 1, 0))
    )
    gate_part = projected[:, margin:, :inner]
    return (summary, (before, inside, from_start, heads_x, c_rows, gate_part))


def normalize(pending, incoming, d_skip, norm_gain):
    before, inside, from_start, heads_x, c_rows, gate_part = pending
    before_decay, before_state = before
    start_state = before_state + before_decay[:, :, :, None, None] * incoming[None]
    start_state = jnp.moveaxis(start_state, 0, 1)
    carried = jnp.einsum(
        "gctn,gchpn->gcthp",
        c_rows.astype(jnp.float32),
        start_state,
        precision=lax.Precision.HIGHEST,
    )
    scanned = (
        inside + from_start[..., None] * carried + d_skip[:, None] * heads_x.astype(jnp.float32)
    )
    count = scanned.shape[0]
    flat = scanned.reshape(count, -1, H * P_SIZE)
    gated = flat * jax.nn.silu(gate_part)
    return (
        gated
        * lax.rsqrt(jnp.mean(gated * gated, axis=-1, keepdims=True) + norm_epsilon)
        * norm_gain
    ).astype(jnp.bfloat16)


def project(normed, w_out):
    return jnp.einsum("grk,kd->grd", normed, w_out, preferred_element_type=jnp.float32)


def chain_states(earlier, later):
    first_decay, first_state = earlier
    next_decay, next_state = later
    return (first_decay * next_decay, next_decay[..., None, None] * first_state + next_state)


def on_device(
    tokens, hidden, base_table, w_in, w_dt, conv_w, conv_b, dt_bias, a_log, d_skip, norm_gain, w_out
):
    slabs = hidden.shape[0]
    rows_here = hidden.shape[1]
    margin = KCONV - 1
    one_hot = (tokens[:, :, None] == jnp.arange(4)[None, None, :]).astype(jnp.bfloat16)
    looked = jnp.einsum("gtb,bd->gtd", one_hot, base_table, preferred_element_type=jnp.float32)
    strand_input = (hidden.astype(jnp.float32) + looked).astype(jnp.bfloat16)
    extended_all = padded(strand_input, (("seq", 1),), margin)
    forward_ext = extended_all[:, : rows_here + margin]
    reverse_ext = extended_all[:, margin:][:, ::-1, ::-1]
    extended = jnp.concatenate([forward_ext, reverse_ext], axis=0)
    summary, pending = local_terms(extended, w_in, w_dt, conv_w, conv_b, dt_bias, a_log)
    sum_decay, sum_state = summary
    neutral = (jnp.ones((slabs, H), jnp.float32), jnp.zeros((slabs, H, P_SIZE, N), jnp.float32))
    forward_in = prefix((sum_decay[:slabs], sum_state[:slabs]), "seq", chain_states, neutral, False)
    reverse_in = prefix((sum_decay[slabs:], sum_state[slabs:]), "seq", chain_states, neutral, True)
    incoming_state = jnp.concatenate([forward_in[1], reverse_in[1]], axis=0)
    outputs = project(normalize(pending, incoming_state, d_skip, norm_gain), w_out)
    mixed = outputs[:slabs] + outputs[slabs:][:, ::-1, ::-1]
    return mixed.astype(jnp.bfloat16)


def solution(mesh):
    placed = (
        P(("groups", "batch"), "seq"),
        P(("groups", "batch"), "seq", None),
        P(),
        P(),
        P(),
        P(),
        P(),
        P(),
        P(),
        P(),
        P(),
        P(),
    )
    return jax.shard_map(
        on_device,
        mesh=mesh,
        in_specs=placed,
        out_specs=P(("groups", "batch"), "seq", None),
        check_vma=False,
    )
```

profile of v0, /device:TPU:0, one launch (start us, length us, event | category | flops | bytes accessed | tf_op | source)
XLA Modules:
  0.0 313.3 jit_solution(1577532329183253447)
XLA Ops:
  6.5 1.9 fusion.32
  9.4 1.3 collective-permute-start.1
  10.7 5.5 %collective-permute-start = (bf16[1,3,1024]{2,1,0:T(4,128)(2,1)S(1)}, bf16[1,3,1024]{2,1,0:T(4,128)(2,1)S(1)}, u32[]{:S(2)}, u32[]{:S(2)}) collective-permute-start(bf16[1,3,1024]{2,1,0:T(4,128)(2,1)S(1)} %get-tuple-element.313), channel_id=1, source_target_pairs={{0,2},{2,4},{4,6},{6,8},{8,10},{10,12},{12,14},{1,3},{3,5},{5,7},{... | collective-permute-start | bytes 18440 | tf_op jit(solution)/shard_map/ppermute | solution.py:23
  17.9 2.3 pad_maximum_fusion
  20.2 20.6 %rev.6 = bf16[1,515,1024]{2,1,0:T(8,128)(2,1)} reverse(bf16[1,515,1024]{2,1,0:T(8,128)(2,1)} %pad_maximum_fusion), dimensions={1,2} | reverse | bytes 2109440 | tf_op jit(solution)/shard_map/rev | solution.py:151
  40.8 8.2 %fusion.12 = f32[2,515,2304]{2,1,0:T(8,128)S(1)} fusion(bf16[1024,2304]{1,0:T(8,128)(2,1)} %param.21, bf16[1,515,1024]{2,1,0:T(8,128)(2,1)} %rev.6, bf16[1,512,1024]{2,1,0:T(8,128)(2,1)} %copy-done.3, bf16[1,3,1024]{2,1,0:T(4,128)(2,1)S(1)} %collective-permute-done), kind=kOutput, calls=%fused_computation.28 | convolution fusion | flops 4866478080 | bytes 16320512 | tf_op jit(solution)/shard_map/grd,de->gre/dot_general | solution.py:70
  49.0 3.4 %multiply_convert_fusion.3 = bf16[2,512,1280]{2,1,0:T(8,128)(2,1)S(1)} fusion(f32[2,515,2304]{2,1,0:T(8,128)S(1)} %fusion.12, f32[1280]{0:T(1024)S(1)} %get-tuple-element.273, f32[1280]{0:T(1024)S(1)} %get-tuple-element.274, f32[1280]{0:T(1024)S(1)} %get-tuple-element.272, f32[1280]{0:T(1024)S(1)} %get-tuple-element.271, f32[1280]{0:T(1024)S(1)} %copy-done.13), kind=kLoop, calls=%fused_computation.27 | loop fusion | flops 17039360 | bytes 23618560 | tf_op jit(solution)/shard_map/convert_element_type | solution.py:75
  53.5 1.6 slice.112
  56.5 4.2 %reduce-window.6 = f32[2,2,16,2,128]{4,2,3,1,0:T(8,128)S(1)} reduce-window(f32[2,2,16,2,128]{4,2,3,1,0:T(8,128)} %copy_bitcast_fusion.1, f32[]{:T(128)} %constant.86.clone.1), window={size=1x1x1x1x128 pad=0_0x0_0x0_0x0_0x127_0}, to_apply=%region_0.1 | reduce-window | flops 2080768 | bytes 131076 | tf_op jit(solution)/shard_map/reduce-window
  62.5 1.8 convert_element_type.37
  64.3 6.4 %reshape.127 = bf16[2,2,256,16,64]{4,3,2,1,0:T(8,128)(2,1)} reshape(bf16[2,512,1024]{2,1,0:T(8,128)(2,1)} %slice.112) | data formatting | bytes 4194304 | tf_op jit(solution)/shard_map/reshape | solution.py:81
  70.7 5.8 %copy.65 = bf16[2,2,256,16,64]{2,4,3,1,0:T(8,128)(2,1)} copy(bf16[2,2,256,16,64]{4,3,2,1,0:T(8,128)(2,1)} %reshape.127) | data formatting | bytes 4194304 | tf_op jit(solution)/shard_map/reshape | solution.py:81
  76.5 5.1 %fusion.37 = f32[2,2,16,64,128]{4,3,2,0,1:T(8,128)} fusion(bf16[2,2,256,16,64]{2,4,3,1,0:T(8,128)(2,1)} %copy.65, f32[2,2,256,16]{2,3,1,0:T(8,128)S(1)} %copy-done.12, f32[2,2,256,128]{3,2,1,0:T(8,128)} %convert_element_type.37), kind=kOutput, calls=%fused_computation.60 | convolution fusion | flops 272629760 | bytes 4784128 | tf_op jit(solution)/shard_map/vmap(vmap(shp,shn->hpn))/dot_general | solution.py:61
  81.7 5.0 %while.45 = (s32[]{:T(128)}, f32[2,16]{1,0:T(2,128)S(1)}, f32[2,16,64,128]{3,2,1,0:T(8,128)S(1)}, f32[2,2,16]{2,1,0:T(2,128)S(1)}, f32[2,2,16,64,128]{4,3,2,1,0:...) while((s32[]{:T(128)}, f32[2,16]{1,0:T(2,128)S(1)}, ...), condition=%wide.region_3.4_spmd.clone, body=%wide.region_2.3_spmd.clone.sunk | while | flops 1048675 | bytes 5246326 | solution.py:99
  82.8 1.4 bitcast_add_fusion.10
  85.3 1.4 bitcast_add_fusion.10
  89.3 19.7 %all-gather.4 = f32[8,1,16]{2,1,0:T(1,128)S(1)} all-gather(f32[1,1,16]{2,1,0:T(1,128)S(1)} %get-tuple-element.319), channel_id=2, replica_groups=mesh['groups'=2,'seq'=8,'batch'=2] {'seq'}, dimensions={0}, use_global_device_ids=true | all-gather | bytes 576 | tf_op jit(solution)/shard_map/all_gather | solution.py:35
  109.0 16.4 %all-gather.5 = f32[8,1,16]{2,1,0:T(1,128)S(1)} all-gather(f32[1,1,16]{2,1,0:T(1,128)S(1)} %get-tuple-element.320), channel_id=4, replica_groups=mesh['groups'=2,'seq'=8,'batch'=2] {'seq'}, dimensions={0}, use_global_device_ids=true | all-gather | bytes 576 | tf_op jit(solution)/shard_map/all_gather | solution.py:35
  125.5 2.2 fusion.53
  127.7 34.8 %all-gather.9.cloned.1.call-done = f32[8,16,64,128]{3,2,1,0:T(8,128)} async-done(((f32[1,16,64,128]{3,2,1,0:T(8,128)}), f32[8,16,64,128]{3,2,1,0:T(8,128)}) %all-gather.9.cloned.1.call-update) | async-done | bytes 4194320 | tf_op jit(solution)/shard_map/all_gather | solution.py:35
  162.6 73.4 %all-gather.11.cloned.1.call-done = f32[8,16,64,128]{3,2,1,0:T(8,128)} async-done(((f32[1,16,64,128]{3,2,1,0:T(8,128)}), f32[8,16,64,128]{3,2,1,0:T(8,128)}) %all-gather.11.cloned.1.call-update) | async-done | bytes 4194320 | tf_op jit(solution)/shard_map/all_gather | solution.py:35
  236.0 8.8 %while.44 = (s32[]{:T(128)}, f32[1,16,64,128]{3,2,1,0:T(8,128)S(1)}, s32[]{:T(128)}, f32[8,1,16]{2,1,0:T(1,128)S(1)}, f32[8,1,16,64,128]{4,3,2,1,0:T(8,128)}, /*index=5*/s32[]{:T(128)}, s32[]{:T(128)}, s32[]{:T(128)}, s32[]{:T(128)}) while((s32[]{:T(128)}, f32[1,16,64,128]{3,2,1,0:T(8,128)S(1)}, s32[]{:T(128)}, f32[8,1,16]{2,1,0:T(1,128)S(1)}, ...), condition=%wide.region_7.8_spmd, body=%wide.region_6.7_spmd.sunk | while | flops 262150 | bytes 1573203 | solution.py:44
  245.0 3.7 %fusion.33 = f32[2,2,256,16,64]{2,4,3,1,0:T(8,128)S(1)} fusion(bf16[2,2,256,128,1]{3,2,4,1,0:T(8,128)(2,1)S(1)} %bitcast.118, f32[2,2,16,64,128]{4,3,2,1,0:T(8,128)} %get-tuple-element.173, f32[2,16,64,128]{3,2,1,0:T(8,128)S(1)} %pad_maximum_fusion.1, f32[2,2,16]{2,1,0:T(2,128)S(1)} %get-tuple-element.174), kind=kOutput, calls=%fused_computation.55 | convolution fusion | flops 1611661312 | bytes 7602432 | tf_op jit(solution)/shard_map/gctn,gchpn->gcthp/dot_general | solution.py:111
  248.7 7.1 %fusion.15 = f32[2,2,256,16,64]{2,4,3,1,0:T(8,128)} fusion(bf16[2,2,256,16,64]{2,4,3,1,0:T(8,128)(2,1)S(1)} %copy-done.6, f32[2,2,256,16,64]{2,4,3,1,0:T(8,128)S(1)} %fusion.33, f32[2,2,16,256]{3,2,1,0:T(8,128)S(1)} %copy.64, f32[2,2,256,256]{3,2,1,0:T(8,128)S(1)} %copy-done.8, f32[2,2,16,256]{3,2,1,0:T(8,128)S(1)} %copy-done.9, ...), kind=kOutput, calls=%fused_computation.32 | convolution fusion | flops 567279616 | bytes 11796544 | tf_op jit(solution)/shard_map/vmap(vmap(hts,shp->thp))/dot_general | solution.py:56
  255.9 8.1 %copy.77 = f32[2,2,256,16,64]{4,3,2,1,0:T(8,128)} copy(f32[2,2,256,16,64]{2,4,3,1,0:T(8,128)} %fusion.15) | data formatting | bytes 8388608 | tf_op jit(solution)/shard_map/reshape | solution.py:121
  263.9 7.6 %reshape.126 = f32[2,512,1024]{2,1,0:T(8,128)} reshape(f32[2,2,256,16,64]{4,3,2,1,0:T(8,128)} %copy.77) | data formatting | bytes 8388608 | tf_op jit(solution)/shard_map/reshape | solution.py:121
  271.5 5.1 %multiply_reduce_fusion = f32[2,512]{1,0:T(2,128)S(1)} fusion(f32[2,512,1024]{2,1,0:T(8,128)} %reshape.126, f32[2,515,2304]{2,1,0:T(8,128)} %copy-done.1), kind=kLoop, calls=%fused_computation.34 | loop fusion | flops 7339008 | bytes 8392704 | tf_op jit(solution)/shard_map/reduce_sum | solution.py:125
  276.7 5.1 %fusion.23 = f32[2,512,1024]{2,1,0:T(8,128)S(1)} fusion(bf16[1024,1024]{1,0:T(8,128)(2,1)S(1)} %copy-done, f32[1024]{0:T(1024)S(1)} %copy-done.16, f32[2,512]{1,0:T(2,128)S(1)} %add_rsqrt_fusion, f32[2,512,1024]{2,1,0:T(8,128)S(1)} %copy-done.2, f32[2,515,2304]{2,1,0:T(8,128)} %copy-done.1), kind=kOutput, calls=%fused_computation.43 | convolution fusion | flops 2155872256 | bytes 14688256 | tf_op jit(solution)/shard_map/grk,kd->grd/dot_general | solution.py:131
  281.8 1.9 copy-done.5
  283.8 1.6 slice.120
  285.4 17.6 %rev.7 = f32[1,512,1024]{2,1,0:T(8,128)} reverse(f32[1,512,1024]{2,1,0:T(8,128)} %slice.120), dimensions={1,2} | reverse | bytes 4194304 | tf_op jit(solution)/shard_map/rev | solution.py:160
  303.0 3.5 %fusion.24 = bf16[1,512,1024]{2,1,0:T(8,128)(2,1)} fusion(f32[1,512,1024]{2,1,0:T(8,128)} %rev.7, f32[2,512,1024]{2,1,0:T(8,128)} %copy-done.5), kind=kLoop, calls=%fused_computation.45 | loop fusion | flops 1048576 | bytes 5242880 | tf_op jit(solution)/shard_map/convert_element_type | solution.py:161
  (92 shorter events, 20.2 us)
Async XLA Ops:
  6.5 270.1 %copy-start = (bf16[1024,1024]{1,0:T(8,128)(2,1)S(1)}, bf16[1024,1024]{1,0:T(8,128)(2,1)}, u32[]{:S(2)}) copy-start(bf16[1024,1024]{1,0:T(8,128)(2,1)} %param.29) | copy-start | bytes 6291460
  6.5 156.0 %all-gather.9.cloned.1.call-start = ((), (), s32[]{:S(2)}) async-start(), calls=%async_computation | async-start | bytes 4718592 | tf_op jit(solution)/shard_map/all_gather | solution.py:35
  8.4 1.0 copy-start.3
  9.4 8.5 %collective-permute-start.1 = (bf16[1,3,1024]{2,1,0:T(4,128)(2,1)S(1)}, bf16[1,3,1024]{2,1,0:T(4,128)(2,1)S(1)}, u32[]{:S(2)}, u32[]{:S(2)}) collective-permute-start(bf16[1,3,1024]{2,1,0:T(4,128)(2,1)S(1)} %get-tuple-element.314), channel_id=1, source_target_pairs={{2,0},{4,2},{6,4},{8,6},{10,8},{12,10},{14,12},{3,1},{5,3},{7,5},{... | collective-permute-start | bytes 18440 | tf_op jit(solution)/shard_map/ppermute | solution.py:26
  10.7 30.1 %collective-permute-start = (bf16[1,3,1024]{2,1,0:T(4,128)(2,1)S(1)}, bf16[1,3,1024]{2,1,0:T(4,128)(2,1)S(1)}, u32[]{:S(2)}, u32[]{:S(2)}) collective-permute-start(bf16[1,3,1024]{2,1,0:T(4,128)(2,1)S(1)} %get-tuple-element.313), channel_id=1, source_target_pairs={{0,2},{2,4},{4,6},{6,8},{8,10},{10,12},{12,14},{1,3},{3,5},{5,7},{... | collective-permute-start | bytes 18440 | tf_op jit(solution)/shard_map/ppermute | solution.py:23
  40.8 8.2 %copy-start.13 = (f32[1280]{0:T(1024)S(1)}, f32[1280]{0:T(1024)}, u32[]{:S(2)}) copy-start(f32[1280]{0:T(1024)} %param.24) | copy-start | bytes 15364
  49.0 3.7 %copy-start.1 = (f32[2,515,2304]{2,1,0:T(8,128)}, f32[2,515,2304]{2,1,0:T(8,128)S(1)}, u32[]{:S(2)}) copy-start(f32[2,515,2304]{2,1,0:T(8,128)S(1)} %fusion.12) | copy-start | bytes 28477444
  52.7 2.4 copy-start.4
  52.7 2.4 copy-start.7
  52.7 2.4 copy-start.15
  52.7 2.4 copy-start.17
  70.7 5.9 %copy-start.12 = (f32[2,2,256,16]{2,3,1,0:T(8,128)S(1)}, f32[2,2,256,16]{2,3,1,0:T(8,128)}, u32[]{:S(2)}) copy-start(f32[2,2,256,16]{2,3,1,0:T(8,128)} %get-tuple-element.316) | copy-start | bytes 196612
  70.7 11.0 %copy-start.14 = (f32[2,2,16]{2,1,0:T(2,128)S(1)}, f32[2,2,16]{2,1,0:T(2,128)}, u32[]{:S(2)}) copy-start(f32[2,2,16]{2,1,0:T(2,128)} %custom-call.2) | copy-start | bytes 772
  87.9 148.1 %all-gather.11.cloned.1.call-start = ((), (), s32[]{:S(2)}) async-start(), calls=%async_computation.1 | async-start | bytes 4718592 | tf_op jit(solution)/shard_map/all_gather | solution.py:35
  245.0 3.7 %copy-start.6 = (bf16[2,2,256,16,64]{2,4,3,1,0:T(8,128)(2,1)S(1)}, bf16[2,2,256,16,64]{2,4,3,1,0:T(8,128)(2,1)}, u32[]{:S(2)}) copy-start(bf16[2,2,256,16,64]{2,4,3,1,0:T(8,128)(2,1)} %copy.65) | copy-start | bytes 6291460
  245.0 3.7 %copy-start.8 = (f32[2,2,256,256]{3,2,1,0:T(8,128)S(1)}, f32[2,2,256,256]{3,2,1,0:T(8,128)}, u32[]{:S(2)}) copy-start(f32[2,2,256,256]{3,2,1,0:T(8,128)} %fusion.53) | copy-start | bytes 3145732
  245.0 3.7 %copy-start.9 = (f32[2,2,16,256]{3,2,1,0:T(8,128)S(1)}, f32[2,2,16,256]{3,2,1,0:T(8,128)}, u32[]{:S(2)}) copy-start(f32[2,2,16,256]{3,2,1,0:T(8,128)} %get-tuple-element.317) | copy-start | bytes 196612
  245.0 3.7 %copy-start.10 = (pred[256,256]{1,0:T(8,128)(4,1)S(1)}, pred[256,256]{1,0:T(8,128)(4,1)}, u32[]{:S(2)}) copy-start(pred[256,256]{1,0:T(8,128)(4,1)} %iota_compare_fusion) | copy-start | bytes 196612
  245.0 3.7 %copy-start.11 = (f32[2,2,256,16]{2,3,1,0:T(8,128)S(1)}, f32[2,2,256,16]{2,3,1,0:T(8,128)}, u32[]{:S(2)}) copy-start(f32[2,2,256,16]{2,3,1,0:T(8,128)} %get-tuple-element.315) | copy-start | bytes 196612
  245.0 3.7 %copy-start.18 = (f32[16]{0:T(128)S(1)}, f32[16]{0:T(128)}, u32[]{:S(2)}) copy-start(f32[16]{0:T(128)} %param.27) | copy-start | bytes 196
  271.5 5.1 %copy-start.2 = (f32[2,512,1024]{2,1,0:T(8,128)S(1)}, f32[2,512,1024]{2,1,0:T(8,128)}, u32[]{:S(2)}) copy-start(f32[2,512,1024]{2,1,0:T(8,128)} %reshape.126) | copy-start | bytes 12582916
  271.5 5.1 %copy-start.16 = (f32[1024]{0:T(1024)S(1)}, f32[1024]{0:T(1024)}, u32[]{:S(2)}) copy-start(f32[1024]{0:T(1024)} %param.28) | copy-start | bytes 12292
  281.8 2.0 copy-start.5
Sparse Core Ops, SparseCore 0:
  88.0 74.4 all-gather.8
  164.6 71.3 all-gather.10
where the time goes:
time: 318 us; the launch traced here: 313 us
  waiting for transfers between devices  109 us (34%)
  local copies, waits for them, and re-layouts  76 us (24%)
  other arithmetic  37.1 us (12%)
  blocking collectives  36.1 us (11%)
  matrix products  34 us (11%)
  between operations  13.8 us (4%)
  starting transfers between devices  6.84 us (2%)
    all_gather x2, waiting for transfers between devices, prefix(): gathered = jax.tree.map(lambda a: lax.all_gather(a, axis), part)  108 us
    all_gather x2, blocking collectives, prefix(): gathered = jax.tree.map(lambda a: lax.all_gather(a, axis), part)  36.1 us
    rev x1, local copies, waits for them, and re-layouts, on_device(): reverse_ext = extended_all[:, margin:][:, ::-1, ::-1]  20.6 us
    rev x1, local copies, waits for them, and re-layouts, on_device(): mixed = outputs[:slabs] + outputs[slabs:][:, ::-1, ::-1]  17.6 us
    reshape x2, local copies, waits for them, and re-layouts, normalize(): flat = scanned.reshape(count, -1, H * P_SIZE)  15.7 us
    reshape x2, local copies, waits for them, and re-layouts, local_terms(): heads_x = activated[:, :, :inner].reshape(count, spans, Q, H, P_SIZE)  12.2 us
    add x7, other arithmetic, chain_states(): next_decay[..., None, None] * first_state + next_state  8.31 us
    dot_general x1, matrix products, local_terms(): jnp.einsum('grd,de->gre', extended, w_in, preferred_element_type=jnp.floa...  8.19 us
  transfers between devices with their start and end apart: 4, of which 2 were waited for; matrix products, arithmetic and copies ran while one was open for 9% of the time, Pallas kernels for 0%

commit v1 on v0

v1 whole, which is shorter than its diff:
```python
import jax
import jax.numpy as jnp
from jax import lax
from jax.sharding import PartitionSpec as P

H = 16
P_SIZE = 64
N = 128
Q = 256
KCONV = 4


norm_epsilon = 1e-05


def exchange(size, dtype):
    row = lax.broadcasted_iota(jnp.int32, (size, size), 0)
    col = lax.broadcasted_iota(jnp.int32, (size, size), 1)
    return (row + col == size - 1).astype(dtype)


def flip_lanes(a):
    j = exchange(a.shape[-1], a.dtype)
    return jnp.einsum("...d,de->...e", a, j, preferred_element_type=jnp.float32).astype(a.dtype)


def chain(earlier, later):
    first_decay, first_state = earlier
    next_decay, next_state = later
    return (first_decay * next_decay, next_decay[..., None, None] * first_state + next_state)


def exclusive_scans(fwd, rev, axis):
    count = lax.axis_size(axis)
    place = lax.axis_index(axis)
    seen = [None, None]
    ahead = [fwd, rev]
    shift = 1
    while shift < count:
        up = [(i, i + shift) for i in range(count - shift)]
        down = [(i + shift, i) for i in range(count - shift)]
        got = []
        for k, pairs in ((0, up), (1, down)):
            decay, state = lax.ppermute(ahead[k], axis, pairs)
            has = (place >= shift) if k == 0 else (place < count - shift)
            decay = jnp.where(has, decay, 1.0)
            got.append((decay, state))
        for k in range(2):
            seen[k] = got[k] if seen[k] is None else chain(got[k], seen[k])
            if 2 * shift < count:
                ahead[k] = chain(got[k], ahead[k])
        shift *= 2
    if seen[0] is None:
        return fwd_identity(fwd), fwd_identity(rev)
    return seen[0], seen[1]


def fwd_identity(summary):
    decay, state = summary
    return (jnp.ones_like(decay), jnp.zeros_like(state))


def block_terms(heads_x, b_rows, c_rows, step_size, rates, reverse):
    log_decay = lax.cumsum(step_size * rates, axis=2, reverse=reverse)
    end = log_decay[:, :, 0] if reverse else log_decay[:, :, -1]
    across = jnp.swapaxes(log_decay, 2, 3)
    width = across.shape[-1]
    t_idx = jnp.arange(width)[:, None]
    s_idx = jnp.arange(width)[None, :]
    keep = (s_idx >= t_idx) if reverse else (t_idx >= s_idx)
    gaps = across[..., :, None] - across[..., None, :]
    decays = jnp.where(keep, jnp.exp(jnp.where(keep, gaps, 0.0)), 0.0)
    scores = jnp.einsum("gjtn,gjsn->gjts", c_rows, b_rows, preferred_element_type=jnp.float32)
    weights = (decays * scores[:, :, None] * jnp.swapaxes(step_size, 2, 3)[:, :, :, None, :]).astype(
        jnp.bfloat16
    )
    inside = jnp.einsum("gjhts,gjshp->gjthp", weights, heads_x, preferred_element_type=jnp.float32)
    to_end = jnp.exp(end[:, :, None, :] - log_decay) * step_size
    state_weights = (b_rows.astype(jnp.float32)[..., None, :] * to_end[..., None]).astype(jnp.bfloat16)
    state = jnp.einsum("gjshp,gjshn->gjhpn", heads_x, state_weights, preferred_element_type=jnp.float32)
    return inside, state, jnp.exp(end), jnp.exp(log_decay)


def strand_terms(projected, halo, step_size, conv_w, conv_b, rates, reverse):
    inner = H * P_SIZE
    count, rows, _ = projected.shape
    margin = KCONV - 1
    source = projected[:, :, inner:]
    if reverse:
        padded = jnp.concatenate([source, halo], axis=1)
        taps = [(tap, margin - tap) for tap in range(KCONV)]
    else:
        padded = jnp.concatenate([halo, source], axis=1)
        taps = [(tap, tap) for tap in range(KCONV)]
    summed = jnp.broadcast_to(conv_b, source.shape)
    for tap, start in taps:
        summed = summed + conv_w[tap] * padded[:, start : start + rows]
    activated = jax.nn.silu(summed).astype(jnp.bfloat16)
    spans = rows // Q
    heads_x = activated[:, :, :inner].reshape(count, spans, Q, H, P_SIZE)
    b_rows = activated[:, :, inner : inner + N].reshape(count, spans, Q, N)
    c_rows = activated[:, :, inner + N :].reshape(count, spans, Q, N)
    steps_cut = step_size.reshape(count, spans, Q, H)
    inside, state, total, from_start = block_terms(
        heads_x, b_rows, c_rows, steps_cut, rates, reverse
    )
    order = list(range(spans))
    if reverse:
        order = order[::-1]
    before = {}
    sofar = (jnp.ones((count, H), jnp.float32), jnp.zeros((count, H, P_SIZE, N), jnp.float32))
    for j in order:
        before[j] = sofar
        sofar = chain(sofar, (total[:, j], state[:, j]))
    before_decay = jnp.stack([before[j][0] for j in range(spans)], axis=1)
    before_state = jnp.stack([before[j][1] for j in range(spans)], axis=1)
    pending = (before_decay, before_state, inside, from_start, heads_x, c_rows)
    return sofar, pending


def finish(pending, incoming, gate_part, d_skip, norm_gain):
    before_decay, before_state, inside, from_start, heads_x, c_rows = pending
    start_state = before_state + before_decay[..., None, None] * incoming[:, None]
    carried = jnp.einsum(
        "gjtn,gjhpn->gjthp",
        c_rows.astype(jnp.float32),
        start_state,
        precision=lax.Precision.HIGHEST,
    )
    scanned = (
        inside
        + from_start[..., None] * carried
        + d_skip[:, None] * heads_x.astype(jnp.float32)
    )
    count = scanned.shape[0]
    flat = scanned.reshape(count, -1, H * P_SIZE)
    gated = flat * jax.nn.silu(gate_part)
    return (
        gated
        * lax.rsqrt(jnp.mean(gated * gated, axis=-1, keepdims=True) + norm_epsilon)
        * norm_gain
    ).astype(jnp.bfloat16)


def on_device(
    tokens, hidden, base_table, w_in, w_dt, conv_w, conv_b, dt_bias, a_log, d_skip, norm_gain, w_out
):
    inner = H * P_SIZE
    margin = KCONV - 1
    one_hot = (tokens[:, :, None] == jnp.arange(4)[None, None, :]).astype(jnp.bfloat16)
    looked = jnp.einsum("gtb,bd->gtd", one_hot, base_table, preferred_element_type=jnp.float32)
    strand = (hidden.astype(jnp.float32) + looked).astype(jnp.bfloat16)
    rows = strand.shape[1]
    count = lax.axis_size("seq")
    low = lax.ppermute(strand[:, rows - margin :], "seq", [(i, i + 1) for i in range(count - 1)])
    high = lax.ppermute(strand[:, :margin], "seq", [(i + 1, i) for i in range(count - 1)])
    mirrored = flip_lanes(strand)
    high_mirrored = flip_lanes(high)
    w_source = w_in[:, inner:]
    proj_f = jnp.einsum("grd,de->gre", strand, w_in, preferred_element_type=jnp.float32)
    proj_r = jnp.einsum("grd,de->gre", mirrored, w_in, preferred_element_type=jnp.float32)
    halo_f = jnp.einsum("grd,de->gre", low, w_source, preferred_element_type=jnp.float32)
    halo_r = jnp.einsum("grd,de->gre", high_mirrored, w_source, preferred_element_type=jnp.float32)
    step_f = jax.nn.softplus(
        jnp.einsum("grd,dh->grh", strand, w_dt, preferred_element_type=jnp.float32) + dt_bias
    )
    step_r = jax.nn.softplus(
        jnp.einsum("grd,dh->grh", mirrored, w_dt, preferred_element_type=jnp.float32) + dt_bias
    )
    rates = -jnp.exp(a_log)
    sum_f, pend_f = strand_terms(proj_f, halo_f, step_f, conv_w, conv_b, rates, False)
    sum_r, pend_r = strand_terms(proj_r, halo_r, step_r, conv_w, conv_b, rates, True)
    in_f, in_r = exclusive_scans(sum_f, sum_r, "seq")
    normed_f = finish(pend_f, in_f[1], proj_f[:, :, :inner], d_skip, norm_gain)
    normed_r = finish(pend_r, in_r[1], proj_r[:, :, :inner], d_skip, norm_gain)
    w_out_mirrored = flip_lanes(w_out)
    out = jnp.einsum(
        "grk,kd->grd", normed_f, w_out, preferred_element_type=jnp.float32
    ) + jnp.einsum("grk,kd->grd", normed_r, w_out_mirrored, preferred_element_type=jnp.float32)
    return out.astype(jnp.bfloat16)


def solution(mesh):
    placed = (
        P(("groups", "batch"), "seq"),
        P(("groups", "batch"), "seq", None),
        P(),
        P(),
        P(),
        P(),
        P(),
        P(),
        P(),
        P(),
        P(),
        P(),
    )
    return jax.shard_map(
        on_device,
        mesh=mesh,
        in_specs=placed,
        out_specs=P(("groups", "batch"), "seq", None),
        check_vma=False,
    )
```

time: 318 us -> 212 us (0.67); the launches traced: 313 us -> 211 us
  waiting for transfers between devices: 109 us -> 7.61 us
  blocking collectives: 36.1 us -> 0 us
  starting transfers between devices: 6.84 us -> 41 us
  matrix products: 34 us -> 51.3 us
  between operations: 13.8 us -> 0.93 us
  local copies, waits for them, and re-layouts: 76 us -> 66.1 us
  other arithmetic: 37.1 us -> 43.6 us
    all_gather x2 -> x0, waiting for transfers between devices: 108 us -> none  [prefix(): gathered = jax.tree.map(lambda a: lax.all_gather(a, axis), part)]
    rev x2 -> x0, local copies, waits for them, and re-layouts: 38.2 us -> none  [the longest x1 20.6 us: on_device(): reverse_ext = extended_all[:, margin:][:, ::-1, ::-1]]
    all_gather x2 -> x0, blocking collectives: 36.1 us -> none  [prefix(): gathered = jax.tree.map(lambda a: lax.all_gather(a, axis), part)]
    ppermute x2 -> x12, starting transfers between devices: 6.79 us -> 41 us  [the longest x10 34.2 us: exclusive_scans(): decay, state = lax.ppermute(ahead[k], axis, pairs)]
    convert_element_type x0 -> x4, local copies, waits for them, and re-layouts: none -> 18.1 us  [finish(): heads_x.astype(jnp.float32)]
    dot_general x7 -> x17, matrix products: 32.2 us -> 49.4 us  [the longest x2 8.74 us: block_terms(): jnp.einsum('gjhts,gjshp->gjthp', weights, heads_x, preferred_element_type...]
    another operation x1 -> x23, local copies, waits for them, and re-layouts: 0.01 us -> 14.2 us
    reshape x5 -> x8, local copies, waits for them, and re-layouts: 27.9 us -> 19.6 us  [the longest x4 19.6 us: finish(): flat = scanned.reshape(count, -1, H * P_SIZE)]
  transfers between devices with their start and end apart: 4 -> 12, of which waited for: 2 -> 3; matrix products, arithmetic and copies ran while one was open for 9% -> 59% of each run, Pallas kernels for 0% -> 0%
where the time goes in v1:
time: 212 us; the launch traced here: 211 us
  local copies, waits for them, and re-layouts  66.1 us (31%)
  matrix products  51.3 us (24%)
  other arithmetic  43.6 us (21%)
  starting transfers between devices  41 us (19%)
  waiting for transfers between devices  7.61 us (4%)
    ppermute x10, starting transfers between devices, exclusive_scans(): decay, state = lax.ppermute(ahead[k], axis, pairs)  34.2 us
    reshape x4, local copies, waits for them, and re-layouts, finish(): flat = scanned.reshape(count, -1, H * P_SIZE)  19.6 us
    convert_element_type x4, local copies, waits for them, and re-layouts, finish(): heads_x.astype(jnp.float32)  18.1 us
    another operation x23, local copies, waits for them, and re-layouts  14.2 us
    convert_element_type x1, other arithmetic, strand_terms(): activated = jax.nn.silu(summed).astype(jnp.bfloat16)  10.1 us
    dot_general x2, matrix products, block_terms(): jnp.einsum('gjhts,gjshp->gjthp', weights, heads_x, preferred_element_type...  8.74 us
    ppermute x10, waiting for transfers between devices, exclusive_scans(): decay, state = lax.ppermute(ahead[k], axis, pairs)  7.61 us
    dot_general x1, matrix products, on_device(): jnp.einsum('grd,de->gre', mirrored, w_in, preferred_element_type=jnp.floa...  7.46 us
  transfers between devices with their start and end apart: 12, of which 3 were waited for; matrix products, arithmetic and copies ran while one was open for 59% of the time, Pallas kernels for 0%

profile of v1, /device:TPU:0, one launch (start us, length us, event | category | flops | bytes accessed | tf_op | source)
XLA Modules:
  0.0 210.5 jit_solution(7298894484794532381)
XLA Ops:
  2.5 5.5 %collective-permute-start = (bf16[1,3,1024]{2,1,0:T(4,128)(2,1)}, bf16[1,3,1024]{2,1,0:T(4,128)(2,1)}, u32[]{:S(2)}, u32[]{:S(2)}) collective-permute-start(bf16[1,3,1024]{2,1,0:T(4,128)(2,1)} %get-tuple-element.21), channel_id=1, source_target_pairs={{0,2},{2,4},{4,6},{6,8},{8,10},{10,12},{12,14},{1,3},{3,5},{5,7},{... | collective-permute-start | bytes 18440 | tf_op jit(solution)/shard_map/ppermute | solution.py:155
  14.7 5.1 %collective-permute-start.1 = (f32[1,16]{1,0:T(1,128)}, f32[1,16]{1,0:T(1,128)}, u32[]{:S(2)}, u32[]{:S(2)}) collective-permute-start(f32[1,16]{1,0:T(1,128)} %get-tuple-element.31), channel_id=1, source_target_pairs={{0,2},{2,4},{4,6},{6,8},{8,10},{10,12},{12,14},{1,3},{3,5},{5,7},{... | collective-permute-start | bytes 200 | tf_op jit(solution)/shard_map/ppermute | solution.py:44
  19.8 5.0 %reduce-window.16 = f32[1,2,16,2,128]{4,2,3,1,0:T(8,128)S(1)} reduce-window(f32[1,2,16,2,128]{4,2,3,1,0:T(8,128)S(1)} %copy.135, f32[]{:T(128)} %constant.13.clone.1), window={size=1x1x1x1x128 pad=0_0x0_0x0_0x0_0x0_127}, to_apply=%region_3.4 | reduce-window | flops 1040384 | bytes 65540 | tf_op jit(solution)/shard_map/reduce-window.2
  27.5 7.5 %convolution_bitcast_fusion = f32[1,512,2304]{2,1,0:T(8,128)} fusion(bf16[512,1024]{1,0:T(8,128)(2,1)} %copy-done.16, bf16[1024,2304]{1,0:T(8,128)(2,1)} %param.15), kind=kOutput, calls=%fused_computation.2 | convolution fusion | flops 2415919104 | bytes 10485760 | tf_op jit(solution)/shard_map/grd,de->gre/dot_general | solution.py:161
  34.9 4.3 %convolution_bitcast_fusion.1 = f32[1,512,2304]{2,1,0:T(8,128)} fusion(bf16[1024,2304]{1,0:T(8,128)(2,1)S(1)} %bitcast.215, bf16[1,512,1024]{2,1,0:T(8,128)(2,1)S(1)} %fusion.51), kind=kOutput, calls=%fused_computation.3 | convolution fusion | flops 2415919104 | bytes 10485760 | tf_op jit(solution)/shard_map/grd,de->gre/dot_general | solution.py:160
  41.8 3.5 %slice.167 = f32[1,512,1280]{2,1,0:T(8,128)} slice(f32[1,512,2304]{2,1,0:T(8,128)} %convolution_bitcast_fusion), slice={[0:1], [0:512], [1024:2304]} | slice | bytes 5242880 | tf_op jit(solution)/shard_map/slice | solution.py:88
  54.4 5.4 %collective-permute-start.2 = (f32[1,16]{1,0:T(1,128)S(1)}, f32[1,16]{1,0:T(1,128)S(1)}, u32[]{:S(2)}, u32[]{:S(2)}) collective-permute-start(f32[1,16]{1,0:T(1,128)S(1)} %fusion.123), channel_id=1, source_target_pairs={{0,4},{2,6},{4,8},{6,10},{8,12},{10,14},{1,5},{3,7},{5,9},{7,11},{... | collective-permute-start | bytes 200 | tf_op jit(solution)/shard_map/ppermute | solution.py:44
  66.6 10.1 %multiply_convert_fusion.7 = (bf16[1,512,1280]{2,1,0:T(8,128)(2,1)S(1)}, bf16[1,512,1280]{2,1,0:T(8,128)(2,1)S(1)}) fusion(f32[1,512,1280]{2,1,0:T(8,128)} %slice.153, f32[1,3,1280]{2,1,0:T(4,128)S(1)} %fusion.39, f32[1280]{0:T(1024)S(1)} %get-tuple-element.7, f32[1280]{0:T(1024)S(1)} %get-tuple-element.8, f32[1280]{0:T(1024)S(1)} %get-tuple-element.6, ...), kind=kLoop, calls=%fused_computation.49 | loop fusion | flops 20971520 | bytes 7920640 | tf_op jit(solution)/shard_map/convert_element_type | solution.py:98
  80.2 4.0 %reshape.701 = bf16[2,256,16,64]{3,2,1,0:T(8,128)(2,1)} reshape(bf16[1,512,1024]{2,1,0:T(8,128)(2,1)} %get-tuple-element.15) | data formatting | bytes 2097152 | tf_op jit(solution)/shard_map/reshape.42
  84.2 3.6 %copy.120 = bf16[2,256,16,64]{1,3,2,0:T(8,128)(2,1)} copy(bf16[2,256,16,64]{3,2,1,0:T(8,128)(2,1)} %reshape.701) | data formatting | bytes 2097152 | tf_op jit(solution)/shard_map/reshape.42
  87.7 2.7 %fusion.64 = f32[1,2,16,64,128]{4,3,2,1,0:T(8,128)S(1)} fusion(bf16[2,256,16,64]{1,3,2,0:T(8,128)(2,1)} %copy.120, f32[2,256,16]{1,2,0:T(8,128)} %copy.127, f32[2,256,128]{2,1,0:T(8,128)} %convert_element_type.116), kind=kOutput, calls=%fused_computation.84 | convolution fusion | flops 136314880 | bytes 2392064 | tf_op jit(solution)/shard_map/gjshp,gjshn->gjhpn/dot_general | solution.py:80
  92.5 3.4 %collective-permute-start.3 = (f32[1,16,64,128]{3,2,1,0:T(8,128)}, f32[1,16,64,128]{3,2,1,0:T(8,128)}, u32[]{:S(2)}, u32[]{:S(2)}) collective-permute-start(f32[1,16,64,128]{3,2,1,0:T(8,128)} %fusion.92), channel_id=1, source_target_pairs={{0,2},{2,4},{4,6},{6,8},{8,10},{10,12},{12,14},{1,3},{3,5},{5,7},{... | collective-permute-start | bytes 1572872 | tf_op jit(solution)/shard_map/ppermute | solution.py:44
  99.5 3.5 %copy.140 = bf16[2,256,16,64]{1,3,2,0:T(8,128)(2,1)} copy(bf16[2,256,16,64]{3,2,1,0:T(8,128)(2,1)} %reshape.702) | data formatting | bytes 2097152 | tf_op jit(solution)/shard_map/reshape.94
  103.0 2.8 %fusion.63 = f32[1,2,16,64,128]{4,3,2,1,0:T(8,128)S(1)} fusion(bf16[2,256,16,64]{1,3,2,0:T(8,128)(2,1)} %copy.140, f32[2,256,16]{1,2,0:T(8,128)} %copy.147, f32[2,256,128]{2,1,0:T(8,128)} %convert_element_type.125), kind=kOutput, calls=%fused_computation.83 | convolution fusion | flops 136314880 | bytes 2392064 | tf_op jit(solution)/shard_map/gjshp,gjshn->gjhpn/dot_general | solution.py:80
  108.6 7.2 %collective-permute-start.4 = (f32[1,16,64,128]{3,2,1,0:T(8,128)S(1)}, f32[1,16,64,128]{3,2,1,0:T(8,128)S(1)}, u32[]{:S(2)}, u32[]{:S(2)}) collective-permute-start(f32[1,16,64,128]{3,2,1,0:T(8,128)S(1)} %multiply_add_fusion.3), channel_id=1, source_target_pairs={{0,4},{2,6},{4,8},{6,10},{8,12},{10,14},{1,5},{3,7},{5,9},{7,11},{... | collective-permute-start | bytes 1572872 | tf_op jit(solution)/shard_map/ppermute | solution.py:44
  117.8 3.3 %collective-permute-done.9 = f32[1,16,64,128]{3,2,1,0:T(8,128)S(1)} collective-permute-done((f32[1,16,64,128]{3,2,1,0:T(8,128)S(1)}, f32[1,16,64,128]{3,2,1,0:T(8,128)S(1)}, u32[]{:S(2)}, u32[]{:S(2)}) %collective-permute-start.9) | collective-permute-done | bytes 524320 | tf_op jit(solution)/shard_map/ppermute | solution.py:44
  126.5 6.2 %collective-permute-start.5 = (f32[1,16,64,128]{3,2,1,0:T(8,128)}, f32[1,16,64,128]{3,2,1,0:T(8,128)}, u32[]{:S(2)}, u32[]{:S(2)}) collective-permute-start(f32[1,16,64,128]{3,2,1,0:T(8,128)} %multiply_add_fusion.2), channel_id=1, source_target_pairs={{0,8},{2,10},{4,12},{6,14},{1,9},{3,11},{5,13},{7,15},{16,24},{18,... | collective-permute-start | bytes 1572872 | tf_op jit(solution)/shard_map/ppermute | solution.py:44
  133.7 4.5 %reshape.696 = f32[1,2,256,16,64]{4,3,2,1,0:T(8,128)} reshape(f32[1,512,1024]{2,1,0:T(8,128)} %get-tuple-element.16) | data formatting | bytes 4194304 | tf_op jit(solution)/shard_map/convert_element_type | solution.py:133
  138.2 4.5 %copy.130 = f32[1,2,256,16,64]{2,4,3,1,0:T(8,128)} copy(f32[1,2,256,16,64]{4,3,2,1,0:T(8,128)} %reshape.696) | data formatting | bytes 4194304 | tf_op jit(solution)/shard_map/convert_element_type | solution.py:133
  142.8 4.5 %reshape.699 = f32[1,2,256,16,64]{4,3,2,1,0:T(8,128)} reshape(f32[1,512,1024]{2,1,0:T(8,128)} %get-tuple-element.47) | data formatting | bytes 4194304 | tf_op jit(solution)/shard_map/convert_element_type | solution.py:133
  147.3 4.6 %copy.150 = f32[1,2,256,16,64]{2,4,3,1,0:T(8,128)} copy(f32[1,2,256,16,64]{4,3,2,1,0:T(8,128)} %reshape.699) | data formatting | bytes 4194304 | tf_op jit(solution)/shard_map/convert_element_type | solution.py:133
  158.2 4.5 %fusion.50 = f32[1,2,256,16,64]{2,4,3,1,0:T(8,128)} fusion(f32[1,2,256,16,64]{2,4,3,1,0:T(8,128)S(1)} %copy-done.5, f32[2,256,16,64]{1,3,2,0:T(8,128)S(1)} %fusion.76, bf16[2,256,16,64]{1,3,2,0:T(8,128)(2,1)S(1)} %copy-done.15, f32[2,16,256]{2,1,0:T(8,128)S(1)} %copy-done.27, f32[2,256,256]{2,1,0:T(8,128)S(1)} %copy-done.18, ...), kind=kOutput, calls=%fused_computation.62 | convolution fusion | flops 283115520 | bytes 8028224 | tf_op jit(solution)/shard_map/gjhts,gjshp->gjthp/dot_general | solution.py:77
  162.7 4.9 %copy.158 = f32[1,2,256,16,64]{4,3,2,1,0:T(8,128)} copy(f32[1,2,256,16,64]{2,4,3,1,0:T(8,128)} %fusion.50) | data formatting | bytes 4194304 | tf_op jit(solution)/shard_map/reshape | solution.py:136
  167.6 4.9 %reshape.697 = f32[1,512,1024]{2,1,0:T(8,128)} reshape(f32[1,2,256,16,64]{4,3,2,1,0:T(8,128)} %copy.158) | data formatting | bytes 4194304 | tf_op jit(solution)/shard_map/reshape | solution.py:136
  172.5 3.0 %multiply_reduce_fusion.1 = f32[512]{0:T(512)S(1)} fusion(f32[1,512,1024]{2,1,0:T(8,128)} %reshape.697, f32[1,512,2304]{2,1,0:T(8,128)} %convolution_bitcast_fusion.1), kind=kLoop, calls=%fused_computation.77 | loop fusion | flops 3669504 | bytes 4196352 | tf_op jit(solution)/shard_map/reduce_sum | solution.py:140
  175.5 2.9 %collective-permute-done.11 = f32[1,16,64,128]{3,2,1,0:T(8,128)S(1)} collective-permute-done((f32[1,16,64,128]{3,2,1,0:T(8,128)S(1)}, f32[1,16,64,128]{3,2,1,0:T(8,128)S(1)}, u32[]{:S(2)}, u32[]{:S(2)}) %collective-permute-start.11) | collective-permute-done | bytes 524320 | tf_op jit(solution)/shard_map/ppermute | solution.py:44
  181.0 4.3 %fusion.49 = f32[1,2,256,16,64]{2,4,3,1,0:T(8,128)} fusion(f32[1,2,256,16,64]{2,4,3,1,0:T(8,128)S(1)} %copy-done.4, f32[2,256,16,64]{1,3,2,0:T(8,128)S(1)} %fusion.74, bf16[2,256,16,64]{1,3,2,0:T(8,128)(2,1)S(1)} %copy-done.14, f32[2,16,256]{2,1,0:T(8,128)S(1)} %copy-done.26, f32[2,256,256]{2,1,0:T(8,128)S(1)} %copy-done.17, ...), kind=kOutput, calls=%fused_computation.60 | convolution fusion | flops 283115520 | bytes 8028224 | tf_op jit(solution)/shard_map/gjhts,gjshp->gjthp/dot_general | solution.py:77
  185.3 4.9 %copy.162 = f32[1,2,256,16,64]{4,3,2,1,0:T(8,128)} copy(f32[1,2,256,16,64]{2,4,3,1,0:T(8,128)} %fusion.49) | data formatting | bytes 4194304 | tf_op jit(solution)/shard_map/reshape | solution.py:136
  190.2 4.9 %reshape.700 = f32[1,512,1024]{2,1,0:T(8,128)} reshape(f32[1,2,256,16,64]{4,3,2,1,0:T(8,128)} %copy.162) | data formatting | bytes 4194304 | tf_op jit(solution)/shard_map/reshape | solution.py:136
  195.1 2.9 %multiply_reduce_fusion = f32[512]{0:T(512)S(1)} fusion(f32[1,512,1024]{2,1,0:T(8,128)} %reshape.700, f32[1,512,2304]{2,1,0:T(8,128)} %convolution_bitcast_fusion), kind=kLoop, calls=%fused_computation.69 | loop fusion | flops 3669504 | bytes 4196352 | tf_op jit(solution)/shard_map/reduce_sum | solution.py:140
  198.0 7.2 %fusion.52 = f32[512,1024]{1,0:T(8,128)} fusion(bf16[1024,1024]{1,0:T(8,128)(2,1)S(1)} %copy-done, f32[512]{0:T(512)S(1)} %add_rsqrt_fusion, f32[1024]{0:T(1024)S(1)} %copy-done.52, f32[1,512,1024]{2,1,0:T(8,128)} %reshape.700, f32[1,512,2304]{2,1,0:T(8,128)} %convolution_bitcast_fusion), kind=kOutput, calls=%fused_computation.66 | convolution fusion | flops 3229614080 | bytes 8394752 | tf_op jit(solution)/shard_map/grk,kd->grd/dot_general | solution.py:179
  205.2 5.3 %fusion.62 = bf16[1,512,1024]{2,1,0:T(8,128)(2,1)} fusion(f32[512,1024]{1,0:T(8,128)} %fusion.52, bf16[1024,1024]{1,0:T(8,128)(2,1)S(1)} %copy-done, f32[1024]{0:T(1024)S(1)} %copy-done.52, f32[512]{0:T(512)S(1)} %add_rsqrt_fusion.1, f32[1,512,1024]{2,1,0:T(8,128)} %reshape.697, f32[1,512,2304]{2,1,0:T(8,128)} %convolution_bitcast_fusion.1), kind=kOutput, calls=%fused_computation.82 | convolution fusion | flops 1078984704 | bytes 9443328 | tf_op jit(solution)/shard_map/grk,kd->grd/dot_general | solution.py:177
  (222 shorter events, 58.7 us)
Async XLA Ops:
  0.0 198.0 %copy-start = (bf16[1024,1024]{1,0:T(8,128)(2,1)S(1)}, bf16[1024,1024]{1,0:T(8,128)(2,1)}, u32[]{:S(2)}) copy-start(bf16[1024,1024]{1,0:T(8,128)(2,1)} %param.23) | copy-start | bytes 6291460
  2.5 59.4 %collective-permute-start = (bf16[1,3,1024]{2,1,0:T(4,128)(2,1)}, bf16[1,3,1024]{2,1,0:T(4,128)(2,1)}, u32[]{:S(2)}, u32[]{:S(2)}) collective-permute-start(bf16[1,3,1024]{2,1,0:T(4,128)(2,1)} %get-tuple-element.21), channel_id=1, source_target_pairs={{0,2},{2,4},{4,6},{6,8},{8,10},{10,12},{12,14},{1,3},{3,5},{5,7},{... | collective-permute-start | bytes 18440 | tf_op jit(solution)/shard_map/ppermute | solution.py:155
  8.0 56.2 %collective-permute-start.6 = (bf16[1,3,1024]{2,1,0:T(4,128)(2,1)}, bf16[1,3,1024]{2,1,0:T(4,128)(2,1)}, u32[]{:S(2)}, u32[]{:S(2)}) collective-permute-start(bf16[1,3,1024]{2,1,0:T(4,128)(2,1)} %get-tuple-element.22), channel_id=1, source_target_pairs={{2,0},{4,2},{6,4},{8,6},{10,8},{12,10},{14,12},{3,1},{5,3},{7,5},{... | collective-permute-start | bytes 18440 | tf_op jit(solution)/shard_map/ppermute | solution.py:156
  14.1 5.7 %copy-start.29 = (f32[1,2,1,16]{3,1,2,0:T(2,128)}, f32[1,2,1,16]{3,1,2,0:T(2,128)S(1)}, u32[]{:S(2)}) copy-start(f32[1,2,1,16]{3,1,2,0:T(2,128)S(1)} %copy.124) | copy-start | bytes 388
  14.7 39.1 %collective-permute-start.1 = (f32[1,16]{1,0:T(1,128)}, f32[1,16]{1,0:T(1,128)}, u32[]{:S(2)}, u32[]{:S(2)}) collective-permute-start(f32[1,16]{1,0:T(1,128)} %get-tuple-element.31), channel_id=1, source_target_pairs={{0,2},{2,4},{4,6},{6,8},{8,10},{10,12},{12,14},{1,3},{3,5},{5,7},{... | collective-permute-start | bytes 200 | tf_op jit(solution)/shard_map/ppermute | solution.py:44
  25.9 9.0 %slice-start = ((s8[4718592]{0:T(1024)(128)(4,1)}), s8[4194304]{0:T(1024)(128)(4,1)S(1)}, s32[]{:S(2)}) async-start(s8[4718592]{0:T(1024)(128)(4,1)} %bitcast.214), calls=%async_computation | async-start | bytes 8388608
  25.9 9.0 %slice-start.1 = ((s8[4718592]{0:T(1024)(128)(4,1)}), s8[524288]{0:T(1024)(128)(4,1)S(1)}, s32[]{:S(2)}) async-start(s8[4718592]{0:T(1024)(128)(4,1)} %bitcast.214), calls=%async_computation.1 | async-start | bytes 1048576
  25.9 33.8 %collective-permute-start.7 = (f32[1,16]{1,0:T(1,128)S(1)}, f32[1,16]{1,0:T(1,128)S(1)}, u32[]{:S(2)}, u32[]{:S(2)}) collective-permute-start(f32[1,16]{1,0:T(1,128)S(1)} %get-tuple-element.36), channel_id=1, source_target_pairs={{2,0},{4,2},{6,4},{8,6},{10,8},{12,10},{14,12},{3,1},{5,3},{7,5},{... | collective-permute-start | bytes 200 | tf_op jit(solution)/shard_map/ppermute | solution.py:44
  54.4 12.2 %copy-start.41 = (f32[1,16]{1,0:T(1,128)}, f32[1,16]{1,0:T(1,128)S(1)}, u32[]{:S(2)}) copy-start(f32[1,16]{1,0:T(1,128)S(1)} %fusion.123) | copy-start | bytes 196
  54.4 6.9 %collective-permute-start.2 = (f32[1,16]{1,0:T(1,128)S(1)}, f32[1,16]{1,0:T(1,128)S(1)}, u32[]{:S(2)}, u32[]{:S(2)}) collective-permute-start(f32[1,16]{1,0:T(1,128)S(1)} %fusion.123), channel_id=1, source_target_pairs={{0,4},{2,6},{4,8},{6,10},{8,12},{10,14},{1,5},{3,7},{5,9},{7,11},{... | collective-permute-start | bytes 200 | tf_op jit(solution)/shard_map/ppermute | solution.py:44
  59.8 6.8 %copy-start.43 = (f32[1,16]{1,0:T(1,128)}, f32[1,16]{1,0:T(1,128)S(1)}, u32[]{:S(2)}) copy-start(f32[1,16]{1,0:T(1,128)S(1)} %collective-permute-done.7) | copy-start | bytes 196
  59.8 6.8 %copy-start.39 = (f32[1,16]{1,0:T(1,128)}, f32[1,16]{1,0:T(1,128)S(1)}, u32[]{:S(2)}) copy-start(f32[1,16]{1,0:T(1,128)S(1)} %fusion.125) | copy-start | bytes 196
  59.8 36.1 %collective-permute-start.8 = (f32[1,16]{1,0:T(1,128)S(1)}, f32[1,16]{1,0:T(1,128)S(1)}, u32[]{:S(2)}, u32[]{:S(2)}) collective-permute-start(f32[1,16]{1,0:T(1,128)S(1)} %fusion.125), channel_id=1, source_target_pairs={{4,0},{6,2},{8,4},{10,6},{12,8},{14,10},{5,1},{7,3},{9,5},{11,7},{... | collective-permute-start | bytes 200 | tf_op jit(solution)/shard_map/ppermute | solution.py:44
  84.2 7.3 %copy-start.32 = (f32[16]{0:T(128)S(1)}, f32[16]{0:T(128)}, u32[]{:S(2)}) copy-start(f32[16]{0:T(128)} %get-tuple-element.33) | copy-start | bytes 196
  84.2 7.3 %copy-start.34 = (f32[16]{0:T(128)S(1)}, f32[16]{0:T(128)}, u32[]{:S(2)}) copy-start(f32[16]{0:T(128)} %get-tuple-element.30) | copy-start | bytes 196
  87.7 8.2 %copy-start.44 = (f32[1,16]{1,0:T(1,128)S(1)}, f32[1,16]{1,0:T(1,128)}, u32[]{:S(2)}) copy-start(f32[1,16]{1,0:T(1,128)} %copy-done.43) | copy-start | bytes 196
  92.5 14.9 %collective-permute-start.3 = (f32[1,16,64,128]{3,2,1,0:T(8,128)}, f32[1,16,64,128]{3,2,1,0:T(8,128)}, u32[]{:S(2)}, u32[]{:S(2)}) collective-permute-start(f32[1,16,64,128]{3,2,1,0:T(8,128)} %fusion.92), channel_id=1, source_target_pairs={{0,2},{2,4},{4,6},{6,8},{8,10},{10,12},{12,14},{1,3},{3,5},{5,7},{... | collective-permute-start | bytes 1572872 | tf_op jit(solution)/shard_map/ppermute | solution.py:44
  99.5 6.4 %copy-start.31 = (f32[16]{0:T(128)S(1)}, f32[16]{0:T(128)}, u32[]{:S(2)}) copy-start(f32[16]{0:T(128)} %get-tuple-element.38) | copy-start | bytes 196
  99.5 6.4 %copy-start.35 = (f32[16]{0:T(128)S(1)}, f32[16]{0:T(128)}, u32[]{:S(2)}) copy-start(f32[16]{0:T(128)} %get-tuple-element.35) | copy-start | bytes 196
  103.0 12.8 %copy-start.13 = (bf16[1,512,128]{2,1,0:T(8,128)(2,1)S(1)}, bf16[1,512,128]{2,1,0:T(8,128)(2,1)}, u32[]{:S(2)}) copy-start(bf16[1,512,128]{2,1,0:T(8,128)(2,1)} %copy-done.12) | copy-start | bytes 393220
  105.9 15.2 %copy-start.37 = (f32[16]{0:T(128)S(1)}, f32[16]{0:T(128)}, u32[]{:S(2)}) copy-start(f32[16]{0:T(128)} %get-tuple-element.37) | copy-start | bytes 196
  106.0 15.1 %collective-permute-start.9 = (f32[1,16,64,128]{3,2,1,0:T(8,128)S(1)}, f32[1,16,64,128]{3,2,1,0:T(8,128)S(1)}, u32[]{:S(2)}, u32[]{:S(2)}) collective-permute-start(f32[1,16,64,128]{3,2,1,0:T(8,128)S(1)} %fusion.91), channel_id=1, source_target_pairs={{2,0},{4,2},{6,4},{8,6},{10,8},{12,10},{14,12},{3,1},{5,3},{7,5},{... | collective-permute-start | bytes 1572872 | tf_op jit(solution)/shard_map/ppermute | solution.py:44
  107.4 18.2 %copy-start.42 = (f32[1,16]{1,0:T(1,128)S(1)}, f32[1,16]{1,0:T(1,128)}, u32[]{:S(2)}) copy-start(f32[1,16]{1,0:T(1,128)} %copy-done.41) | copy-start | bytes 196
  108.6 16.1 %collective-permute-start.4 = (f32[1,16,64,128]{3,2,1,0:T(8,128)S(1)}, f32[1,16,64,128]{3,2,1,0:T(8,128)S(1)}, u32[]{:S(2)}, u32[]{:S(2)}) collective-permute-start(f32[1,16,64,128]{3,2,1,0:T(8,128)S(1)} %multiply_add_fusion.3), channel_id=1, source_target_pairs={{0,4},{2,6},{4,8},{6,10},{8,12},{10,14},{1,5},{3,7},{5,9},{7,11},{... | collective-permute-start | bytes 1572872 | tf_op jit(solution)/shard_map/ppermute | solution.py:44
  122.1 30.7 %collective-permute-start.10 = (f32[1,16,64,128]{3,2,1,0:T(8,128)}, f32[1,16,64,128]{3,2,1,0:T(8,128)}, u32[]{:S(2)}, u32[]{:S(2)}) collective-permute-start(f32[1,16,64,128]{3,2,1,0:T(8,128)} %multiply_add_fusion.1), channel_id=1, source_target_pairs={{4,0},{6,2},{8,4},{10,6},{12,8},{14,10},{5,1},{7,3},{9,5},{11,7},{... | collective-permute-start | bytes 1572872 | tf_op jit(solution)/shard_map/ppermute | solution.py:44
  126.5 28.9 %collective-permute-start.5 = (f32[1,16,64,128]{3,2,1,0:T(8,128)}, f32[1,16,64,128]{3,2,1,0:T(8,128)}, u32[]{:S(2)}, u32[]{:S(2)}) collective-permute-start(f32[1,16,64,128]{3,2,1,0:T(8,128)} %multiply_add_fusion.2), channel_id=1, source_target_pairs={{0,8},{2,10},{4,12},{6,14},{1,9},{3,11},{5,13},{7,15},{16,24},{18,... | collective-permute-start | bytes 1572872 | tf_op jit(solution)/shard_map/ppermute | solution.py:44
  154.1 24.3 %collective-permute-start.11 = (f32[1,16,64,128]{3,2,1,0:T(8,128)S(1)}, f32[1,16,64,128]{3,2,1,0:T(8,128)S(1)}, u32[]{:S(2)}, u32[]{:S(2)}) collective-permute-start(f32[1,16,64,128]{3,2,1,0:T(8,128)S(1)} %multiply_add_fusion), channel_id=1, source_target_pairs={{8,0},{10,2},{12,4},{14,6},{9,1},{11,3},{13,5},{15,7},{24,16},{26,... | collective-permute-start | bytes 1572872 | tf_op jit(solution)/shard_map/ppermute | solution.py:44
  172.5 5.9 %copy-start.9 = (f32[1,16,64,128]{3,2,1,0:T(8,128)S(1)}, f32[1,16,64,128]{3,2,1,0:T(8,128)}, u32[]{:S(2)}) copy-start(f32[1,16,64,128]{3,2,1,0:T(8,128)} %copy-done.8) | copy-start | bytes 1572868
  172.5 5.9 %copy-start.47 = (f32[16]{0:T(128)S(1)}, f32[16]{0:T(128)}, u32[]{:S(2)}) copy-start(f32[16]{0:T(128)} %get-tuple-element.43) | copy-start | bytes 196
  172.5 5.9 %copy-start.48 = (f32[16]{0:T(128)S(1)}, f32[16]{0:T(128)}, u32[]{:S(2)}) copy-start(f32[16]{0:T(128)} %get-tuple-element.44) | copy-start | bytes 196
  172.5 7.4 %copy-start.11 = (f32[1,1,16,64,128]{4,3,2,1,0:T(8,128)S(1)}, f32[1,1,16,64,128]{4,3,2,1,0:T(8,128)}, u32[]{:S(2)}) copy-start(f32[1,1,16,64,128]{4,3,2,1,0:T(8,128)} %slice_add_fusion) | copy-start | bytes 1572868
  172.5 7.4 %copy-start.49 = (f32[2,16]{1,0:T(2,128)S(1)}, f32[2,16]{1,0:T(2,128)}, u32[]{:S(2)}) copy-start(f32[2,16]{1,0:T(2,128)} %pad_bitcast_fusion) | copy-start | bytes 388
  (37 other events, 112.5 us)

commit v2 on v1

--- a/solution.py
+++ b/solution.py
@@ -1,6 +1,10 @@
+from functools import partial
+
 import jax
 import jax.numpy as jnp
 from jax import lax
+from jax.experimental import pallas as pl
+from jax.experimental.pallas import tpu as pltpu
 from jax.sharding import PartitionSpec as P
 
 H = 16
@@ -60,24 +64,58 @@
     return (jnp.ones_like(decay), jnp.zeros_like(state))
 
 
-def block_terms(heads_x, b_rows, c_rows, step_size, rates, reverse):
-    log_decay = lax.cumsum(step_size * rates, axis=2, reverse=reverse)
+def block_kernel(xbc_ref, cum_ref, cum_t_ref, step_t_ref, to_end_ref, inside_ref, state_ref, *, reverse):
+    inner = H * P_SIZE
+    x_all = xbc_ref[:, :inner]
+    b_rows = xbc_ref[:, inner : inner + N]
+    c_rows = xbc_ref[:, inner + N :]
+    scores = lax.dot_general(
+        c_rows, b_rows, (((1,), (1,)), ((), ())), preferred_element_type=jnp.float32
+    )
+    t_idx = lax.broadcasted_iota(jnp.int32, (Q, Q), 0)
+    s_idx = lax.broadcasted_iota(jnp.int32, (Q, Q), 1)
+    keep = (s_idx >= t_idx) if reverse else (t_idx >= s_idx)
+    b_wide = b_rows.astype(jnp.float32)
+    for h in range(H):
+        gaps = cum_ref[:, h : h + 1] - cum_t_ref[h : h + 1, :]
+        decays = jnp.where(keep, jnp.exp(jnp.where(keep, gaps, 0.0)), 0.0)
+        weights = (decays * scores * step_t_ref[h : h + 1, :]).astype(jnp.bfloat16)
+        x_h = x_all[:, h * P_SIZE : (h + 1) * P_SIZE]
+        inside_ref[:, h * P_SIZE : (h + 1) * P_SIZE] = jnp.dot(
+            weights, x_h, preferred_element_type=jnp.float32
+        )
+        state_weights = (b_wide * to_end_ref[:, h : h + 1]).astype(jnp.bfloat16)
+        state_ref[h] = lax.dot_general(
+            x_h, state_weights, (((0,), (0,)), ((), ())), preferred_element_type=jnp.float32
+        )
+
+
+def block_terms(activated, step_size, rates, reverse):
+    count, rows, width = activated.shape
+    spans = rows // Q
+    blocks = count * spans
+    steps_cut = step_size.reshape(count, spans, Q, H)
+    log_decay = lax.cumsum(steps_cut * rates, axis=2, reverse=reverse)
     end = log_decay[:, :, 0] if reverse else log_decay[:, :, -1]
-    across = jnp.swapaxes(log_decay, 2, 3)
-    width = across.shape[-1]
-    t_idx = jnp.arange(width)[:, None]
-    s_idx = jnp.arange(width)[None, :]
-    keep = (s_idx >= t_idx) if reverse else (t_idx >= s_idx)
-    gaps = across[..., :, None] - across[..., None, :]
-    decays = jnp.where(keep, jnp.exp(jnp.where(keep, gaps, 0.0)), 0.0)
-    scores = jnp.einsum("gjtn,gjsn->gjts", c_rows, b_rows, preferred_element_type=jnp.float32)
-    weights = (decays * scores[:, :, None] * jnp.swapaxes(step_size, 2, 3)[:, :, :, None, :]).astype(
-        jnp.bfloat16
-    )
-    inside = jnp.einsum("gjhts,gjshp->gjthp", weights, heads_x, preferred_element_type=jnp.float32)
-    to_end = jnp.exp(end[:, :, None, :] - log_decay) * step_size
-    state_weights = (b_rows.astype(jnp.float32)[..., None, :] * to_end[..., None]).astype(jnp.bfloat16)
-    state = jnp.einsum("gjshp,gjshn->gjhpn", heads_x, state_weights, preferred_element_type=jnp.float32)
+    to_end = jnp.exp(end[:, :, None, :] - log_decay) * steps_cut
+    flat = lambda a: a.reshape((blocks,) + a.shape[2:])
+    cum = flat(log_decay)
+    cum_t = jnp.swapaxes(cum, 1, 2)
+    step_t = jnp.swapaxes(flat(steps_cut), 1, 2)
+    xbc = activated.reshape(blocks, Q, width)
+    spec = lambda shape: pl.BlockSpec((None,) + shape, lambda i: (i,) + (0,) * len(shape))
+    inside, state = pl.pallas_call(
+        partial(block_kernel, reverse=reverse),
+        grid=(blocks,),
+        in_specs=[spec((Q, width)), spec((Q, H)), spec((H, Q)), spec((H, Q)), spec((Q, H))],
+        out_specs=[spec((Q, H * P_SIZE)), spec((H, P_SIZE, N))],
+        out_shape=[
+            jax.ShapeDtypeStruct((blocks, Q, H * P_SIZE), jnp.float32),
+            jax.ShapeDtypeStruct((blocks, H, P_SIZE, N), jnp.float32),
+        ],
+    )(xbc, cum, cum_t, step_t, flat(to_end))
+    inside = inside.reshape(count, rows, H * P_SIZE)
+    state = state.reshape(count, spans, H, P_SIZE, N)
     return inside, state, jnp.exp(end), jnp.exp(log_decay)
 
 
@@ -97,13 +135,7 @@
         summed = summed + conv_w[tap] * padded[:, start : start + rows]
     activated = jax.nn.silu(summed).astype(jnp.bfloat16)
     spans = rows // Q
-    heads_x = activated[:, :, :inner].reshape(count, spans, Q, H, P_SIZE)
-    b_rows = activated[:, :, inner : inner + N].reshape(count, spans, Q, N)
-    c_rows = activated[:, :, inner + N :].reshape(count, spans, Q, N)
-    steps_cut = step_size.reshape(count, spans, Q, H)
-    inside, state, total, from_start = block_terms(
-        heads_x, b_rows, c_rows, steps_cut, rates, reverse
-    )
+    inside, state, total, from_start = block_terms(activated, step_size, rates, reverse)
     order = list(range(spans))
     if reverse:
         order = order[::-1]
@@ -114,27 +146,27 @@
         sofar = chain(sofar, (total[:, j], state[:, j]))
     before_decay = jnp.stack([before[j][0] for j in range(spans)], axis=1)
     before_state = jnp.stack([before[j][1] for j in range(spans)], axis=1)
-    pending = (before_decay, before_state, inside, from_start, heads_x, c_rows)
+    pending = (before_decay, before_state, inside, from_start, activated)
     return sofar, pending
 
 
 def finish(pending, incoming, gate_part, d_skip, norm_gain):
-    before_decay, before_state, inside, from_start, heads_x, c_rows = pending
+    before_decay, before_state, inside, from_start, activated = pending
+    inner = H * P_SIZE
+    count, rows, _ = activated.shape
+    spans = rows // Q
     start_state = before_state + before_decay[..., None, None] * incoming[:, None]
+    c_rows = activated[:, :, inner + N :].reshape(count, spans, Q, N)
     carried = jnp.einsum(
-        "gjtn,gjhpn->gjthp",
+        "gjtn,gjkn->gjtk",
         c_rows.astype(jnp.float32),
-        start_state,
+        start_state.reshape(count, spans, inner, N),
         precision=lax.Precision.HIGHEST,
-    )
-    scanned = (
-        inside
-        + from_start[..., None] * carried
-        + d_skip[:, None] * heads_x.astype(jnp.float32)
-    )
-    count = scanned.shape[0]
-    flat = scanned.reshape(count, -1, H * P_SIZE)
-    gated = flat * jax.nn.silu(gate_part)
+    ).reshape(count, rows, inner)
+    scale = jnp.repeat(from_start.reshape(count, rows, H), P_SIZE, axis=-1)
+    skip = jnp.repeat(d_skip, P_SIZE)
+    scanned = inside + scale * carried + skip * activated[:, :, :inner].astype(jnp.float32)
+    gated = scanned * jax.nn.silu(gate_part)
     return (
         gated
         * lax.rsqrt(jnp.mean(gated * gated, axis=-1, keepdims=True) + norm_epsilon)

time: 212 us -> 193 us (0.910)
  the two profiles are of different devices: /device:TPU:0 before, /device:TPU:24 now
where the time goes in v2:
time: 193 us; the launch traced here: 192 us
  other arithmetic  38.4 us (20%)
  starting transfers between devices  34.8 us (18%)
  matrix products  34.5 us (18%)
  waiting for transfers between devices  33.4 us (17%)
  local copies, waits for them, and re-layouts  30.4 us (16%)
  Pallas kernels  19.8 us (10%)
    ppermute x10, waiting for transfers between devices, exclusive_scans(): decay, state = lax.ppermute(ahead[k], axis, pairs)  33.4 us
    ppermute x10, starting transfers between devices, exclusive_scans(): decay, state = lax.ppermute(ahead[k], axis, pairs)  27.9 us
    pallas_call x2, Pallas kernels, block_terms(): pl.pallas_call(partial(block_kernel, reverse=reverse), grid=(blocks,), in...  19.8 us
    convert_element_type x1, other arithmetic, strand_terms(): activated = jax.nn.silu(summed).astype(jnp.bfloat16)  11.4 us
    broadcast_in_dim x4, local copies, waits for them, and re-layouts, finish(): scale = jnp.repeat(from_start.reshape(count, rows, H), P_SIZE, axis=-1)  8.98 us
    dot_general x1, matrix products, on_device(): jnp.einsum('grd,de->gre', mirrored, w_in, preferred_element_type=jnp.floa...  7.52 us
    slice x2, local copies, waits for them, and re-layouts, strand_terms(): source = projected[:, :, inner:]  6.95 us
    dot_general x1, matrix products, on_device(): jnp.einsum('grk,kd->grd', normed_r, w_out_mirrored, preferred_element_typ...  6.38 us
  transfers between devices with their start and end apart: 12, of which 5 were waited for; matrix products, arithmetic and copies ran while one was open for 42% of the time, Pallas kernels for 10%

profile of v2, /device:TPU:24, one launch (start us, length us, event | category | flops | bytes accessed | tf_op | source)
XLA Modules:
  0.0 191.9 jit_solution(7771311409738184415)
XLA Ops:
  0.0 1.9 fusion.39
  2.5 3.4 %collective-permute-start = (bf16[1,3,1024]{2,1,0:T(4,128)(2,1)}, bf16[1,3,1024]{2,1,0:T(4,128)(2,1)}, u32[]{:S(2)}, u32[]{:S(2)}) collective-permute-start(bf16[1,3,1024]{2,1,0:T(4,128)(2,1)} %get-tuple-element.25), channel_id=1, source_target_pairs={{0,2},{2,4},{4,6},{6,8},{8,10},{10,12},{12,14},{1,3},{3,5},{5,7},{... | collective-permute-start | bytes 18440 | tf_op jit(solution)/shard_map/ppermute | solution.py:187
  5.9 3.5 %collective-permute-start.6 = (bf16[1,3,1024]{2,1,0:T(4,128)(2,1)S(1)}, bf16[1,3,1024]{2,1,0:T(4,128)(2,1)}, u32[]{:S(2)}, u32[]{:S(2)}) collective-permute-start(bf16[1,3,1024]{2,1,0:T(4,128)(2,1)S(1)} %get-tuple-element.26), channel_id=1, source_target_pairs={{2,0},{4,2},{6,4},{8,6},{10,8},{12,10},{14,12},{3,1},{5,3},{7,5},{... | collective-permute-start | bytes 18440 | tf_op jit(solution)/shard_map/ppermute | solution.py:188
  9.4 2.2 %fusion.45 = bf16[512,1024]{1,0:T(8,128)(2,1)} fusion(bf16[1,512,1024]{2,1,0:T(8,128)(2,1)S(1)} %fusion.39), kind=kOutput, calls=%fused_computation.59 | convolution fusion | flops 1076363264 | bytes 2097152 | tf_op jit(solution)/shard_map/...d,de->...e/dot_general | solution.py:28
  12.2 1.7 compare_select_fusion
  14.8 1.8 broadcast_multiply_fusion.1
  17.6 5.0 %reduce-window.16 = f32[1,2,16,2,128]{4,2,3,1,0:T(8,128)S(1)} reduce-window(f32[1,2,16,2,128]{4,2,3,1,0:T(8,128)S(1)} %copy.29, f32[]{:T(128)} %constant.13.clone.1), window={size=1x1x1x1x128 pad=0_0x0_0x0_0x0_0x0_127}, to_apply=%region_3.4 | reduce-window | flops 1040384 | bytes 65540 | tf_op jit(solution)/shard_map/reduce-window.2
  27.1 2.4 %collective-permute-start.7 = (f32[1,16]{1,0:T(1,128)}, f32[1,16]{1,0:T(1,128)}, u32[]{:S(2)}, u32[]{:S(2)}) collective-permute-start(f32[1,16]{1,0:T(1,128)} %get-tuple-element.42), channel_id=1, source_target_pairs={{2,0},{4,2},{6,4},{8,6},{10,8},{12,10},{14,12},{3,1},{5,3},{7,5},{... | collective-permute-start | bytes 200 | tf_op jit(solution)/shard_map/ppermute | solution.py:48
  32.7 1.9 bitcast_exponential_fusion.1
  34.6 4.2 %collective-permute-start.1 = (f32[1,16]{1,0:T(1,128)S(1)}, f32[1,16]{1,0:T(1,128)S(1)}, u32[]{:S(2)}, u32[]{:S(2)}) collective-permute-start(f32[1,16]{1,0:T(1,128)S(1)} %get-tuple-element.37), channel_id=1, source_target_pairs={{0,2},{2,4},{4,6},{6,8},{8,10},{10,12},{12,14},{1,3},{3,5},{5,7},{... | collective-permute-start | bytes 200 | tf_op jit(solution)/shard_map/ppermute | solution.py:48
  38.8 7.5 %convolution_bitcast_fusion = f32[1,512,2304]{2,1,0:T(8,128)} fusion(bf16[512,1024]{1,0:T(8,128)(2,1)} %fusion.45, bf16[1024,2304]{1,0:T(8,128)(2,1)} %param.15), kind=kOutput, calls=%fused_computation | convolution fusion | flops 2415919104 | bytes 10485760 | tf_op jit(solution)/shard_map/grd,de->gre/dot_general | solution.py:193
  46.4 4.3 %convolution_bitcast_fusion.1 = f32[1,512,2304]{2,1,0:T(8,128)} fusion(bf16[1024,2304]{1,0:T(8,128)(2,1)S(1)} %bitcast.239, bf16[1,512,1024]{2,1,0:T(8,128)(2,1)S(1)} %fusion.39), kind=kOutput, calls=%fused_computation.1 | convolution fusion | flops 2415919104 | bytes 10485760 | tf_op jit(solution)/shard_map/grd,de->gre/dot_general | solution.py:192
  59.8 2.9 %copy.27 = f32[1,512,1024]{2,1,0:T(8,128)} copy(f32[1,512,1024]{1,2,0:T(8,128)} %bitcast.214) | data formatting | bytes 4194304 | tf_op jit(solution)/shard_map/broadcast_in_dim | solution.py:166
  64.2 2.9 %copy.34 = f32[1,512,1024]{2,1,0:T(8,128)} copy(f32[1,512,1024]{1,2,0:T(8,128)} %bitcast.215) | data formatting | bytes 4194304 | tf_op jit(solution)/shard_map/broadcast_in_dim | solution.py:166
  67.2 3.6 %slice.158 = f32[1,512,1280]{2,1,0:T(8,128)} slice(f32[1,512,2304]{2,1,0:T(8,128)} %convolution_bitcast_fusion), slice={[0:1], [0:512], [1024:2304]} | slice | bytes 5242880 | tf_op jit(solution)/shard_map/slice | solution.py:126
  70.8 3.4 %slice.145 = f32[1,512,1280]{2,1,0:T(8,128)} slice(f32[1,512,2304]{2,1,0:T(8,128)} %convolution_bitcast_fusion.1), slice={[0:1], [0:512], [1024:2304]} | slice | bytes 5242880 | tf_op jit(solution)/shard_map/slice | solution.py:126
  75.3 2.4 %fusion.28 = f32[1,3,1280]{2,1,0:T(4,128)S(1)} fusion(bf16[1024,2304]{1,0:T(8,128)(2,1)} %param.15, bf16[1,3,1024]{2,1,0:T(4,128)(2,1)} %collective-permute-done.6), kind=kOutput, calls=%fused_computation.37 | convolution fusion | flops 16256000 | bytes 2644992 | tf_op jit(solution)/shard_map/grd,de->gre/dot_general | solution.py:195
  77.7 11.4 %multiply_convert_fusion.1 = (bf16[1,512,1280]{2,1,0:T(8,128)(2,1)}, bf16[1,512,1280]{2,1,0:T(8,128)(2,1)}) fusion(f32[1,512,1280]{2,1,0:T(8,128)} %slice.145, f32[1,3,1280]{2,1,0:T(4,128)S(1)} %fusion.25, f32[1280]{0:T(1024)S(1)} %get-tuple-element.15, f32[1280]{0:T(1024)S(1)} %get-tuple-element.16, f32[1280]{0:T(1024)S(1)} %get-tuple-element.14, ...), kind=kLoop, calls=%fused_computation.31 | loop fusion | flops 20971520 | bytes 7920640 | tf_op jit(solution)/shard_map/convert_element_type | solution.py:136
  89.1 9.9 %shard_map.119 = (f32[2,256,1024]{2,1,0:T(8,128)}, f32[2,16,64,128]{3,2,1,0:T(8,128)}) custom-call(bf16[2,256,1280]{2,1,0:T(8,128)(2,1)} %bitcast.213, f32[2,256,16]{2,1,0:T(8,128)} %bitcast.229, f32[2,16,256]{2,1,0:T(8,128)} %copy.32.cum_t_ref, f32[2,16,256]{2,1,0:T(8,128)} %bitcast.251, f32[2,256,16]{2,1,0:T(8,128)} %multiply_bitcast_fusion.to_end_ref), custom_call_target="tpu_custom_call" | custom-call | tf_op jit(solution)/shard_map/pallas_call | solution.py:107
  99.0 2.2 %fusion.63 = f32[1,16,64,128]{3,2,1,0:T(8,128)} fusion(f32[1,2,16,64,128]{4,3,2,1,0:T(8,128)} %bitcast.218, f32[16]{0:T(128)S(1)} %get-tuple-element.44, f32[16]{0:T(128)S(1)} %get-tuple-element.41), kind=kLoop, calls=%fused_computation.76 | loop fusion | flops 393216 | bytes 1572992 | tf_op jit(solution)/shard_map/add | solution.py:34
  101.2 2.7 %collective-permute-start.9 = (f32[1,16,64,128]{3,2,1,0:T(8,128)}, f32[1,16,64,128]{3,2,1,0:T(8,128)}, u32[]{:S(2)}, u32[]{:S(2)}) collective-permute-start(f32[1,16,64,128]{3,2,1,0:T(8,128)} %fusion.63), channel_id=1, source_target_pairs={{2,0},{4,2},{6,4},{8,6},{10,8},{12,10},{14,12},{3,1},{5,3},{7,5},{... | collective-permute-start | bytes 1572872 | tf_op jit(solution)/shard_map/ppermute | solution.py:48
  104.7 2.3 %collective-permute-start.8 = (f32[1,16]{1,0:T(1,128)S(1)}, f32[1,16]{1,0:T(1,128)S(1)}, u32[]{:S(2)}, u32[]{:S(2)}) collective-permute-start(f32[1,16]{1,0:T(1,128)S(1)} %fusion.85), channel_id=1, source_target_pairs={{4,0},{6,2},{8,4},{10,6},{12,8},{14,10},{5,1},{7,3},{9,5},{11,7},{... | collective-permute-start | bytes 200 | tf_op jit(solution)/shard_map/ppermute | solution.py:48
  108.6 9.9 %shard_map.118 = (f32[2,256,1024]{2,1,0:T(8,128)}, f32[2,16,64,128]{3,2,1,0:T(8,128)}) custom-call(bf16[2,256,1280]{2,1,0:T(8,128)(2,1)} %bitcast.212, f32[2,256,16]{2,1,0:T(8,128)} %bitcast.226, f32[2,16,256]{2,1,0:T(8,128)} %copy.25.cum_t_ref, f32[2,16,256]{2,1,0:T(8,128)} %bitcast.250, f32[2,256,16]{2,1,0:T(8,128)} %multiply_bitcast_fusion.1.to_end_ref), custom_call_target="tpu_custom_call" | custom-call | tf_op jit(solution)/shard_map/pallas_call | solution.py:107
  119.9 2.8 %collective-permute-start.3 = (f32[1,16,64,128]{3,2,1,0:T(8,128)S(1)}, f32[1,16,64,128]{3,2,1,0:T(8,128)S(1)}, u32[]{:S(2)}, u32[]{:S(2)}) collective-permute-start(f32[1,16,64,128]{3,2,1,0:T(8,128)S(1)} %fusion.64), channel_id=1, source_target_pairs={{0,2},{2,4},{4,6},{6,8},{8,10},{10,12},{12,14},{1,3},{3,5},{5,7},{... | collective-permute-start | bytes 1572872 | tf_op jit(solution)/shard_map/ppermute | solution.py:48
  123.9 4.7 %collective-permute-start.10 = (f32[1,16,64,128]{3,2,1,0:T(8,128)S(1)}, f32[1,16,64,128]{3,2,1,0:T(8,128)S(1)}, u32[]{:S(2)}, u32[]{:S(2)}) collective-permute-start(f32[1,16,64,128]{3,2,1,0:T(8,128)S(1)} %multiply_add_fusion.3), channel_id=1, source_target_pairs={{4,0},{6,2},{8,4},{10,6},{12,8},{14,10},{5,1},{7,3},{9,5},{11,7},{... | collective-permute-start | bytes 1572872 | tf_op jit(solution)/shard_map/ppermute | solution.py:48
  129.3 5.6 %collective-permute-done.3 = f32[1,16,64,128]{3,2,1,0:T(8,128)S(1)} collective-permute-done((f32[1,16,64,128]{3,2,1,0:T(8,128)S(1)}, f32[1,16,64,128]{3,2,1,0:T(8,128)S(1)}, u32[]{:S(2)}, u32[]{:S(2)}) %collective-permute-start.3) | collective-permute-done | bytes 524320 | tf_op jit(solution)/shard_map/ppermute | solution.py:48
  138.0 4.7 %collective-permute-start.11 = (f32[1,16,64,128]{3,2,1,0:T(8,128)S(1)}, f32[1,16,64,128]{3,2,1,0:T(8,128)S(1)}, u32[]{:S(2)}, u32[]{:S(2)}) collective-permute-start(f32[1,16,64,128]{3,2,1,0:T(8,128)S(1)} %multiply_add_fusion.2), channel_id=1, source_target_pairs={{8,0},{10,2},{12,4},{14,6},{9,1},{11,3},{13,5},{15,7},{24,16},{26,... | collective-permute-start | bytes 1572872 | tf_op jit(solution)/shard_map/ppermute | solution.py:48
  143.0 5.5 %collective-permute-done.4 = f32[1,16,64,128]{3,2,1,0:T(8,128)S(1)} collective-permute-done((f32[1,16,64,128]{3,2,1,0:T(8,128)S(1)}, f32[1,16,64,128]{3,2,1,0:T(8,128)S(1)}, u32[]{:S(2)}, u32[]{:S(2)}) %collective-permute-start.4) | collective-permute-done | bytes 524320 | tf_op jit(solution)/shard_map/ppermute | solution.py:48
  153.2 20.0 %collective-permute-done.5 = f32[1,16,64,128]{3,2,1,0:T(8,128)S(1)} collective-permute-done((f32[1,16,64,128]{3,2,1,0:T(8,128)S(1)}, f32[1,16,64,128]{3,2,1,0:T(8,128)S(1)}, u32[]{:S(2)}, u32[]{:S(2)}) %collective-permute-start.5) | collective-permute-done | bytes 524320 | tf_op jit(solution)/shard_map/ppermute | solution.py:48
  176.1 4.9 %multiply_reduce_fusion.1 = (f32[512]{0:T(512)S(1)}, f32[1,512,1024]{2,1,0:T(8,128)}, f32[512]{0:T(512)S(1)}, f32[1,512,1024]{2,1,0:T(8,128)}) fusion(f32[1,512,2304]{2,1,0:T(8,128)} %convolution_bitcast_fusion.1, bf16[1,512,1280]{2,1,0:T(8,128)(2,1)S(1)} %copy-done.1, f32[1024]{0:T(1024)S(1)} %mul.480, f32[1,512,1024]{2,1,0:T(8,128)S(1)} %copy-done.3, ...), kind=kLoop, calls=%fused_computation.58 | loop fusion | flops 12581888 | bytes 23076864 | tf_op jit(solution)/shard_map/reduce_sum | solution.py:172
  181.0 6.4 %fusion.40 = f32[512,1024]{1,0:T(8,128)} fusion(bf16[1024,1024]{1,0:T(8,128)(2,1)S(1)} %copy-done, f32[1,512,1024]{2,1,0:T(8,128)} %get-tuple-element.34, f32[512]{0:T(512)S(1)} %get-tuple-element.51, f32[1024]{0:T(1024)S(1)} %copy-done.22), kind=kOutput, calls=%fused_computation.50 | convolution fusion | flops 3226992640 | bytes 6297600 | tf_op jit(solution)/shard_map/grk,kd->grd/dot_general | solution.py:211
  187.4 4.5 %fusion.46 = bf16[1,512,1024]{2,1,0:T(8,128)(2,1)} fusion(f32[512,1024]{1,0:T(8,128)} %fusion.40, bf16[1024,1024]{1,0:T(8,128)(2,1)S(1)} %copy-done, f32[1,512,1024]{2,1,0:T(8,128)} %get-tuple-element.18, f32[1024]{0:T(1024)S(1)} %copy-done.22, f32[512]{0:T(512)S(1)} %get-tuple-element.52), kind=kOutput, calls=%fused_computation.60 | convolution fusion | flops 1076363264 | bytes 7346176 | tf_op jit(solution)/shard_map/grk,kd->grd/dot_general | solution.py:209
  (129 shorter events, 38.8 us)
Async XLA Ops:
  0.0 181.0 %copy-start = (bf16[1024,1024]{1,0:T(8,128)(2,1)S(1)}, bf16[1024,1024]{1,0:T(8,128)(2,1)}, u32[]{:S(2)}) copy-start(bf16[1024,1024]{1,0:T(8,128)(2,1)} %param.23) | copy-start | bytes 6291460
  2.5 71.6 %collective-permute-start = (bf16[1,3,1024]{2,1,0:T(4,128)(2,1)}, bf16[1,3,1024]{2,1,0:T(4,128)(2,1)}, u32[]{:S(2)}, u32[]{:S(2)}) collective-permute-start(bf16[1,3,1024]{2,1,0:T(4,128)(2,1)} %get-tuple-element.25), channel_id=1, source_target_pairs={{0,2},{2,4},{4,6},{6,8},{8,10},{10,12},{12,14},{1,3},{3,5},{5,7},{... | collective-permute-start | bytes 18440 | tf_op jit(solution)/shard_map/ppermute | solution.py:187
  5.9 5.7 %copy-start.23 = (f32[16]{0:T(128)S(1)}, f32[16]{0:T(128)}, u32[]{:S(2)}) copy-start(f32[16]{0:T(128)} %param.20) | copy-start | bytes 196
  5.9 5.7 %copy-start.15 = (bf16[1024,16]{0,1:T(8,128)(2,1)S(1)}, bf16[1024,16]{0,1:T(8,128)(2,1)}, u32[]{:S(2)}) copy-start(bf16[1024,16]{0,1:T(8,128)(2,1)} %param.16) | copy-start | bytes 98308
  5.9 5.7 %copy-start.19 = (f32[16]{0:T(128)S(1)}, f32[16]{0:T(128)}, u32[]{:S(2)}) copy-start(f32[16]{0:T(128)} %param.19) | copy-start | bytes 196
  5.9 69.4 %collective-permute-start.6 = (bf16[1,3,1024]{2,1,0:T(4,128)(2,1)S(1)}, bf16[1,3,1024]{2,1,0:T(4,128)(2,1)}, u32[]{:S(2)}, u32[]{:S(2)}) collective-permute-start(bf16[1,3,1024]{2,1,0:T(4,128)(2,1)S(1)} %get-tuple-element.26), channel_id=1, source_target_pairs={{2,0},{4,2},{6,4},{8,6},{10,8},{12,10},{14,12},{3,1},{5,3},{7,5},{... | collective-permute-start | bytes 18440 | tf_op jit(solution)/shard_map/ppermute | solution.py:188
  12.2 20.5 %copy-start.10 = (f32[512,16]{1,0:T(8,128)}, f32[512,16]{1,0:T(8,128)S(1)}, u32[]{:S(2)}) copy-start(f32[512,16]{1,0:T(8,128)S(1)} %copy.21) | copy-start | bytes 98308
  27.1 76.9 %collective-permute-start.7 = (f32[1,16]{1,0:T(1,128)}, f32[1,16]{1,0:T(1,128)}, u32[]{:S(2)}, u32[]{:S(2)}) collective-permute-start(f32[1,16]{1,0:T(1,128)} %get-tuple-element.42), channel_id=1, source_target_pairs={{2,0},{4,2},{6,4},{8,6},{10,8},{12,10},{14,12},{3,1},{5,3},{7,5},{... | collective-permute-start | bytes 200 | tf_op jit(solution)/shard_map/ppermute | solution.py:48
  32.7 13.6 %slice-start = ((s8[4718592]{0:T(1024)(128)(4,1)}), s8[4194304]{0:T(1024)(128)(4,1)S(1)}, s32[]{:S(2)}) async-start(s8[4718592]{0:T(1024)(128)(4,1)} %bitcast.238), calls=%async_computation | async-start | bytes 8388608
  34.5 22.9 %copy-start.7 = (f32[1,2,16,256]{2,3,1,0:T(8,128)}, f32[1,2,16,256]{2,3,1,0:T(8,128)S(1)}, u32[]{:S(2)}) copy-start(f32[1,2,16,256]{2,3,1,0:T(8,128)S(1)} %get-tuple-element.20) | copy-start | bytes 98308
  34.6 72.5 %collective-permute-start.1 = (f32[1,16]{1,0:T(1,128)S(1)}, f32[1,16]{1,0:T(1,128)S(1)}, u32[]{:S(2)}, u32[]{:S(2)}) collective-permute-start(f32[1,16]{1,0:T(1,128)S(1)} %get-tuple-element.37), channel_id=1, source_target_pairs={{0,2},{2,4},{4,6},{6,8},{8,10},{10,12},{12,14},{1,3},{3,5},{5,7},{... | collective-permute-start | bytes 200 | tf_op jit(solution)/shard_map/ppermute | solution.py:48
  38.8 7.5 %slice-start.1 = ((s8[4718592]{0:T(1024)(128)(4,1)}), s8[524288]{0:T(1024)(128)(4,1)S(1)}, s32[]{:S(2)}) async-start(s8[4718592]{0:T(1024)(128)(4,1)} %bitcast.238), calls=%async_computation.1 | async-start | bytes 1048576
  46.3 4.4 %copy-start.9 = (f32[1,2,16,256]{2,3,1,0:T(8,128)S(1)}, f32[1,2,16,256]{2,3,1,0:T(8,128)}, u32[]{:S(2)}) copy-start(f32[1,2,16,256]{2,3,1,0:T(8,128)} %copy-done.8) | copy-start | bytes 98308
  46.4 5.2 %copy-start.21 = (f32[1,1,16]{2,1,0:T(1,128)S(1)}, f32[1,1,16]{2,1,0:T(1,128)}, u32[]{:S(2)}) copy-start(f32[1,1,16]{2,1,0:T(1,128)} %get-tuple-element.40) | copy-start | bytes 196
  46.4 5.2 %copy-start.11 = (f32[512,16]{1,0:T(8,128)S(1)}, f32[512,16]{1,0:T(8,128)}, u32[]{:S(2)}) copy-start(f32[512,16]{1,0:T(8,128)} %copy-done.10) | copy-start | bytes 98308
  46.4 5.9 %copy-start.20 = (f32[16]{0:T(128)S(1)}, f32[16]{0:T(128)}, u32[]{:S(2)}) copy-start(f32[16]{0:T(128)} %param.21) | copy-start | bytes 196
  64.2 9.9 %slice-start.2 = ((s8[4718592]{0:T(1024)(128)(4,1)}), s8[524288]{0:T(1024)(128)(4,1)S(1)}, s32[]{:S(2)}) async-start(s8[4718592]{0:T(1024)(128)(4,1)} %bitcast.240), calls=%async_computation.2 | async-start | bytes 1048576
  67.2 7.0 %slice-start.3 = ((s8[4718592]{0:T(1024)(128)(4,1)}), s8[4194304]{0:T(1024)(128)(4,1)S(1)}, s32[]{:S(2)}) async-start(s8[4718592]{0:T(1024)(128)(4,1)} %bitcast.240), calls=%async_computation.3 | async-start | bytes 8388608
  99.0 23.7 %copy-start.5 = (f32[2,16,64,128]{3,2,1,0:T(8,128)S(1)}, f32[2,16,64,128]{3,2,1,0:T(8,128)}, u32[]{:S(2)}) copy-start(f32[2,16,64,128]{3,2,1,0:T(8,128)} %get-tuple-element.12) | copy-start | bytes 3145732
  101.2 21.4 %collective-permute-start.9 = (f32[1,16,64,128]{3,2,1,0:T(8,128)}, f32[1,16,64,128]{3,2,1,0:T(8,128)}, u32[]{:S(2)}, u32[]{:S(2)}) collective-permute-start(f32[1,16,64,128]{3,2,1,0:T(8,128)} %fusion.63), channel_id=1, source_target_pairs={{2,0},{4,2},{6,4},{8,6},{10,8},{12,10},{14,12},{3,1},{5,3},{7,5},{... | collective-permute-start | bytes 1572872 | tf_op jit(solution)/shard_map/ppermute | solution.py:48
  104.7 24.0 %collective-permute-start.8 = (f32[1,16]{1,0:T(1,128)S(1)}, f32[1,16]{1,0:T(1,128)S(1)}, u32[]{:S(2)}, u32[]{:S(2)}) collective-permute-start(f32[1,16]{1,0:T(1,128)S(1)} %fusion.85), channel_id=1, source_target_pairs={{4,0},{6,2},{8,4},{10,6},{12,8},{14,10},{5,1},{7,3},{9,5},{11,7},{... | collective-permute-start | bytes 200 | tf_op jit(solution)/shard_map/ppermute | solution.py:48
  107.0 22.3 %collective-permute-start.2 = (f32[1,16]{1,0:T(1,128)S(1)}, f32[1,16]{1,0:T(1,128)S(1)}, u32[]{:S(2)}, u32[]{:S(2)}) collective-permute-start(f32[1,16]{1,0:T(1,128)S(1)} %fusion.83), channel_id=1, source_target_pairs={{0,4},{2,6},{4,8},{6,10},{8,12},{10,14},{1,5},{3,7},{5,9},{7,11},{... | collective-permute-start | bytes 200 | tf_op jit(solution)/shard_map/ppermute | solution.py:48
  118.5 16.5 %copy-start.6 = (f32[2,16,64,128]{3,2,1,0:T(8,128)S(1)}, f32[2,16,64,128]{3,2,1,0:T(8,128)}, u32[]{:S(2)}) copy-start(f32[2,16,64,128]{3,2,1,0:T(8,128)} %get-tuple-element.10) | copy-start | bytes 3145732
  119.9 15.1 %collective-permute-start.3 = (f32[1,16,64,128]{3,2,1,0:T(8,128)S(1)}, f32[1,16,64,128]{3,2,1,0:T(8,128)S(1)}, u32[]{:S(2)}, u32[]{:S(2)}) collective-permute-start(f32[1,16,64,128]{3,2,1,0:T(8,128)S(1)} %fusion.64), channel_id=1, source_target_pairs={{0,2},{2,4},{4,6},{6,8},{8,10},{10,12},{12,14},{1,3},{3,5},{5,7},{... | collective-permute-start | bytes 1572872 | tf_op jit(solution)/shard_map/ppermute | solution.py:48
  123.9 18.9 %copy-start.1 = (bf16[1,512,1280]{2,1,0:T(8,128)(2,1)S(1)}, bf16[1,512,1280]{2,1,0:T(8,128)(2,1)}, u32[]{:S(2)}) copy-start(bf16[1,512,1280]{2,1,0:T(8,128)(2,1)} %get-tuple-element.31) | copy-start | bytes 3932164
  123.9 18.9 %copy-start.2 = (bf16[1,512,1280]{2,1,0:T(8,128)(2,1)S(1)}, bf16[1,512,1280]{2,1,0:T(8,128)(2,1)}, u32[]{:S(2)}) copy-start(bf16[1,512,1280]{2,1,0:T(8,128)(2,1)} %get-tuple-element.32) | copy-start | bytes 3932164
  123.9 13.9 %collective-permute-start.10 = (f32[1,16,64,128]{3,2,1,0:T(8,128)S(1)}, f32[1,16,64,128]{3,2,1,0:T(8,128)S(1)}, u32[]{:S(2)}, u32[]{:S(2)}) collective-permute-start(f32[1,16,64,128]{3,2,1,0:T(8,128)S(1)} %multiply_add_fusion.3), channel_id=1, source_target_pairs={{4,0},{6,2},{8,4},{10,6},{12,8},{14,10},{5,1},{7,3},{9,5},{11,7},{... | collective-permute-start | bytes 1572872 | tf_op jit(solution)/shard_map/ppermute | solution.py:48
  135.2 13.3 %collective-permute-start.4 = (f32[1,16,64,128]{3,2,1,0:T(8,128)S(1)}, f32[1,16,64,128]{3,2,1,0:T(8,128)S(1)}, u32[]{:S(2)}, u32[]{:S(2)}) collective-permute-start(f32[1,16,64,128]{3,2,1,0:T(8,128)S(1)} %multiply_add_fusion.5), channel_id=1, source_target_pairs={{0,4},{2,6},{4,8},{6,10},{8,12},{10,14},{1,5},{3,7},{5,9},{7,11},{... | collective-permute-start | bytes 1572872 | tf_op jit(solution)/shard_map/ppermute | solution.py:48
  138.0 12.8 %collective-permute-start.11 = (f32[1,16,64,128]{3,2,1,0:T(8,128)S(1)}, f32[1,16,64,128]{3,2,1,0:T(8,128)S(1)}, u32[]{:S(2)}, u32[]{:S(2)}) collective-permute-start(f32[1,16,64,128]{3,2,1,0:T(8,128)S(1)} %multiply_add_fusion.2), channel_id=1, source_target_pairs={{8,0},{10,2},{12,4},{14,6},{9,1},{11,3},{13,5},{15,7},{24,16},{26,... | collective-permute-start | bytes 1572872 | tf_op jit(solution)/shard_map/ppermute | solution.py:48
  148.6 24.5 %collective-permute-start.5 = (f32[1,16,64,128]{3,2,1,0:T(8,128)S(1)}, f32[1,16,64,128]{3,2,1,0:T(8,128)S(1)}, u32[]{:S(2)}, u32[]{:S(2)}) collective-permute-start(f32[1,16,64,128]{3,2,1,0:T(8,128)S(1)} %multiply_add_fusion.4), channel_id=1, source_target_pairs={{0,8},{2,10},{4,12},{6,14},{1,9},{3,11},{5,13},{7,15},{16,24},{18,... | collective-permute-start | bytes 1572872 | tf_op jit(solution)/shard_map/ppermute | solution.py:48
  152.1 22.4 %copy-start.14 = (f32[2,256,1024]{2,1,0:T(8,128)S(1)}, f32[2,256,1024]{2,1,0:T(8,128)}, u32[]{:S(2)}) copy-start(f32[2,256,1024]{2,1,0:T(8,128)} %get-tuple-element.9) | copy-start | bytes 6291460
  176.0 4.9 %copy-start.22 = (f32[1024]{0:T(1024)S(1)}, f32[1024]{0:T(1024)}, u32[]{:S(2)}) copy-start(f32[1024]{0:T(1024)} %param.22) | copy-start | bytes 12292
  (8 other events, 22.8 us)

commit v3 on v2

--- a/solution.py
+++ b/solution.py
@@ -64,9 +64,8 @@
     return (jnp.ones_like(decay), jnp.zeros_like(state))
 
 
-def block_kernel(xbc_ref, cum_ref, cum_t_ref, step_t_ref, to_end_ref, inside_ref, state_ref, *, reverse):
-    inner = H * P_SIZE
-    x_all = xbc_ref[:, :inner]
+def inside_kernel(xbc_ref, cum_ref, cum_t_ref, step_t_ref, inside_ref, *, reverse):
+    inner = H * P_SIZE
     b_rows = xbc_ref[:, inner : inner + N]
     c_rows = xbc_ref[:, inner + N :]
     scores = lax.dot_general(
@@ -75,16 +74,22 @@
     t_idx = lax.broadcasted_iota(jnp.int32, (Q, Q), 0)
     s_idx = lax.broadcasted_iota(jnp.int32, (Q, Q), 1)
     keep = (s_idx >= t_idx) if reverse else (t_idx >= s_idx)
-    b_wide = b_rows.astype(jnp.float32)
     for h in range(H):
         gaps = cum_ref[:, h : h + 1] - cum_t_ref[h : h + 1, :]
         decays = jnp.where(keep, jnp.exp(jnp.where(keep, gaps, 0.0)), 0.0)
         weights = (decays * scores * step_t_ref[h : h + 1, :]).astype(jnp.bfloat16)
-        x_h = x_all[:, h * P_SIZE : (h + 1) * P_SIZE]
+        x_h = xbc_ref[:, h * P_SIZE : (h + 1) * P_SIZE]
         inside_ref[:, h * P_SIZE : (h + 1) * P_SIZE] = jnp.dot(
             weights, x_h, preferred_element_type=jnp.float32
         )
+
+
+def state_kernel(xbc_ref, to_end_ref, state_ref):
+    inner = H * P_SIZE
+    b_wide = xbc_ref[:, inner : inner + N].astype(jnp.float32)
+    for h in range(H):
         state_weights = (b_wide * to_end_ref[:, h : h + 1]).astype(jnp.bfloat16)
+        x_h = xbc_ref[:, h * P_SIZE : (h + 1) * P_SIZE]
         state_ref[h] = lax.dot_general(
             x_h, state_weights, (((0,), (0,)), ((), ())), preferred_element_type=jnp.float32
         )
@@ -104,16 +109,20 @@
     step_t = jnp.swapaxes(flat(steps_cut), 1, 2)
     xbc = activated.reshape(blocks, Q, width)
     spec = lambda shape: pl.BlockSpec((None,) + shape, lambda i: (i,) + (0,) * len(shape))
-    inside, state = pl.pallas_call(
-        partial(block_kernel, reverse=reverse),
+    state = pl.pallas_call(
+        state_kernel,
         grid=(blocks,),
-        in_specs=[spec((Q, width)), spec((Q, H)), spec((H, Q)), spec((H, Q)), spec((Q, H))],
-        out_specs=[spec((Q, H * P_SIZE)), spec((H, P_SIZE, N))],
-        out_shape=[
-            jax.ShapeDtypeStruct((blocks, Q, H * P_SIZE), jnp.float32),
-            jax.ShapeDtypeStruct((blocks, H, P_SIZE, N), jnp.float32),
-        ],
-    )(xbc, cum, cum_t, step_t, flat(to_end))
+        in_specs=[spec((Q, width)), spec((Q, H))],
+        out_specs=spec((H, P_SIZE, N)),
+        out_shape=jax.ShapeDtypeStruct((blocks, H, P_SIZE, N), jnp.float32),
+    )(xbc, flat(to_end))
+    inside = pl.pallas_call(
+        partial(inside_kernel, reverse=reverse),
+        grid=(blocks,),
+        in_specs=[spec((Q, width)), spec((Q, H)), spec((H, Q)), spec((H, Q))],
+        out_specs=spec((Q, H * P_SIZE)),
+        out_shape=jax.ShapeDtypeStruct((blocks, Q, H * P_SIZE), jnp.float32),
+    )(xbc, cum, cum_t, step_t)
     inside = inside.reshape(count, rows, H * P_SIZE)
     state = state.reshape(count, spans, H, P_SIZE, N)
     return inside, state, jnp.exp(end), jnp.exp(log_decay)

time: 193 us -> 198 us (1.026)
  the two profiles are of different devices: /device:TPU:24 before, /device:TPU:0 now
where the time goes in v3:
time: 198 us; the launch traced here: 197 us
  other arithmetic  43.4 us (22%)
  starting transfers between devices  39.4 us (20%)
  matrix products  34.5 us (17%)
  local copies, waits for them, and re-layouts  31.3 us (16%)
  waiting for transfers between devices  26.8 us (14%)
  Pallas kernels  21.3 us (11%)
    ppermute x10, starting transfers between devices, exclusive_scans(): decay, state = lax.ppermute(ahead[k], axis, pairs)  32.6 us
    ppermute x10, waiting for transfers between devices, exclusive_scans(): decay, state = lax.ppermute(ahead[k], axis, pairs)  26.8 us
    convert_element_type x1, other arithmetic, strand_terms(): activated = jax.nn.silu(summed).astype(jnp.bfloat16)  11.2 us
    pallas_call x2, Pallas kernels, block_terms(): pl.pallas_call(partial(inside_kernel, reverse=reverse), grid=(blocks,), i...  11.1 us
    pallas_call x2, Pallas kernels, block_terms(): pl.pallas_call(state_kernel, grid=(blocks,), in_specs=[spec((Q, width)),...  10.2 us
    add x8, other arithmetic, chain(): next_decay[..., None, None] * first_state + next_state  9.26 us
    broadcast_in_dim x4, local copies, waits for them, and re-layouts, finish(): scale = jnp.repeat(from_start.reshape(count, rows, H), P_SIZE, axis=-1)  8.99 us
    dot_general x1, matrix products, on_device(): jnp.einsum('grd,de->gre', mirrored, w_in, preferred_element_type=jnp.floa...  7.51 us
  transfers between devices with their start and end apart: 12, of which 2 were waited for; matrix products, arithmetic and copies ran while one was open for 44% of the time, Pallas kernels for 11%

profile of v3, /device:TPU:0, one launch (start us, length us, event | category | flops | bytes accessed | tf_op | source)
XLA Modules:
  0.0 197.3 jit_solution(11907564845951185161)
XLA Ops:
  0.0 1.9 fusion.39
  2.5 5.5 %collective-permute-start = (bf16[1,3,1024]{2,1,0:T(4,128)(2,1)}, bf16[1,3,1024]{2,1,0:T(4,128)(2,1)}, u32[]{:S(2)}, u32[]{:S(2)}) collective-permute-start(bf16[1,3,1024]{2,1,0:T(4,128)(2,1)} %get-tuple-element.17), channel_id=1, source_target_pairs={{0,2},{2,4},{4,6},{6,8},{8,10},{10,12},{12,14},{1,3},{3,5},{5,7},{... | collective-permute-start | bytes 18440 | tf_op jit(solution)/shard_map/ppermute | solution.py:196
  9.4 2.2 %fusion.45 = bf16[512,1024]{1,0:T(8,128)(2,1)} fusion(bf16[1,512,1024]{2,1,0:T(8,128)(2,1)S(1)} %fusion.39), kind=kOutput, calls=%fused_computation.59 | convolution fusion | flops 1076363264 | bytes 2097152 | tf_op jit(solution)/shard_map/...d,de->...e/dot_general | solution.py:28
  12.1 1.7 compare_select_fusion
  14.7 1.8 broadcast_multiply_fusion.1
  17.6 5.0 %reduce-window.16 = f32[1,2,16,2,128]{4,2,3,1,0:T(8,128)S(1)} reduce-window(f32[1,2,16,2,128]{4,2,3,1,0:T(8,128)S(1)} %copy.29, f32[]{:T(128)} %constant.13.clone.1), window={size=1x1x1x1x128 pad=0_0x0_0x0_0x0_0x0_127}, to_apply=%region_3.4 | reduce-window | flops 1040384 | bytes 65540 | tf_op jit(solution)/shard_map/reduce-window.2
  23.5 1.7 bitcast_exponential_fusion
  31.0 1.8 bitcast_exponential_fusion.1
  32.8 5.4 %collective-permute-start.1 = (f32[1,16]{1,0:T(1,128)S(1)}, f32[1,16]{1,0:T(1,128)S(1)}, u32[]{:S(2)}, u32[]{:S(2)}) collective-permute-start(f32[1,16]{1,0:T(1,128)S(1)} %get-tuple-element.29), channel_id=1, source_target_pairs={{0,2},{2,4},{4,6},{6,8},{8,10},{10,12},{12,14},{1,3},{3,5},{5,7},{... | collective-permute-start | bytes 200 | tf_op jit(solution)/shard_map/ppermute | solution.py:48
  38.2 7.5 %convolution_bitcast_fusion = f32[1,512,2304]{2,1,0:T(8,128)} fusion(bf16[512,1024]{1,0:T(8,128)(2,1)} %fusion.45, bf16[1024,2304]{1,0:T(8,128)(2,1)} %param.15), kind=kOutput, calls=%fused_computation | convolution fusion | flops 2415919104 | bytes 10485760 | tf_op jit(solution)/shard_map/grd,de->gre/dot_general | solution.py:202
  45.8 4.3 %convolution_bitcast_fusion.1 = f32[1,512,2304]{2,1,0:T(8,128)} fusion(bf16[1024,2304]{1,0:T(8,128)(2,1)S(1)} %bitcast.241, bf16[1,512,1024]{2,1,0:T(8,128)(2,1)S(1)} %fusion.39), kind=kOutput, calls=%fused_computation.1 | convolution fusion | flops 2415919104 | bytes 10485760 | tf_op jit(solution)/shard_map/grd,de->gre/dot_general | solution.py:201
  55.9 1.7 copy.25.cum_t_ref
  59.2 2.9 %copy.27 = f32[1,512,1024]{2,1,0:T(8,128)} copy(f32[1,512,1024]{1,2,0:T(8,128)} %bitcast.222) | data formatting | bytes 4194304 | tf_op jit(solution)/shard_map/broadcast_in_dim | solution.py:175
  63.7 3.0 %copy.34 = f32[1,512,1024]{2,1,0:T(8,128)} copy(f32[1,512,1024]{1,2,0:T(8,128)} %bitcast.223) | data formatting | bytes 4194304 | tf_op jit(solution)/shard_map/broadcast_in_dim | solution.py:175
  66.6 3.6 %slice.158 = f32[1,512,1280]{2,1,0:T(8,128)} slice(f32[1,512,2304]{2,1,0:T(8,128)} %convolution_bitcast_fusion), slice={[0:1], [0:512], [1024:2304]} | slice | bytes 5242880 | tf_op jit(solution)/shard_map/slice | solution.py:135
  70.2 3.4 %slice.145 = f32[1,512,1280]{2,1,0:T(8,128)} slice(f32[1,512,2304]{2,1,0:T(8,128)} %convolution_bitcast_fusion.1), slice={[0:1], [0:512], [1024:2304]} | slice | bytes 5242880 | tf_op jit(solution)/shard_map/slice | solution.py:135
  74.7 2.4 %fusion.28 = f32[1,3,1280]{2,1,0:T(4,128)S(1)} fusion(bf16[1024,2304]{1,0:T(8,128)(2,1)} %param.15, bf16[1,3,1024]{2,1,0:T(4,128)(2,1)} %collective-permute-done.6), kind=kOutput, calls=%fused_computation.37 | convolution fusion | flops 16256000 | bytes 2644992 | tf_op jit(solution)/shard_map/grd,de->gre/dot_general | solution.py:204
  77.2 11.2 %multiply_convert_fusion.1 = (bf16[1,512,1280]{2,1,0:T(8,128)(2,1)}, bf16[1,512,1280]{2,1,0:T(8,128)(2,1)}) fusion(f32[1,512,1280]{2,1,0:T(8,128)} %slice.145, f32[1,3,1280]{2,1,0:T(4,128)S(1)} %fusion.25, f32[1280]{0:T(1024)S(1)} %get-tuple-element.7, f32[1280]{0:T(1024)S(1)} %get-tuple-element.8, f32[1280]{0:T(1024)S(1)} %get-tuple-element.6, ...), kind=kLoop, calls=%fused_computation.31 | loop fusion | flops 20971520 | bytes 7920640 | tf_op jit(solution)/shard_map/convert_element_type | solution.py:145
  88.3 5.1 %shard_map.119 = f32[2,16,64,128]{3,2,1,0:T(8,128)} custom-call(bf16[2,256,1280]{2,1,0:T(8,128)(2,1)} %bitcast.212, f32[2,256,16]{2,1,0:T(8,128)} %multiply_bitcast_fusion.1.to_end_ref), custom_call_target="tpu_custom_call" | custom-call | tf_op jit(solution)/shard_map/pallas_call | solution.py:112
  93.4 2.2 %fusion.64 = f32[1,16,64,128]{3,2,1,0:T(8,128)} fusion(f32[1,2,16,64,128]{4,3,2,1,0:T(8,128)} %bitcast.216, f32[16]{0:T(128)S(1)} %get-tuple-element.31, f32[16]{0:T(128)S(1)} %get-tuple-element.28), kind=kLoop, calls=%fused_computation.78 | loop fusion | flops 393216 | bytes 1572992 | tf_op jit(solution)/shard_map/add | solution.py:34
  95.7 5.6 %collective-permute-start.3 = (f32[1,16,64,128]{3,2,1,0:T(8,128)}, f32[1,16,64,128]{3,2,1,0:T(8,128)}, u32[]{:S(2)}, u32[]{:S(2)}) collective-permute-start(f32[1,16,64,128]{3,2,1,0:T(8,128)} %fusion.64), channel_id=1, source_target_pairs={{0,2},{2,4},{4,6},{6,8},{8,10},{10,12},{12,14},{1,3},{3,5},{5,7},{... | collective-permute-start | bytes 1572872 | tf_op jit(solution)/shard_map/ppermute | solution.py:48
  103.3 4.5 %collective-permute-start.2 = (f32[1,16]{1,0:T(1,128)S(1)}, f32[1,16]{1,0:T(1,128)S(1)}, u32[]{:S(2)}, u32[]{:S(2)}) collective-permute-start(f32[1,16]{1,0:T(1,128)S(1)} %fusion.83), channel_id=1, source_target_pairs={{0,4},{2,6},{4,8},{6,10},{8,12},{10,14},{1,5},{3,7},{5,9},{7,11},{... | collective-permute-start | bytes 200 | tf_op jit(solution)/shard_map/ppermute | solution.py:48
  107.8 5.1 %shard_map.121 = f32[2,16,64,128]{3,2,1,0:T(8,128)} custom-call(bf16[2,256,1280]{2,1,0:T(8,128)(2,1)} %bitcast.214, f32[2,256,16]{2,1,0:T(8,128)} %multiply_bitcast_fusion.to_end_ref), custom_call_target="tpu_custom_call" | custom-call | tf_op jit(solution)/shard_map/pallas_call | solution.py:112
  116.9 4.2 %collective-permute-start.4 = (f32[1,16,64,128]{3,2,1,0:T(8,128)S(1)}, f32[1,16,64,128]{3,2,1,0:T(8,128)S(1)}, u32[]{:S(2)}, u32[]{:S(2)}) collective-permute-start(f32[1,16,64,128]{3,2,1,0:T(8,128)S(1)} %multiply_add_fusion.5), channel_id=1, source_target_pairs={{0,4},{2,6},{4,8},{6,10},{8,12},{10,14},{1,5},{3,7},{5,9},{7,11},{... | collective-permute-start | bytes 1572872 | tf_op jit(solution)/shard_map/ppermute | solution.py:48
  121.9 6.1 %collective-permute-done.9 = f32[1,16,64,128]{3,2,1,0:T(8,128)S(1)} collective-permute-done((f32[1,16,64,128]{3,2,1,0:T(8,128)S(1)}, f32[1,16,64,128]{3,2,1,0:T(8,128)S(1)}, u32[]{:S(2)}, u32[]{:S(2)}) %collective-permute-start.9) | collective-permute-done | bytes 524320 | tf_op jit(solution)/shard_map/ppermute | solution.py:48
  131.3 6.4 %collective-permute-start.5 = (f32[1,16,64,128]{3,2,1,0:T(8,128)}, f32[1,16,64,128]{3,2,1,0:T(8,128)}, u32[]{:S(2)}, u32[]{:S(2)}) collective-permute-start(f32[1,16,64,128]{3,2,1,0:T(8,128)} %multiply_add_fusion.4), channel_id=1, source_target_pairs={{0,8},{2,10},{4,12},{6,14},{1,9},{3,11},{5,13},{7,15},{16,24},{18,... | collective-permute-start | bytes 1572872 | tf_op jit(solution)/shard_map/ppermute | solution.py:48
  140.5 5.5 %shard_map.120 = f32[2,256,1024]{2,1,0:T(8,128)} custom-call(bf16[2,256,1280]{2,1,0:T(8,128)(2,1)} %bitcast.215, f32[2,256,16]{2,1,0:T(8,128)} %bitcast.230, f32[2,16,256]{2,1,0:T(8,128)} %copy.32.cum_t_ref, f32[2,16,256]{2,1,0:T(8,128)} %bitcast.253), custom_call_target="tpu_custom_call" | custom-call | tf_op jit(solution)/shard_map/pallas_call | solution.py:119
  145.9 5.6 %shard_map.118 = f32[2,256,1024]{2,1,0:T(8,128)} custom-call(bf16[2,256,1280]{2,1,0:T(8,128)(2,1)} %bitcast.213, f32[2,256,16]{2,1,0:T(8,128)} %bitcast.233, f32[2,16,256]{2,1,0:T(8,128)} %copy.25.cum_t_ref, f32[2,16,256]{2,1,0:T(8,128)} %bitcast.252), custom_call_target="tpu_custom_call" | custom-call | tf_op jit(solution)/shard_map/pallas_call | solution.py:119
  156.9 20.7 %collective-permute-done.11 = f32[1,16,64,128]{3,2,1,0:T(8,128)S(1)} collective-permute-done((f32[1,16,64,128]{3,2,1,0:T(8,128)S(1)}, f32[1,16,64,128]{3,2,1,0:T(8,128)S(1)}, u32[]{:S(2)}, u32[]{:S(2)}) %collective-permute-start.11) | collective-permute-done | bytes 524320 | tf_op jit(solution)/shard_map/ppermute | solution.py:48
  181.5 4.9 %multiply_reduce_fusion.1 = (f32[512]{0:T(512)S(1)}, f32[1,512,1024]{2,1,0:T(8,128)}, f32[512]{0:T(512)S(1)}, f32[1,512,1024]{2,1,0:T(8,128)}) fusion(f32[1,512,2304]{2,1,0:T(8,128)} %convolution_bitcast_fusion.1, bf16[1,512,1280]{2,1,0:T(8,128)(2,1)S(1)} %copy-done.1, f32[1024]{0:T(1024)S(1)} %mul.480, f32[1,512,1024]{2,1,0:T(8,128)S(1)} %copy-done.7, ...), kind=kLoop, calls=%fused_computation.58 | loop fusion | flops 12581888 | bytes 23076864 | tf_op jit(solution)/shard_map/reduce_sum | solution.py:181
  186.4 6.4 %fusion.40 = f32[512,1024]{1,0:T(8,128)} fusion(bf16[1024,1024]{1,0:T(8,128)(2,1)S(1)} %copy-done, f32[1,512,1024]{2,1,0:T(8,128)} %get-tuple-element.26, f32[512]{0:T(512)S(1)} %get-tuple-element.43, f32[1024]{0:T(1024)S(1)} %copy-done.26), kind=kOutput, calls=%fused_computation.50 | convolution fusion | flops 3226992640 | bytes 6297600 | tf_op jit(solution)/shard_map/grk,kd->grd/dot_general | solution.py:220
  192.8 4.5 %fusion.46 = bf16[1,512,1024]{2,1,0:T(8,128)(2,1)} fusion(f32[512,1024]{1,0:T(8,128)} %fusion.40, bf16[1024,1024]{1,0:T(8,128)(2,1)S(1)} %copy-done, f32[1,512,1024]{2,1,0:T(8,128)} %get-tuple-element.10, f32[1024]{0:T(1024)S(1)} %copy-done.26, f32[512]{0:T(512)S(1)} %get-tuple-element.44), kind=kOutput, calls=%fused_computation.60 | convolution fusion | flops 1076363264 | bytes 7346176 | tf_op jit(solution)/shard_map/grk,kd->grd/dot_general | solution.py:218
  (139 shorter events, 43.0 us)
Async XLA Ops:
  0.0 186.4 %copy-start = (bf16[1024,1024]{1,0:T(8,128)(2,1)S(1)}, bf16[1024,1024]{1,0:T(8,128)(2,1)}, u32[]{:S(2)}) copy-start(bf16[1024,1024]{1,0:T(8,128)(2,1)} %param.23) | copy-start | bytes 6291460
  2.5 71.1 %collective-permute-start = (bf16[1,3,1024]{2,1,0:T(4,128)(2,1)}, bf16[1,3,1024]{2,1,0:T(4,128)(2,1)}, u32[]{:S(2)}, u32[]{:S(2)}) collective-permute-start(bf16[1,3,1024]{2,1,0:T(4,128)(2,1)} %get-tuple-element.17), channel_id=1, source_target_pairs={{0,2},{2,4},{4,6},{6,8},{8,10},{10,12},{12,14},{1,3},{3,5},{5,7},{... | collective-permute-start | bytes 18440 | tf_op jit(solution)/shard_map/ppermute | solution.py:196
  8.0 66.8 %collective-permute-start.6 = (bf16[1,3,1024]{2,1,0:T(4,128)(2,1)S(1)}, bf16[1,3,1024]{2,1,0:T(4,128)(2,1)}, u32[]{:S(2)}, u32[]{:S(2)}) collective-permute-start(bf16[1,3,1024]{2,1,0:T(4,128)(2,1)S(1)} %get-tuple-element.18), channel_id=1, source_target_pairs={{2,0},{4,2},{6,4},{8,6},{10,8},{12,10},{14,12},{3,1},{5,3},{7,5},{... | collective-permute-start | bytes 18440 | tf_op jit(solution)/shard_map/ppermute | solution.py:197
  12.1 11.4 %copy-start.11 = (f32[512,16]{1,0:T(8,128)}, f32[512,16]{1,0:T(8,128)S(1)}, u32[]{:S(2)}) copy-start(f32[512,16]{1,0:T(8,128)S(1)} %copy.21) | copy-start | bytes 98308
  25.2 28.9 %copy-start.9 = (f32[1,2,16,256]{2,3,1,0:T(8,128)}, f32[1,2,16,256]{2,3,1,0:T(8,128)S(1)}, u32[]{:S(2)}) copy-start(f32[1,2,16,256]{2,3,1,0:T(8,128)S(1)} %get-tuple-element.16) | copy-start | bytes 98308
  26.4 74.9 %collective-permute-start.7 = (f32[1,16]{1,0:T(1,128)}, f32[1,16]{1,0:T(1,128)}, u32[]{:S(2)}, u32[]{:S(2)}) collective-permute-start(f32[1,16]{1,0:T(1,128)} %get-tuple-element.34), channel_id=1, source_target_pairs={{2,0},{4,2},{6,4},{8,6},{10,8},{12,10},{14,12},{3,1},{5,3},{7,5},{... | collective-permute-start | bytes 200 | tf_op jit(solution)/shard_map/ppermute | solution.py:48
  31.0 14.8 %slice-start = ((s8[4718592]{0:T(1024)(128)(4,1)}), s8[4194304]{0:T(1024)(128)(4,1)S(1)}, s32[]{:S(2)}) async-start(s8[4718592]{0:T(1024)(128)(4,1)} %bitcast.240), calls=%async_computation | async-start | bytes 8388608
  32.8 18.2 %copy-start.10 = (f32[1,2,16,256]{2,3,1,0:T(8,128)}, f32[1,2,16,256]{2,3,1,0:T(8,128)S(1)}, u32[]{:S(2)}) copy-start(f32[1,2,16,256]{2,3,1,0:T(8,128)S(1)} %get-tuple-element.12) | copy-start | bytes 98308
  32.8 70.4 %collective-permute-start.1 = (f32[1,16]{1,0:T(1,128)S(1)}, f32[1,16]{1,0:T(1,128)S(1)}, u32[]{:S(2)}, u32[]{:S(2)}) collective-permute-start(f32[1,16]{1,0:T(1,128)S(1)} %get-tuple-element.29), channel_id=1, source_target_pairs={{0,2},{2,4},{4,6},{6,8},{8,10},{10,12},{12,14},{1,3},{3,5},{5,7},{... | collective-permute-start | bytes 200 | tf_op jit(solution)/shard_map/ppermute | solution.py:48
  38.2 7.5 %slice-start.1 = ((s8[4718592]{0:T(1024)(128)(4,1)}), s8[524288]{0:T(1024)(128)(4,1)S(1)}, s32[]{:S(2)}) async-start(s8[4718592]{0:T(1024)(128)(4,1)} %bitcast.240), calls=%async_computation.1 | async-start | bytes 1048576
  45.8 5.2 %copy-start.25 = (f32[1,1,16]{2,1,0:T(1,128)S(1)}, f32[1,1,16]{2,1,0:T(1,128)}, u32[]{:S(2)}) copy-start(f32[1,1,16]{2,1,0:T(1,128)} %get-tuple-element.32) | copy-start | bytes 196
  45.8 5.2 %copy-start.12 = (f32[512,16]{1,0:T(8,128)S(1)}, f32[512,16]{1,0:T(8,128)}, u32[]{:S(2)}) copy-start(f32[512,16]{1,0:T(8,128)} %copy-done.11) | copy-start | bytes 98308
  45.8 6.0 %copy-start.24 = (f32[16]{0:T(128)S(1)}, f32[16]{0:T(128)}, u32[]{:S(2)}) copy-start(f32[16]{0:T(128)} %param.21) | copy-start | bytes 196
  63.7 9.9 %slice-start.2 = ((s8[4718592]{0:T(1024)(128)(4,1)}), s8[524288]{0:T(1024)(128)(4,1)S(1)}, s32[]{:S(2)}) async-start(s8[4718592]{0:T(1024)(128)(4,1)} %bitcast.242), calls=%async_computation.2 | async-start | bytes 1048576
  66.6 6.9 %slice-start.3 = ((s8[4718592]{0:T(1024)(128)(4,1)}), s8[4194304]{0:T(1024)(128)(4,1)S(1)}, s32[]{:S(2)}) async-start(s8[4718592]{0:T(1024)(128)(4,1)} %bitcast.242), calls=%async_computation.3 | async-start | bytes 8388608
  93.4 22.3 %copy-start.3 = (f32[2,16,64,128]{3,2,1,0:T(8,128)S(1)}, f32[2,16,64,128]{3,2,1,0:T(8,128)}, u32[]{:S(2)}) copy-start(f32[2,16,64,128]{3,2,1,0:T(8,128)} %shard_map.119) | copy-start | bytes 3145732
  95.7 20.0 %collective-permute-start.3 = (f32[1,16,64,128]{3,2,1,0:T(8,128)}, f32[1,16,64,128]{3,2,1,0:T(8,128)}, u32[]{:S(2)}, u32[]{:S(2)}) collective-permute-start(f32[1,16,64,128]{3,2,1,0:T(8,128)} %fusion.64), channel_id=1, source_target_pairs={{0,2},{2,4},{4,6},{6,8},{8,10},{10,12},{12,14},{1,3},{3,5},{5,7},{... | collective-permute-start | bytes 1572872 | tf_op jit(solution)/shard_map/ppermute | solution.py:48
  102.0 19.2 %collective-permute-start.8 = (f32[1,16]{1,0:T(1,128)S(1)}, f32[1,16]{1,0:T(1,128)S(1)}, u32[]{:S(2)}, u32[]{:S(2)}) collective-permute-start(f32[1,16]{1,0:T(1,128)S(1)} %fusion.85), channel_id=1, source_target_pairs={{4,0},{6,2},{8,4},{10,6},{12,8},{14,10},{5,1},{7,3},{9,5},{11,7},{... | collective-permute-start | bytes 200 | tf_op jit(solution)/shard_map/ppermute | solution.py:48
  103.3 18.6 %collective-permute-start.2 = (f32[1,16]{1,0:T(1,128)S(1)}, f32[1,16]{1,0:T(1,128)S(1)}, u32[]{:S(2)}, u32[]{:S(2)}) collective-permute-start(f32[1,16]{1,0:T(1,128)S(1)} %fusion.83), channel_id=1, source_target_pairs={{0,4},{2,6},{4,8},{6,10},{8,12},{10,14},{1,5},{3,7},{5,9},{7,11},{... | collective-permute-start | bytes 200 | tf_op jit(solution)/shard_map/ppermute | solution.py:48
  113.0 15.0 %copy-start.4 = (f32[2,16,64,128]{3,2,1,0:T(8,128)S(1)}, f32[2,16,64,128]{3,2,1,0:T(8,128)}, u32[]{:S(2)}) copy-start(f32[2,16,64,128]{3,2,1,0:T(8,128)} %shard_map.121) | copy-start | bytes 3145732
  114.4 13.6 %collective-permute-start.9 = (f32[1,16,64,128]{3,2,1,0:T(8,128)S(1)}, f32[1,16,64,128]{3,2,1,0:T(8,128)S(1)}, u32[]{:S(2)}, u32[]{:S(2)}) collective-permute-start(f32[1,16,64,128]{3,2,1,0:T(8,128)S(1)} %fusion.63), channel_id=1, source_target_pairs={{2,0},{4,2},{6,4},{8,6},{10,8},{12,10},{14,12},{3,1},{5,3},{7,5},{... | collective-permute-start | bytes 1572872 | tf_op jit(solution)/shard_map/ppermute | solution.py:48
  116.9 13.4 %collective-permute-start.4 = (f32[1,16,64,128]{3,2,1,0:T(8,128)S(1)}, f32[1,16,64,128]{3,2,1,0:T(8,128)S(1)}, u32[]{:S(2)}, u32[]{:S(2)}) collective-permute-start(f32[1,16,64,128]{3,2,1,0:T(8,128)S(1)} %multiply_add_fusion.5), channel_id=1, source_target_pairs={{0,4},{2,6},{4,8},{6,10},{8,12},{10,14},{1,5},{3,7},{5,9},{7,11},{... | collective-permute-start | bytes 1572872 | tf_op jit(solution)/shard_map/ppermute | solution.py:48
  128.0 12.5 %copy-start.16 = (f32[1,16,64,128]{3,2,1,0:T(8,128)}, f32[1,16,64,128]{3,2,1,0:T(8,128)S(1)}, u32[]{:S(2)}) copy-start(f32[1,16,64,128]{3,2,1,0:T(8,128)S(1)} %collective-permute-done.9) | copy-start | bytes 1572868
  129.0 22.6 %collective-permute-start.10 = (f32[1,16,64,128]{3,2,1,0:T(8,128)}, f32[1,16,64,128]{3,2,1,0:T(8,128)}, u32[]{:S(2)}, u32[]{:S(2)}) collective-permute-start(f32[1,16,64,128]{3,2,1,0:T(8,128)} %multiply_add_fusion.3), channel_id=1, source_target_pairs={{4,0},{6,2},{8,4},{10,6},{12,8},{14,10},{5,1},{7,3},{9,5},{11,7},{... | collective-permute-start | bytes 1572872 | tf_op jit(solution)/shard_map/ppermute | solution.py:48
  130.3 8.3 %copy-start.14 = (f32[1,16,64,128]{3,2,1,0:T(8,128)}, f32[1,16,64,128]{3,2,1,0:T(8,128)S(1)}, u32[]{:S(2)}) copy-start(f32[1,16,64,128]{3,2,1,0:T(8,128)S(1)} %collective-permute-done.4) | copy-start | bytes 1572868
  131.3 23.0 %collective-permute-start.5 = (f32[1,16,64,128]{3,2,1,0:T(8,128)}, f32[1,16,64,128]{3,2,1,0:T(8,128)}, u32[]{:S(2)}, u32[]{:S(2)}) collective-permute-start(f32[1,16,64,128]{3,2,1,0:T(8,128)} %multiply_add_fusion.4), channel_id=1, source_target_pairs={{0,8},{2,10},{4,12},{6,14},{1,9},{3,11},{5,13},{7,15},{16,24},{18,... | collective-permute-start | bytes 1572872 | tf_op jit(solution)/shard_map/ppermute | solution.py:48
  153.0 24.6 %collective-permute-start.11 = (f32[1,16,64,128]{3,2,1,0:T(8,128)S(1)}, f32[1,16,64,128]{3,2,1,0:T(8,128)S(1)}, u32[]{:S(2)}, u32[]{:S(2)}) collective-permute-start(f32[1,16,64,128]{3,2,1,0:T(8,128)S(1)} %multiply_add_fusion.2), channel_id=1, source_target_pairs={{8,0},{10,2},{12,4},{14,6},{9,1},{11,3},{13,5},{15,7},{24,16},{26,... | collective-permute-start | bytes 1572872 | tf_op jit(solution)/shard_map/ppermute | solution.py:48
  155.7 21.9 %copy-start.17 = (f32[1,16,64,128]{3,2,1,0:T(8,128)S(1)}, f32[1,16,64,128]{3,2,1,0:T(8,128)}, u32[]{:S(2)}) copy-start(f32[1,16,64,128]{3,2,1,0:T(8,128)} %copy-done.16) | copy-start | bytes 1572868
  155.7 24.5 %copy-start.8 = (f32[1,512,1024]{2,1,0:T(8,128)S(1)}, f32[1,512,1024]{2,1,0:T(8,128)}, u32[]{:S(2)}) copy-start(f32[1,512,1024]{2,1,0:T(8,128)} %copy.34) | copy-start | bytes 6291460
  155.9 23.1 %copy-start.18 = (f32[1,1,16,64,128]{4,3,2,1,0:T(8,128)S(1)}, f32[1,1,16,64,128]{4,3,2,1,0:T(8,128)}, u32[]{:S(2)}) copy-start(f32[1,1,16,64,128]{4,3,2,1,0:T(8,128)} %slice_add_fusion) | copy-start | bytes 1572868
  155.9 24.3 %copy-start.7 = (f32[1,512,1024]{2,1,0:T(8,128)S(1)}, f32[1,512,1024]{2,1,0:T(8,128)}, u32[]{:S(2)}) copy-start(f32[1,512,1024]{2,1,0:T(8,128)} %copy.27) | copy-start | bytes 6291460
  181.4 4.9 %copy-start.26 = (f32[1024]{0:T(1024)S(1)}, f32[1024]{0:T(1024)}, u32[]{:S(2)}) copy-start(f32[1024]{0:T(1024)} %param.22) | copy-start | bytes 12292
  (12 other events, 37.6 us)

commit v4 on v3

--- a/solution.py
+++ b/solution.py
@@ -45,7 +45,7 @@
         down = [(i + shift, i) for i in range(count - shift)]
         got = []
         for k, pairs in ((0, up), (1, down)):
-            decay, state = lax.ppermute(ahead[k], axis, pairs)
+            decay, state = unpack(lax.ppermute(pack(*ahead[k]), axis, pairs))
             has = (place >= shift) if k == 0 else (place < count - shift)
             decay = jnp.where(has, decay, 1.0)
             got.append((decay, state))
@@ -57,6 +57,15 @@
     if seen[0] is None:
         return fwd_identity(fwd), fwd_identity(rev)
     return seen[0], seen[1]
+
+
+def pack(decay, state):
+    extra = jnp.broadcast_to(decay[:, :, None, None], decay.shape + (8, state.shape[-1]))
+    return jnp.concatenate([state, extra], axis=2)
+
+
+def unpack(packed):
+    return packed[:, :, P_SIZE, 0], packed[:, :, :P_SIZE]
 
 
 def fwd_identity(summary):

time: 198 us -> 198 us (level)
  the two profiles are of different devices: /device:TPU:0 before, /device:TPU:24 now
where the time goes in v4:
time: 198 us; the launch traced here: 195 us
  other arithmetic  46.7 us (24%)
  waiting for transfers between devices  40.2 us (20%)
  matrix products  34.5 us (17%)
  local copies, waits for them, and re-layouts  29.1 us (15%)
  starting transfers between devices  22.9 us (12%)
  Pallas kernels  21.5 us (11%)
    ppermute x6, waiting for transfers between devices, exclusive_scans(): decay, state = unpack(lax.ppermute(pack(*ahead[k]), axis, pairs))  40.2 us
    ppermute x6, starting transfers between devices, exclusive_scans(): decay, state = unpack(lax.ppermute(pack(*ahead[k]), axis, pairs))  16 us
    convert_element_type x1, other arithmetic, strand_terms(): activated = jax.nn.silu(summed).astype(jnp.bfloat16)  11.2 us
    pallas_call x2, Pallas kernels, block_terms(): pl.pallas_call(partial(inside_kernel, reverse=reverse), grid=(blocks,), i...  11.1 us
    pallas_call x2, Pallas kernels, block_terms(): pl.pallas_call(state_kernel, grid=(blocks,), in_specs=[spec((Q, width)),...  10.4 us
    broadcast_in_dim x4, local copies, waits for them, and re-layouts, finish(): scale = jnp.repeat(from_start.reshape(count, rows, H), P_SIZE, axis=-1)  9.06 us
    add x8, other arithmetic, chain(): next_decay[..., None, None] * first_state + next_state  7.97 us
    dot_general x1, matrix products, on_device(): jnp.einsum('grd,de->gre', mirrored, w_in, preferred_element_type=jnp.floa...  7.52 us
  transfers between devices with their start and end apart: 8, of which 3 were waited for; matrix products, arithmetic and copies ran while one was open for 36% of the time, Pallas kernels for 8%

profile of v4, /device:TPU:24, one launch (start us, length us, event | category | flops | bytes accessed | tf_op | source)
XLA Modules:
  0.0 195.4 jit_solution(16959759953572172107)
XLA Ops:
  0.0 1.9 fusion.39
  2.5 3.4 %collective-permute-start = (bf16[1,3,1024]{2,1,0:T(4,128)(2,1)}, bf16[1,3,1024]{2,1,0:T(4,128)(2,1)}, u32[]{:S(2)}, u32[]{:S(2)}) collective-permute-start(bf16[1,3,1024]{2,1,0:T(4,128)(2,1)} %get-tuple-element.27), channel_id=1, source_target_pairs={{0,2},{2,4},{4,6},{6,8},{8,10},{10,12},{12,14},{1,3},{3,5},{5,7},{... | collective-permute-start | bytes 18440 | tf_op jit(solution)/shard_map/ppermute | solution.py:205
  5.9 3.5 %collective-permute-start.4 = (bf16[1,3,1024]{2,1,0:T(4,128)(2,1)S(1)}, bf16[1,3,1024]{2,1,0:T(4,128)(2,1)}, u32[]{:S(2)}, u32[]{:S(2)}) collective-permute-start(bf16[1,3,1024]{2,1,0:T(4,128)(2,1)S(1)} %get-tuple-element.28), channel_id=1, source_target_pairs={{2,0},{4,2},{6,4},{8,6},{10,8},{12,10},{14,12},{3,1},{5,3},{7,5},{... | collective-permute-start | bytes 18440 | tf_op jit(solution)/shard_map/ppermute | solution.py:206
  9.4 2.2 %fusion.45 = bf16[512,1024]{1,0:T(8,128)(2,1)} fusion(bf16[1,512,1024]{2,1,0:T(8,128)(2,1)S(1)} %fusion.39), kind=kOutput, calls=%fused_computation.59 | convolution fusion | flops 1076363264 | bytes 2097152 | tf_op jit(solution)/shard_map/...d,de->...e/dot_general | solution.py:28
  12.2 1.7 compare_select_fusion
  14.8 1.8 broadcast_multiply_fusion.1
  20.8 5.0 %reduce-window.16 = f32[1,2,16,2,128]{4,2,3,1,0:T(8,128)S(1)} reduce-window(f32[1,2,16,2,128]{4,2,3,1,0:T(8,128)S(1)} %copy.32, f32[]{:T(128)} %constant.13.clone.1), window={size=1x1x1x1x128 pad=0_0x0_0x0_0x0_0x0_127}, to_apply=%region_3.4 | reduce-window | flops 1040384 | bytes 65540 | tf_op jit(solution)/shard_map/reduce-window.2
  26.7 1.8 bitcast_exponential_fusion
  28.6 7.5 %convolution_bitcast_fusion = f32[1,512,2304]{2,1,0:T(8,128)} fusion(bf16[512,1024]{1,0:T(8,128)(2,1)} %fusion.45, bf16[1024,2304]{1,0:T(8,128)(2,1)} %param.15), kind=kOutput, calls=%fused_computation | convolution fusion | flops 2415919104 | bytes 10485760 | tf_op jit(solution)/shard_map/grd,de->gre/dot_general | solution.py:211
  36.2 4.3 %convolution_bitcast_fusion.1 = f32[1,512,2304]{2,1,0:T(8,128)} fusion(bf16[1024,2304]{1,0:T(8,128)(2,1)S(1)} %bitcast.231, bf16[1,512,1024]{2,1,0:T(8,128)(2,1)S(1)} %fusion.39), kind=kOutput, calls=%fused_computation.1 | convolution fusion | flops 2415919104 | bytes 10485760 | tf_op jit(solution)/shard_map/grd,de->gre/dot_general | solution.py:210
  40.6 1.7 multiply_bitcast_fusion.to_end_ref
  43.3 1.8 multiply_bitcast_fusion.1.to_end_ref
  49.8 2.9 %copy.30 = f32[1,512,1024]{2,1,0:T(8,128)} copy(f32[1,512,1024]{1,2,0:T(8,128)} %bitcast.212) | data formatting | bytes 4194304 | tf_op jit(solution)/shard_map/broadcast_in_dim | solution.py:184
  54.3 3.0 %copy.38 = f32[1,512,1024]{2,1,0:T(8,128)} copy(f32[1,512,1024]{1,2,0:T(8,128)} %bitcast.213) | data formatting | bytes 4194304 | tf_op jit(solution)/shard_map/broadcast_in_dim | solution.py:184
  57.3 3.6 %slice.203 = f32[1,512,1280]{2,1,0:T(8,128)} slice(f32[1,512,2304]{2,1,0:T(8,128)} %convolution_bitcast_fusion), slice={[0:1], [0:512], [1024:2304]} | slice | bytes 5242880 | tf_op jit(solution)/shard_map/slice | solution.py:144
  60.9 3.4 %slice.185 = f32[1,512,1280]{2,1,0:T(8,128)} slice(f32[1,512,2304]{2,1,0:T(8,128)} %convolution_bitcast_fusion.1), slice={[0:1], [0:512], [1024:2304]} | slice | bytes 5242880 | tf_op jit(solution)/shard_map/slice | solution.py:144
  65.5 2.4 %fusion.28 = f32[1,3,1280]{2,1,0:T(4,128)S(1)} fusion(bf16[1024,2304]{1,0:T(8,128)(2,1)} %param.15, bf16[1,3,1024]{2,1,0:T(4,128)(2,1)} %collective-permute-done.4), kind=kOutput, calls=%fused_computation.37 | convolution fusion | flops 16256000 | bytes 2644992 | tf_op jit(solution)/shard_map/grd,de->gre/dot_general | solution.py:213
  67.9 11.2 %multiply_convert_fusion.1 = (bf16[1,512,1280]{2,1,0:T(8,128)(2,1)}, bf16[1,512,1280]{2,1,0:T(8,128)(2,1)}) fusion(f32[1,512,1280]{2,1,0:T(8,128)} %slice.185, f32[1,3,1280]{2,1,0:T(4,128)S(1)} %fusion.25, f32[1280]{0:T(1024)S(1)} %get-tuple-element.13, f32[1280]{0:T(1024)S(1)} %get-tuple-element.14, f32[1280]{0:T(1024)S(1)} %get-tuple-element.12, ...), kind=kLoop, calls=%fused_computation.31 | loop fusion | flops 20971520 | bytes 7920640 | tf_op jit(solution)/shard_map/convert_element_type | solution.py:154
  79.1 5.1 %shard_map.121 = f32[2,16,64,128]{3,2,1,0:T(8,128)} custom-call(bf16[2,256,1280]{2,1,0:T(8,128)(2,1)} %bitcast.204, f32[2,256,16]{2,1,0:T(8,128)} %multiply_bitcast_fusion.to_end_ref), custom_call_target="tpu_custom_call" | custom-call | tf_op jit(solution)/shard_map/pallas_call | solution.py:121
  86.4 2.4 %collective-permute-start.5 = (f32[1,16,72,128]{3,2,1,0:T(8,128)}, f32[1,16,72,128]{3,2,1,0:T(8,128)}, u32[]{:S(2)}, u32[]{:S(2)}) collective-permute-start(f32[1,16,72,128]{3,2,1,0:T(8,128)} %pad_maximum_fusion.5), channel_id=1, source_target_pairs={{2,0},{4,2},{6,4},{8,6},{10,8},{12,10},{14,12},{3,1},{5,3},{7,5},{... | collective-permute-start | bytes 1769480 | tf_op jit(solution)/shard_map/ppermute | solution.py:48
  88.8 5.3 %shard_map.119 = f32[2,16,64,128]{3,2,1,0:T(8,128)} custom-call(bf16[2,256,1280]{2,1,0:T(8,128)(2,1)} %bitcast.202, f32[2,256,16]{2,1,0:T(8,128)} %multiply_bitcast_fusion.1.to_end_ref), custom_call_target="tpu_custom_call" | custom-call | tf_op jit(solution)/shard_map/pallas_call | solution.py:121
  95.7 4.2 %collective-permute-start.1 = (f32[1,16,72,128]{3,2,1,0:T(8,128)S(1)}, f32[1,16,72,128]{3,2,1,0:T(8,128)S(1)}, u32[]{:S(2)}, u32[]{:S(2)}) collective-permute-start(f32[1,16,72,128]{3,2,1,0:T(8,128)S(1)} %pad_maximum_fusion.2), channel_id=1, source_target_pairs={{0,2},{2,4},{4,6},{6,8},{8,10},{10,12},{12,14},{1,3},{3,5},{5,7},{... | collective-permute-start | bytes 1769480 | tf_op jit(solution)/shard_map/ppermute | solution.py:48
  99.9 15.9 %collective-permute-done.5 = f32[1,16,72,128]{3,2,1,0:T(8,128)} collective-permute-done((f32[1,16,72,128]{3,2,1,0:T(8,128)}, f32[1,16,72,128]{3,2,1,0:T(8,128)}, u32[]{:S(2)}, u32[]{:S(2)}) %collective-permute-start.5) | collective-permute-done | bytes 589856 | tf_op jit(solution)/shard_map/ppermute | solution.py:48
  119.1 3.2 %collective-permute-start.6 = (f32[1,16,72,128]{3,2,1,0:T(8,128)}, f32[1,16,72,128]{3,2,1,0:T(8,128)}, u32[]{:S(2)}, u32[]{:S(2)}) collective-permute-start(f32[1,16,72,128]{3,2,1,0:T(8,128)} %pad_maximum_fusion.6), channel_id=1, source_target_pairs={{4,0},{6,2},{8,4},{10,6},{12,8},{14,10},{5,1},{7,3},{9,5},{11,7},{... | collective-permute-start | bytes 1769480 | tf_op jit(solution)/shard_map/ppermute | solution.py:48
  127.3 5.5 %shard_map.120 = f32[2,256,1024]{2,1,0:T(8,128)} custom-call(bf16[2,256,1280]{2,1,0:T(8,128)(2,1)} %bitcast.205, f32[2,256,16]{2,1,0:T(8,128)} %bitcast.220, f32[2,16,256]{2,1,0:T(8,128)} %copy.35.cum_t_ref, f32[2,16,256]{2,1,0:T(8,128)} %bitcast.243), custom_call_target="tpu_custom_call" | custom-call | tf_op jit(solution)/shard_map/pallas_call | solution.py:128
  132.8 5.6 %shard_map.118 = f32[2,256,1024]{2,1,0:T(8,128)} custom-call(bf16[2,256,1280]{2,1,0:T(8,128)(2,1)} %bitcast.203, f32[2,256,16]{2,1,0:T(8,128)} %bitcast.223, f32[2,16,256]{2,1,0:T(8,128)} %copy.27.cum_t_ref, f32[2,16,256]{2,1,0:T(8,128)} %bitcast.242), custom_call_target="tpu_custom_call" | custom-call | tf_op jit(solution)/shard_map/pallas_call | solution.py:128
  142.3 3.7 %collective-permute-start.7 = (f32[1,16,72,128]{3,2,1,0:T(8,128)S(1)}, f32[1,16,72,128]{3,2,1,0:T(8,128)S(1)}, u32[]{:S(2)}, u32[]{:S(2)}) collective-permute-start(f32[1,16,72,128]{3,2,1,0:T(8,128)S(1)} %pad_maximum_fusion.7), channel_id=1, source_target_pairs={{8,0},{10,2},{12,4},{14,6},{9,1},{11,3},{13,5},{15,7},{24,16},{26,... | collective-permute-start | bytes 1769480 | tf_op jit(solution)/shard_map/ppermute | solution.py:48
  148.7 7.9 %collective-permute-done.7 = f32[1,16,72,128]{3,2,1,0:T(8,128)S(1)} collective-permute-done((f32[1,16,72,128]{3,2,1,0:T(8,128)S(1)}, f32[1,16,72,128]{3,2,1,0:T(8,128)S(1)}, u32[]{:S(2)}, u32[]{:S(2)}) %collective-permute-start.7) | collective-permute-done | bytes 589856 | tf_op jit(solution)/shard_map/ppermute | solution.py:48
  159.2 16.5 %collective-permute-done.3 = f32[1,16,72,128]{3,2,1,0:T(8,128)S(1)} collective-permute-done((f32[1,16,72,128]{3,2,1,0:T(8,128)S(1)}, f32[1,16,72,128]{3,2,1,0:T(8,128)S(1)}, u32[]{:S(2)}, u32[]{:S(2)}) %collective-permute-start.3) | collective-permute-done | bytes 589856 | tf_op jit(solution)/shard_map/ppermute | solution.py:48
  179.5 4.9 %multiply_reduce_fusion.1 = (f32[512]{0:T(512)S(1)}, f32[1,512,1024]{2,1,0:T(8,128)}, f32[512]{0:T(512)S(1)}, f32[1,512,1024]{2,1,0:T(8,128)}) fusion(f32[1,512,2304]{2,1,0:T(8,128)} %convolution_bitcast_fusion.1, bf16[1,512,1280]{2,1,0:T(8,128)(2,1)S(1)} %copy-done.1, f32[1024]{0:T(1024)S(1)} %mul.508, f32[1,512,1024]{2,1,0:T(8,128)S(1)} %copy-done.7, ...), kind=kLoop, calls=%fused_computation.58 | loop fusion | flops 12581888 | bytes 23076864 | tf_op jit(solution)/shard_map/reduce_sum | solution.py:190
  184.5 6.4 %fusion.40 = f32[512,1024]{1,0:T(8,128)} fusion(bf16[1024,1024]{1,0:T(8,128)(2,1)S(1)} %copy-done, f32[1,512,1024]{2,1,0:T(8,128)} %get-tuple-element.36, f32[512]{0:T(512)S(1)} %add_rsqrt_fusion, f32[1024]{0:T(1024)S(1)} %copy-done.23), kind=kOutput, calls=%fused_computation.50 | convolution fusion | flops 3226992640 | bytes 6297600 | tf_op jit(solution)/shard_map/grk,kd->grd/dot_general | solution.py:229
  190.9 4.5 %fusion.46 = bf16[1,512,1024]{2,1,0:T(8,128)(2,1)} fusion(f32[512,1024]{1,0:T(8,128)} %fusion.40, bf16[1024,1024]{1,0:T(8,128)(2,1)S(1)} %copy-done, f32[1,512,1024]{2,1,0:T(8,128)} %get-tuple-element.16, f32[1024]{0:T(1024)S(1)} %copy-done.23, f32[512]{0:T(512)S(1)} %add_rsqrt_fusion.1), kind=kOutput, calls=%fused_computation.60 | convolution fusion | flops 1076363264 | bytes 7346176 | tf_op jit(solution)/shard_map/grk,kd->grd/dot_general | solution.py:227
  (139 shorter events, 40.8 us)
Async XLA Ops:
  0.0 184.5 %copy-start = (bf16[1024,1024]{1,0:T(8,128)(2,1)S(1)}, bf16[1024,1024]{1,0:T(8,128)(2,1)}, u32[]{:S(2)}) copy-start(bf16[1024,1024]{1,0:T(8,128)(2,1)} %param.23) | copy-start | bytes 6291460
  2.5 61.8 %collective-permute-start = (bf16[1,3,1024]{2,1,0:T(4,128)(2,1)}, bf16[1,3,1024]{2,1,0:T(4,128)(2,1)}, u32[]{:S(2)}, u32[]{:S(2)}) collective-permute-start(bf16[1,3,1024]{2,1,0:T(4,128)(2,1)} %get-tuple-element.27), channel_id=1, source_target_pairs={{0,2},{2,4},{4,6},{6,8},{8,10},{10,12},{12,14},{1,3},{3,5},{5,7},{... | collective-permute-start | bytes 18440 | tf_op jit(solution)/shard_map/ppermute | solution.py:205
  5.9 5.7 %copy-start.24 = (f32[16]{0:T(128)S(1)}, f32[16]{0:T(128)}, u32[]{:S(2)}) copy-start(f32[16]{0:T(128)} %param.20) | copy-start | bytes 196
  5.9 5.7 %copy-start.18 = (bf16[1024,16]{0,1:T(8,128)(2,1)S(1)}, bf16[1024,16]{0,1:T(8,128)(2,1)}, u32[]{:S(2)}) copy-start(bf16[1024,16]{0,1:T(8,128)(2,1)} %param.16) | copy-start | bytes 98308
  5.9 5.7 %copy-start.21 = (f32[16]{0:T(128)S(1)}, f32[16]{0:T(128)}, u32[]{:S(2)}) copy-start(f32[16]{0:T(128)} %param.19) | copy-start | bytes 196
  5.9 59.5 %collective-permute-start.4 = (bf16[1,3,1024]{2,1,0:T(4,128)(2,1)S(1)}, bf16[1,3,1024]{2,1,0:T(4,128)(2,1)}, u32[]{:S(2)}, u32[]{:S(2)}) collective-permute-start(bf16[1,3,1024]{2,1,0:T(4,128)(2,1)S(1)} %get-tuple-element.28), channel_id=1, source_target_pairs={{2,0},{4,2},{6,4},{8,6},{10,8},{12,10},{14,12},{3,1},{5,3},{7,5},{... | collective-permute-start | bytes 18440 | tf_op jit(solution)/shard_map/ppermute | solution.py:206
  12.2 14.6 %copy-start.14 = (f32[512,16]{1,0:T(8,128)}, f32[512,16]{1,0:T(8,128)S(1)}, u32[]{:S(2)}) copy-start(f32[512,16]{1,0:T(8,128)S(1)} %copy.23) | copy-start | bytes 98308
  26.7 9.4 %slice-start = ((s8[4718592]{0:T(1024)(128)(4,1)}), s8[4194304]{0:T(1024)(128)(4,1)S(1)}, s32[]{:S(2)}) async-start(s8[4718592]{0:T(1024)(128)(4,1)} %bitcast.230), calls=%async_computation | async-start | bytes 8388608
  28.6 18.0 %copy-start.12 = (f32[1,2,16,256]{2,3,1,0:T(8,128)}, f32[1,2,16,256]{2,3,1,0:T(8,128)S(1)}, u32[]{:S(2)}) copy-start(f32[1,2,16,256]{2,3,1,0:T(8,128)S(1)} %get-tuple-element.26) | copy-start | bytes 98308
  28.6 7.5 %slice-start.1 = ((s8[4718592]{0:T(1024)(128)(4,1)}), s8[524288]{0:T(1024)(128)(4,1)S(1)}, s32[]{:S(2)}) async-start(s8[4718592]{0:T(1024)(128)(4,1)} %bitcast.230), calls=%async_computation.1 | async-start | bytes 1048576
  36.2 4.3 %copy-start.19 = (f32[4,1280]{1,0:T(4,128)S(1)}, f32[4,1280]{1,0:T(4,128)}, u32[]{:S(2)}) copy-start(f32[4,1280]{1,0:T(4,128)} %param.17) | copy-start | bytes 61444
  36.2 8.9 %copy-start.22 = (f32[16]{0:T(128)S(1)}, f32[16]{0:T(128)}, u32[]{:S(2)}) copy-start(f32[16]{0:T(128)} %param.21) | copy-start | bytes 196
  40.5 6.0 %copy-start.17 = (f32[1,2,256,16]{3,2,1,0:T(8,128)S(1)}, f32[1,2,256,16]{3,2,1,0:T(8,128)}, u32[]{:S(2)}) copy-start(f32[1,2,256,16]{3,2,1,0:T(8,128)} %get-tuple-element.25) | copy-start | bytes 98308
  43.2 9.5 %copy-start.13 = (f32[1,2,16,256]{2,3,1,0:T(8,128)}, f32[1,2,16,256]{2,3,1,0:T(8,128)S(1)}, u32[]{:S(2)}) copy-start(f32[1,2,16,256]{2,3,1,0:T(8,128)S(1)} %get-tuple-element.20) | copy-start | bytes 98308
  54.3 10.0 %slice-start.2 = ((s8[4718592]{0:T(1024)(128)(4,1)}), s8[524288]{0:T(1024)(128)(4,1)S(1)}, s32[]{:S(2)}) async-start(s8[4718592]{0:T(1024)(128)(4,1)} %bitcast.232), calls=%async_computation.2 | async-start | bytes 1048576
  57.3 7.0 %slice-start.3 = ((s8[4718592]{0:T(1024)(128)(4,1)}), s8[4194304]{0:T(1024)(128)(4,1)S(1)}, s32[]{:S(2)}) async-start(s8[4718592]{0:T(1024)(128)(4,1)} %bitcast.232), calls=%async_computation.3 | async-start | bytes 8388608
  86.4 29.4 %collective-permute-start.5 = (f32[1,16,72,128]{3,2,1,0:T(8,128)}, f32[1,16,72,128]{3,2,1,0:T(8,128)}, u32[]{:S(2)}, u32[]{:S(2)}) collective-permute-start(f32[1,16,72,128]{3,2,1,0:T(8,128)} %pad_maximum_fusion.5), channel_id=1, source_target_pairs={{2,0},{4,2},{6,4},{8,6},{10,8},{12,10},{14,12},{3,1},{5,3},{7,5},{... | collective-permute-start | bytes 1769480 | tf_op jit(solution)/shard_map/ppermute | solution.py:48
  94.1 22.7 %copy-start.4 = (f32[2,16,64,128]{3,2,1,0:T(8,128)S(1)}, f32[2,16,64,128]{3,2,1,0:T(8,128)}, u32[]{:S(2)}) copy-start(f32[2,16,64,128]{3,2,1,0:T(8,128)} %shard_map.121) | copy-start | bytes 3145732
  95.5 26.7 %copy-start.3 = (f32[2,16,64,128]{3,2,1,0:T(8,128)S(1)}, f32[2,16,64,128]{3,2,1,0:T(8,128)}, u32[]{:S(2)}) copy-start(f32[2,16,64,128]{3,2,1,0:T(8,128)} %shard_map.119) | copy-start | bytes 3145732
  95.7 26.6 %collective-permute-start.1 = (f32[1,16,72,128]{3,2,1,0:T(8,128)S(1)}, f32[1,16,72,128]{3,2,1,0:T(8,128)S(1)}, u32[]{:S(2)}, u32[]{:S(2)}) collective-permute-start(f32[1,16,72,128]{3,2,1,0:T(8,128)S(1)} %pad_maximum_fusion.2), channel_id=1, source_target_pairs={{0,2},{2,4},{4,6},{6,8},{8,10},{10,12},{12,14},{1,3},{3,5},{5,7},{... | collective-permute-start | bytes 1769480 | tf_op jit(solution)/shard_map/ppermute | solution.py:48
  118.1 6.1 %copy-start.11 = (f32[1,16,64,128]{3,2,1,0:T(8,128)}, f32[1,16,64,128]{3,2,1,0:T(8,128)S(1)}, u32[]{:S(2)}) copy-start(f32[1,16,64,128]{3,2,1,0:T(8,128)S(1)} %multiply_add_fusion.3) | copy-start | bytes 1572868
  119.1 20.6 %collective-permute-start.6 = (f32[1,16,72,128]{3,2,1,0:T(8,128)}, f32[1,16,72,128]{3,2,1,0:T(8,128)}, u32[]{:S(2)}, u32[]{:S(2)}) collective-permute-start(f32[1,16,72,128]{3,2,1,0:T(8,128)} %pad_maximum_fusion.6), channel_id=1, source_target_pairs={{4,0},{6,2},{8,4},{10,6},{12,8},{14,10},{5,1},{7,3},{9,5},{11,7},{... | collective-permute-start | bytes 1769480 | tf_op jit(solution)/shard_map/ppermute | solution.py:48
  122.3 3.2 %copy-start.15 = (f32[1,16,72,128]{3,2,1,0:T(8,128)}, f32[1,16,72,128]{3,2,1,0:T(8,128)S(1)}, u32[]{:S(2)}) copy-start(f32[1,16,72,128]{3,2,1,0:T(8,128)S(1)} %collective-permute-done.1) | copy-start | bytes 1769476
  124.2 16.8 %collective-permute-start.2 = (f32[1,16,72,128]{3,2,1,0:T(8,128)}, f32[1,16,72,128]{3,2,1,0:T(8,128)}, u32[]{:S(2)}, u32[]{:S(2)}) collective-permute-start(f32[1,16,72,128]{3,2,1,0:T(8,128)} %pad_maximum_fusion.3), channel_id=1, source_target_pairs={{0,4},{2,6},{4,8},{6,10},{8,12},{10,14},{1,5},{3,7},{5,9},{7,11},{... | collective-permute-start | bytes 1769480 | tf_op jit(solution)/shard_map/ppermute | solution.py:48
  138.4 2.6 %copy-start.16 = (f32[1,16,72,128]{3,2,1,0:T(8,128)S(1)}, f32[1,16,72,128]{3,2,1,0:T(8,128)}, u32[]{:S(2)}) copy-start(f32[1,16,72,128]{3,2,1,0:T(8,128)} %copy-done.15) | copy-start | bytes 1769476
  138.4 7.7 %copy-start.10 = (f32[1,16,64,128]{3,2,1,0:T(8,128)S(1)}, f32[1,16,64,128]{3,2,1,0:T(8,128)}, u32[]{:S(2)}) copy-start(f32[1,16,64,128]{3,2,1,0:T(8,128)} %copy-done.9) | copy-start | bytes 1572868
  142.3 14.3 %collective-permute-start.7 = (f32[1,16,72,128]{3,2,1,0:T(8,128)S(1)}, f32[1,16,72,128]{3,2,1,0:T(8,128)S(1)}, u32[]{:S(2)}, u32[]{:S(2)}) collective-permute-start(f32[1,16,72,128]{3,2,1,0:T(8,128)S(1)} %pad_maximum_fusion.7), channel_id=1, source_target_pairs={{8,0},{10,2},{12,4},{14,6},{9,1},{11,3},{13,5},{15,7},{24,16},{26,... | collective-permute-start | bytes 1769480 | tf_op jit(solution)/shard_map/ppermute | solution.py:48
  147.4 28.3 %collective-permute-start.3 = (f32[1,16,72,128]{3,2,1,0:T(8,128)S(1)}, f32[1,16,72,128]{3,2,1,0:T(8,128)S(1)}, u32[]{:S(2)}, u32[]{:S(2)}) collective-permute-start(f32[1,16,72,128]{3,2,1,0:T(8,128)S(1)} %pad_maximum_fusion.4), channel_id=1, source_target_pairs={{0,8},{2,10},{4,12},{6,14},{1,9},{3,11},{5,13},{7,15},{16,24},{18,... | collective-permute-start | bytes 1769480 | tf_op jit(solution)/shard_map/ppermute | solution.py:48
  158.0 20.3 %copy-start.8 = (f32[1,512,1024]{2,1,0:T(8,128)S(1)}, f32[1,512,1024]{2,1,0:T(8,128)}, u32[]{:S(2)}) copy-start(f32[1,512,1024]{2,1,0:T(8,128)} %copy.38) | copy-start | bytes 6291460
  158.2 20.1 %copy-start.7 = (f32[1,512,1024]{2,1,0:T(8,128)S(1)}, f32[1,512,1024]{2,1,0:T(8,128)}, u32[]{:S(2)}) copy-start(f32[1,512,1024]{2,1,0:T(8,128)} %copy.30) | copy-start | bytes 6291460
  175.7 2.6 %copy-start.6 = (f32[2,256,1024]{2,1,0:T(8,128)S(1)}, f32[2,256,1024]{2,1,0:T(8,128)}, u32[]{:S(2)}) copy-start(f32[2,256,1024]{2,1,0:T(8,128)} %shard_map.118) | copy-start | bytes 6291460
  179.5 4.9 %copy-start.23 = (f32[1024]{0:T(1024)S(1)}, f32[1024]{0:T(1024)}, u32[]{:S(2)}) copy-start(f32[1024]{0:T(1024)} %param.22) | copy-start | bytes 12292
  (5 other events, 8.9 us)

commit v5 on v4

--- a/solution.py
+++ b/solution.py
@@ -109,7 +109,10 @@
     spans = rows // Q
     blocks = count * spans
     steps_cut = step_size.reshape(count, spans, Q, H)
-    log_decay = lax.cumsum(steps_cut * rates, axis=2, reverse=reverse)
+    rated = steps_cut * rates
+    log_decay = jnp.cumsum(rated, axis=2)
+    if reverse:
+        log_decay = log_decay[:, :, -1:] - log_decay + rated
     end = log_decay[:, :, 0] if reverse else log_decay[:, :, -1]
     to_end = jnp.exp(end[:, :, None, :] - log_decay) * steps_cut
     flat = lambda a: a.reshape((blocks,) + a.shape[2:])
@@ -137,21 +140,70 @@
     return inside, state, jnp.exp(end), jnp.exp(log_decay)
 
 
+CONV_LANES = 256
+
+
+def conv_kernel(src_ref, halo_ref, w_ref, b_ref, out_ref, *, reverse):
+    margin = KCONV - 1
+    src = src_ref[...]
+    rows = src.shape[0]
+    edge = halo_ref.shape[0]
+    w = w_ref[...]
+    if reverse:
+        near = jnp.concatenate([src[rows - edge :], halo_ref[...]], axis=0)
+    else:
+        near = jnp.concatenate([halo_ref[...], src[:edge]], axis=0)
+    span = near.shape[0]
+    main = jnp.broadcast_to(b_ref[...], src.shape)
+    side = jnp.broadcast_to(b_ref[...], (edge, src.shape[1]))
+    for tap in range(KCONV):
+        shift = margin - tap
+        if shift == 0:
+            piece, near_piece = src, near
+        elif reverse:
+            piece = pltpu.roll(src, rows - shift, 0)
+            near_piece = pltpu.roll(near, span - shift, 0)
+        else:
+            piece = pltpu.roll(src, shift, 0)
+            near_piece = pltpu.roll(near, shift, 0)
+        main = main + w[tap : tap + 1] * piece
+        part = near_piece[:edge] if reverse else near_piece[edge:]
+        side = side + w[tap : tap + 1] * part
+    out_ref[...] = jax.nn.silu(main).astype(out_ref.dtype)
+    if reverse:
+        out_ref[rows - edge :, :] = jax.nn.silu(side).astype(out_ref.dtype)
+    else:
+        out_ref[:edge, :] = jax.nn.silu(side).astype(out_ref.dtype)
+
+
+def convolve(projected, halo, conv_w, conv_b, reverse):
+    inner = H * P_SIZE
+    count, rows, _ = projected.shape
+    width = conv_w.shape[1]
+    edge = 8
+    margin = KCONV - 1
+    pad = ((0, 0), (0, edge - margin), (0, 0)) if reverse else ((0, 0), (edge - margin, 0), (0, 0))
+    halo8 = jnp.pad(halo, pad)
+    lanes = CONV_LANES
+    skip = inner // lanes
+    return pl.pallas_call(
+        partial(conv_kernel, reverse=reverse),
+        grid=(count, width // lanes),
+        in_specs=[
+            pl.BlockSpec((None, rows, lanes), lambda g, j: (g, 0, j + skip)),
+            pl.BlockSpec((None, edge, lanes), lambda g, j: (g, 0, j)),
+            pl.BlockSpec((KCONV, lanes), lambda g, j: (0, j)),
+            pl.BlockSpec((1, lanes), lambda g, j: (0, j)),
+        ],
+        out_specs=pl.BlockSpec((None, rows, lanes), lambda g, j: (g, 0, j)),
+        out_shape=jax.ShapeDtypeStruct((count, rows, width), jnp.bfloat16),
+    )(projected, halo8, conv_w, conv_b.reshape(1, width))
+
+
 def strand_terms(projected, halo, step_size, conv_w, conv_b, rates, reverse):
     inner = H * P_SIZE
     count, rows, _ = projected.shape
-    margin = KCONV - 1
-    source = projected[:, :, inner:]
-    if reverse:
-        padded = jnp.concatenate([source, halo], axis=1)
-        taps = [(tap, margin - tap) for tap in range(KCONV)]
-    else:
-        padded = jnp.concatenate([halo, source], axis=1)
-        taps = [(tap, tap) for tap in range(KCONV)]
-    summed = jnp.broadcast_to(conv_b, source.shape)
-    for tap, start in taps:
-        summed = summed + conv_w[tap] * padded[:, start : start + rows]
-    activated = jax.nn.silu(summed).astype(jnp.bfloat16)
+    activated = convolve(projected, halo, conv_w, conv_b, reverse)
     spans = rows // Q
     inside, state, total, from_start = block_terms(activated, step_size, rates, reverse)
     order = list(range(spans))

time: 198 us -> 184 us (0.929)
  other arithmetic: 46.7 us -> 32.4 us
  Pallas kernels: 21.5 us -> 31.5 us
  waiting for transfers between devices: 40.2 us -> 31.2 us
  local copies, waits for them, and re-layouts: 29.1 us -> 26.2 us
    convert_element_type x1 -> x0, other arithmetic: 11.2 us -> none  [strand_terms(): activated = jax.nn.silu(summed).astype(jnp.bfloat16)]
    pallas_call x0 -> x2, Pallas kernels: none -> 10.2 us  [convolve(): pl.pallas_call(partial(conv_kernel, reverse=reverse), grid=(count, width...]
    ppermute x6, waiting for transfers between devices: 40.2 us -> 31.2 us  [exclusive_scans(): decay, state = unpack(lax.ppermute(pack(*ahead[k]), axis, pairs))]
    slice x4 -> x2, local copies, waits for them, and re-layouts: 7.21 us -> 0.16 us  [the longest x2 7 us: strand_terms(): source = projected[:, :, inner:]]
    another operation x4 -> x5, other arithmetic: 6.18 us -> 3.32 us
  transfers between devices with their start and end apart: 8 -> 8, of which waited for: 3 -> 3; matrix products, arithmetic and copies ran while one was open for 36% -> 39% of each run, Pallas kernels for 8% -> 17%
where the time goes in v5:
time: 184 us; the launch traced here: 181 us
  matrix products  35.5 us (19%)
  other arithmetic  32.4 us (18%)
  Pallas kernels  31.5 us (17%)
  waiting for transfers between devices  31.2 us (17%)
  local copies, waits for them, and re-layouts  26.2 us (14%)
  starting transfers between devices  23.2 us (13%)
    ppermute x6, waiting for transfers between devices, exclusive_scans(): decay, state = unpack(lax.ppermute(pack(*ahead[k]), axis, pairs))  31.2 us
    ppermute x6, starting transfers between devices, exclusive_scans(): decay, state = unpack(lax.ppermute(pack(*ahead[k]), axis, pairs))  16.4 us
    pallas_call x2, Pallas kernels, block_terms(): pl.pallas_call(partial(inside_kernel, reverse=reverse), grid=(blocks,), i...  11.1 us
    pallas_call x2, Pallas kernels, convolve(): pl.pallas_call(partial(conv_kernel, reverse=reverse), grid=(count, width...  10.2 us
    pallas_call x2, Pallas kernels, block_terms(): pl.pallas_call(state_kernel, grid=(blocks,), in_specs=[spec((Q, width)),...  10.2 us
    broadcast_in_dim x4, local copies, waits for them, and re-layouts, finish(): scale = jnp.repeat(from_start.reshape(count, rows, H), P_SIZE, axis=-1)  9.13 us
    add x8, other arithmetic, chain(): next_decay[..., None, None] * first_state + next_state  7.99 us
    dot_general x1, matrix products, on_device(): jnp.einsum('grd,de->gre', mirrored, w_in, preferred_element_type=jnp.floa...  7.52 us
  transfers between devices with their start and end apart: 8, of which 3 were waited for; matrix products, arithmetic and copies ran while one was open for 39% of the time, Pallas kernels for 17%

profile of v5, /device:TPU:24, one launch (start us, length us, event | category | flops | bytes accessed | tf_op | source)
XLA Modules:
  0.0 180.6 jit_solution(9392338403020872519)
XLA Ops:
  0.0 1.9 %fusion.21 = bf16[1,512,1024]{2,1,0:T(8,128)(2,1)S(1)} fusion(bf16[1,512,1024]{2,1,0:T(8,128)(2,1)} %param.13, bf16[4,1024]{1,0:T(4,128)(2,1)} %param.14, s32[512]{0:T(512)} %bitcast.249), kind=kOutput, calls=%fused_computation.22 | convolution fusion | flops 5769216 | bytes 2107392 | tf_op jit(solution)/shard_map/gtb,bd->gtd/dot_general | solution.py:253
  2.5 3.4 %collective-permute-start = (bf16[1,3,1024]{2,1,0:T(4,128)(2,1)S(1)}, bf16[1,3,1024]{2,1,0:T(4,128)(2,1)}, u32[]{:S(2)}, u32[]{:S(2)}) collective-permute-start(bf16[1,3,1024]{2,1,0:T(4,128)(2,1)S(1)} %get-tuple-element.23), channel_id=1, source_target_pairs={{0,2},{2,4},{4,6},{6,8},{8,10},{10,12},{12,14},{1,3},{3,5},{5,7},{... | collective-permute-start | bytes 18440 | tf_op jit(solution)/shard_map/ppermute | solution.py:257
  5.9 3.5 %collective-permute-start.4 = (bf16[1,3,1024]{2,1,0:T(4,128)(2,1)}, bf16[1,3,1024]{2,1,0:T(4,128)(2,1)}, u32[]{:S(2)}, u32[]{:S(2)}) collective-permute-start(bf16[1,3,1024]{2,1,0:T(4,128)(2,1)} %get-tuple-element.24), channel_id=1, source_target_pairs={{2,0},{4,2},{6,4},{8,6},{10,8},{12,10},{14,12},{3,1},{5,3},{7,5},{... | collective-permute-start | bytes 18440 | tf_op jit(solution)/shard_map/ppermute | solution.py:258
  9.4 2.2 %fusion.27 = bf16[512,1024]{1,0:T(8,128)(2,1)} fusion(bf16[1,512,1024]{2,1,0:T(8,128)(2,1)S(1)} %fusion.21), kind=kOutput, calls=%fused_computation.33 | convolution fusion | flops 1076363264 | bytes 2097152 | tf_op jit(solution)/shard_map/...d,de->...e/dot_general | solution.py:28
  12.9 1.6 compare_select_fusion
  15.3 1.8 broadcast_multiply_fusion.1
  20.4 1.7 fusion.74
  27.0 1.9 %bitcast_exponential_fusion = (f32[1,2,256,16]{3,2,1,0:T(8,128)}, f32[1,2,16,256]{2,3,1,0:T(8,128)S(1)}) fusion(f32[2,16,2]{1,2,0:T(2,128)S(1)} %slice_bitcast_fusion.3, f32[1,2,16,2,128]{2,4,3,1,0:T(8,128)} %copy.25), kind=kLoop, calls=%fused_computation.115 | loop fusion | flops 8192 | bytes 98560 | tf_op jit(solution)/shard_map/exp | solution.py:140
  28.9 7.5 %convolution_bitcast_fusion.src_ref = f32[1,512,2304]{2,1,0:T(8,128)} fusion(bf16[512,1024]{1,0:T(8,128)(2,1)} %fusion.27, bf16[1024,2304]{1,0:T(8,128)(2,1)} %param.15), kind=kOutput, calls=%fused_computation | convolution fusion | flops 2415919104 | bytes 10485760 | tf_op jit(solution)/shard_map/grd,de->gre/dot_general | solution.py:263
  36.5 4.3 %convolution_bitcast_fusion.1.src_ref = f32[1,512,2304]{2,1,0:T(8,128)} fusion(bf16[1024,2304]{1,0:T(8,128)(2,1)S(1)} %bitcast.229, bf16[1,512,1024]{2,1,0:T(8,128)(2,1)S(1)} %fusion.21), kind=kOutput, calls=%fused_computation.1 | convolution fusion | flops 2415919104 | bytes 10485760 | tf_op jit(solution)/shard_map/grd,de->gre/dot_general | solution.py:262
  46.3 1.7 copy.27.cum_t_ref
  47.9 1.7 broadcast_in_dim.37
  49.6 2.9 %copy.30 = f32[1,512,1024]{2,1,0:T(8,128)} copy(f32[1,512,1024]{1,2,0:T(8,128)} %bitcast.210) | data formatting | bytes 4194304 | tf_op jit(solution)/shard_map/broadcast_in_dim | solution.py:236
  54.1 3.0 %copy.38 = f32[1,512,1024]{2,1,0:T(8,128)} copy(f32[1,512,1024]{1,2,0:T(8,128)} %bitcast.211) | data formatting | bytes 4194304 | tf_op jit(solution)/shard_map/broadcast_in_dim | solution.py:236
  57.1 2.4 %fusion.10 = f32[1,3,1280]{2,1,0:T(4,128)S(1)} fusion(bf16[1024,2304]{1,0:T(8,128)(2,1)} %param.15, bf16[1,3,1024]{2,1,0:T(4,128)(2,1)} %collective-permute-done.4), kind=kOutput, calls=%fused_computation.11 | convolution fusion | flops 16256000 | bytes 2644992 | tf_op jit(solution)/shard_map/grd,de->gre/dot_general | solution.py:265
  60.1 5.1 %shard_map.121 = bf16[1,512,1280]{2,1,0:T(8,128)(2,1)} custom-call(f32[1,512,2304]{2,1,0:T(8,128)} %convolution_bitcast_fusion.src_ref, f32[1,8,1280]{2,1,0:T(8,128)} %pad.13.halo_ref, f32[4,1280]{1,0:T(4,128)} %w_ref.3, f32[1,1280]{1,0:T(1,128)} %reshape.614.b_ref), custom_call_target="tpu_custom_call" | custom-call | tf_op jit(solution)/shard_map/pallas_call | solution.py:189
  65.3 5.1 %shard_map.123 = f32[2,16,64,128]{3,2,1,0:T(8,128)} custom-call(bf16[2,256,1280]{2,1,0:T(8,128)(2,1)} %bitcast.200, f32[2,256,16]{2,1,0:T(8,128)} %multiply_bitcast_fusion.to_end_ref), custom_call_target="tpu_custom_call" | custom-call | tf_op jit(solution)/shard_map/pallas_call | solution.py:124
  72.7 2.4 %collective-permute-start.5 = (f32[1,16,72,128]{3,2,1,0:T(8,128)}, f32[1,16,72,128]{3,2,1,0:T(8,128)}, u32[]{:S(2)}, u32[]{:S(2)}) collective-permute-start(f32[1,16,72,128]{3,2,1,0:T(8,128)} %pad_maximum_fusion.3), channel_id=1, source_target_pairs={{2,0},{4,2},{6,4},{8,6},{10,8},{12,10},{14,12},{3,1},{5,3},{7,5},{... | collective-permute-start | bytes 1769480 | tf_op jit(solution)/shard_map/ppermute | solution.py:48
  75.1 2.2 %fusion.7 = f32[1,3,1280]{2,1,0:T(4,128)S(1)} fusion(bf16[1024,2304]{1,0:T(8,128)(2,1)} %param.15, bf16[1,3,1024]{2,1,0:T(4,128)(2,1)} %collective-permute-done), kind=kOutput, calls=%fused_computation.10 | convolution fusion | flops 7864320 | bytes 2644992 | tf_op jit(solution)/shard_map/grd,de->gre/dot_general | solution.py:264
  77.9 5.1 %shard_map.118 = bf16[1,512,1280]{2,1,0:T(8,128)(2,1)} custom-call(f32[1,512,2304]{2,1,0:T(8,128)} %convolution_bitcast_fusion.1.src_ref, f32[1,8,1280]{2,1,0:T(8,128)} %pad.12.halo_ref, f32[4,1280]{1,0:T(4,128)} %w_ref.3, f32[1,1280]{1,0:T(1,128)} %reshape.614.b_ref), custom_call_target="tpu_custom_call" | custom-call | tf_op jit(solution)/shard_map/pallas_call | solution.py:189
  83.0 5.1 %shard_map.120 = f32[2,16,64,128]{3,2,1,0:T(8,128)} custom-call(bf16[2,256,1280]{2,1,0:T(8,128)(2,1)} %bitcast.202, f32[2,256,16]{2,1,0:T(8,128)} %multiply_bitcast_fusion.1.to_end_ref), custom_call_target="tpu_custom_call" | custom-call | tf_op jit(solution)/shard_map/pallas_call | solution.py:124
  89.7 4.6 %collective-permute-start.1 = (f32[1,16,72,128]{3,2,1,0:T(8,128)S(1)}, f32[1,16,72,128]{3,2,1,0:T(8,128)S(1)}, u32[]{:S(2)}, u32[]{:S(2)}) collective-permute-start(f32[1,16,72,128]{3,2,1,0:T(8,128)S(1)} %pad_maximum_fusion), channel_id=1, source_target_pairs={{0,2},{2,4},{4,6},{6,8},{8,10},{10,12},{12,14},{1,3},{3,5},{5,7},{... | collective-permute-start | bytes 1769480 | tf_op jit(solution)/shard_map/ppermute | solution.py:48
  97.6 2.4 %collective-permute-start.6 = (f32[1,16,72,128]{3,2,1,0:T(8,128)}, f32[1,16,72,128]{3,2,1,0:T(8,128)}, u32[]{:S(2)}, u32[]{:S(2)}) collective-permute-start(f32[1,16,72,128]{3,2,1,0:T(8,128)} %pad_maximum_fusion.4), channel_id=1, source_target_pairs={{4,0},{6,2},{8,4},{10,6},{12,8},{14,10},{5,1},{7,3},{9,5},{11,7},{... | collective-permute-start | bytes 1769480 | tf_op jit(solution)/shard_map/ppermute | solution.py:48
  100.0 6.9 %collective-permute-done.1 = f32[1,16,72,128]{3,2,1,0:T(8,128)S(1)} collective-permute-done((f32[1,16,72,128]{3,2,1,0:T(8,128)S(1)}, f32[1,16,72,128]{3,2,1,0:T(8,128)S(1)}, u32[]{:S(2)}, u32[]{:S(2)}) %collective-permute-start.1) | collective-permute-done | bytes 589856 | tf_op jit(solution)/shard_map/ppermute | solution.py:48
  111.9 5.5 %shard_map.122 = f32[2,256,1024]{2,1,0:T(8,128)} custom-call(bf16[2,256,1280]{2,1,0:T(8,128)(2,1)} %bitcast.201, f32[2,256,16]{2,1,0:T(8,128)} %bitcast.217, f32[2,16,256]{2,1,0:T(8,128)} %copy.35.cum_t_ref, f32[2,16,256]{2,1,0:T(8,128)} %bitcast.239), custom_call_target="tpu_custom_call" | custom-call | tf_op jit(solution)/shard_map/pallas_call | solution.py:131
  117.4 5.5 %shard_map.119 = f32[2,256,1024]{2,1,0:T(8,128)} custom-call(bf16[2,256,1280]{2,1,0:T(8,128)(2,1)} %bitcast.203, f32[2,256,16]{2,1,0:T(8,128)} %bitcast.220, f32[2,16,256]{2,1,0:T(8,128)} %copy.27.cum_t_ref, f32[2,16,256]{2,1,0:T(8,128)} %bitcast.238), custom_call_target="tpu_custom_call" | custom-call | tf_op jit(solution)/shard_map/pallas_call | solution.py:131
  126.9 4.5 %collective-permute-start.7 = (f32[1,16,72,128]{3,2,1,0:T(8,128)S(1)}, f32[1,16,72,128]{3,2,1,0:T(8,128)S(1)}, u32[]{:S(2)}, u32[]{:S(2)}) collective-permute-start(f32[1,16,72,128]{3,2,1,0:T(8,128)S(1)} %pad_maximum_fusion.5), channel_id=1, source_target_pairs={{8,0},{10,2},{12,4},{14,6},{9,1},{11,3},{13,5},{15,7},{24,16},{26,... | collective-permute-start | bytes 1769480 | tf_op jit(solution)/shard_map/ppermute | solution.py:48
  134.1 7.9 %collective-permute-done.7 = f32[1,16,72,128]{3,2,1,0:T(8,128)S(1)} collective-permute-done((f32[1,16,72,128]{3,2,1,0:T(8,128)S(1)}, f32[1,16,72,128]{3,2,1,0:T(8,128)S(1)}, u32[]{:S(2)}, u32[]{:S(2)}) %collective-permute-start.7) | collective-permute-done | bytes 589856 | tf_op jit(solution)/shard_map/ppermute | solution.py:48
  144.6 16.5 %collective-permute-done.3 = f32[1,16,72,128]{3,2,1,0:T(8,128)S(1)} collective-permute-done((f32[1,16,72,128]{3,2,1,0:T(8,128)S(1)}, f32[1,16,72,128]{3,2,1,0:T(8,128)S(1)}, u32[]{:S(2)}, u32[]{:S(2)}) %collective-permute-start.3) | collective-permute-done | bytes 589856 | tf_op jit(solution)/shard_map/ppermute | solution.py:48
  164.8 4.9 %multiply_reduce_fusion.1 = (f32[512]{0:T(512)S(1)}, f32[1,512,1024]{2,1,0:T(8,128)}, f32[512]{0:T(512)S(1)}, f32[1,512,1024]{2,1,0:T(8,128)}) fusion(f32[1,512,2304]{2,1,0:T(8,128)} %convolution_bitcast_fusion.1.src_ref, bf16[1,512,1280]{2,1,0:T(8,128)(2,1)S(1)} %copy-done.2, f32[1024]{0:T(1024)S(1)} %mul.424, f32[1,512,1024]{2,1,0:T(8,128)S(1)} %copy-done.7, ...), kind=kLoop, calls=%fused_computation.32 | loop fusion | flops 12581888 | bytes 23076864 | tf_op jit(solution)/shard_map/reduce_sum | solution.py:242
  169.8 6.4 %fusion.22 = f32[512,1024]{1,0:T(8,128)} fusion(bf16[1024,1024]{1,0:T(8,128)(2,1)S(1)} %copy-done, f32[1,512,1024]{2,1,0:T(8,128)} %get-tuple-element.30, f32[512]{0:T(512)S(1)} %add_rsqrt_fusion, f32[1024]{0:T(1024)S(1)} %copy-done.28), kind=kOutput, calls=%fused_computation.24 | convolution fusion | flops 3226992640 | bytes 6297600 | tf_op jit(solution)/shard_map/grk,kd->grd/dot_general | solution.py:281
  176.1 4.5 %fusion.28 = bf16[1,512,1024]{2,1,0:T(8,128)(2,1)} fusion(f32[512,1024]{1,0:T(8,128)} %fusion.22, bf16[1024,1024]{1,0:T(8,128)(2,1)S(1)} %copy-done, f32[1,512,1024]{2,1,0:T(8,128)} %get-tuple-element.12, f32[1024]{0:T(1024)S(1)} %copy-done.28, f32[512]{0:T(512)S(1)} %add_rsqrt_fusion.1), kind=kOutput, calls=%fused_computation.34 | convolution fusion | flops 1076363264 | bytes 7346176 | tf_op jit(solution)/shard_map/grk,kd->grd/dot_general | solution.py:279
  (147 shorter events, 44.1 us)
Async XLA Ops:
  0.0 169.7 %copy-start = (bf16[1024,1024]{1,0:T(8,128)(2,1)S(1)}, bf16[1024,1024]{1,0:T(8,128)(2,1)}, u32[]{:S(2)}) copy-start(bf16[1024,1024]{1,0:T(8,128)(2,1)} %param.23) | copy-start | bytes 6291460
  2.5 72.6 %collective-permute-start = (bf16[1,3,1024]{2,1,0:T(4,128)(2,1)S(1)}, bf16[1,3,1024]{2,1,0:T(4,128)(2,1)}, u32[]{:S(2)}, u32[]{:S(2)}) collective-permute-start(bf16[1,3,1024]{2,1,0:T(4,128)(2,1)S(1)} %get-tuple-element.23), channel_id=1, source_target_pairs={{0,2},{2,4},{4,6},{6,8},{8,10},{10,12},{12,14},{1,3},{3,5},{5,7},{... | collective-permute-start | bytes 18440 | tf_op jit(solution)/shard_map/ppermute | solution.py:257
  5.9 5.7 %copy-start.29 = (f32[16]{0:T(128)S(1)}, f32[16]{0:T(128)}, u32[]{:S(2)}) copy-start(f32[16]{0:T(128)} %param.20) | copy-start | bytes 196
  5.9 5.7 %copy-start.20 = (bf16[1024,16]{0,1:T(8,128)(2,1)S(1)}, bf16[1024,16]{0,1:T(8,128)(2,1)}, u32[]{:S(2)}) copy-start(bf16[1024,16]{0,1:T(8,128)(2,1)} %param.16) | copy-start | bytes 98308
  5.9 5.7 %copy-start.24 = (f32[16]{0:T(128)S(1)}, f32[16]{0:T(128)}, u32[]{:S(2)}) copy-start(f32[16]{0:T(128)} %param.19) | copy-start | bytes 196
  5.9 51.2 %collective-permute-start.4 = (bf16[1,3,1024]{2,1,0:T(4,128)(2,1)}, bf16[1,3,1024]{2,1,0:T(4,128)(2,1)}, u32[]{:S(2)}, u32[]{:S(2)}) collective-permute-start(bf16[1,3,1024]{2,1,0:T(4,128)(2,1)} %get-tuple-element.24), channel_id=1, source_target_pairs={{2,0},{4,2},{6,4},{8,6},{10,8},{12,10},{14,12},{3,1},{5,3},{7,5},{... | collective-permute-start | bytes 18440 | tf_op jit(solution)/shard_map/ppermute | solution.py:258
  22.1 23.3 %copy-start.12 = (f32[1,2,256,16]{3,2,1,0:T(8,128)}, f32[1,2,256,16]{3,2,1,0:T(8,128)S(1)}, u32[]{:S(2)}) copy-start(f32[1,2,256,16]{3,2,1,0:T(8,128)S(1)} %get-tuple-element.22) | copy-start | bytes 98308
  27.0 9.4 %slice-start = ((s8[4718592]{0:T(1024)(128)(4,1)}), s8[4194304]{0:T(1024)(128)(4,1)S(1)}, s32[]{:S(2)}) async-start(s8[4718592]{0:T(1024)(128)(4,1)} %bitcast.228), calls=%async_computation | async-start | bytes 8388608
  28.8 12.7 %copy-start.13 = (f32[1,2,16,256]{2,3,1,0:T(8,128)}, f32[1,2,16,256]{2,3,1,0:T(8,128)S(1)}, u32[]{:S(2)}) copy-start(f32[1,2,16,256]{2,3,1,0:T(8,128)S(1)} %get-tuple-element.16) | copy-start | bytes 98308
  28.9 7.5 %slice-start.1 = ((s8[4718592]{0:T(1024)(128)(4,1)}), s8[524288]{0:T(1024)(128)(4,1)S(1)}, s32[]{:S(2)}) async-start(s8[4718592]{0:T(1024)(128)(4,1)} %bitcast.228), calls=%async_computation.1 | async-start | bytes 1048576
  36.4 4.4 %copy-start.16 = (f32[512,16]{1,0:T(8,128)S(1)}, f32[512,16]{1,0:T(8,128)}, u32[]{:S(2)}) copy-start(f32[512,16]{1,0:T(8,128)} %copy.31) | copy-start | bytes 98308
  36.4 4.4 %copy-start.23 = (f32[1,2,1,16]{3,2,1,0:T(1,128)S(1)}, f32[1,2,1,16]{3,2,1,0:T(1,128)}, u32[]{:S(2)}) copy-start(f32[1,2,1,16]{3,2,1,0:T(1,128)} %get-tuple-element.28) | copy-start | bytes 388
  36.4 5.1 %copy-start.15 = (f32[512,16]{1,0:T(8,128)S(1)}, f32[512,16]{1,0:T(8,128)}, u32[]{:S(2)}) copy-start(f32[512,16]{1,0:T(8,128)} %copy.23) | copy-start | bytes 98308
  36.4 5.8 %copy-start.27 = (f32[1,1,16]{2,1,0:T(1,128)S(1)}, f32[1,1,16]{2,1,0:T(1,128)}, u32[]{:S(2)}) copy-start(f32[1,1,16]{2,1,0:T(1,128)} %get-tuple-element.36) | copy-start | bytes 196
  36.4 5.8 %copy-start.21 = (f32[1280]{0:T(1024)S(1)}, f32[1280]{0:T(1024)}, u32[]{:S(2)}) copy-start(f32[1280]{0:T(1024)} %param.18) | copy-start | bytes 15364
  36.4 6.4 %copy-start.26 = (f32[16]{0:T(128)S(1)}, f32[16]{0:T(128)}, u32[]{:S(2)}) copy-start(f32[16]{0:T(128)} %param.21) | copy-start | bytes 196
  36.5 8.8 %copy-start.25 = (f32[1,16,1,1]{1,3,2,0:T(1,128)S(1)}, f32[1,16,1,1]{1,3,2,0:T(1,128)}, u32[]{:S(2)}) copy-start(f32[1,16,1,1]{1,3,2,0:T(1,128)} %get-tuple-element.37) | copy-start | bytes 196
  40.8 5.3 %copy-start.19 = (f32[1,2,256,16]{3,2,1,0:T(8,128)S(1)}, f32[1,2,256,16]{3,2,1,0:T(8,128)}, u32[]{:S(2)}) copy-start(f32[1,2,256,16]{3,2,1,0:T(8,128)} %get-tuple-element.15) | copy-start | bytes 98308
  65.3 6.5 %copy-start.22 = (f32[16]{0:T(128)S(1)}, f32[16]{0:T(128)}, u32[]{:S(2)}) copy-start(f32[16]{0:T(128)} %get-tuple-element.39) | copy-start | bytes 196
  72.7 21.6 %collective-permute-start.5 = (f32[1,16,72,128]{3,2,1,0:T(8,128)}, f32[1,16,72,128]{3,2,1,0:T(8,128)}, u32[]{:S(2)}, u32[]{:S(2)}) collective-permute-start(f32[1,16,72,128]{3,2,1,0:T(8,128)} %pad_maximum_fusion.3), channel_id=1, source_target_pairs={{2,0},{4,2},{6,4},{8,6},{10,8},{12,10},{14,12},{3,1},{5,3},{7,5},{... | collective-permute-start | bytes 1769480 | tf_op jit(solution)/shard_map/ppermute | solution.py:48
  88.1 7.2 %copy-start.4 = (f32[2,16,64,128]{3,2,1,0:T(8,128)S(1)}, f32[2,16,64,128]{3,2,1,0:T(8,128)}, u32[]{:S(2)}) copy-start(f32[2,16,64,128]{3,2,1,0:T(8,128)} %shard_map.123) | copy-start | bytes 3145732
  89.6 17.2 %copy-start.3 = (f32[2,16,64,128]{3,2,1,0:T(8,128)S(1)}, f32[2,16,64,128]{3,2,1,0:T(8,128)}, u32[]{:S(2)}) copy-start(f32[2,16,64,128]{3,2,1,0:T(8,128)} %shard_map.120) | copy-start | bytes 3145732
  89.7 17.2 %collective-permute-start.1 = (f32[1,16,72,128]{3,2,1,0:T(8,128)S(1)}, f32[1,16,72,128]{3,2,1,0:T(8,128)S(1)}, u32[]{:S(2)}, u32[]{:S(2)}) collective-permute-start(f32[1,16,72,128]{3,2,1,0:T(8,128)S(1)} %pad_maximum_fusion), channel_id=1, source_target_pairs={{0,2},{2,4},{4,6},{6,8},{8,10},{10,12},{12,14},{1,3},{3,5},{5,7},{... | collective-permute-start | bytes 1769480 | tf_op jit(solution)/shard_map/ppermute | solution.py:48
  96.6 12.2 %copy-start.11 = (f32[1,16,64,128]{3,2,1,0:T(8,128)}, f32[1,16,64,128]{3,2,1,0:T(8,128)S(1)}, u32[]{:S(2)}) copy-start(f32[1,16,64,128]{3,2,1,0:T(8,128)S(1)} %multiply_add_fusion.3) | copy-start | bytes 1572868
  97.6 26.6 %collective-permute-start.6 = (f32[1,16,72,128]{3,2,1,0:T(8,128)}, f32[1,16,72,128]{3,2,1,0:T(8,128)}, u32[]{:S(2)}, u32[]{:S(2)}) collective-permute-start(f32[1,16,72,128]{3,2,1,0:T(8,128)} %pad_maximum_fusion.4), channel_id=1, source_target_pairs={{4,0},{6,2},{8,4},{10,6},{12,8},{14,10},{5,1},{7,3},{9,5},{11,7},{... | collective-permute-start | bytes 1769480 | tf_op jit(solution)/shard_map/ppermute | solution.py:48
  108.8 16.8 %collective-permute-start.2 = (f32[1,16,72,128]{3,2,1,0:T(8,128)}, f32[1,16,72,128]{3,2,1,0:T(8,128)}, u32[]{:S(2)}, u32[]{:S(2)}) collective-permute-start(f32[1,16,72,128]{3,2,1,0:T(8,128)} %pad_maximum_fusion.1), channel_id=1, source_target_pairs={{0,4},{2,6},{4,8},{6,10},{8,12},{10,14},{1,5},{3,7},{5,9},{7,11},{... | collective-permute-start | bytes 1769480 | tf_op jit(solution)/shard_map/ppermute | solution.py:48
  124.2 7.3 %copy-start.10 = (f32[1,16,64,128]{3,2,1,0:T(8,128)S(1)}, f32[1,16,64,128]{3,2,1,0:T(8,128)}, u32[]{:S(2)}) copy-start(f32[1,16,64,128]{3,2,1,0:T(8,128)} %copy-done.9) | copy-start | bytes 1572868
  126.9 15.1 %collective-permute-start.7 = (f32[1,16,72,128]{3,2,1,0:T(8,128)S(1)}, f32[1,16,72,128]{3,2,1,0:T(8,128)S(1)}, u32[]{:S(2)}, u32[]{:S(2)}) collective-permute-start(f32[1,16,72,128]{3,2,1,0:T(8,128)S(1)} %pad_maximum_fusion.5), channel_id=1, source_target_pairs={{8,0},{10,2},{12,4},{14,6},{9,1},{11,3},{13,5},{15,7},{24,16},{26,... | collective-permute-start | bytes 1769480 | tf_op jit(solution)/shard_map/ppermute | solution.py:48
  132.8 28.2 %collective-permute-start.3 = (f32[1,16,72,128]{3,2,1,0:T(8,128)S(1)}, f32[1,16,72,128]{3,2,1,0:T(8,128)S(1)}, u32[]{:S(2)}, u32[]{:S(2)}) collective-permute-start(f32[1,16,72,128]{3,2,1,0:T(8,128)S(1)} %pad_maximum_fusion.2), channel_id=1, source_target_pairs={{0,8},{2,10},{4,12},{6,14},{1,9},{3,11},{5,13},{7,15},{16,24},{18,... | collective-permute-start | bytes 1769480 | tf_op jit(solution)/shard_map/ppermute | solution.py:48
  143.4 20.3 %copy-start.8 = (f32[1,512,1024]{2,1,0:T(8,128)S(1)}, f32[1,512,1024]{2,1,0:T(8,128)}, u32[]{:S(2)}) copy-start(f32[1,512,1024]{2,1,0:T(8,128)} %copy.38) | copy-start | bytes 6291460
  143.5 20.1 %copy-start.7 = (f32[1,512,1024]{2,1,0:T(8,128)S(1)}, f32[1,512,1024]{2,1,0:T(8,128)}, u32[]{:S(2)}) copy-start(f32[1,512,1024]{2,1,0:T(8,128)} %copy.30) | copy-start | bytes 6291460
  164.8 4.9 %copy-start.28 = (f32[1024]{0:T(1024)S(1)}, f32[1024]{0:T(1024)}, u32[]{:S(2)}) copy-start(f32[1024]{0:T(1024)} %param.22) | copy-start | bytes 12292
  (8 other events, 18.3 us)

commit v6 on v5

--- a/solution.py
+++ b/solution.py
@@ -256,21 +256,22 @@
     count = lax.axis_size("seq")
     low = lax.ppermute(strand[:, rows - margin :], "seq", [(i, i + 1) for i in range(count - 1)])
     high = lax.ppermute(strand[:, :margin], "seq", [(i + 1, i) for i in range(count - 1)])
-    mirrored = flip_lanes(strand)
-    high_mirrored = flip_lanes(high)
     w_source = w_in[:, inner:]
+    rates = -jnp.exp(a_log)
     proj_f = jnp.einsum("grd,de->gre", strand, w_in, preferred_element_type=jnp.float32)
-    proj_r = jnp.einsum("grd,de->gre", mirrored, w_in, preferred_element_type=jnp.float32)
     halo_f = jnp.einsum("grd,de->gre", low, w_source, preferred_element_type=jnp.float32)
-    halo_r = jnp.einsum("grd,de->gre", high_mirrored, w_source, preferred_element_type=jnp.float32)
     step_f = jax.nn.softplus(
         jnp.einsum("grd,dh->grh", strand, w_dt, preferred_element_type=jnp.float32) + dt_bias
     )
+    sum_f, pend_f = strand_terms(proj_f, halo_f, step_f, conv_w, conv_b, rates, False)
+    sum_f, (strand_late, high) = lax.optimization_barrier((sum_f, (strand, high)))
+    mirrored = flip_lanes(strand_late)
+    high_mirrored = flip_lanes(high)
+    proj_r = jnp.einsum("grd,de->gre", mirrored, w_in, preferred_element_type=jnp.float32)
+    halo_r = jnp.einsum("grd,de->gre", high_mirrored, w_source, preferred_element_type=jnp.float32)
     step_r = jax.nn.softplus(
         jnp.einsum("grd,dh->grh", mirrored, w_dt, preferred_element_type=jnp.float32) + dt_bias
     )
-    rates = -jnp.exp(a_log)
-    sum_f, pend_f = strand_terms(proj_f, halo_f, step_f, conv_w, conv_b, rates, False)
     sum_r, pend_r = strand_terms(proj_r, halo_r, step_r, conv_w, conv_b, rates, True)
     in_f, in_r = exclusive_scans(sum_f, sum_r, "seq")
     normed_f = finish(pend_f, in_f[1], proj_f[:, :, :inner], d_skip, norm_gain)

time: 184 us -> 186 us (1.011)
  the two profiles are of different devices: /device:TPU:24 before, /device:TPU:0 now
where the time goes in v6:
time: 186 us; the launch traced here: 185 us
  matrix products  37.3 us (20%)
  waiting for transfers between devices  32.2 us (17%)
  Pallas kernels  31.5 us (17%)
  other arithmetic  30.4 us (16%)
  local copies, waits for them, and re-layouts  26.7 us (14%)
  starting transfers between devices  25.8 us (14%)
    ppermute x6, waiting for transfers between devices, exclusive_scans(): decay, state = unpack(lax.ppermute(pack(*ahead[k]), axis, pairs))  32.2 us
    ppermute x6, starting transfers between devices, exclusive_scans(): decay, state = unpack(lax.ppermute(pack(*ahead[k]), axis, pairs))  19 us
    pallas_call x2, Pallas kernels, block_terms(): pl.pallas_call(partial(inside_kernel, reverse=reverse), grid=(blocks,), i...  11.1 us
    pallas_call x2, Pallas kernels, convolve(): pl.pallas_call(partial(conv_kernel, reverse=reverse), grid=(count, width...  10.2 us
    pallas_call x2, Pallas kernels, block_terms(): pl.pallas_call(state_kernel, grid=(blocks,), in_specs=[spec((Q, width)),...  10.2 us
    broadcast_in_dim x4, local copies, waits for them, and re-layouts, finish(): scale = jnp.repeat(from_start.reshape(count, rows, H), P_SIZE, axis=-1)  9.07 us
    dot_general x1, matrix products, on_device(): jnp.einsum('grd,de->gre', mirrored, w_in, preferred_element_type=jnp.floa...  7.45 us
    add x8, other arithmetic, chain(): next_decay[..., None, None] * first_state + next_state  6.58 us
  transfers between devices with their start and end apart: 8, of which 3 were waited for; matrix products, arithmetic and copies ran while one was open for 26% of the time, Pallas kernels for 17%

profile of v6, /device:TPU:0, one launch (start us, length us, event | category | flops | bytes accessed | tf_op | source)
XLA Modules:
  0.0 184.5 jit_solution(8941738518200132076)
XLA Ops:
  0.0 1.9 %fusion.21 = bf16[1,512,1024]{2,1,0:T(8,128)(2,1)S(1)} fusion(bf16[1,512,1024]{2,1,0:T(8,128)(2,1)} %param.13, bf16[4,1024]{1,0:T(4,128)(2,1)} %param.14, s32[512]{0:T(512)} %bitcast.257), kind=kOutput, calls=%fused_computation.22 | convolution fusion | flops 5769216 | bytes 2107392 | tf_op jit(solution)/shard_map/gtb,bd->gtd/dot_general | solution.py:253
  3.2 5.5 %collective-permute-start = (bf16[1,3,1024]{2,1,0:T(4,128)(2,1)S(1)}, bf16[1,3,1024]{2,1,0:T(4,128)(2,1)S(1)}, u32[]{:S(2)}, u32[]{:S(2)}) collective-permute-start(bf16[1,3,1024]{2,1,0:T(4,128)(2,1)S(1)} %get-tuple-element.29), channel_id=1, source_target_pairs={{0,2},{2,4},{4,6},{6,8},{8,10},{10,12},{12,14},{1,3},{3,5},{5,7},{... | collective-permute-start | bytes 18440 | tf_op jit(solution)/shard_map/ppermute | solution.py:257
  13.3 1.7 bitcast_exponential_fusion
  15.0 1.8 multiply_bitcast_fusion.1.to_end_ref
  17.4 6.6 %convolution_bitcast_fusion.1.src_ref = f32[1,512,2304]{2,1,0:T(8,128)} fusion(bf16[1024,2304]{1,0:T(8,128)(2,1)} %param.15, bf16[1,512,1024]{2,1,0:T(8,128)(2,1)S(1)} %fusion.21), kind=kOutput, calls=%fused_computation.1 | convolution fusion | flops 2415919104 | bytes 10485760 | tf_op jit(solution)/shard_map/grd,de->gre/dot_general | solution.py:261
  27.6 1.6 broadcast_in_dim.37
  29.3 2.9 %copy.28 = f32[1,512,1024]{2,1,0:T(8,128)} copy(f32[1,512,1024]{1,2,0:T(8,128)} %bitcast.216) | data formatting | bytes 4194304 | tf_op jit(solution)/shard_map/broadcast_in_dim | solution.py:236
  32.1 2.2 %fusion.7 = f32[1,3,1280]{2,1,0:T(4,128)S(1)} fusion(bf16[1024,2304]{1,0:T(8,128)(2,1)} %param.15, bf16[1,3,1024]{2,1,0:T(4,128)(2,1)S(1)} %collective-permute-done), kind=kOutput, calls=%fused_computation.10 | convolution fusion | flops 7864320 | bytes 2642944 | tf_op jit(solution)/shard_map/grd,de->gre/dot_general | solution.py:262
  35.0 5.1 %shard_map.118 = bf16[1,512,1280]{2,1,0:T(8,128)(2,1)} custom-call(f32[1,512,2304]{2,1,0:T(8,128)} %convolution_bitcast_fusion.1.src_ref, f32[1,8,1280]{2,1,0:T(8,128)} %pad.12.halo_ref, f32[4,1280]{1,0:T(4,128)} %w_ref.3, f32[1,1280]{1,0:T(1,128)} %reshape.627.b_ref), custom_call_target="tpu_custom_call" | custom-call | tf_op jit(solution)/shard_map/pallas_call | solution.py:189
  40.1 5.1 %shard_map.120 = f32[2,16,64,128]{3,2,1,0:T(8,128)} custom-call(bf16[2,256,1280]{2,1,0:T(8,128)(2,1)} %bitcast.209, f32[2,256,16]{2,1,0:T(8,128)} %multiply_bitcast_fusion.1.to_end_ref), custom_call_target="tpu_custom_call" | custom-call | tf_op jit(solution)/shard_map/pallas_call | solution.py:124
  47.6 2.4 %fusion.27 = bf16[512,1024]{1,0:T(8,128)(2,1)S(1)} fusion(bf16[1,512,1024]{2,1,0:T(8,128)(2,1)} %copy-done.10), kind=kOutput, calls=%fused_computation.33 | convolution fusion | flops 1076363264 | bytes 2097152 | tf_op jit(solution)/shard_map/...d,de->...e/dot_general | solution.py:28
  55.7 7.4 %convolution_bitcast_fusion.src_ref = f32[1,512,2304]{2,1,0:T(8,128)} fusion(bf16[512,1024]{1,0:T(8,128)(2,1)} %copy-done.15, bf16[1024,2304]{1,0:T(8,128)(2,1)} %param.15), kind=kOutput, calls=%fused_computation | convolution fusion | flops 2415919104 | bytes 10485760 | tf_op jit(solution)/shard_map/grd,de->gre/dot_general | solution.py:270
  63.1 3.1 %fusion.10 = f32[1,3,1280]{2,1,0:T(4,128)} fusion(bf16[1024,2304]{1,0:T(8,128)(2,1)} %param.15, bf16[1,3,1024]{2,1,0:T(4,128)(2,1)} %collective-permute-done.1), kind=kOutput, calls=%fused_computation.11 | convolution fusion | flops 16256000 | bytes 2644992 | tf_op jit(solution)/shard_map/grd,de->gre/dot_general | solution.py:271
  66.2 1.3 pad.13.halo_ref
  67.6 1.4 copy.41
  73.4 5.6 %collective-permute-start.2 = (f32[1,16,72,128]{3,2,1,0:T(8,128)}, f32[1,16,72,128]{3,2,1,0:T(8,128)}, u32[]{:S(2)}, u32[]{:S(2)}) collective-permute-start(f32[1,16,72,128]{3,2,1,0:T(8,128)} %pad_maximum_fusion), channel_id=1, source_target_pairs={{0,2},{2,4},{4,6},{6,8},{8,10},{10,12},{12,14},{1,3},{3,5},{5,7},{... | collective-permute-start | bytes 1769480 | tf_op jit(solution)/shard_map/ppermute | solution.py:48
  79.1 1.6 broadcast_in_dim.46
  80.6 3.0 %copy.36 = f32[1,512,1024]{2,1,0:T(8,128)} copy(f32[1,512,1024]{1,2,0:T(8,128)} %bitcast.217) | data formatting | bytes 4194304 | tf_op jit(solution)/shard_map/broadcast_in_dim | solution.py:236
  83.6 5.1 %shard_map.121 = bf16[1,512,1280]{2,1,0:T(8,128)(2,1)} custom-call(f32[1,512,2304]{2,1,0:T(8,128)} %convolution_bitcast_fusion.src_ref, f32[1,8,1280]{2,1,0:T(8,128)} %pad.13.halo_ref, f32[4,1280]{1,0:T(4,128)} %w_ref.3, f32[1,1280]{1,0:T(1,128)} %reshape.627.b_ref), custom_call_target="tpu_custom_call" | custom-call | tf_op jit(solution)/shard_map/pallas_call | solution.py:189
  89.6 5.1 %shard_map.123 = f32[2,16,64,128]{3,2,1,0:T(8,128)} custom-call(bf16[2,256,1280]{2,1,0:T(8,128)(2,1)} %bitcast.211, f32[2,256,16]{2,1,0:T(8,128)} %multiply_bitcast_fusion.to_end_ref), custom_call_target="tpu_custom_call" | custom-call | tf_op jit(solution)/shard_map/pallas_call | solution.py:124
  97.0 1.5 collective-permute-start.5
  98.5 5.6 %shard_map.119 = f32[2,256,1024]{2,1,0:T(8,128)} custom-call(bf16[2,256,1280]{2,1,0:T(8,128)(2,1)} %bitcast.210, f32[2,256,16]{2,1,0:T(8,128)} %bitcast.226, f32[2,16,256]{2,1,0:T(8,128)} %copy.26.cum_t_ref, f32[2,16,256]{2,1,0:T(8,128)} %bitcast.245), custom_call_target="tpu_custom_call" | custom-call | tf_op jit(solution)/shard_map/pallas_call | solution.py:131
  104.1 5.6 %shard_map.122 = f32[2,256,1024]{2,1,0:T(8,128)} custom-call(bf16[2,256,1280]{2,1,0:T(8,128)(2,1)} %bitcast.212, f32[2,256,16]{2,1,0:T(8,128)} %bitcast.228, f32[2,16,256]{2,1,0:T(8,128)} %copy.33.cum_t_ref, f32[2,16,256]{2,1,0:T(8,128)} %bitcast.246), custom_call_target="tpu_custom_call" | custom-call | tf_op jit(solution)/shard_map/pallas_call | solution.py:131
  113.3 3.9 %collective-permute-start.3 = (f32[1,16,72,128]{3,2,1,0:T(8,128)S(1)}, f32[1,16,72,128]{3,2,1,0:T(8,128)S(1)}, u32[]{:S(2)}, u32[]{:S(2)}) collective-permute-start(f32[1,16,72,128]{3,2,1,0:T(8,128)S(1)} %pad_maximum_fusion.1), channel_id=1, source_target_pairs={{0,4},{2,6},{4,8},{6,10},{8,12},{10,14},{1,5},{3,7},{5,9},{7,11},{... | collective-permute-start | bytes 1769480 | tf_op jit(solution)/shard_map/ppermute | solution.py:48
  120.9 7.7 %collective-permute-done.3 = f32[1,16,72,128]{3,2,1,0:T(8,128)S(1)} collective-permute-done((f32[1,16,72,128]{3,2,1,0:T(8,128)S(1)}, f32[1,16,72,128]{3,2,1,0:T(8,128)S(1)}, u32[]{:S(2)}, u32[]{:S(2)}) %collective-permute-start.3) | collective-permute-done | bytes 589856 | tf_op jit(solution)/shard_map/ppermute | solution.py:48
  129.9 5.4 %collective-permute-start.4 = (f32[1,16,72,128]{3,2,1,0:T(8,128)S(1)}, f32[1,16,72,128]{3,2,1,0:T(8,128)S(1)}, u32[]{:S(2)}, u32[]{:S(2)}) collective-permute-start(f32[1,16,72,128]{3,2,1,0:T(8,128)S(1)} %pad_maximum_fusion.2), channel_id=1, source_target_pairs={{0,8},{2,10},{4,12},{6,14},{1,9},{3,11},{5,13},{7,15},{16,24},{18,... | collective-permute-start | bytes 1769480 | tf_op jit(solution)/shard_map/ppermute | solution.py:48
  138.0 8.0 %collective-permute-done.4 = f32[1,16,72,128]{3,2,1,0:T(8,128)S(1)} collective-permute-done((f32[1,16,72,128]{3,2,1,0:T(8,128)S(1)}, f32[1,16,72,128]{3,2,1,0:T(8,128)S(1)}, u32[]{:S(2)}, u32[]{:S(2)}) %collective-permute-start.4) | collective-permute-done | bytes 589856 | tf_op jit(solution)/shard_map/ppermute | solution.py:48
  148.4 16.6 %collective-permute-done.7 = f32[1,16,72,128]{3,2,1,0:T(8,128)S(1)} collective-permute-done((f32[1,16,72,128]{3,2,1,0:T(8,128)S(1)}, f32[1,16,72,128]{3,2,1,0:T(8,128)S(1)}, u32[]{:S(2)}, u32[]{:S(2)}) %collective-permute-start.7) | collective-permute-done | bytes 589856 | tf_op jit(solution)/shard_map/ppermute | solution.py:48
  165.0 1.4 fusion.46
  168.7 4.9 %multiply_reduce_fusion.1 = (f32[512]{0:T(512)S(1)}, f32[1,512,1024]{2,1,0:T(8,128)}, f32[512]{0:T(512)S(1)}, f32[1,512,1024]{2,1,0:T(8,128)}) fusion(f32[1,512,2304]{2,1,0:T(8,128)} %convolution_bitcast_fusion.1.src_ref, bf16[1,512,1280]{2,1,0:T(8,128)(2,1)S(1)} %copy-done.1, f32[1024]{0:T(1024)S(1)} %mul.414, f32[1,512,1024]{2,1,0:T(8,128)S(1)} %copy-done.6, ...), kind=kLoop, calls=%fused_computation.32 | loop fusion | flops 12581888 | bytes 23076864 | tf_op jit(solution)/shard_map/reduce_sum | solution.py:242
  173.7 6.4 %fusion.22 = f32[512,1024]{1,0:T(8,128)} fusion(bf16[1024,1024]{1,0:T(8,128)(2,1)S(1)} %copy-done, f32[1,512,1024]{2,1,0:T(8,128)} %get-tuple-element.35, f32[512]{0:T(512)S(1)} %get-tuple-element.45, f32[1024]{0:T(1024)S(1)} %copy-done.31), kind=kOutput, calls=%fused_computation.24 | convolution fusion | flops 3226992640 | bytes 6297600 | tf_op jit(solution)/shard_map/grk,kd->grd/dot_general | solution.py:282
  180.0 4.5 %fusion.28 = bf16[1,512,1024]{2,1,0:T(8,128)(2,1)} fusion(f32[512,1024]{1,0:T(8,128)} %fusion.22, bf16[1024,1024]{1,0:T(8,128)(2,1)S(1)} %copy-done, f32[1,512,1024]{2,1,0:T(8,128)} %get-tuple-element.19, f32[1024]{0:T(1024)S(1)} %copy-done.31, f32[512]{0:T(512)S(1)} %get-tuple-element.46), kind=kOutput, calls=%fused_computation.34 | convolution fusion | flops 1076363264 | bytes 7346176 | tf_op jit(solution)/shard_map/grk,kd->grd/dot_general | solution.py:280
  (149 shorter events, 42.3 us)
Async XLA Ops:
  0.0 173.6 %copy-start = (bf16[1024,1024]{1,0:T(8,128)(2,1)S(1)}, bf16[1024,1024]{1,0:T(8,128)(2,1)}, u32[]{:S(2)}) copy-start(bf16[1024,1024]{1,0:T(8,128)(2,1)} %param.23) | copy-start | bytes 6291460
  0.0 8.8 %copy-start.32 = (f32[16]{0:T(128)S(1)}, f32[16]{0:T(128)}, u32[]{:S(2)}) copy-start(f32[16]{0:T(128)} %param.20) | copy-start | bytes 196
  0.0 8.8 %copy-start.26 = (f32[16]{0:T(128)S(1)}, f32[16]{0:T(128)}, u32[]{:S(2)}) copy-start(f32[16]{0:T(128)} %param.19) | copy-start | bytes 196
  0.0 8.8 %copy-start.18 = (bf16[1024,16]{0,1:T(8,128)(2,1)S(1)}, bf16[1024,16]{0,1:T(8,128)(2,1)}, u32[]{:S(2)}) copy-start(bf16[1024,16]{0,1:T(8,128)(2,1)} %param.16) | copy-start | bytes 98308
  1.9 15.4 %copy-start.10 = (bf16[1,512,1024]{2,1,0:T(8,128)(2,1)}, bf16[1,512,1024]{2,1,0:T(8,128)(2,1)S(1)}, u32[]{:S(2)}) copy-start(bf16[1,512,1024]{2,1,0:T(8,128)(2,1)S(1)} %fusion.21) | copy-start | bytes 3145732
  1.9 45.7 %collective-permute-start.1 = (bf16[1,3,1024]{2,1,0:T(4,128)(2,1)S(1)}, bf16[1,3,1024]{2,1,0:T(4,128)(2,1)}, u32[]{:S(2)}, u32[]{:S(2)}) collective-permute-start(bf16[1,3,1024]{2,1,0:T(4,128)(2,1)S(1)} %get-tuple-element.28), channel_id=1, source_target_pairs={{2,0},{4,2},{6,4},{8,6},{10,8},{12,10},{14,12},{3,1},{5,3},{7,5},{... | collective-permute-start | bytes 18440 | tf_op jit(solution)/shard_map/ppermute | solution.py:258
  3.2 28.9 %collective-permute-start = (bf16[1,3,1024]{2,1,0:T(4,128)(2,1)S(1)}, bf16[1,3,1024]{2,1,0:T(4,128)(2,1)S(1)}, u32[]{:S(2)}, u32[]{:S(2)}) collective-permute-start(bf16[1,3,1024]{2,1,0:T(4,128)(2,1)S(1)} %get-tuple-element.29), channel_id=1, source_target_pairs={{0,2},{2,4},{4,6},{6,8},{8,10},{10,12},{12,14},{1,3},{3,5},{5,7},{... | collective-permute-start | bytes 18440 | tf_op jit(solution)/shard_map/ppermute | solution.py:257
  9.3 4.0 %copy-start.13 = (f32[512,16]{1,0:T(8,128)}, f32[512,16]{1,0:T(8,128)S(1)}, u32[]{:S(2)}) copy-start(f32[512,16]{1,0:T(8,128)S(1)} %copy.22) | copy-start | bytes 98308
  15.0 11.9 %copy-start.11 = (f32[1,2,16,256]{2,3,1,0:T(8,128)}, f32[1,2,16,256]{2,3,1,0:T(8,128)S(1)}, u32[]{:S(2)}) copy-start(f32[1,2,16,256]{2,3,1,0:T(8,128)S(1)} %get-tuple-element.21) | copy-start | bytes 98308
  17.3 27.9 %copy-start.23 = (f32[16]{0:T(128)}, f32[16]{0:T(128)S(1)}, u32[]{:S(2)}) copy-start(f32[16]{0:T(128)S(1)} %get-tuple-element.37) | copy-start | bytes 196
  17.3 7.1 %copy-start.21 = (f32[1280]{0:T(1024)S(1)}, f32[1280]{0:T(1024)}, u32[]{:S(2)}) copy-start(f32[1280]{0:T(1024)} %param.18) | copy-start | bytes 15364
  17.3 7.7 %copy-start.29 = (f32[16]{0:T(128)S(1)}, f32[16]{0:T(128)}, u32[]{:S(2)}) copy-start(f32[16]{0:T(128)} %param.21) | copy-start | bytes 196
  46.5 26.0 %copy-start.8 = (f32[1,16,64,128]{3,2,1,0:T(8,128)}, f32[1,16,64,128]{3,2,1,0:T(8,128)S(1)}, u32[]{:S(2)}) copy-start(f32[1,16,64,128]{3,2,1,0:T(8,128)S(1)} %fusion.50) | copy-start | bytes 1572868
  54.5 16.6 %copy-start.12 = (f32[1,2,256,16]{3,2,1,0:T(8,128)}, f32[1,2,256,16]{3,2,1,0:T(8,128)S(1)}, u32[]{:S(2)}) copy-start(f32[1,2,256,16]{3,2,1,0:T(8,128)S(1)} %get-tuple-element.27) | copy-start | bytes 98308
  63.1 5.8 %copy-start.14 = (f32[1,2,256,16]{3,2,1,0:T(8,128)S(1)}, f32[1,2,256,16]{3,2,1,0:T(8,128)}, u32[]{:S(2)}) copy-start(f32[1,2,256,16]{3,2,1,0:T(8,128)} %get-tuple-element.26) | copy-start | bytes 98308
  69.6 9.4 %copy-start.17 = (f32[512,16]{0,1:T(8,128)S(1)}, f32[512,16]{0,1:T(8,128)}, u32[]{:S(2)}) copy-start(f32[512,16]{0,1:T(8,128)} %copy.34) | copy-start | bytes 98308
  73.4 37.6 %collective-permute-start.2 = (f32[1,16,72,128]{3,2,1,0:T(8,128)}, f32[1,16,72,128]{3,2,1,0:T(8,128)}, u32[]{:S(2)}, u32[]{:S(2)}) collective-permute-start(f32[1,16,72,128]{3,2,1,0:T(8,128)} %pad_maximum_fusion), channel_id=1, source_target_pairs={{0,2},{2,4},{4,6},{6,8},{8,10},{10,12},{12,14},{1,3},{3,5},{5,7},{... | collective-permute-start | bytes 1769480 | tf_op jit(solution)/shard_map/ppermute | solution.py:48
  88.7 6.0 %copy-start.22 = (f32[16]{0:T(128)S(1)}, f32[16]{0:T(128)}, u32[]{:S(2)}) copy-start(f32[16]{0:T(128)} %get-tuple-element.42) | copy-start | bytes 196
  89.6 6.5 %copy-start.25 = (f32[16]{0:T(128)S(1)}, f32[16]{0:T(128)}, u32[]{:S(2)}) copy-start(f32[16]{0:T(128)} %get-tuple-element.43) | copy-start | bytes 196
  97.0 20.2 %collective-permute-start.5 = (f32[1,16,72,128]{3,2,1,0:T(8,128)}, f32[1,16,72,128]{3,2,1,0:T(8,128)}, u32[]{:S(2)}, u32[]{:S(2)}) collective-permute-start(f32[1,16,72,128]{3,2,1,0:T(8,128)} %pad_maximum_fusion.3), channel_id=1, source_target_pairs={{2,0},{4,2},{6,4},{8,6},{10,8},{12,10},{14,12},{3,1},{5,3},{7,5},{... | collective-permute-start | bytes 1769480 | tf_op jit(solution)/shard_map/ppermute | solution.py:48
  104.1 5.6 %copy-start.24 = (f32[16]{0:T(128)S(1)}, f32[16]{0:T(128)}, u32[]{:S(2)}) copy-start(f32[16]{0:T(128)} %copy-done.23) | copy-start | bytes 196
  104.1 6.8 %copy-start.3 = (f32[2,16,64,128]{3,2,1,0:T(8,128)S(1)}, f32[2,16,64,128]{3,2,1,0:T(8,128)}, u32[]{:S(2)}) copy-start(f32[2,16,64,128]{3,2,1,0:T(8,128)} %shard_map.123) | copy-start | bytes 3145732
  104.1 8.0 %copy-start.20 = (f32[1,16]{1,0:T(1,128)S(1)}, f32[1,16]{1,0:T(1,128)}, u32[]{:S(2)}) copy-start(f32[1,16]{1,0:T(1,128)} %get-tuple-element.9) | copy-start | bytes 196
  113.3 15.3 %collective-permute-start.3 = (f32[1,16,72,128]{3,2,1,0:T(8,128)S(1)}, f32[1,16,72,128]{3,2,1,0:T(8,128)S(1)}, u32[]{:S(2)}, u32[]{:S(2)}) collective-permute-start(f32[1,16,72,128]{3,2,1,0:T(8,128)S(1)} %pad_maximum_fusion.1), channel_id=1, source_target_pairs={{0,4},{2,6},{4,8},{6,10},{8,12},{10,14},{1,5},{3,7},{5,9},{7,11},{... | collective-permute-start | bytes 1769480 | tf_op jit(solution)/shard_map/ppermute | solution.py:48
  119.5 15.9 %copy-start.30 = (f32[1,1,16]{2,1,0:T(1,128)S(1)}, f32[1,1,16]{2,1,0:T(1,128)}, u32[]{:S(2)}) copy-start(f32[1,1,16]{2,1,0:T(1,128)} %get-tuple-element.40) | copy-start | bytes 196
  119.6 15.8 %collective-permute-start.6 = (f32[1,16,72,128]{3,2,1,0:T(8,128)S(1)}, f32[1,16,72,128]{3,2,1,0:T(8,128)S(1)}, u32[]{:S(2)}, u32[]{:S(2)}) collective-permute-start(f32[1,16,72,128]{3,2,1,0:T(8,128)S(1)} %pad_maximum_fusion.4), channel_id=1, source_target_pairs={{4,0},{6,2},{8,4},{10,6},{12,8},{14,10},{5,1},{7,3},{9,5},{11,7},{... | collective-permute-start | bytes 1769480 | tf_op jit(solution)/shard_map/ppermute | solution.py:48
  129.9 16.0 %collective-permute-start.4 = (f32[1,16,72,128]{3,2,1,0:T(8,128)S(1)}, f32[1,16,72,128]{3,2,1,0:T(8,128)S(1)}, u32[]{:S(2)}, u32[]{:S(2)}) collective-permute-start(f32[1,16,72,128]{3,2,1,0:T(8,128)S(1)} %pad_maximum_fusion.2), channel_id=1, source_target_pairs={{0,8},{2,10},{4,12},{6,14},{1,9},{3,11},{5,13},{7,15},{16,24},{18,... | collective-permute-start | bytes 1769480 | tf_op jit(solution)/shard_map/ppermute | solution.py:48
  136.4 10.7 %copy-start.28 = (f32[2,16]{1,0:T(2,128)S(1)}, f32[2,16]{1,0:T(2,128)}, u32[]{:S(2)}) copy-start(f32[2,16]{1,0:T(2,128)} %pad_bitcast_fusion.1) | copy-start | bytes 388
  136.7 28.2 %collective-permute-start.7 = (f32[1,16,72,128]{3,2,1,0:T(8,128)S(1)}, f32[1,16,72,128]{3,2,1,0:T(8,128)S(1)}, u32[]{:S(2)}, u32[]{:S(2)}) collective-permute-start(f32[1,16,72,128]{3,2,1,0:T(8,128)S(1)} %pad_maximum_fusion.5), channel_id=1, source_target_pairs={{8,0},{10,2},{12,4},{14,6},{9,1},{11,3},{13,5},{15,7},{24,16},{26,... | collective-permute-start | bytes 1769480 | tf_op jit(solution)/shard_map/ppermute | solution.py:48
  147.2 20.3 %copy-start.7 = (f32[1,512,1024]{2,1,0:T(8,128)S(1)}, f32[1,512,1024]{2,1,0:T(8,128)}, u32[]{:S(2)}) copy-start(f32[1,512,1024]{2,1,0:T(8,128)} %copy.36) | copy-start | bytes 6291460
  147.4 20.2 %copy-start.6 = (f32[1,512,1024]{2,1,0:T(8,128)S(1)}, f32[1,512,1024]{2,1,0:T(8,128)}, u32[]{:S(2)}) copy-start(f32[1,512,1024]{2,1,0:T(8,128)} %copy.28) | copy-start | bytes 6291460
  168.7 4.9 %copy-start.31 = (f32[1024]{0:T(1024)S(1)}, f32[1024]{0:T(1024)}, u32[]{:S(2)}) copy-start(f32[1024]{0:T(1024)} %param.22) | copy-start | bytes 12292
  (9 other events, 19.2 us)

commit v7 on v6

--- a/solution.py
+++ b/solution.py
@@ -233,7 +233,12 @@
         start_state.reshape(count, spans, inner, N),
         precision=lax.Precision.HIGHEST,
     ).reshape(count, rows, inner)
-    scale = jnp.repeat(from_start.reshape(count, rows, H), P_SIZE, axis=-1)
+    heads = lax.broadcasted_iota(jnp.int32, (H, inner), 0)
+    lanes = lax.broadcasted_iota(jnp.int32, (H, inner), 1)
+    spread = (lanes // P_SIZE == heads).astype(jnp.float32)
+    scale = jnp.einsum(
+        "grh,hk->grk", from_start.reshape(count, rows, H), spread, precision=lax.Precision.HIGHEST
+    )
     skip = jnp.repeat(d_skip, P_SIZE)
     scanned = inside + scale * carried + skip * activated[:, :, :inner].astype(jnp.float32)
     gated = scanned * jax.nn.silu(gate_part)

time: 186 us -> 171 us (0.919)
  the two profiles are of different devices: /device:TPU:0 before, /device:TPU:24 now
where the time goes in v7:
time: 171 us; the launch traced here: 169 us
  matrix products  43.7 us (26%)
  Pallas kernels  31.6 us (18%)
  waiting for transfers between devices  28.2 us (16%)
  other arithmetic  25.8 us (15%)
  starting transfers between devices  25.1 us (15%)
  local copies, waits for them, and re-layouts  14.2 us (8%)
    ppermute x6, waiting for transfers between devices, exclusive_scans(): decay, state = unpack(lax.ppermute(pack(*ahead[k]), axis, pairs))  28.2 us
    ppermute x6, starting transfers between devices, exclusive_scans(): decay, state = unpack(lax.ppermute(pack(*ahead[k]), axis, pairs))  18.6 us
    pallas_call x2, Pallas kernels, block_terms(): pl.pallas_call(partial(inside_kernel, reverse=reverse), grid=(blocks,), i...  11.2 us
    pallas_call x2, Pallas kernels, convolve(): pl.pallas_call(partial(conv_kernel, reverse=reverse), grid=(count, width...  10.2 us
    pallas_call x2, Pallas kernels, block_terms(): pl.pallas_call(state_kernel, grid=(blocks,), in_specs=[spec((Q, width)),...  10.2 us
    dot_general x1, matrix products, on_device(): jnp.einsum('grd,de->gre', mirrored, w_in, preferred_element_type=jnp.floa...  7.5 us
    dot_general x2, matrix products, finish(): jnp.einsum('grh,hk->grk', from_start.reshape(count, rows, H), spread, pre...  7.04 us
    add x8, other arithmetic, chain(): next_decay[..., None, None] * first_state + next_state  6.61 us
  transfers between devices with their start and end apart: 8, of which 3 were waited for; matrix products, arithmetic and copies ran while one was open for 24% of the time, Pallas kernels for 19%

profile of v7, /device:TPU:24, one launch (start us, length us, event | category | flops | bytes accessed | tf_op | source)
XLA Modules:
  0.0 169.1 jit_solution(5653033302316272025)
XLA Ops:
  0.0 1.9 %fusion.19 = bf16[1,512,1024]{2,1,0:T(8,128)(2,1)S(1)} fusion(bf16[1,512,1024]{2,1,0:T(8,128)(2,1)} %param.13, bf16[4,1024]{1,0:T(4,128)(2,1)} %param.14, s32[512]{0:T(512)} %bitcast.251), kind=kOutput, calls=%fused_computation.22 | convolution fusion | flops 5769216 | bytes 2107392 | tf_op jit(solution)/shard_map/gtb,bd->gtd/dot_general | solution.py:258
  1.9 3.3 %collective-permute-start.1 = (bf16[1,3,1024]{2,1,0:T(4,128)(2,1)S(1)}, bf16[1,3,1024]{2,1,0:T(4,128)(2,1)}, u32[]{:S(2)}, u32[]{:S(2)}) collective-permute-start(bf16[1,3,1024]{2,1,0:T(4,128)(2,1)S(1)} %get-tuple-element.24), channel_id=1, source_target_pairs={{2,0},{4,2},{6,4},{8,6},{10,8},{12,10},{14,12},{3,1},{5,3},{7,5},{... | collective-permute-start | bytes 18440 | tf_op jit(solution)/shard_map/ppermute | solution.py:263
  5.2 3.1 %collective-permute-start = (bf16[1,3,1024]{2,1,0:T(4,128)(2,1)S(1)}, bf16[1,3,1024]{2,1,0:T(4,128)(2,1)}, u32[]{:S(2)}, u32[]{:S(2)}) collective-permute-start(bf16[1,3,1024]{2,1,0:T(4,128)(2,1)S(1)} %get-tuple-element.25), channel_id=1, source_target_pairs={{0,2},{2,4},{4,6},{6,8},{8,10},{10,12},{12,14},{1,3},{3,5},{5,7},{... | collective-permute-start | bytes 18440 | tf_op jit(solution)/shard_map/ppermute | solution.py:262
  14.2 1.7 %bitcast_exponential_fusion = (f32[1,2,256,16]{3,2,1,0:T(8,128)}, f32[1,2,16,256]{2,3,1,0:T(8,128)S(1)}) fusion(f32[2,16,2]{1,2,0:T(2,128)S(1)} %slice_bitcast_fusion.3, f32[1,2,16,2,128]{2,4,3,1,0:T(8,128)} %copy.24), kind=kLoop, calls=%fused_computation.133 | loop fusion | flops 8192 | bytes 98560 | tf_op jit(solution)/shard_map/exp | solution.py:140
  15.9 1.8 %multiply_bitcast_fusion.1.to_end_ref = f32[2,256,16]{2,1,0:T(8,128)} fusion(f32[1,2,256,16]{3,2,1,0:T(8,128)} %bitcast.229, f32[2,16]{1,0:T(2,128)S(1)} %bitcast.248, f32[1,2,16,256]{2,3,1,0:T(8,128)S(1)} %get-tuple-element.19), kind=kLoop, calls=%fused_computation.79 | loop fusion | flops 16384 | bytes 98432 | tf_op jit(solution)/shard_map/reshape | solution.py:118
  17.7 6.5 %convolution_bitcast_fusion.1.src_ref = f32[1,512,2304]{2,1,0:T(8,128)} fusion(bf16[1024,2304]{1,0:T(8,128)(2,1)} %param.15, bf16[1,512,1024]{2,1,0:T(8,128)(2,1)S(1)} %fusion.19), kind=kOutput, calls=%fused_computation.1 | convolution fusion | flops 2415919104 | bytes 10485760 | tf_op jit(solution)/shard_map/grd,de->gre/dot_general | solution.py:266
  26.4 2.2 %fusion.7 = f32[1,3,1280]{2,1,0:T(4,128)S(1)} fusion(bf16[1024,2304]{1,0:T(8,128)(2,1)} %param.15, bf16[1,3,1024]{2,1,0:T(4,128)(2,1)} %collective-permute-done), kind=kOutput, calls=%fused_computation.10 | convolution fusion | flops 7864320 | bytes 2644992 | tf_op jit(solution)/shard_map/grd,de->gre/dot_general | solution.py:267
  29.2 5.1 %shard_map.118 = bf16[1,512,1280]{2,1,0:T(8,128)(2,1)} custom-call(f32[1,512,2304]{2,1,0:T(8,128)} %convolution_bitcast_fusion.1.src_ref, f32[1,8,1280]{2,1,0:T(8,128)} %pad.12.halo_ref, f32[4,1280]{1,0:T(4,128)} %w_ref.3, f32[1,1280]{1,0:T(1,128)} %reshape.565.b_ref), custom_call_target="tpu_custom_call" | custom-call | tf_op jit(solution)/shard_map/pallas_call | solution.py:189
  34.3 5.1 %shard_map.120 = f32[2,16,64,128]{3,2,1,0:T(8,128)} custom-call(bf16[2,256,1280]{2,1,0:T(8,128)(2,1)} %bitcast.212, f32[2,256,16]{2,1,0:T(8,128)} %multiply_bitcast_fusion.1.to_end_ref), custom_call_target="tpu_custom_call" | custom-call | tf_op jit(solution)/shard_map/pallas_call | solution.py:124
  39.4 1.3 fusion.48
  41.8 2.4 %fusion.25 = bf16[512,1024]{1,0:T(8,128)(2,1)S(1)} fusion(bf16[1,512,1024]{2,1,0:T(8,128)(2,1)} %copy-done.6), kind=kOutput, calls=%fused_computation.33 | convolution fusion | flops 1076363264 | bytes 2097152 | tf_op jit(solution)/shard_map/...d,de->...e/dot_general | solution.py:28
  48.2 7.5 %convolution_bitcast_fusion.src_ref = f32[1,512,2304]{2,1,0:T(8,128)} fusion(bf16[512,1024]{1,0:T(8,128)(2,1)} %copy-done.14, bf16[1024,2304]{1,0:T(8,128)(2,1)} %param.15), kind=kOutput, calls=%fused_computation | convolution fusion | flops 2415919104 | bytes 10485760 | tf_op jit(solution)/shard_map/grd,de->gre/dot_general | solution.py:275
  55.7 2.4 %fusion.10 = f32[1,3,1280]{2,1,0:T(4,128)S(1)} fusion(bf16[1024,2304]{1,0:T(8,128)(2,1)} %param.15, bf16[1,3,1024]{2,1,0:T(4,128)(2,1)} %collective-permute-done.1), kind=kOutput, calls=%fused_computation.11 | convolution fusion | flops 16256000 | bytes 2644992 | tf_op jit(solution)/shard_map/grd,de->gre/dot_general | solution.py:276
  61.9 1.9 %collective-permute-start.2 = (f32[1,16,72,128]{3,2,1,0:T(8,128)}, f32[1,16,72,128]{3,2,1,0:T(8,128)}, u32[]{:S(2)}, u32[]{:S(2)}) collective-permute-start(f32[1,16,72,128]{3,2,1,0:T(8,128)} %pad_maximum_fusion), channel_id=1, source_target_pairs={{0,2},{2,4},{4,6},{6,8},{8,10},{10,12},{12,14},{1,3},{3,5},{5,7},{... | collective-permute-start | bytes 1769480 | tf_op jit(solution)/shard_map/ppermute | solution.py:48
  63.8 5.1 %shard_map.121 = bf16[1,512,1280]{2,1,0:T(8,128)(2,1)} custom-call(f32[1,512,2304]{2,1,0:T(8,128)} %convolution_bitcast_fusion.src_ref, f32[1,8,1280]{2,1,0:T(8,128)} %pad.13.halo_ref, f32[4,1280]{1,0:T(4,128)} %w_ref.3, f32[1,1280]{1,0:T(1,128)} %reshape.565.b_ref), custom_call_target="tpu_custom_call" | custom-call | tf_op jit(solution)/shard_map/pallas_call | solution.py:189
  69.9 5.1 %shard_map.123 = f32[2,16,64,128]{3,2,1,0:T(8,128)} custom-call(bf16[2,256,1280]{2,1,0:T(8,128)(2,1)} %bitcast.214, f32[2,256,16]{2,1,0:T(8,128)} %multiply_bitcast_fusion.to_end_ref), custom_call_target="tpu_custom_call" | custom-call | tf_op jit(solution)/shard_map/pallas_call | solution.py:124
  74.9 1.3 fusion.45
  77.2 5.0 %collective-permute-start.5 = (f32[1,16,72,128]{3,2,1,0:T(8,128)}, f32[1,16,72,128]{3,2,1,0:T(8,128)}, u32[]{:S(2)}, u32[]{:S(2)}) collective-permute-start(f32[1,16,72,128]{3,2,1,0:T(8,128)} %pad_maximum_fusion.3), channel_id=1, source_target_pairs={{2,0},{4,2},{6,4},{8,6},{10,8},{12,10},{14,12},{3,1},{5,3},{7,5},{... | collective-permute-start | bytes 1769480 | tf_op jit(solution)/shard_map/ppermute | solution.py:48
  82.2 5.6 %shard_map.119 = f32[2,256,1024]{2,1,0:T(8,128)} custom-call(bf16[2,256,1280]{2,1,0:T(8,128)(2,1)} %bitcast.213, f32[2,256,16]{2,1,0:T(8,128)} %bitcast.220, f32[2,16,256]{2,1,0:T(8,128)} %copy.26.cum_t_ref, f32[2,16,256]{2,1,0:T(8,128)} %bitcast.239), custom_call_target="tpu_custom_call" | custom-call | tf_op jit(solution)/shard_map/pallas_call | solution.py:131
  87.8 5.6 %shard_map.122 = f32[2,256,1024]{2,1,0:T(8,128)} custom-call(bf16[2,256,1280]{2,1,0:T(8,128)(2,1)} %bitcast.215, f32[2,256,16]{2,1,0:T(8,128)} %bitcast.222, f32[2,16,256]{2,1,0:T(8,128)} %copy.31.cum_t_ref, f32[2,16,256]{2,1,0:T(8,128)} %bitcast.240), custom_call_target="tpu_custom_call" | custom-call | tf_op jit(solution)/shard_map/pallas_call | solution.py:131
  97.1 1.3 collective-permute-start.3
  100.8 4.6 %collective-permute-start.6 = (f32[1,16,72,128]{3,2,1,0:T(8,128)S(1)}, f32[1,16,72,128]{3,2,1,0:T(8,128)S(1)}, u32[]{:S(2)}, u32[]{:S(2)}) collective-permute-start(f32[1,16,72,128]{3,2,1,0:T(8,128)S(1)} %pad_maximum_fusion.4), channel_id=1, source_target_pairs={{4,0},{6,2},{8,4},{10,6},{12,8},{14,10},{5,1},{7,3},{9,5},{11,7},{... | collective-permute-start | bytes 1769480 | tf_op jit(solution)/shard_map/ppermute | solution.py:48
  105.4 7.5 %collective-permute-done.3 = f32[1,16,72,128]{3,2,1,0:T(8,128)S(1)} collective-permute-done((f32[1,16,72,128]{3,2,1,0:T(8,128)S(1)}, f32[1,16,72,128]{3,2,1,0:T(8,128)S(1)}, u32[]{:S(2)}, u32[]{:S(2)}) %collective-permute-start.3) | collective-permute-done | bytes 589856 | tf_op jit(solution)/shard_map/ppermute | solution.py:48
  114.3 1.3 collective-permute-start.4
  117.8 4.6 %collective-permute-start.7 = (f32[1,16,72,128]{3,2,1,0:T(8,128)S(1)}, f32[1,16,72,128]{3,2,1,0:T(8,128)S(1)}, u32[]{:S(2)}, u32[]{:S(2)}) collective-permute-start(f32[1,16,72,128]{3,2,1,0:T(8,128)S(1)} %pad_maximum_fusion.5), channel_id=1, source_target_pairs={{8,0},{10,2},{12,4},{14,6},{9,1},{11,3},{13,5},{15,7},{24,16},{26,... | collective-permute-start | bytes 1769480 | tf_op jit(solution)/shard_map/ppermute | solution.py:48
  122.4 19.7 %collective-permute-done.4 = f32[1,16,72,128]{3,2,1,0:T(8,128)S(1)} collective-permute-done((f32[1,16,72,128]{3,2,1,0:T(8,128)S(1)}, f32[1,16,72,128]{3,2,1,0:T(8,128)S(1)}, u32[]{:S(2)}, u32[]{:S(2)}) %collective-permute-start.4) | collective-permute-done | bytes 589856 | tf_op jit(solution)/shard_map/ppermute | solution.py:48
  145.3 3.5 %fusion.17 = f32[1,512,1024]{2,1,0:T(8,128)S(1)} fusion(f32[2,256,1024]{2,1,0:T(8,128)S(1)} %fusion.84, f32[2,256,1024]{2,1,0:T(8,128)S(1)} %copy-done.11, f32[1,512,2304]{2,1,0:T(8,128)} %convolution_bitcast_fusion.1.src_ref, f32[512,16]{1,0:T(8,128)S(1)} %bitcast.237, bf16[1,512,1280]{2,1,0:T(8,128)(2,1)S(1)} %copy-done.2, f32[1024]{0:T(1024)S(1)} %mul.400, ...), kind=kOutput, calls=%fused_computation.18 | convolution fusion | flops 105938944 | bytes 9483264 | tf_op jit(solution)/shard_map/grh,hk->grk/dot_general | solution.py:239
  149.1 1.6 fusion.44
  152.8 3.5 %fusion.15 = f32[1,512,1024]{2,1,0:T(8,128)S(1)} fusion(f32[2,256,1024]{2,1,0:T(8,128)S(1)} %fusion.85, f32[2,256,1024]{2,1,0:T(8,128)S(1)} %copy-done.10, f32[1,512,2304]{2,1,0:T(8,128)} %convolution_bitcast_fusion.src_ref, f32[512,16]{1,0:T(8,128)S(1)} %bitcast.238, bf16[1,512,1280]{2,1,0:T(8,128)(2,1)S(1)} %copy-done.3, f32[1024]{0:T(1024)S(1)} %mul.400, ...), kind=kOutput, calls=%fused_computation.14 | convolution fusion | flops 105938944 | bytes 9483264 | tf_op jit(solution)/shard_map/grh,hk->grk/dot_general | solution.py:239
  156.3 1.3 copy-done.13
  158.3 6.4 %fusion.20 = f32[512,1024]{1,0:T(8,128)} fusion(bf16[1024,1024]{1,0:T(8,128)(2,1)S(1)} %copy-done, f32[1,512,1024]{2,1,0:T(8,128)} %copy-done.13, f32[512]{0:T(512)S(1)} %add_rsqrt_fusion, f32[1024]{0:T(1024)S(1)} %copy-done.26), kind=kOutput, calls=%fused_computation.24 | convolution fusion | flops 3226992640 | bytes 6297600 | tf_op jit(solution)/shard_map/grk,kd->grd/dot_general | solution.py:287
  164.6 4.5 %fusion.26 = bf16[1,512,1024]{2,1,0:T(8,128)(2,1)} fusion(f32[512,1024]{1,0:T(8,128)} %fusion.20, bf16[1024,1024]{1,0:T(8,128)(2,1)S(1)} %copy-done, f32[1,512,1024]{2,1,0:T(8,128)} %copy-done.12, f32[1024]{0:T(1024)S(1)} %copy-done.26, f32[512]{0:T(512)S(1)} %add_rsqrt_fusion.1), kind=kOutput, calls=%fused_computation.34 | convolution fusion | flops 1076363264 | bytes 7346176 | tf_op jit(solution)/shard_map/grk,kd->grd/dot_general | solution.py:285
  (141 shorter events, 34.7 us)
Async XLA Ops:
  0.0 157.8 %copy-start = (bf16[1024,1024]{1,0:T(8,128)(2,1)S(1)}, bf16[1024,1024]{1,0:T(8,128)(2,1)}, u32[]{:S(2)}) copy-start(bf16[1024,1024]{1,0:T(8,128)(2,1)} %param.23) | copy-start | bytes 6291460
  0.0 9.6 %copy-start.27 = (f32[16]{0:T(128)S(1)}, f32[16]{0:T(128)}, u32[]{:S(2)}) copy-start(f32[16]{0:T(128)} %param.20) | copy-start | bytes 196
  0.0 9.6 %copy-start.23 = (f32[16]{0:T(128)S(1)}, f32[16]{0:T(128)}, u32[]{:S(2)}) copy-start(f32[16]{0:T(128)} %param.19) | copy-start | bytes 196
  0.0 9.6 %copy-start.17 = (bf16[1024,16]{0,1:T(8,128)(2,1)S(1)}, bf16[1024,16]{0,1:T(8,128)(2,1)}, u32[]{:S(2)}) copy-start(bf16[1024,16]{0,1:T(8,128)(2,1)} %param.16) | copy-start | bytes 98308
  1.9 15.8 %copy-start.6 = (bf16[1,512,1024]{2,1,0:T(8,128)(2,1)}, bf16[1,512,1024]{2,1,0:T(8,128)(2,1)S(1)}, u32[]{:S(2)}) copy-start(bf16[1,512,1024]{2,1,0:T(8,128)(2,1)S(1)} %fusion.19) | copy-start | bytes 3145732
  1.9 39.9 %collective-permute-start.1 = (bf16[1,3,1024]{2,1,0:T(4,128)(2,1)S(1)}, bf16[1,3,1024]{2,1,0:T(4,128)(2,1)}, u32[]{:S(2)}, u32[]{:S(2)}) collective-permute-start(bf16[1,3,1024]{2,1,0:T(4,128)(2,1)S(1)} %get-tuple-element.24), channel_id=1, source_target_pairs={{2,0},{4,2},{6,4},{8,6},{10,8},{12,10},{14,12},{3,1},{5,3},{7,5},{... | collective-permute-start | bytes 18440 | tf_op jit(solution)/shard_map/ppermute | solution.py:263
  5.2 21.1 %collective-permute-start = (bf16[1,3,1024]{2,1,0:T(4,128)(2,1)S(1)}, bf16[1,3,1024]{2,1,0:T(4,128)(2,1)}, u32[]{:S(2)}, u32[]{:S(2)}) collective-permute-start(bf16[1,3,1024]{2,1,0:T(4,128)(2,1)S(1)} %get-tuple-element.25), channel_id=1, source_target_pairs={{0,2},{2,4},{4,6},{6,8},{8,10},{10,12},{12,14},{1,3},{3,5},{5,7},{... | collective-permute-start | bytes 18440 | tf_op jit(solution)/shard_map/ppermute | solution.py:262
  10.1 4.0 %copy-start.9 = (f32[512,16]{1,0:T(8,128)}, f32[512,16]{1,0:T(8,128)S(1)}, u32[]{:S(2)}) copy-start(f32[512,16]{1,0:T(8,128)S(1)} %copy.22) | copy-start | bytes 98308
  15.9 9.7 %copy-start.7 = (f32[1,2,16,256]{2,3,1,0:T(8,128)}, f32[1,2,16,256]{2,3,1,0:T(8,128)S(1)}, u32[]{:S(2)}) copy-start(f32[1,2,16,256]{2,3,1,0:T(8,128)S(1)} %get-tuple-element.19) | copy-start | bytes 98308
  17.7 6.6 %copy-start.18 = (f32[1280]{0:T(1024)S(1)}, f32[1280]{0:T(1024)}, u32[]{:S(2)}) copy-start(f32[1280]{0:T(1024)} %param.18) | copy-start | bytes 15364
  17.7 7.2 %copy-start.25 = (f32[16]{0:T(128)S(1)}, f32[16]{0:T(128)}, u32[]{:S(2)}) copy-start(f32[16]{0:T(128)} %param.21) | copy-start | bytes 196
  40.7 20.3 %copy-start.4 = (f32[1,16,64,128]{3,2,1,0:T(8,128)}, f32[1,16,64,128]{3,2,1,0:T(8,128)S(1)}, u32[]{:S(2)}) copy-start(f32[1,16,64,128]{3,2,1,0:T(8,128)S(1)} %fusion.48) | copy-start | bytes 1572868
  41.8 3.4 %copy-start.24 = (f32[16]{0:T(128)S(1)}, f32[16]{0:T(128)}, u32[]{:S(2)}) copy-start(f32[16]{0:T(128)} %param.19) | copy-start | bytes 196
  41.8 4.0 %copy-start.20 = (f32[16]{0:T(128)S(1)}, f32[16]{0:T(128)}, u32[]{:S(2)}) copy-start(f32[16]{0:T(128)} %copy-done.19) | copy-start | bytes 196
  48.2 12.0 %copy-start.8 = (f32[1,2,256,16]{3,2,1,0:T(8,128)}, f32[1,2,256,16]{3,2,1,0:T(8,128)S(1)}, u32[]{:S(2)}) copy-start(f32[1,2,256,16]{3,2,1,0:T(8,128)S(1)} %get-tuple-element.21) | copy-start | bytes 98308
  61.9 32.8 %collective-permute-start.2 = (f32[1,16,72,128]{3,2,1,0:T(8,128)}, f32[1,16,72,128]{3,2,1,0:T(8,128)}, u32[]{:S(2)}, u32[]{:S(2)}) collective-permute-start(f32[1,16,72,128]{3,2,1,0:T(8,128)} %pad_maximum_fusion), channel_id=1, source_target_pairs={{0,2},{2,4},{4,6},{6,8},{8,10},{10,12},{12,14},{1,3},{3,5},{5,7},{... | collective-permute-start | bytes 1769480 | tf_op jit(solution)/shard_map/ppermute | solution.py:48
  77.2 21.2 %collective-permute-start.5 = (f32[1,16,72,128]{3,2,1,0:T(8,128)}, f32[1,16,72,128]{3,2,1,0:T(8,128)}, u32[]{:S(2)}, u32[]{:S(2)}) collective-permute-start(f32[1,16,72,128]{3,2,1,0:T(8,128)} %pad_maximum_fusion.3), channel_id=1, source_target_pairs={{2,0},{4,2},{6,4},{8,6},{10,8},{12,10},{14,12},{3,1},{5,3},{7,5},{... | collective-permute-start | bytes 1769480 | tf_op jit(solution)/shard_map/ppermute | solution.py:48
  87.8 6.8 %copy-start.1 = (f32[2,16,64,128]{3,2,1,0:T(8,128)S(1)}, f32[2,16,64,128]{3,2,1,0:T(8,128)}, u32[]{:S(2)}) copy-start(f32[2,16,64,128]{3,2,1,0:T(8,128)} %shard_map.123) | copy-start | bytes 3145732
  93.4 2.4 %copy-start.5 = (f32[1,16,64,128]{3,2,1,0:T(8,128)S(1)}, f32[1,16,64,128]{3,2,1,0:T(8,128)}, u32[]{:S(2)}) copy-start(f32[1,16,64,128]{3,2,1,0:T(8,128)} %copy-done.4) | copy-start | bytes 1572868
  97.1 15.8 %collective-permute-start.3 = (f32[1,16,72,128]{3,2,1,0:T(8,128)S(1)}, f32[1,16,72,128]{3,2,1,0:T(8,128)S(1)}, u32[]{:S(2)}, u32[]{:S(2)}) collective-permute-start(f32[1,16,72,128]{3,2,1,0:T(8,128)S(1)} %pad_maximum_fusion.1), channel_id=1, source_target_pairs={{0,4},{2,6},{4,8},{6,10},{8,12},{10,14},{1,5},{3,7},{5,9},{7,11},{... | collective-permute-start | bytes 1769480 | tf_op jit(solution)/shard_map/ppermute | solution.py:48
  100.8 15.7 %collective-permute-start.6 = (f32[1,16,72,128]{3,2,1,0:T(8,128)S(1)}, f32[1,16,72,128]{3,2,1,0:T(8,128)S(1)}, u32[]{:S(2)}, u32[]{:S(2)}) collective-permute-start(f32[1,16,72,128]{3,2,1,0:T(8,128)S(1)} %pad_maximum_fusion.4), channel_id=1, source_target_pairs={{4,0},{6,2},{8,4},{10,6},{12,8},{14,10},{5,1},{7,3},{9,5},{11,7},{... | collective-permute-start | bytes 1769480 | tf_op jit(solution)/shard_map/ppermute | solution.py:48
  114.3 27.8 %collective-permute-start.4 = (f32[1,16,72,128]{3,2,1,0:T(8,128)S(1)}, f32[1,16,72,128]{3,2,1,0:T(8,128)S(1)}, u32[]{:S(2)}, u32[]{:S(2)}) collective-permute-start(f32[1,16,72,128]{3,2,1,0:T(8,128)S(1)} %pad_maximum_fusion.2), channel_id=1, source_target_pairs={{0,8},{2,10},{4,12},{6,14},{1,9},{3,11},{5,13},{7,15},{16,24},{18,... | collective-permute-start | bytes 1769480 | tf_op jit(solution)/shard_map/ppermute | solution.py:48
  117.8 31.3 %collective-permute-start.7 = (f32[1,16,72,128]{3,2,1,0:T(8,128)S(1)}, f32[1,16,72,128]{3,2,1,0:T(8,128)S(1)}, u32[]{:S(2)}, u32[]{:S(2)}) collective-permute-start(f32[1,16,72,128]{3,2,1,0:T(8,128)S(1)} %pad_maximum_fusion.5), channel_id=1, source_target_pairs={{8,0},{10,2},{12,4},{14,6},{9,1},{11,3},{13,5},{15,7},{24,16},{26,... | collective-permute-start | bytes 1769480 | tf_op jit(solution)/shard_map/ppermute | solution.py:48
  143.3 1.6 copy-start.11
  143.5 1.8 %copy-start.2 = (bf16[1,512,1280]{2,1,0:T(8,128)(2,1)S(1)}, bf16[1,512,1280]{2,1,0:T(8,128)(2,1)}, u32[]{:S(2)}) copy-start(bf16[1,512,1280]{2,1,0:T(8,128)(2,1)} %shard_map.118) | copy-start | bytes 3932164
  143.5 1.8 %copy-start.15 = (f32[1,2,256,16]{3,2,1,0:T(8,128)S(1)}, f32[1,2,256,16]{3,2,1,0:T(8,128)}, u32[]{:S(2)}) copy-start(f32[1,2,256,16]{3,2,1,0:T(8,128)} %get-tuple-element.18) | copy-start | bytes 98308
  143.5 1.8 %copy-start.21 = (s32[1024]{0:T(1024)S(1)}, s32[1024]{0:T(1024)}, u32[]{:S(2)}) copy-start(s32[1024]{0:T(1024)} %get-tuple-element.39) | copy-start | bytes 12292
  143.5 1.8 %copy-start.22 = (s32[1024]{0:T(1024)S(1)}, s32[1024]{0:T(1024)}, u32[]{:S(2)}) copy-start(s32[1024]{0:T(1024)} %get-tuple-element.40) | copy-start | bytes 12292
  143.6 1.8 %copy-start.28 = (pred[1024]{0:T(1024)(128)(4,1)S(1)}, pred[1024]{0:T(1024)(128)(4,1)}, u32[]{:S(2)}) copy-start(pred[1024]{0:T(1024)(128)(4,1)} %fusion.65) | copy-start | bytes 3076
  148.9 1.9 %copy-start.12 = (f32[1,512,1024]{2,1,0:T(8,128)}, f32[1,512,1024]{2,1,0:T(8,128)S(1)}, u32[]{:S(2)}) copy-start(f32[1,512,1024]{2,1,0:T(8,128)S(1)} %fusion.17) | copy-start | bytes 6291460
  150.9 1.8 %copy-start.3 = (bf16[1,512,1280]{2,1,0:T(8,128)(2,1)S(1)}, bf16[1,512,1280]{2,1,0:T(8,128)(2,1)}, u32[]{:S(2)}) copy-start(bf16[1,512,1280]{2,1,0:T(8,128)(2,1)} %shard_map.121) | copy-start | bytes 3932164
  150.9 1.8 %copy-start.16 = (f32[1,2,256,16]{3,2,1,0:T(8,128)S(1)}, f32[1,2,256,16]{3,2,1,0:T(8,128)}, u32[]{:S(2)}) copy-start(f32[1,2,256,16]{3,2,1,0:T(8,128)} %get-tuple-element.20) | copy-start | bytes 98308
  (5 other events, 5.9 us)

commit v8 on v7

--- a/solution.py
+++ b/solution.py
@@ -34,29 +34,41 @@
     return (first_decay * next_decay, next_decay[..., None, None] * first_state + next_state)
 
 
-def exclusive_scans(fwd, rev, axis):
+def scan(summary, axis, reverse, fillers):
     count = lax.axis_size(axis)
     place = lax.axis_index(axis)
-    seen = [None, None]
-    ahead = [fwd, rev]
+    seen = None
+    ahead = summary
     shift = 1
+    done = []
+    fillers = list(fillers)
     while shift < count:
-        up = [(i, i + shift) for i in range(count - shift)]
-        down = [(i + shift, i) for i in range(count - shift)]
-        got = []
-        for k, pairs in ((0, up), (1, down)):
-            decay, state = unpack(lax.ppermute(pack(*ahead[k]), axis, pairs))
-            has = (place >= shift) if k == 0 else (place < count - shift)
-            decay = jnp.where(has, decay, 1.0)
-            got.append((decay, state))
-        for k in range(2):
-            seen[k] = got[k] if seen[k] is None else chain(got[k], seen[k])
-            if 2 * shift < count:
-                ahead[k] = chain(got[k], ahead[k])
+        fill = fillers.pop(0)(done) if fillers else None
+        if fill is not None:
+            fn, args = fill
+            ahead, args = lax.optimization_barrier((ahead, args))
+        if reverse:
+            pairs = [(i + shift, i) for i in range(count - shift)]
+            has = place < count - shift
+        else:
+            pairs = [(i, i + shift) for i in range(count - shift)]
+            has = place >= shift
+        decay, state = unpack(lax.ppermute(pack(*ahead), axis, pairs))
+        got = (jnp.where(has, decay, 1.0), state)
+        if fill is not None:
+            got, out = lax.optimization_barrier((got, fn(*args)))
+            done.append(out)
+        seen = got if seen is None else chain(got, seen)
+        if 2 * shift < count:
+            ahead = chain(got, ahead)
         shift *= 2
-    if seen[0] is None:
-        return fwd_identity(fwd), fwd_identity(rev)
-    return seen[0], seen[1]
+    for make in fillers:
+        fill = make(done)
+        if fill is not None:
+            done.append(fill[0](*fill[1]))
+    if seen is None:
+        seen = fwd_identity(summary)
+    return seen, done
 
 
 def pack(decay, state):
@@ -128,6 +140,14 @@
         out_specs=spec((H, P_SIZE, N)),
         out_shape=jax.ShapeDtypeStruct((blocks, H, P_SIZE, N), jnp.float32),
     )(xbc, flat(to_end))
+    state = state.reshape(count, spans, H, P_SIZE, N)
+    return state, jnp.exp(end), jnp.exp(log_decay), (xbc, cum, cum_t, step_t)
+
+
+def inside_terms(inside_args, reverse, count, rows):
+    xbc, cum, cum_t, step_t = inside_args
+    blocks, _, width = xbc.shape
+    spec = lambda shape: pl.BlockSpec((None,) + shape, lambda i: (i,) + (0,) * len(shape))
     inside = pl.pallas_call(
         partial(inside_kernel, reverse=reverse),
         grid=(blocks,),
@@ -135,9 +155,7 @@
         out_specs=spec((Q, H * P_SIZE)),
         out_shape=jax.ShapeDtypeStruct((blocks, Q, H * P_SIZE), jnp.float32),
     )(xbc, cum, cum_t, step_t)
-    inside = inside.reshape(count, rows, H * P_SIZE)
-    state = state.reshape(count, spans, H, P_SIZE, N)
-    return inside, state, jnp.exp(end), jnp.exp(log_decay)
+    return inside.reshape(count, rows, H * P_SIZE)
 
 
 CONV_LANES = 256
@@ -205,7 +223,7 @@
     count, rows, _ = projected.shape
     activated = convolve(projected, halo, conv_w, conv_b, reverse)
     spans = rows // Q
-    inside, state, total, from_start = block_terms(activated, step_size, rates, reverse)
+    state, total, from_start, inside_args = block_terms(activated, step_size, rates, reverse)
     order = list(range(spans))
     if reverse:
         order = order[::-1]
@@ -216,12 +234,12 @@
         sofar = chain(sofar, (total[:, j], state[:, j]))
     before_decay = jnp.stack([before[j][0] for j in range(spans)], axis=1)
     before_state = jnp.stack([before[j][1] for j in range(spans)], axis=1)
-    pending = (before_decay, before_state, inside, from_start, activated)
-    return sofar, pending
-
-
-def finish(pending, incoming, gate_part, d_skip, norm_gain):
-    before_decay, before_state, inside, from_start, activated = pending
+    pending = (before_decay, before_state, from_start, activated)
+    return sofar, pending, inside_args
+
+
+def finish(pending, inside, incoming, gate_part, d_skip, norm_gain):
+    before_decay, before_state, from_start, activated = pending
     inner = H * P_SIZE
     count, rows, _ = activated.shape
     spans = rows // Q
@@ -268,23 +286,54 @@
     step_f = jax.nn.softplus(
         jnp.einsum("grd,dh->grh", strand, w_dt, preferred_element_type=jnp.float32) + dt_bias
     )
-    sum_f, pend_f = strand_terms(proj_f, halo_f, step_f, conv_w, conv_b, rates, False)
-    sum_f, (strand_late, high) = lax.optimization_barrier((sum_f, (strand, high)))
-    mirrored = flip_lanes(strand_late)
-    high_mirrored = flip_lanes(high)
-    proj_r = jnp.einsum("grd,de->gre", mirrored, w_in, preferred_element_type=jnp.float32)
-    halo_r = jnp.einsum("grd,de->gre", high_mirrored, w_source, preferred_element_type=jnp.float32)
-    step_r = jax.nn.softplus(
-        jnp.einsum("grd,dh->grh", mirrored, w_dt, preferred_element_type=jnp.float32) + dt_bias
-    )
-    sum_r, pend_r = strand_terms(proj_r, halo_r, step_r, conv_w, conv_b, rates, True)
-    in_f, in_r = exclusive_scans(sum_f, sum_r, "seq")
-    normed_f = finish(pend_f, in_f[1], proj_f[:, :, :inner], d_skip, norm_gain)
-    normed_r = finish(pend_r, in_r[1], proj_r[:, :, :inner], d_skip, norm_gain)
+    sum_f, pend_f, args_f = strand_terms(proj_f, halo_f, step_f, conv_w, conv_b, rates, False)
+    count_g = strand.shape[0]
+
+    def reverse_prep(strand_late, high_late):
+        mirrored = flip_lanes(strand_late)
+        high_mirrored = flip_lanes(high_late)
+        proj_r = jnp.einsum("grd,de->gre", mirrored, w_in, preferred_element_type=jnp.float32)
+        halo_r = jnp.einsum(
+            "grd,de->gre", high_mirrored, w_source, preferred_element_type=jnp.float32
+        )
+        step_r = jax.nn.softplus(
+            jnp.einsum("grd,dh->grh", mirrored, w_dt, preferred_element_type=jnp.float32) + dt_bias
+        )
+        sum_r, pend_r, args_r = strand_terms(proj_r, halo_r, step_r, conv_w, conv_b, rates, True)
+        return sum_r, pend_r, args_r, proj_r[:, :, :inner]
+
+    def inside_f_fill(done):
+        return (lambda *a: inside_terms(a, False, count_g, rows), args_f)
+
+    def inside_r_fill(done):
+        args_r = done[0][2]
+        return (lambda *a: inside_terms(a, True, count_g, rows), args_r)
+
+    in_f, done_f = scan(
+        sum_f,
+        "seq",
+        False,
+        [lambda done: (reverse_prep, (strand, high)), inside_f_fill, inside_r_fill],
+    )
+    sum_r, pend_r, args_r, gate_r = done_f[0]
+    inside_f, inside_r = done_f[1], done_f[2]
+
+    def forward_out(inside_f, in_state):
+        normed_f = finish(pend_f, inside_f, in_state, proj_f[:, :, :inner], d_skip, norm_gain)
+        return jnp.einsum("grk,kd->grd", normed_f, w_out, preferred_element_type=jnp.float32)
+
+    in_r, done_r = scan(
+        sum_r,
+        "seq",
+        True,
+        [lambda done: None, lambda done: (forward_out, (inside_f, in_f[1]))],
+    )
+    out_f = done_r[0]
+    normed_r = finish(pend_r, inside_r, in_r[1], gate_r, d_skip, norm_gain)
     w_out_mirrored = flip_lanes(w_out)
-    out = jnp.einsum(
-        "grk,kd->grd", normed_f, w_out, preferred_element_type=jnp.float32
-    ) + jnp.einsum("grk,kd->grd", normed_r, w_out_mirrored, preferred_element_type=jnp.float32)
+    out = out_f + jnp.einsum(
+        "grk,kd->grd", normed_r, w_out_mirrored, preferred_element_type=jnp.float32
+    )
     return out.astype(jnp.bfloat16)
 
 

time: 171 us -> 191 us (1.12)
  the two profiles are of different devices: /device:TPU:24 before, /device:TPU:0 now
where the time goes in v8:
time: 191 us; the launch traced here: 190 us
  waiting for transfers between devices  53.6 us (28%)
  matrix products  36.2 us (19%)
  Pallas kernels  31.5 us (16%)
  starting transfers between devices  26.2 us (14%)
  other arithmetic  24.9 us (13%)
  local copies, waits for them, and re-layouts  17 us (9%)
    ppermute x6, waiting for transfers between devices, scan(): decay, state = unpack(lax.ppermute(pack(*ahead), axis, pairs))  53.6 us
    ppermute x6, starting transfers between devices, scan(): decay, state = unpack(lax.ppermute(pack(*ahead), axis, pairs))  20 us
    pallas_call x2, Pallas kernels, inside_terms(): pl.pallas_call(partial(inside_kernel, reverse=reverse), grid=(blocks,), i...  11.1 us
    pallas_call x2, Pallas kernels, convolve(): pl.pallas_call(partial(conv_kernel, reverse=reverse), grid=(count, width...  10.2 us
    pallas_call x2, Pallas kernels, block_terms(): pl.pallas_call(state_kernel, grid=(blocks,), in_specs=[spec((Q, width)),...  10.2 us
    add x9, other arithmetic, chain(): next_decay[..., None, None] * first_state + next_state  7.1 us
    dot_general x1, matrix products, on_device(): jnp.einsum('grd,de->gre', strand, w_in, preferred_element_type=jnp.float32)  6.53 us
    dot_general x1, matrix products, on_device(): jnp.einsum('grk,kd->grd', normed_r, w_out_mirrored, preferred_element_typ...  6.41 us
  transfers between devices with their start and end apart: 8, of which 4 were waited for; matrix products, arithmetic and copies ran while one was open for 19% of the time, Pallas kernels for 17%

profile of v8, /device:TPU:0, one launch (start us, length us, event | category | flops | bytes accessed | tf_op | source)
XLA Modules:
  0.0 190.1 jit_solution(18380316206579937823)
XLA Ops:
  0.0 1.9 fusion.20
  1.9 4.9 %collective-permute-start = (bf16[1,3,1024]{2,1,0:T(4,128)(2,1)S(1)}, bf16[1,3,1024]{2,1,0:T(4,128)(2,1)S(1)}, u32[]{:S(2)}, u32[]{:S(2)}) collective-permute-start(bf16[1,3,1024]{2,1,0:T(4,128)(2,1)S(1)} %get-tuple-element.96), channel_id=1, source_target_pairs={{0,2},{2,4},{4,6},{6,8},{8,10},{10,12},{12,14},{1,3},{3,5},{5,7},{... | collective-permute-start | bytes 18440 | tf_op jit(solution)/shard_map/ppermute | solution.py:280
  6.8 1.3 collective-permute-start.1
  10.6 6.5 %convolution_bitcast_fusion.1.src_ref = f32[1,512,2304]{2,1,0:T(8,128)} fusion(bf16[1024,2304]{1,0:T(8,128)(2,1)} %param.15, bf16[1,512,1024]{2,1,0:T(8,128)(2,1)S(1)} %fusion.20), kind=kOutput, calls=%fused_computation.1 | convolution fusion | flops 2415919104 | bytes 10485760 | tf_op jit(solution)/shard_map/grd,de->gre/dot_general | solution.py:284
  19.4 2.2 %fusion.7 = f32[1,3,1280]{2,1,0:T(4,128)S(1)} fusion(bf16[1024,2304]{1,0:T(8,128)(2,1)} %param.15, bf16[1,3,1024]{2,1,0:T(4,128)(2,1)S(1)} %collective-permute-done), kind=kOutput, calls=%fused_computation.10 | convolution fusion | flops 7864320 | bytes 2642944 | tf_op jit(solution)/shard_map/grd,de->gre/dot_general | solution.py:285
  22.2 5.1 %shard_map.118 = bf16[1,512,1280]{2,1,0:T(8,128)(2,1)} custom-call(f32[1,512,2304]{2,1,0:T(8,128)} %convolution_bitcast_fusion.1.src_ref, f32[1,8,1280]{2,1,0:T(8,128)} %pad.12.halo_ref, f32[4,1280]{1,0:T(4,128)} %w_ref.3, f32[1,1280]{1,0:T(1,128)} %reshape.573.b_ref), custom_call_target="tpu_custom_call" | custom-call | tf_op jit(solution)/shard_map/pallas_call | solution.py:207
  27.3 5.1 %shard_map.119 = f32[2,16,64,128]{3,2,1,0:T(8,128)} custom-call(bf16[2,256,1280]{2,1,0:T(8,128)(2,1)} %bitcast.224, f32[2,256,16]{2,1,0:T(8,128)} %copy.28.to_end_ref), custom_call_target="tpu_custom_call" | custom-call | tf_op jit(solution)/shard_map/pallas_call | solution.py:136
  32.4 1.5 fusion.46
  33.9 2.5 %fusion.26 = bf16[512,1024]{1,0:T(8,128)(2,1)S(1)} fusion(bf16[1,512,1024]{2,1,0:T(8,128)(2,1)} %copy-done.12), kind=kOutput, calls=%fused_computation.35 | convolution fusion | flops 1076363264 | bytes 2097152 | tf_op jit(solution)/shard_map/...d,de->...e/dot_general | solution.py:28
  36.9 4.3 %convolution_bitcast_fusion.src_ref = f32[1,512,2304]{2,1,0:T(8,128)} fusion(bf16[512,1024]{1,0:T(8,128)(2,1)S(1)} %fusion.26, bf16[1024,2304]{1,0:T(8,128)(2,1)S(1)} %bitcast.236), kind=kOutput, calls=%fused_computation | convolution fusion | flops 2415919104 | bytes 10485760 | tf_op jit(solution)/shard_map/grd,de->gre/dot_general | solution.py:295
  43.3 2.4 %fusion.10 = f32[1,3,1280]{2,1,0:T(4,128)S(1)} fusion(bf16[1024,2304]{1,0:T(8,128)(2,1)} %param.15, bf16[1,3,1024]{2,1,0:T(4,128)(2,1)S(1)} %collective-permute-done.1), kind=kOutput, calls=%fused_computation.11 | convolution fusion | flops 16256000 | bytes 2642944 | tf_op jit(solution)/shard_map/grd,de->gre/dot_general | solution.py:296
  46.7 5.4 %collective-permute-start.2 = (f32[1,16,72,128]{3,2,1,0:T(8,128)}, f32[1,16,72,128]{3,2,1,0:T(8,128)}, u32[]{:S(2)}, u32[]{:S(2)}) collective-permute-start(f32[1,16,72,128]{3,2,1,0:T(8,128)} %pad_maximum_fusion), channel_id=1, source_target_pairs={{0,2},{2,4},{4,6},{6,8},{8,10},{10,12},{12,14},{1,3},{3,5},{5,7},{... | collective-permute-start | bytes 1769480 | tf_op jit(solution)/shard_map/ppermute | solution.py:56
  53.5 5.1 %shard_map.120 = bf16[1,512,1280]{2,1,0:T(8,128)(2,1)} custom-call(f32[1,512,2304]{2,1,0:T(8,128)} %convolution_bitcast_fusion.src_ref, f32[1,8,1280]{2,1,0:T(8,128)} %pad.13.halo_ref, f32[4,1280]{1,0:T(4,128)} %w_ref.3, f32[1,1280]{1,0:T(1,128)} %reshape.573.b_ref), custom_call_target="tpu_custom_call" | custom-call | tf_op jit(solution)/shard_map/pallas_call | solution.py:207
  58.6 5.1 %shard_map.121 = f32[2,16,64,128]{3,2,1,0:T(8,128)} custom-call(bf16[2,256,1280]{2,1,0:T(8,128)(2,1)} %bitcast.222, f32[2,256,16]{2,1,0:T(8,128)} %copy.34.to_end_ref), custom_call_target="tpu_custom_call" | custom-call | tf_op jit(solution)/shard_map/pallas_call | solution.py:136
  71.0 3.5 %collective-permute-start.4 = (f32[1,16,72,128]{3,2,1,0:T(8,128)}, f32[1,16,72,128]{3,2,1,0:T(8,128)}, u32[]{:S(2)}, u32[]{:S(2)}) collective-permute-start(f32[1,16,72,128]{3,2,1,0:T(8,128)} %pad_maximum_fusion.2), channel_id=1, source_target_pairs={{0,4},{2,6},{4,8},{6,10},{8,12},{10,14},{1,5},{3,7},{5,9},{7,11},{... | collective-permute-start | bytes 1769480 | tf_op jit(solution)/shard_map/ppermute | solution.py:56
  78.2 1.5 collective-permute-start.3
  79.7 5.6 %shard_map.122 = f32[2,256,1024]{2,1,0:T(8,128)} custom-call(bf16[2,256,1280]{2,1,0:T(8,128)(2,1)} %bitcast.225, f32[2,256,16]{2,1,0:T(8,128)} %copy.37.cum_ref, f32[2,16,256]{2,1,0:T(8,128)} %bitcast.239, f32[2,16,256]{2,1,0:T(8,128)} %bitcast.246), custom_call_target="tpu_custom_call" | custom-call | tf_op jit(solution)/shard_map/pallas_call | solution.py:151
  89.8 1.9 %pad_maximum_fusion.3 = f32[1,16,72,128]{3,2,1,0:T(8,128)} fusion(f32[1,16,8,128]{3,2,1,0:T(8,128)S(1)} %broadcast_in_dim.42, f32[1,16,64,128]{3,2,1,0:T(8,128)} %multiply_add_fusion.3), kind=kLoop, calls=%fused_computation.53 | loop fusion | flops 147456 | bytes 1179648 | tf_op jit(solution)/shard_map/concatenate | solution.py:76
  91.7 6.9 %collective-permute-start.5 = (f32[1,16,72,128]{3,2,1,0:T(8,128)}, f32[1,16,72,128]{3,2,1,0:T(8,128)}, u32[]{:S(2)}, u32[]{:S(2)}) collective-permute-start(f32[1,16,72,128]{3,2,1,0:T(8,128)} %pad_maximum_fusion.3), channel_id=1, source_target_pairs={{0,8},{2,10},{4,12},{6,14},{1,9},{3,11},{5,13},{7,15},{16,24},{18,... | collective-permute-start | bytes 1769480 | tf_op jit(solution)/shard_map/ppermute | solution.py:56
  98.6 5.6 %shard_map.123 = f32[2,256,1024]{2,1,0:T(8,128)} custom-call(bf16[2,256,1280]{2,1,0:T(8,128)(2,1)} %bitcast.223, f32[2,256,16]{2,1,0:T(8,128)} %copy.38.cum_ref, f32[2,16,256]{2,1,0:T(8,128)} %bitcast.241, f32[2,16,256]{2,1,0:T(8,128)} %bitcast.247), custom_call_target="tpu_custom_call" | custom-call | tf_op jit(solution)/shard_map/pallas_call | solution.py:151
  106.6 2.8 %collective-permute-done.5 = f32[1,16,72,128]{3,2,1,0:T(8,128)} collective-permute-done((f32[1,16,72,128]{3,2,1,0:T(8,128)}, f32[1,16,72,128]{3,2,1,0:T(8,128)}, u32[]{:S(2)}, u32[]{:S(2)}) %collective-permute-start.5) | collective-permute-done | bytes 589856 | tf_op jit(solution)/shard_map/ppermute | solution.py:56
  112.6 3.5 %fusion.19 = f32[1,512,1024]{2,1,0:T(8,128)S(1)} fusion(f32[1,512,1024]{2,1,0:T(8,128)S(1)} %bitcast.233, f32[2,256,1024]{2,1,0:T(8,128)S(1)} %fusion.81, f32[1,512,2304]{2,1,0:T(8,128)} %convolution_bitcast_fusion.1.src_ref, f32[512,16]{0,1:T(8,128)S(1)} %bitcast.251, bf16[1,512,1280]{2,1,0:T(8,128)(2,1)S(1)} %copy-done.2, f32[1024]{0:T(1024)S(1)} %mul.397, ...), kind=kOutput, calls=%fused_computation.21 | convolution fusion | flops 105938944 | bytes 9483264 | tf_op jit(solution)/shard_map/grh,hk->grk/dot_general | solution.py:257
  116.5 1.3 collective-permute-start.6
  117.8 2.6 %convolution_bitcast_fusion.2 = f32[1,512,1024]{2,1,0:T(8,128)} fusion(bf16[1024,1024]{1,0:T(8,128)(2,1)S(1)} %copy-done, f32[1,512,1024]{2,1,0:T(8,128)S(1)} %fusion.19, f32[1024]{0:T(1024)S(1)} %copy-done.22, f32[512]{0:T(512)S(1)} %add_rsqrt_fusion.1), kind=kOutput, calls=%fused_computation.34 | convolution fusion | flops 1075314688 | bytes 6297600 | tf_op jit(solution)/shard_map/grk,kd->grd/dot_general | solution.py:323
  120.4 23.7 %collective-permute-done.6 = f32[1,16,72,128]{3,2,1,0:T(8,128)S(1)} collective-permute-done((f32[1,16,72,128]{3,2,1,0:T(8,128)S(1)}, f32[1,16,72,128]{3,2,1,0:T(8,128)S(1)}, u32[]{:S(2)}, u32[]{:S(2)}) %collective-permute-start.6) | collective-permute-done | bytes 589856 | tf_op jit(solution)/shard_map/ppermute | solution.py:56
  144.7 1.5 collective-permute-start.7
  147.3 26.6 %collective-permute-done.7 = f32[1,16,72,128]{3,2,1,0:T(8,128)S(1)} collective-permute-done((f32[1,16,72,128]{3,2,1,0:T(8,128)S(1)}, f32[1,16,72,128]{3,2,1,0:T(8,128)S(1)}, u32[]{:S(2)}, u32[]{:S(2)}) %collective-permute-start.7) | collective-permute-done | bytes 589856 | tf_op jit(solution)/shard_map/ppermute | solution.py:56
  173.9 1.2 fusion.44
  177.4 1.3 fusion.17
  178.7 1.3 copy-done.4
  180.2 6.4 %fusion.21 = f32[512,1024]{1,0:T(8,128)} fusion(bf16[1024,1024]{1,0:T(8,128)(2,1)S(1)} %copy-done, f32[1,512,1024]{2,1,0:T(8,128)} %copy-done.4, f32[512]{0:T(512)S(1)} %add_rsqrt_fusion, f32[1024]{0:T(1024)S(1)} %copy-done.22), kind=kOutput, calls=%fused_computation.25 | convolution fusion | flops 3226992640 | bytes 6297600 | tf_op jit(solution)/shard_map/grk,kd->grd/dot_general | solution.py:334
  186.6 3.5 %fusion.15 = bf16[1,512,1024]{2,1,0:T(8,128)(2,1)} fusion(f32[1,512,1024]{2,1,0:T(8,128)} %convolution_bitcast_fusion.2, f32[512,1024]{1,0:T(8,128)} %fusion.21), kind=kLoop, calls=%fused_computation.14 | loop fusion | flops 1048576 | bytes 5242880 | tf_op jit(solution)/shard_map/convert_element_type | solution.py:337
  (153 shorter events, 35.6 us)
Async XLA Ops:
  0.0 117.8 %copy-start = (bf16[1024,1024]{1,0:T(8,128)(2,1)S(1)}, bf16[1024,1024]{1,0:T(8,128)(2,1)}, u32[]{:S(2)}) copy-start(bf16[1024,1024]{1,0:T(8,128)(2,1)} %param.23) | copy-start | bytes 6291460
  0.0 8.1 %copy-start.18 = (bf16[1024,16]{0,1:T(8,128)(2,1)S(1)}, bf16[1024,16]{0,1:T(8,128)(2,1)}, u32[]{:S(2)}) copy-start(bf16[1024,16]{0,1:T(8,128)(2,1)} %param.16) | copy-start | bytes 98308
  0.0 8.1 %copy-start.20 = (f32[16]{0:T(128)S(1)}, f32[16]{0:T(128)}, u32[]{:S(2)}) copy-start(f32[16]{0:T(128)} %param.19) | copy-start | bytes 196
  0.0 8.6 %copy-start.23 = (f32[16]{0:T(128)S(1)}, f32[16]{0:T(128)}, u32[]{:S(2)}) copy-start(f32[16]{0:T(128)} %param.20) | copy-start | bytes 196
  1.9 15.2 %copy-start.12 = (bf16[1,512,1024]{2,1,0:T(8,128)(2,1)}, bf16[1,512,1024]{2,1,0:T(8,128)(2,1)S(1)}, u32[]{:S(2)}) copy-start(bf16[1,512,1024]{2,1,0:T(8,128)(2,1)S(1)} %fusion.20) | copy-start | bytes 3145732
  1.9 17.4 %collective-permute-start = (bf16[1,3,1024]{2,1,0:T(4,128)(2,1)S(1)}, bf16[1,3,1024]{2,1,0:T(4,128)(2,1)S(1)}, u32[]{:S(2)}, u32[]{:S(2)}) collective-permute-start(bf16[1,3,1024]{2,1,0:T(4,128)(2,1)S(1)} %get-tuple-element.96), channel_id=1, source_target_pairs={{0,2},{2,4},{4,6},{6,8},{8,10},{10,12},{12,14},{1,3},{3,5},{5,7},{... | collective-permute-start | bytes 18440 | tf_op jit(solution)/shard_map/ppermute | solution.py:280
  6.8 27.1 %collective-permute-start.1 = (bf16[1,3,1024]{2,1,0:T(4,128)(2,1)S(1)}, bf16[1,3,1024]{2,1,0:T(4,128)(2,1)S(1)}, u32[]{:S(2)}, u32[]{:S(2)}) collective-permute-start(bf16[1,3,1024]{2,1,0:T(4,128)(2,1)S(1)} %get-tuple-element.95), channel_id=1, source_target_pairs={{2,0},{4,2},{6,4},{8,6},{10,8},{12,10},{14,12},{3,1},{5,3},{7,5},{... | collective-permute-start | bytes 18440 | tf_op jit(solution)/shard_map/ppermute | solution.py:281
  10.3 66.1 %copy-start.16 = (f32[1,2,16,256]{3,2,1,0:T(8,128)}, f32[1,2,16,256]{3,2,1,0:T(8,128)S(1)}, u32[]{:S(2)}) copy-start(f32[1,2,16,256]{3,2,1,0:T(8,128)S(1)} %get-tuple-element.92) | copy-start | bytes 98308
  10.5 7.4 %copy-start.19 = (f32[1280]{0:T(1024)S(1)}, f32[1280]{0:T(1024)}, u32[]{:S(2)}) copy-start(f32[1280]{0:T(1024)} %param.18) | copy-start | bytes 15364
  10.6 8.7 %copy-start.21 = (f32[16]{0:T(128)S(1)}, f32[16]{0:T(128)}, u32[]{:S(2)}) copy-start(f32[16]{0:T(128)} %param.21) | copy-start | bytes 196
  32.4 4.5 %slice-start.1 = ((s8[4718592]{0:T(1024)(128)(4,1)}), s8[4194304]{0:T(1024)(128)(4,1)S(1)}, s32[]{:S(2)}) async-start(s8[4718592]{0:T(1024)(128)(4,1)} %bitcast.235), calls=%async_computation.1 | async-start | bytes 8388608
  33.9 3.0 %slice-start.2 = ((s8[4718592]{0:T(1024)(128)(4,1)}), s8[524288]{0:T(1024)(128)(4,1)S(1)}, s32[]{:S(2)}) async-start(s8[4718592]{0:T(1024)(128)(4,1)} %bitcast.235), calls=%async_computation.2 | async-start | bytes 1048576
  43.1 45.8 %copy-start.17 = (f32[1,2,256,16]{2,3,1,0:T(8,128)}, f32[1,2,256,16]{2,3,1,0:T(8,128)S(1)}, u32[]{:S(2)}) copy-start(f32[1,2,256,16]{2,3,1,0:T(8,128)S(1)} %get-tuple-element.94) | copy-start | bytes 98308
  46.7 20.9 %collective-permute-start.2 = (f32[1,16,72,128]{3,2,1,0:T(8,128)}, f32[1,16,72,128]{3,2,1,0:T(8,128)}, u32[]{:S(2)}, u32[]{:S(2)}) collective-permute-start(f32[1,16,72,128]{3,2,1,0:T(8,128)} %pad_maximum_fusion), channel_id=1, source_target_pairs={{0,2},{2,4},{4,6},{6,8},{8,10},{10,12},{12,14},{1,3},{3,5},{5,7},{... | collective-permute-start | bytes 1769480 | tf_op jit(solution)/shard_map/ppermute | solution.py:56
  63.7 3.0 %copy-start.6 = (f32[2,16,64,128]{3,2,1,0:T(8,128)S(1)}, f32[2,16,64,128]{3,2,1,0:T(8,128)}, u32[]{:S(2)}) copy-start(f32[2,16,64,128]{3,2,1,0:T(8,128)} %shard_map.121) | copy-start | bytes 3145732
  67.6 7.8 %copy-start.5 = (f32[2,16,64,128]{3,2,1,0:T(8,128)S(1)}, f32[2,16,64,128]{3,2,1,0:T(8,128)}, u32[]{:S(2)}) copy-start(f32[2,16,64,128]{3,2,1,0:T(8,128)} %shard_map.119) | copy-start | bytes 3145732
  70.1 7.2 %copy-start.9 = (f32[1,16,64,128]{3,2,1,0:T(8,128)S(1)}, f32[1,16,64,128]{3,2,1,0:T(8,128)}, u32[]{:S(2)}) copy-start(f32[1,16,64,128]{3,2,1,0:T(8,128)} %fusion.45) | copy-start | bytes 1572868
  71.0 14.7 %collective-permute-start.4 = (f32[1,16,72,128]{3,2,1,0:T(8,128)}, f32[1,16,72,128]{3,2,1,0:T(8,128)}, u32[]{:S(2)}, u32[]{:S(2)}) collective-permute-start(f32[1,16,72,128]{3,2,1,0:T(8,128)} %pad_maximum_fusion.2), channel_id=1, source_target_pairs={{0,4},{2,6},{4,8},{6,10},{8,12},{10,14},{1,5},{3,7},{5,9},{7,11},{... | collective-permute-start | bytes 1769480 | tf_op jit(solution)/shard_map/ppermute | solution.py:56
  78.2 26.0 %collective-permute-start.3 = (f32[1,16,72,128]{3,2,1,0:T(8,128)}, f32[1,16,72,128]{3,2,1,0:T(8,128)}, u32[]{:S(2)}, u32[]{:S(2)}) collective-permute-start(f32[1,16,72,128]{3,2,1,0:T(8,128)} %pad_maximum_fusion.1), channel_id=1, source_target_pairs={{2,0},{4,2},{6,4},{8,6},{10,8},{12,10},{14,12},{3,1},{5,3},{7,5},{... | collective-permute-start | bytes 1769480 | tf_op jit(solution)/shard_map/ppermute | solution.py:56
  86.8 2.0 %copy-start.10 = (f32[1,16,64,128]{3,2,1,0:T(8,128)}, f32[1,16,64,128]{3,2,1,0:T(8,128)S(1)}, u32[]{:S(2)}) copy-start(f32[1,16,64,128]{3,2,1,0:T(8,128)S(1)} %slice.156) | copy-start | bytes 1572868
  91.7 17.6 %collective-permute-start.5 = (f32[1,16,72,128]{3,2,1,0:T(8,128)}, f32[1,16,72,128]{3,2,1,0:T(8,128)}, u32[]{:S(2)}, u32[]{:S(2)}) collective-permute-start(f32[1,16,72,128]{3,2,1,0:T(8,128)} %pad_maximum_fusion.3), channel_id=1, source_target_pairs={{0,8},{2,10},{4,12},{6,14},{1,9},{3,11},{5,13},{7,15},{16,24},{18,... | collective-permute-start | bytes 1769480 | tf_op jit(solution)/shard_map/ppermute | solution.py:56
  104.2 6.3 %copy-start.8 = (f32[1,16,64,128]{3,2,1,0:T(8,128)S(1)}, f32[1,16,64,128]{3,2,1,0:T(8,128)}, u32[]{:S(2)}) copy-start(f32[1,16,64,128]{3,2,1,0:T(8,128)} %copy-done.7) | copy-start | bytes 1572868
  104.2 6.3 %copy-start.11 = (f32[1,16,64,128]{3,2,1,0:T(8,128)S(1)}, f32[1,16,64,128]{3,2,1,0:T(8,128)}, u32[]{:S(2)}) copy-start(f32[1,16,64,128]{3,2,1,0:T(8,128)} %copy-done.10) | copy-start | bytes 1572868
  105.3 5.3 %copy-start.15 = (f32[1,1,16,64,128]{4,3,2,1,0:T(8,128)S(1)}, f32[1,1,16,64,128]{4,3,2,1,0:T(8,128)}, u32[]{:S(2)}) copy-start(f32[1,1,16,64,128]{4,3,2,1,0:T(8,128)} %slice_add_fusion.1) | copy-start | bytes 1572868
  110.6 1.6 copy-start.14
  110.8 1.8 copy-start.2
  116.1 1.7 copy-start.22
  116.5 27.7 %collective-permute-start.6 = (f32[1,16,72,128]{3,2,1,0:T(8,128)S(1)}, f32[1,16,72,128]{3,2,1,0:T(8,128)S(1)}, u32[]{:S(2)}, u32[]{:S(2)}) collective-permute-start(f32[1,16,72,128]{3,2,1,0:T(8,128)S(1)} %pad_maximum_fusion.4), channel_id=1, source_target_pairs={{4,0},{6,2},{8,4},{10,6},{12,8},{14,10},{5,1},{7,3},{9,5},{11,7},{... | collective-permute-start | bytes 1769480 | tf_op jit(solution)/shard_map/ppermute | solution.py:56
  120.4 25.8 %copy-start.1 = (bf16[1,512,1280]{2,1,0:T(8,128)(2,1)S(1)}, bf16[1,512,1280]{2,1,0:T(8,128)(2,1)}, u32[]{:S(2)}) copy-start(bf16[1,512,1280]{2,1,0:T(8,128)(2,1)} %shard_map.120) | copy-start | bytes 3932164
  144.7 29.2 %collective-permute-start.7 = (f32[1,16,72,128]{3,2,1,0:T(8,128)S(1)}, f32[1,16,72,128]{3,2,1,0:T(8,128)S(1)}, u32[]{:S(2)}, u32[]{:S(2)}) collective-permute-start(f32[1,16,72,128]{3,2,1,0:T(8,128)S(1)} %pad_maximum_fusion.5), channel_id=1, source_target_pairs={{8,0},{10,2},{12,4},{14,6},{9,1},{11,3},{13,5},{15,7},{24,16},{26,... | collective-permute-start | bytes 1769480 | tf_op jit(solution)/shard_map/ppermute | solution.py:56
  146.3 28.9 %copy-start.13 = (f32[1,2,16,64,128]{4,3,2,1,0:T(8,128)S(1)}, f32[1,2,16,64,128]{4,3,2,1,0:T(8,128)}, u32[]{:S(2)}) copy-start(f32[1,2,16,64,128]{4,3,2,1,0:T(8,128)} %stack.15) | copy-start | bytes 3145732
  175.3 2.1 %slice-start = ((f32[1,512,2304]{2,1,0:T(8,128)}), f32[1,512,1024]{2,1,0:T(8,128)S(1)}, s32[]{:S(2)}) async-start(f32[1,512,2304]{2,1,0:T(8,128)} %convolution_bitcast_fusion.src_ref), calls=%async_computation | async-start | bytes 4194304 | tf_op jit(solution)/shard_map/slice | solution.py:303
  (3 other events, 4.1 us)

commit v9 on v7

--- a/solution.py
+++ b/solution.py
@@ -60,12 +60,16 @@
 
 
 def pack(decay, state):
-    extra = jnp.broadcast_to(decay[:, :, None, None], decay.shape + (8, state.shape[-1]))
-    return jnp.concatenate([state, extra], axis=2)
+    count = state.shape[0]
+    flat = state.reshape(count, H * P_SIZE, N)
+    extra = jnp.zeros((count, 8, N), jnp.float32).at[:, 0, :H].set(decay)
+    return jnp.concatenate([flat, extra], axis=1)
 
 
 def unpack(packed):
-    return packed[:, :, P_SIZE, 0], packed[:, :, :P_SIZE]
+    count = packed.shape[0]
+    rows = H * P_SIZE
+    return packed[:, rows, :H], packed[:, :rows].reshape(count, H, P_SIZE, N)
 
 
 def fwd_identity(summary):

time: 171 us -> 169 us (0.988)
  local copies, waits for them, and re-layouts: 14.2 us -> 19.3 us
  waiting for transfers between devices: 28.2 us -> 23.9 us
  other arithmetic: 25.8 us -> 22.4 us
    ppermute x6, waiting for transfers between devices: 28.2 us -> 23.9 us  [exclusive_scans(): decay, state = unpack(lax.ppermute(pack(*ahead[k]), axis, pairs))]
    unnamed x58 -> x70, local copies, waits for them, and re-layouts: 4.37 us -> 7.19 us
    slice x2 -> x3, other arithmetic: 0.01 us -> 2.13 us  [strand_terms(): sofar = chain(sofar, (total[:, j], state[:, j]))]
    mul x2, other arithmetic: 2.86 us -> 0.75 us  [chain(): next_decay[..., None, None] * first_state + next_state]
    slice x1 -> x4, local copies, waits for them, and re-layouts: 0.16 us -> 2.22 us  [unpack(): return (packed[:, rows, :H], packed[:, :rows].reshape(count, H, P_SIZE, N))]
    add x8 -> x9, other arithmetic: 6.61 us -> 4.62 us  [chain(): next_decay[..., None, None] * first_state + next_state]
    mul x4 -> x5, other arithmetic: 3.15 us -> 1.39 us  [chain(): first_decay * next_decay]
  transfers between devices with their start and end apart: 8 -> 8, of which waited for: 3 -> 2; matrix products, arithmetic and copies ran while one was open for 24% -> 25% of each run, Pallas kernels for 19% -> 19%
where the time goes in v9:
time: 169 us; the launch traced here: 168 us
  matrix products  43.8 us (26%)
  Pallas kernels  31.6 us (19%)
  starting transfers between devices  26.1 us (15%)
  waiting for transfers between devices  23.9 us (14%)
  other arithmetic  22.4 us (13%)
  local copies, waits for them, and re-layouts  19.3 us (11%)
    ppermute x6, waiting for transfers between devices, exclusive_scans(): decay, state = unpack(lax.ppermute(pack(*ahead[k]), axis, pairs))  23.9 us
    ppermute x6, starting transfers between devices, exclusive_scans(): decay, state = unpack(lax.ppermute(pack(*ahead[k]), axis, pairs))  19.7 us
    pallas_call x2, Pallas kernels, block_terms(): pl.pallas_call(partial(inside_kernel, reverse=reverse), grid=(blocks,), i...  11.1 us
    pallas_call x2, Pallas kernels, convolve(): pl.pallas_call(partial(conv_kernel, reverse=reverse), grid=(count, width...  10.2 us
    pallas_call x2, Pallas kernels, block_terms(): pl.pallas_call(state_kernel, grid=(blocks,), in_specs=[spec((Q, width)),...  10.2 us
    dot_general x1, matrix products, on_device(): jnp.einsum('grd,de->gre', mirrored, w_in, preferred_element_type=jnp.floa...  7.51 us
    unnamed x70, local copies, waits for them, and re-layouts  7.19 us
    dot_general x2, matrix products, finish(): jnp.einsum('grh,hk->grk', from_start.reshape(count, rows, H), spread, pre...  7.04 us
  transfers between devices with their start and end apart: 8, of which 2 were waited for; matrix products, arithmetic and copies ran while one was open for 25% of the time, Pallas kernels for 19%

profile of v9, /device:TPU:24, one launch (start us, length us, event | category | flops | bytes accessed | tf_op | source)
XLA Modules:
  0.0 167.7 jit_solution(812098297787643716)
XLA Ops:
  0.0 1.9 %fusion.19 = bf16[1,512,1024]{2,1,0:T(8,128)(2,1)S(1)} fusion(bf16[1,512,1024]{2,1,0:T(8,128)(2,1)} %param.25, bf16[4,1024]{1,0:T(4,128)(2,1)} %param.26, s32[512]{0:T(512)} %bitcast.278), kind=kOutput, calls=%fused_computation.22 | convolution fusion | flops 5769216 | bytes 2107392 | tf_op jit(solution)/shard_map/gtb,bd->gtd/dot_general | solution.py:262
  1.9 3.3 %collective-permute-start.1 = (bf16[1,3,1024]{2,1,0:T(4,128)(2,1)S(1)}, bf16[1,3,1024]{2,1,0:T(4,128)(2,1)}, u32[]{:S(2)}, u32[]{:S(2)}) collective-permute-start(bf16[1,3,1024]{2,1,0:T(4,128)(2,1)S(1)} %get-tuple-element.97), channel_id=1, source_target_pairs={{2,0},{4,2},{6,4},{8,6},{10,8},{12,10},{14,12},{3,1},{5,3},{7,5},{... | collective-permute-start | bytes 18440 | tf_op jit(solution)/shard_map/ppermute | solution.py:267
  5.2 3.1 %collective-permute-start = (bf16[1,3,1024]{2,1,0:T(4,128)(2,1)S(1)}, bf16[1,3,1024]{2,1,0:T(4,128)(2,1)}, u32[]{:S(2)}, u32[]{:S(2)}) collective-permute-start(bf16[1,3,1024]{2,1,0:T(4,128)(2,1)S(1)} %get-tuple-element.98), channel_id=1, source_target_pairs={{0,2},{2,4},{4,6},{6,8},{8,10},{10,12},{12,14},{1,3},{3,5},{5,7},{... | collective-permute-start | bytes 18440 | tf_op jit(solution)/shard_map/ppermute | solution.py:266
  14.2 1.7 %bitcast_exponential_fusion = (f32[1,2,256,16]{3,2,1,0:T(8,128)}, f32[1,2,16,256]{2,3,1,0:T(8,128)S(1)}) fusion(f32[2,16,2]{1,2,0:T(2,128)S(1)} %slice_bitcast_fusion.2, f32[1,2,16,2,128]{2,4,3,1,0:T(8,128)} %copy.23), kind=kLoop, calls=%fused_computation.126 | loop fusion | flops 8192 | bytes 98560 | tf_op jit(solution)/shard_map/exp | solution.py:144
  15.9 1.8 %multiply_bitcast_fusion.1.to_end_ref = f32[2,256,16]{2,1,0:T(8,128)} fusion(f32[1,2,256,16]{3,2,1,0:T(8,128)} %bitcast.248, f32[2,16]{1,0:T(2,128)S(1)} %bitcast.275, f32[1,2,16,256]{2,3,1,0:T(8,128)S(1)} %get-tuple-element.86), kind=kLoop, calls=%fused_computation.75 | loop fusion | flops 16384 | bytes 98432 | tf_op jit(solution)/shard_map/reshape | solution.py:122
  17.7 6.6 %convolution_bitcast_fusion.1.src_ref = f32[1,512,2304]{2,1,0:T(8,128)} fusion(bf16[1024,2304]{1,0:T(8,128)(2,1)} %param.27, bf16[1,512,1024]{2,1,0:T(8,128)(2,1)S(1)} %fusion.19), kind=kOutput, calls=%fused_computation.1 | convolution fusion | flops 2415919104 | bytes 10485760 | tf_op jit(solution)/shard_map/grd,de->gre/dot_general | solution.py:270
  26.4 2.2 %fusion.7 = f32[1,3,1280]{2,1,0:T(4,128)S(1)} fusion(bf16[1024,2304]{1,0:T(8,128)(2,1)} %param.27, bf16[1,3,1024]{2,1,0:T(4,128)(2,1)} %collective-permute-done), kind=kOutput, calls=%fused_computation.10 | convolution fusion | flops 7864320 | bytes 2644992 | tf_op jit(solution)/shard_map/grd,de->gre/dot_general | solution.py:271
  29.2 5.1 %shard_map.118 = bf16[1,512,1280]{2,1,0:T(8,128)(2,1)} custom-call(f32[1,512,2304]{2,1,0:T(8,128)} %convolution_bitcast_fusion.1.src_ref, f32[1,8,1280]{2,1,0:T(8,128)} %pad.42.halo_ref, f32[4,1280]{1,0:T(4,128)} %w_ref.3, f32[1,1280]{1,0:T(1,128)} %reshape.994.b_ref), custom_call_target="tpu_custom_call" | custom-call | tf_op jit(solution)/shard_map/pallas_call | solution.py:193
  34.3 5.1 %shard_map.120 = f32[2,16,64,128]{3,2,1,0:T(8,128)} custom-call(bf16[2,256,1280]{2,1,0:T(8,128)(2,1)} %bitcast.224, f32[2,256,16]{2,1,0:T(8,128)} %multiply_bitcast_fusion.1.to_end_ref), custom_call_target="tpu_custom_call" | custom-call | tf_op jit(solution)/shard_map/pallas_call | solution.py:128
  39.4 1.3 fusion.43
  41.9 2.4 %fusion.25 = bf16[512,1024]{1,0:T(8,128)(2,1)S(1)} fusion(bf16[1,512,1024]{2,1,0:T(8,128)(2,1)} %copy-done.10), kind=kOutput, calls=%fused_computation.33 | convolution fusion | flops 1076363264 | bytes 2097152 | tf_op jit(solution)/shard_map/...d,de->...e/dot_general | solution.py:28
  48.3 7.5 %convolution_bitcast_fusion.src_ref = f32[1,512,2304]{2,1,0:T(8,128)} fusion(bf16[512,1024]{1,0:T(8,128)(2,1)} %copy-done.20, bf16[1024,2304]{1,0:T(8,128)(2,1)} %param.27), kind=kOutput, calls=%fused_computation | convolution fusion | flops 2415919104 | bytes 10485760 | tf_op jit(solution)/shard_map/grd,de->gre/dot_general | solution.py:279
  55.8 2.4 %fusion.10 = f32[1,3,1280]{2,1,0:T(4,128)S(1)} fusion(bf16[1024,2304]{1,0:T(8,128)(2,1)} %param.27, bf16[1,3,1024]{2,1,0:T(4,128)(2,1)} %collective-permute-done.1), kind=kOutput, calls=%fused_computation.11 | convolution fusion | flops 16256000 | bytes 2644992 | tf_op jit(solution)/shard_map/grd,de->gre/dot_general | solution.py:280
  62.1 1.9 %collective-permute-start.2 = (f32[1,1032,128]{2,1,0:T(8,128)}, f32[1,1032,128]{2,1,0:T(8,128)}, u32[]{:S(2)}, u32[]{:S(2)}) collective-permute-start(f32[1,1032,128]{2,1,0:T(8,128)} %select_maximum_fusion.5), channel_id=1, source_target_pairs={{0,2},{2,4},{4,6},{6,8},{8,10},{10,12},{12,14},{1,3},{3,5},{5,7},{... | collective-permute-start | bytes 1585160 | tf_op jit(solution)/shard_map/ppermute | solution.py:48
  64.0 5.1 %shard_map.121 = bf16[1,512,1280]{2,1,0:T(8,128)(2,1)} custom-call(f32[1,512,2304]{2,1,0:T(8,128)} %convolution_bitcast_fusion.src_ref, f32[1,8,1280]{2,1,0:T(8,128)} %pad.43.halo_ref, f32[4,1280]{1,0:T(4,128)} %w_ref.3, f32[1,1280]{1,0:T(1,128)} %reshape.994.b_ref), custom_call_target="tpu_custom_call" | custom-call | tf_op jit(solution)/shard_map/pallas_call | solution.py:193
  70.0 5.1 %shard_map.123 = f32[2,16,64,128]{3,2,1,0:T(8,128)} custom-call(bf16[2,256,1280]{2,1,0:T(8,128)(2,1)} %bitcast.226, f32[2,256,16]{2,1,0:T(8,128)} %multiply_bitcast_fusion.to_end_ref), custom_call_target="tpu_custom_call" | custom-call | tf_op jit(solution)/shard_map/pallas_call | solution.py:128
  75.1 2.1 %fusion.71 = (f32[1,1,16,64,128]{4,3,2,1,0:T(8,128)S(1)}, f32[1,1,16,64,128]{4,3,2,1,0:T(8,128)}, f32[1,1,16,64,128]{4,3,2,1,0:T(8,128)S(1)}) fusion(f32[1,2,16,64,128]{4,3,2,1,0:T(8,128)} %bitcast.246, f32[16]{0:T(128)S(1)} %bitcast_multiply_fusion.4), kind=kLoop, calls=%fused_computation.136 | loop fusion | flops 131072 | bytes 2621504 | tf_op jit(solution)/shard_map/slice | solution.py:220
  79.2 5.0 %collective-permute-start.5 = (f32[1,1032,128]{2,1,0:T(8,128)}, f32[1,1032,128]{2,1,0:T(8,128)}, u32[]{:S(2)}, u32[]{:S(2)}) collective-permute-start(f32[1,1032,128]{2,1,0:T(8,128)} %select_maximum_fusion.2), channel_id=1, source_target_pairs={{2,0},{4,2},{6,4},{8,6},{10,8},{12,10},{14,12},{3,1},{5,3},{7,5},{... | collective-permute-start | bytes 1585160 | tf_op jit(solution)/shard_map/ppermute | solution.py:48
  84.2 5.6 %shard_map.119 = f32[2,256,1024]{2,1,0:T(8,128)} custom-call(bf16[2,256,1280]{2,1,0:T(8,128)(2,1)} %bitcast.225, f32[2,256,16]{2,1,0:T(8,128)} %bitcast.238, f32[2,16,256]{2,1,0:T(8,128)} %copy.25.cum_t_ref, f32[2,16,256]{2,1,0:T(8,128)} %bitcast.263), custom_call_target="tpu_custom_call" | custom-call | tf_op jit(solution)/shard_map/pallas_call | solution.py:135
  89.8 5.6 %shard_map.122 = f32[2,256,1024]{2,1,0:T(8,128)} custom-call(bf16[2,256,1280]{2,1,0:T(8,128)(2,1)} %bitcast.227, f32[2,256,16]{2,1,0:T(8,128)} %bitcast.240, f32[2,16,256]{2,1,0:T(8,128)} %copy.30.cum_t_ref, f32[2,16,256]{2,1,0:T(8,128)} %bitcast.264), custom_call_target="tpu_custom_call" | custom-call | tf_op jit(solution)/shard_map/pallas_call | solution.py:135
  99.9 1.3 collective-permute-start.3
  102.1 1.3 multiply_add_fusion.3
  103.5 4.6 %collective-permute-start.6 = (f32[1,1032,128]{2,1,0:T(8,128)S(1)}, f32[1,1032,128]{2,1,0:T(8,128)S(1)}, u32[]{:S(2)}, u32[]{:S(2)}) collective-permute-start(f32[1,1032,128]{2,1,0:T(8,128)S(1)} %select_maximum_fusion.1), channel_id=1, source_target_pairs={{4,0},{6,2},{8,4},{10,6},{12,8},{14,10},{5,1},{7,3},{9,5},{11,7},{... | collective-permute-start | bytes 1585160 | tf_op jit(solution)/shard_map/ppermute | solution.py:48
  108.1 6.6 %collective-permute-done.3 = f32[1,1032,128]{2,1,0:T(8,128)} collective-permute-done((f32[1,1032,128]{2,1,0:T(8,128)}, f32[1,1032,128]{2,1,0:T(8,128)}, u32[]{:S(2)}, u32[]{:S(2)}) %collective-permute-start.3) | collective-permute-done | bytes 528416 | tf_op jit(solution)/shard_map/ppermute | solution.py:48
  116.6 1.3 collective-permute-start.4
  118.2 5.6 %collective-permute-start.7 = (f32[1,1032,128]{2,1,0:T(8,128)S(1)}, f32[1,1032,128]{2,1,0:T(8,128)S(1)}, u32[]{:S(2)}, u32[]{:S(2)}) collective-permute-start(f32[1,1032,128]{2,1,0:T(8,128)S(1)} %select_maximum_fusion), channel_id=1, source_target_pairs={{8,0},{10,2},{12,4},{14,6},{9,1},{11,3},{13,5},{15,7},{24,16},{26,... | collective-permute-start | bytes 1585160 | tf_op jit(solution)/shard_map/ppermute | solution.py:48
  124.6 17.3 %collective-permute-done.4 = f32[1,1032,128]{2,1,0:T(8,128)S(1)} collective-permute-done((f32[1,1032,128]{2,1,0:T(8,128)S(1)}, f32[1,1032,128]{2,1,0:T(8,128)S(1)}, u32[]{:S(2)}, u32[]{:S(2)}) %collective-permute-start.4) | collective-permute-done | bytes 528416 | tf_op jit(solution)/shard_map/ppermute | solution.py:48
  144.1 3.5 %fusion.17 = f32[1,512,1024]{2,1,0:T(8,128)S(1)} fusion(f32[2,256,1024]{2,1,0:T(8,128)S(1)} %fusion.77, f32[2,256,1024]{2,1,0:T(8,128)S(1)} %copy-done.15, f32[1,512,2304]{2,1,0:T(8,128)} %convolution_bitcast_fusion.1.src_ref, f32[512,16]{1,0:T(8,128)S(1)} %bitcast.261, bf16[1,512,1280]{2,1,0:T(8,128)(2,1)S(1)} %copy-done.1, f32[1024]{0:T(1024)S(1)} %mul.475, ...), kind=kOutput, calls=%fused_computation.18 | convolution fusion | flops 105938944 | bytes 9483264 | tf_op jit(solution)/shard_map/grh,hk->grk/dot_general | solution.py:243
  151.3 3.5 %fusion.15 = f32[1,512,1024]{2,1,0:T(8,128)S(1)} fusion(f32[2,256,1024]{2,1,0:T(8,128)S(1)} %fusion.78, f32[2,256,1024]{2,1,0:T(8,128)S(1)} %copy-done.14, f32[1,512,2304]{2,1,0:T(8,128)} %convolution_bitcast_fusion.src_ref, f32[512,16]{1,0:T(8,128)S(1)} %bitcast.262, bf16[1,512,1280]{2,1,0:T(8,128)(2,1)S(1)} %copy-done.2, f32[1024]{0:T(1024)S(1)} %mul.475, ...), kind=kOutput, calls=%fused_computation.14 | convolution fusion | flops 105938944 | bytes 9483264 | tf_op jit(solution)/shard_map/grh,hk->grk/dot_general | solution.py:243
  154.8 1.4 copy-done.17
  156.8 6.4 %fusion.20 = f32[512,1024]{1,0:T(8,128)} fusion(bf16[1024,1024]{1,0:T(8,128)(2,1)S(1)} %copy-done, f32[1,512,1024]{2,1,0:T(8,128)} %copy-done.17, f32[512]{0:T(512)S(1)} %add_rsqrt_fusion, f32[1024]{0:T(1024)S(1)} %copy-done.32), kind=kOutput, calls=%fused_computation.24 | convolution fusion | flops 3226992640 | bytes 6297600 | tf_op jit(solution)/shard_map/grk,kd->grd/dot_general | solution.py:291
  163.2 4.5 %fusion.26 = bf16[1,512,1024]{2,1,0:T(8,128)(2,1)} fusion(f32[512,1024]{1,0:T(8,128)} %fusion.20, bf16[1024,1024]{1,0:T(8,128)(2,1)S(1)} %copy-done, f32[1,512,1024]{2,1,0:T(8,128)} %copy-done.16, f32[1024]{0:T(1024)S(1)} %copy-done.32, f32[512]{0:T(512)S(1)} %add_rsqrt_fusion.1), kind=kOutput, calls=%fused_computation.34 | convolution fusion | flops 1076363264 | bytes 7346176 | tf_op jit(solution)/shard_map/grk,kd->grd/dot_general | solution.py:289
  (160 shorter events, 34.9 us)
Async XLA Ops:
  0.0 156.4 %copy-start = (bf16[1024,1024]{1,0:T(8,128)(2,1)S(1)}, bf16[1024,1024]{1,0:T(8,128)(2,1)}, u32[]{:S(2)}) copy-start(bf16[1024,1024]{1,0:T(8,128)(2,1)} %param.35) | copy-start | bytes 6291460
  0.0 9.5 %copy-start.33 = (f32[16]{0:T(128)S(1)}, f32[16]{0:T(128)}, u32[]{:S(2)}) copy-start(f32[16]{0:T(128)} %param.32) | copy-start | bytes 196
  0.0 9.6 %copy-start.29 = (f32[16]{0:T(128)S(1)}, f32[16]{0:T(128)}, u32[]{:S(2)}) copy-start(f32[16]{0:T(128)} %param.31) | copy-start | bytes 196
  0.0 9.6 %copy-start.23 = (bf16[1024,16]{0,1:T(8,128)(2,1)S(1)}, bf16[1024,16]{0,1:T(8,128)(2,1)}, u32[]{:S(2)}) copy-start(bf16[1024,16]{0,1:T(8,128)(2,1)} %param.28) | copy-start | bytes 98308
  1.9 15.8 %copy-start.10 = (bf16[1,512,1024]{2,1,0:T(8,128)(2,1)}, bf16[1,512,1024]{2,1,0:T(8,128)(2,1)S(1)}, u32[]{:S(2)}) copy-start(bf16[1,512,1024]{2,1,0:T(8,128)(2,1)S(1)} %fusion.19) | copy-start | bytes 3145732
  1.9 39.9 %collective-permute-start.1 = (bf16[1,3,1024]{2,1,0:T(4,128)(2,1)S(1)}, bf16[1,3,1024]{2,1,0:T(4,128)(2,1)}, u32[]{:S(2)}, u32[]{:S(2)}) collective-permute-start(bf16[1,3,1024]{2,1,0:T(4,128)(2,1)S(1)} %get-tuple-element.97), channel_id=1, source_target_pairs={{2,0},{4,2},{6,4},{8,6},{10,8},{12,10},{14,12},{3,1},{5,3},{7,5},{... | collective-permute-start | bytes 18440 | tf_op jit(solution)/shard_map/ppermute | solution.py:267
  5.2 21.1 %collective-permute-start = (bf16[1,3,1024]{2,1,0:T(4,128)(2,1)S(1)}, bf16[1,3,1024]{2,1,0:T(4,128)(2,1)}, u32[]{:S(2)}, u32[]{:S(2)}) collective-permute-start(bf16[1,3,1024]{2,1,0:T(4,128)(2,1)S(1)} %get-tuple-element.98), channel_id=1, source_target_pairs={{0,2},{2,4},{4,6},{6,8},{8,10},{10,12},{12,14},{1,3},{3,5},{5,7},{... | collective-permute-start | bytes 18440 | tf_op jit(solution)/shard_map/ppermute | solution.py:266
  10.1 4.0 %copy-start.13 = (f32[512,16]{1,0:T(8,128)}, f32[512,16]{1,0:T(8,128)S(1)}, u32[]{:S(2)}) copy-start(f32[512,16]{1,0:T(8,128)S(1)} %copy.21) | copy-start | bytes 98308
  15.9 9.8 %copy-start.11 = (f32[1,2,16,256]{2,3,1,0:T(8,128)}, f32[1,2,16,256]{2,3,1,0:T(8,128)S(1)}, u32[]{:S(2)}) copy-start(f32[1,2,16,256]{2,3,1,0:T(8,128)S(1)} %get-tuple-element.86) | copy-start | bytes 98308
  17.7 6.6 %copy-start.24 = (f32[1280]{0:T(1024)S(1)}, f32[1280]{0:T(1024)}, u32[]{:S(2)}) copy-start(f32[1280]{0:T(1024)} %param.30) | copy-start | bytes 15364
  17.7 7.2 %copy-start.31 = (f32[16]{0:T(128)S(1)}, f32[16]{0:T(128)}, u32[]{:S(2)}) copy-start(f32[16]{0:T(128)} %param.33) | copy-start | bytes 196
  40.8 20.4 %copy-start.4 = (f32[1,16,64,128]{3,2,1,0:T(8,128)}, f32[1,16,64,128]{3,2,1,0:T(8,128)S(1)}, u32[]{:S(2)}) copy-start(f32[1,16,64,128]{3,2,1,0:T(8,128)S(1)} %fusion.43) | copy-start | bytes 1572868
  41.8 3.4 %copy-start.30 = (f32[16]{0:T(128)S(1)}, f32[16]{0:T(128)}, u32[]{:S(2)}) copy-start(f32[16]{0:T(128)} %param.31) | copy-start | bytes 196
  41.9 4.0 %copy-start.26 = (f32[16]{0:T(128)S(1)}, f32[16]{0:T(128)}, u32[]{:S(2)}) copy-start(f32[16]{0:T(128)} %copy-done.25) | copy-start | bytes 196
  48.3 12.2 %copy-start.12 = (f32[1,2,256,16]{3,2,1,0:T(8,128)}, f32[1,2,256,16]{3,2,1,0:T(8,128)S(1)}, u32[]{:S(2)}) copy-start(f32[1,2,256,16]{3,2,1,0:T(8,128)S(1)} %get-tuple-element.90) | copy-start | bytes 98308
  62.1 34.2 %collective-permute-start.2 = (f32[1,1032,128]{2,1,0:T(8,128)}, f32[1,1032,128]{2,1,0:T(8,128)}, u32[]{:S(2)}, u32[]{:S(2)}) collective-permute-start(f32[1,1032,128]{2,1,0:T(8,128)} %select_maximum_fusion.5), channel_id=1, source_target_pairs={{0,2},{2,4},{4,6},{6,8},{8,10},{10,12},{12,14},{1,3},{3,5},{5,7},{... | collective-permute-start | bytes 1585160 | tf_op jit(solution)/shard_map/ppermute | solution.py:48
  79.2 22.0 %collective-permute-start.5 = (f32[1,1032,128]{2,1,0:T(8,128)}, f32[1,1032,128]{2,1,0:T(8,128)}, u32[]{:S(2)}, u32[]{:S(2)}) collective-permute-start(f32[1,1032,128]{2,1,0:T(8,128)} %select_maximum_fusion.2), channel_id=1, source_target_pairs={{2,0},{4,2},{6,4},{8,6},{10,8},{12,10},{14,12},{3,1},{5,3},{7,5},{... | collective-permute-start | bytes 1585160 | tf_op jit(solution)/shard_map/ppermute | solution.py:48
  89.8 5.6 %copy-start.3 = (f32[2,16,64,128]{3,2,1,0:T(8,128)S(1)}, f32[2,16,64,128]{3,2,1,0:T(8,128)}, u32[]{:S(2)}) copy-start(f32[2,16,64,128]{3,2,1,0:T(8,128)} %shard_map.120) | copy-start | bytes 3145732
  95.3 2.8 %copy-start.5 = (f32[1,16,64,128]{3,2,1,0:T(8,128)S(1)}, f32[1,16,64,128]{3,2,1,0:T(8,128)}, u32[]{:S(2)}) copy-start(f32[1,16,64,128]{3,2,1,0:T(8,128)} %copy-done.4) | copy-start | bytes 1572868
  96.3 5.9 %copy-start.7 = (f32[1,1024,128]{2,1,0:T(8,128)S(1)}, f32[1,1024,128]{2,1,0:T(8,128)}, u32[]{:S(2)}) copy-start(f32[1,1024,128]{2,1,0:T(8,128)} %copy-done.6) | copy-start | bytes 1572868
  99.9 14.8 %collective-permute-start.3 = (f32[1,1032,128]{2,1,0:T(8,128)}, f32[1,1032,128]{2,1,0:T(8,128)}, u32[]{:S(2)}, u32[]{:S(2)}) collective-permute-start(f32[1,1032,128]{2,1,0:T(8,128)} %select_maximum_fusion.4), channel_id=1, source_target_pairs={{0,4},{2,6},{4,8},{6,10},{8,12},{10,14},{1,5},{3,7},{5,9},{7,11},{... | collective-permute-start | bytes 1585160 | tf_op jit(solution)/shard_map/ppermute | solution.py:48
  102.1 14.3 %copy-start.9 = (f32[1,16,64,128]{3,2,1,0:T(8,128)S(1)}, f32[1,16,64,128]{3,2,1,0:T(8,128)}, u32[]{:S(2)}) copy-start(f32[1,16,64,128]{3,2,1,0:T(8,128)} %copy-done.8) | copy-start | bytes 1572868
  103.5 14.4 %collective-permute-start.6 = (f32[1,1032,128]{2,1,0:T(8,128)S(1)}, f32[1,1032,128]{2,1,0:T(8,128)S(1)}, u32[]{:S(2)}, u32[]{:S(2)}) collective-permute-start(f32[1,1032,128]{2,1,0:T(8,128)S(1)} %select_maximum_fusion.1), channel_id=1, source_target_pairs={{4,0},{6,2},{8,4},{10,6},{12,8},{14,10},{5,1},{7,3},{9,5},{11,7},{... | collective-permute-start | bytes 1585160 | tf_op jit(solution)/shard_map/ppermute | solution.py:48
  116.6 25.2 %collective-permute-start.4 = (f32[1,1032,128]{2,1,0:T(8,128)S(1)}, f32[1,1032,128]{2,1,0:T(8,128)S(1)}, u32[]{:S(2)}, u32[]{:S(2)}) collective-permute-start(f32[1,1032,128]{2,1,0:T(8,128)S(1)} %select_maximum_fusion.3), channel_id=1, source_target_pairs={{0,8},{2,10},{4,12},{6,14},{1,9},{3,11},{5,13},{7,15},{16,24},{18,... | collective-permute-start | bytes 1585160 | tf_op jit(solution)/shard_map/ppermute | solution.py:48
  118.2 23.9 %copy-start.19 = (f32[1,1,16,64,128]{4,3,2,1,0:T(8,128)S(1)}, f32[1,1,16,64,128]{4,3,2,1,0:T(8,128)}, u32[]{:S(2)}) copy-start(f32[1,1,16,64,128]{4,3,2,1,0:T(8,128)} %slice_add_fusion) | copy-start | bytes 1572868
  118.2 29.6 %collective-permute-start.7 = (f32[1,1032,128]{2,1,0:T(8,128)S(1)}, f32[1,1032,128]{2,1,0:T(8,128)S(1)}, u32[]{:S(2)}, u32[]{:S(2)}) collective-permute-start(f32[1,1032,128]{2,1,0:T(8,128)S(1)} %select_maximum_fusion), channel_id=1, source_target_pairs={{8,0},{10,2},{12,4},{14,6},{9,1},{11,3},{13,5},{15,7},{24,16},{26,... | collective-permute-start | bytes 1585160 | tf_op jit(solution)/shard_map/ppermute | solution.py:48
  142.2 1.8 %copy-start.1 = (bf16[1,512,1280]{2,1,0:T(8,128)(2,1)S(1)}, bf16[1,512,1280]{2,1,0:T(8,128)(2,1)}, u32[]{:S(2)}) copy-start(bf16[1,512,1280]{2,1,0:T(8,128)(2,1)} %shard_map.118) | copy-start | bytes 3932164
  142.3 1.8 %copy-start.21 = (f32[1,2,256,16]{3,2,1,0:T(8,128)S(1)}, f32[1,2,256,16]{3,2,1,0:T(8,128)}, u32[]{:S(2)}) copy-start(f32[1,2,256,16]{3,2,1,0:T(8,128)} %get-tuple-element.85) | copy-start | bytes 98308
  142.3 1.8 %copy-start.27 = (s32[1024]{0:T(1024)S(1)}, s32[1024]{0:T(1024)}, u32[]{:S(2)}) copy-start(s32[1024]{0:T(1024)} %get-tuple-element.114) | copy-start | bytes 12292
  142.3 1.8 %copy-start.28 = (s32[1024]{0:T(1024)S(1)}, s32[1024]{0:T(1024)}, u32[]{:S(2)}) copy-start(s32[1024]{0:T(1024)} %get-tuple-element.115) | copy-start | bytes 12292
  149.4 1.8 %copy-start.2 = (bf16[1,512,1280]{2,1,0:T(8,128)(2,1)S(1)}, bf16[1,512,1280]{2,1,0:T(8,128)(2,1)}, u32[]{:S(2)}) copy-start(bf16[1,512,1280]{2,1,0:T(8,128)(2,1)} %shard_map.121) | copy-start | bytes 3932164
  149.4 1.8 %copy-start.22 = (f32[1,2,256,16]{3,2,1,0:T(8,128)S(1)}, f32[1,2,256,16]{3,2,1,0:T(8,128)}, u32[]{:S(2)}) copy-start(f32[1,2,256,16]{3,2,1,0:T(8,128)} %get-tuple-element.89) | copy-start | bytes 98308
  (11 other events, 13.7 us)

commit v10 on v9

--- a/solution.py
+++ b/solution.py
@@ -180,14 +180,11 @@
         out_ref[:edge, :] = jax.nn.silu(side).astype(out_ref.dtype)
 
 
-def convolve(projected, halo, conv_w, conv_b, reverse):
-    inner = H * P_SIZE
-    count, rows, _ = projected.shape
+def convolve(projected, rows, conv_w, conv_b, reverse):
+    inner = H * P_SIZE
+    count = projected.shape[0]
     width = conv_w.shape[1]
     edge = 8
-    margin = KCONV - 1
-    pad = ((0, 0), (0, edge - margin), (0, 0)) if reverse else ((0, 0), (edge - margin, 0), (0, 0))
-    halo8 = jnp.pad(halo, pad)
     lanes = CONV_LANES
     skip = inner // lanes
     return pl.pallas_call(
@@ -195,19 +192,19 @@
         grid=(count, width // lanes),
         in_specs=[
             pl.BlockSpec((None, rows, lanes), lambda g, j: (g, 0, j + skip)),
-            pl.BlockSpec((None, edge, lanes), lambda g, j: (g, 0, j)),
+            pl.BlockSpec((None, edge, lanes), lambda g, j: (g, rows // edge, j + skip)),
             pl.BlockSpec((KCONV, lanes), lambda g, j: (0, j)),
             pl.BlockSpec((1, lanes), lambda g, j: (0, j)),
         ],
         out_specs=pl.BlockSpec((None, rows, lanes), lambda g, j: (g, 0, j)),
         out_shape=jax.ShapeDtypeStruct((count, rows, width), jnp.bfloat16),
-    )(projected, halo8, conv_w, conv_b.reshape(1, width))
-
-
-def strand_terms(projected, halo, step_size, conv_w, conv_b, rates, reverse):
-    inner = H * P_SIZE
-    count, rows, _ = projected.shape
-    activated = convolve(projected, halo, conv_w, conv_b, reverse)
+    )(projected, projected, conv_w, conv_b.reshape(1, width))
+
+
+def strand_terms(projected, step_size, conv_w, conv_b, rates, reverse):
+    inner = H * P_SIZE
+    count, rows, _ = step_size.shape
+    activated = convolve(projected, rows, conv_w, conv_b, reverse)
     spans = rows // Q
     inside, state, total, from_start = block_terms(activated, step_size, rates, reverse)
     order = list(range(spans))
@@ -265,26 +262,25 @@
     count = lax.axis_size("seq")
     low = lax.ppermute(strand[:, rows - margin :], "seq", [(i, i + 1) for i in range(count - 1)])
     high = lax.ppermute(strand[:, :margin], "seq", [(i + 1, i) for i in range(count - 1)])
-    w_source = w_in[:, inner:]
     rates = -jnp.exp(a_log)
-    proj_f = jnp.einsum("grd,de->gre", strand, w_in, preferred_element_type=jnp.float32)
-    halo_f = jnp.einsum("grd,de->gre", low, w_source, preferred_element_type=jnp.float32)
+    gap = jnp.zeros((strand.shape[0], 8 - margin, strand.shape[2]), strand.dtype)
+    ext_f = jnp.concatenate([strand, gap, low], axis=1)
+    proj_f = jnp.einsum("grd,de->gre", ext_f, w_in, preferred_element_type=jnp.float32)
     step_f = jax.nn.softplus(
         jnp.einsum("grd,dh->grh", strand, w_dt, preferred_element_type=jnp.float32) + dt_bias
     )
-    sum_f, pend_f = strand_terms(proj_f, halo_f, step_f, conv_w, conv_b, rates, False)
+    sum_f, pend_f = strand_terms(proj_f, step_f, conv_w, conv_b, rates, False)
     sum_f, (strand_late, high) = lax.optimization_barrier((sum_f, (strand, high)))
-    mirrored = flip_lanes(strand_late)
-    high_mirrored = flip_lanes(high)
-    proj_r = jnp.einsum("grd,de->gre", mirrored, w_in, preferred_element_type=jnp.float32)
-    halo_r = jnp.einsum("grd,de->gre", high_mirrored, w_source, preferred_element_type=jnp.float32)
+    ext_r = flip_lanes(jnp.concatenate([strand_late, high, gap], axis=1))
+    mirrored = ext_r[:, :rows]
+    proj_r = jnp.einsum("grd,de->gre", ext_r, w_in, preferred_element_type=jnp.float32)
     step_r = jax.nn.softplus(
         jnp.einsum("grd,dh->grh", mirrored, w_dt, preferred_element_type=jnp.float32) + dt_bias
     )
-    sum_r, pend_r = strand_terms(proj_r, halo_r, step_r, conv_w, conv_b, rates, True)
+    sum_r, pend_r = strand_terms(proj_r, step_r, conv_w, conv_b, rates, True)
     in_f, in_r = exclusive_scans(sum_f, sum_r, "seq")
-    normed_f = finish(pend_f, in_f[1], proj_f[:, :, :inner], d_skip, norm_gain)
-    normed_r = finish(pend_r, in_r[1], proj_r[:, :, :inner], d_skip, norm_gain)
+    normed_f = finish(pend_f, in_f[1], proj_f[:, :rows, :inner], d_skip, norm_gain)
+    normed_r = finish(pend_r, in_r[1], proj_r[:, :rows, :inner], d_skip, norm_gain)
     w_out_mirrored = flip_lanes(w_out)
     out = jnp.einsum(
         "grk,kd->grd", normed_f, w_out, preferred_element_type=jnp.float32

time: 169 us -> 165 us (0.976)
  matrix products: 43.8 us -> 39.8 us
    dot_general x4 -> x2, matrix products: 18.7 us -> 14.7 us  [the longest x1 7.58 us: on_device(): jnp.einsum('grd,de->gre', ext_r, w_in, preferred_element_type=jnp.float32)]
    unnamed x70 -> x68, local copies, waits for them, and re-layouts: 7.19 us -> 7.24 us
  transfers between devices with their start and end apart: 8 -> 8, of which waited for: 2 -> 2; matrix products, arithmetic and copies ran while one was open for 25% -> 24% of each run, Pallas kernels for 19% -> 19%
where the time goes in v10:
time: 165 us; the launch traced here: 164 us
  matrix products  39.8 us (24%)
  Pallas kernels  31.5 us (19%)
  starting transfers between devices  26.1 us (16%)
  waiting for transfers between devices  23.9 us (14%)
  other arithmetic  22.3 us (14%)
  local copies, waits for them, and re-layouts  19.4 us (12%)
    ppermute x6, waiting for transfers between devices, exclusive_scans(): decay, state = unpack(lax.ppermute(pack(*ahead[k]), axis, pairs))  23.9 us
    ppermute x6, starting transfers between devices, exclusive_scans(): decay, state = unpack(lax.ppermute(pack(*ahead[k]), axis, pairs))  19.7 us
    pallas_call x2, Pallas kernels, block_terms(): pl.pallas_call(partial(inside_kernel, reverse=reverse), grid=(blocks,), i...  11.1 us
    pallas_call x2, Pallas kernels, convolve(): pl.pallas_call(partial(conv_kernel, reverse=reverse), grid=(count, width...  10.2 us
    pallas_call x2, Pallas kernels, block_terms(): pl.pallas_call(state_kernel, grid=(blocks,), in_specs=[spec((Q, width)),...  10.2 us
    dot_general x1, matrix products, on_device(): jnp.einsum('grd,de->gre', ext_r, w_in, preferred_element_type=jnp.float32)  7.58 us
    unnamed x68, local copies, waits for them, and re-layouts  7.24 us
    dot_general x1, matrix products, on_device(): jnp.einsum('grd,de->gre', ext_f, w_in, preferred_element_type=jnp.float32)  7.16 us
  transfers between devices with their start and end apart: 8, of which 2 were waited for; matrix products, arithmetic and copies ran while one was open for 24% of the time, Pallas kernels for 19%

profile of v10, /device:TPU:24, one launch (start us, length us, event | category | flops | bytes accessed | tf_op | source)
XLA Modules:
  0.0 163.7 jit_solution(7503267857917947173)
XLA Ops:
  0.0 1.9 %fusion.8 = bf16[1,512,1024]{2,1,0:T(8,128)(2,1)S(1)} fusion(bf16[1,512,1024]{2,1,0:T(8,128)(2,1)} %param.25, bf16[4,1024]{1,0:T(4,128)(2,1)} %param.26, s32[512]{0:T(512)} %bitcast.273), kind=kOutput, calls=%fused_computation.15 | convolution fusion | flops 5769216 | bytes 2107392 | tf_op jit(solution)/shard_map/gtb,bd->gtd/dot_general | solution.py:259
  2.6 3.3 %collective-permute-start.1 = (bf16[1,3,1024]{2,1,0:T(4,128)(2,1)S(1)}, bf16[1,3,1024]{2,1,0:T(4,128)(2,1)}, u32[]{:S(2)}, u32[]{:S(2)}) collective-permute-start(bf16[1,3,1024]{2,1,0:T(4,128)(2,1)S(1)} %get-tuple-element.97), channel_id=1, source_target_pairs={{2,0},{4,2},{6,4},{8,6},{10,8},{12,10},{14,12},{3,1},{5,3},{7,5},{... | collective-permute-start | bytes 18440 | tf_op jit(solution)/shard_map/ppermute | solution.py:264
  5.8 3.1 %collective-permute-start = (bf16[1,3,1024]{2,1,0:T(4,128)(2,1)}, bf16[1,3,1024]{2,1,0:T(4,128)(2,1)}, u32[]{:S(2)}, u32[]{:S(2)}) collective-permute-start(bf16[1,3,1024]{2,1,0:T(4,128)(2,1)} %get-tuple-element.98), channel_id=1, source_target_pairs={{0,2},{2,4},{4,6},{6,8},{8,10},{10,12},{12,14},{1,3},{3,5},{5,7},{... | collective-permute-start | bytes 18440 | tf_op jit(solution)/shard_map/ppermute | solution.py:263
  12.6 1.1 reduce-window.14
  14.8 1.7 %bitcast_exponential_fusion = (f32[1,2,256,16]{3,2,1,0:T(8,128)}, f32[1,2,16,256]{2,3,1,0:T(8,128)S(1)}) fusion(f32[2,16,2]{1,2,0:T(2,128)S(1)} %slice_bitcast_fusion.6, f32[1,2,16,2,128]{2,4,3,1,0:T(8,128)} %copy.23), kind=kLoop, calls=%fused_computation.126 | loop fusion | flops 8192 | bytes 98560 | tf_op jit(solution)/shard_map/exp | solution.py:144
  16.5 1.8 %multiply_bitcast_fusion.1.to_end_ref = f32[2,256,16]{2,1,0:T(8,128)} fusion(f32[1,2,256,16]{3,2,1,0:T(8,128)} %bitcast.243, f32[2,16]{1,0:T(2,128)S(1)} %bitcast.270, f32[1,2,16,256]{2,3,1,0:T(8,128)S(1)} %get-tuple-element.86), kind=kLoop, calls=%fused_computation.75 | loop fusion | flops 16384 | bytes 98432 | tf_op jit(solution)/shard_map/reshape | solution.py:122
  21.1 7.2 %convolution_bitcast_fusion.1.src_ref.halo_ref = f32[1,520,2304]{2,1,0:T(8,128)} fusion(bf16[1024,2304]{1,0:T(8,128)(2,1)} %param.27, bf16[1,3,1024]{2,1,0:T(4,128)(2,1)} %collective-permute-done, bf16[1,5,1024]{2,1,0:T(8,128)(2,1)S(1)} %broadcast_in_dim.11, bf16[1,512,1024]{2,1,0:T(8,128)(2,1)S(1)} %fusion.8), kind=kOutput, calls=%fused_computation.1 | convolution fusion | flops 2456862720 | bytes 10575872 | tf_op jit(solution)/shard_map/grd,de->gre/dot_general | solution.py:268
  28.3 5.1 %shard_map.118 = bf16[1,512,1280]{2,1,0:T(8,128)(2,1)} custom-call(f32[1,520,2304]{2,1,0:T(8,128)} %convolution_bitcast_fusion.1.src_ref.halo_ref, f32[1,520,2304]{2,1,0:T(8,128)} %convolution_bitcast_fusion.1.src_ref.halo_ref, f32[4,1280]{1,0:T(4,128)} %w_ref.3, f32[1,1280]{1,0:T(1,128)} %reshape.984.b_ref), custom_call_target="tpu_custom_call" | custom-call | tf_op jit(solution)/shard_map/pallas_call | solution.py:190
  33.4 5.1 %shard_map.120 = f32[2,16,64,128]{3,2,1,0:T(8,128)} custom-call(bf16[2,256,1280]{2,1,0:T(8,128)(2,1)} %bitcast.219, f32[2,256,16]{2,1,0:T(8,128)} %multiply_bitcast_fusion.1.to_end_ref), custom_call_target="tpu_custom_call" | custom-call | tf_op jit(solution)/shard_map/pallas_call | solution.py:128
  38.5 1.3 fusion.36
  40.9 2.5 %fusion.13 = bf16[520,1024]{1,0:T(8,128)(2,1)S(1)} fusion(bf16[1,5,1024]{2,1,0:T(8,128)(2,1)S(1)} %broadcast_in_dim.11, bf16[1,3,1024]{2,1,0:T(4,128)(2,1)} %collective-permute-done.1, bf16[1,512,1024]{2,1,0:T(8,128)(2,1)} %copy-done.10), kind=kOutput, calls=%fused_computation.25 | convolution fusion | flops 1096343552 | bytes 2129920 | tf_op jit(solution)/shard_map/...d,de->...e/dot_general | solution.py:28
  45.0 1.1 reduce-window.16
  47.3 7.6 %convolution_bitcast_fusion.src_ref.halo_ref = f32[1,520,2304]{2,1,0:T(8,128)} fusion(bf16[520,1024]{1,0:T(8,128)(2,1)} %copy-done.32, bf16[1024,2304]{1,0:T(8,128)(2,1)} %param.27), kind=kOutput, calls=%fused_computation | convolution fusion | flops 2453667840 | bytes 10575872 | tf_op jit(solution)/shard_map/grd,de->gre/dot_general | solution.py:276
  58.1 1.9 %collective-permute-start.2 = (f32[1,1032,128]{2,1,0:T(8,128)}, f32[1,1032,128]{2,1,0:T(8,128)}, u32[]{:S(2)}, u32[]{:S(2)}) collective-permute-start(f32[1,1032,128]{2,1,0:T(8,128)} %select_maximum_fusion.5), channel_id=1, source_target_pairs={{0,2},{2,4},{4,6},{6,8},{8,10},{10,12},{12,14},{1,3},{3,5},{5,7},{... | collective-permute-start | bytes 1585160 | tf_op jit(solution)/shard_map/ppermute | solution.py:48
  60.0 5.1 %shard_map.121 = bf16[1,512,1280]{2,1,0:T(8,128)(2,1)} custom-call(f32[1,520,2304]{2,1,0:T(8,128)} %convolution_bitcast_fusion.src_ref.halo_ref, f32[1,520,2304]{2,1,0:T(8,128)} %convolution_bitcast_fusion.src_ref.halo_ref, f32[4,1280]{1,0:T(4,128)} %w_ref.3, f32[1,1280]{1,0:T(1,128)} %reshape.984.b_ref), custom_call_target="tpu_custom_call" | custom-call | tf_op jit(solution)/shard_map/pallas_call | solution.py:190
  66.1 5.1 %shard_map.123 = f32[2,16,64,128]{3,2,1,0:T(8,128)} custom-call(bf16[2,256,1280]{2,1,0:T(8,128)(2,1)} %bitcast.221, f32[2,256,16]{2,1,0:T(8,128)} %multiply_bitcast_fusion.to_end_ref), custom_call_target="tpu_custom_call" | custom-call | tf_op jit(solution)/shard_map/pallas_call | solution.py:128
  71.2 2.1 %fusion.61 = (f32[1,1,16,64,128]{4,3,2,1,0:T(8,128)S(1)}, f32[1,1,16,64,128]{4,3,2,1,0:T(8,128)}, f32[1,1,16,64,128]{4,3,2,1,0:T(8,128)S(1)}) fusion(f32[1,2,16,64,128]{4,3,2,1,0:T(8,128)} %bitcast.241, f32[16]{0:T(128)S(1)} %bitcast_multiply_fusion.4), kind=kLoop, calls=%fused_computation.135 | loop fusion | flops 131072 | bytes 2621504 | tf_op jit(solution)/shard_map/slice | solution.py:217
  75.3 5.0 %collective-permute-start.5 = (f32[1,1032,128]{2,1,0:T(8,128)}, f32[1,1032,128]{2,1,0:T(8,128)}, u32[]{:S(2)}, u32[]{:S(2)}) collective-permute-start(f32[1,1032,128]{2,1,0:T(8,128)} %select_maximum_fusion.2), channel_id=1, source_target_pairs={{2,0},{4,2},{6,4},{8,6},{10,8},{12,10},{14,12},{3,1},{5,3},{7,5},{... | collective-permute-start | bytes 1585160 | tf_op jit(solution)/shard_map/ppermute | solution.py:48
  80.3 5.5 %shard_map.119 = f32[2,256,1024]{2,1,0:T(8,128)} custom-call(bf16[2,256,1280]{2,1,0:T(8,128)(2,1)} %bitcast.220, f32[2,256,16]{2,1,0:T(8,128)} %bitcast.233, f32[2,16,256]{2,1,0:T(8,128)} %copy.25.cum_t_ref, f32[2,16,256]{2,1,0:T(8,128)} %bitcast.257), custom_call_target="tpu_custom_call" | custom-call | tf_op jit(solution)/shard_map/pallas_call | solution.py:135
  85.8 5.5 %shard_map.122 = f32[2,256,1024]{2,1,0:T(8,128)} custom-call(bf16[2,256,1280]{2,1,0:T(8,128)(2,1)} %bitcast.222, f32[2,256,16]{2,1,0:T(8,128)} %bitcast.235, f32[2,16,256]{2,1,0:T(8,128)} %copy.30.cum_t_ref, f32[2,16,256]{2,1,0:T(8,128)} %bitcast.258), custom_call_target="tpu_custom_call" | custom-call | tf_op jit(solution)/shard_map/pallas_call | solution.py:135
  95.9 1.3 collective-permute-start.3
  98.1 1.3 multiply_add_fusion.3
  99.5 4.6 %collective-permute-start.6 = (f32[1,1032,128]{2,1,0:T(8,128)S(1)}, f32[1,1032,128]{2,1,0:T(8,128)S(1)}, u32[]{:S(2)}, u32[]{:S(2)}) collective-permute-start(f32[1,1032,128]{2,1,0:T(8,128)S(1)} %select_maximum_fusion.1), channel_id=1, source_target_pairs={{4,0},{6,2},{8,4},{10,6},{12,8},{14,10},{5,1},{7,3},{9,5},{11,7},{... | collective-permute-start | bytes 1585160 | tf_op jit(solution)/shard_map/ppermute | solution.py:48
  104.1 6.6 %collective-permute-done.3 = f32[1,1032,128]{2,1,0:T(8,128)} collective-permute-done((f32[1,1032,128]{2,1,0:T(8,128)}, f32[1,1032,128]{2,1,0:T(8,128)}, u32[]{:S(2)}, u32[]{:S(2)}) %collective-permute-start.3) | collective-permute-done | bytes 528416 | tf_op jit(solution)/shard_map/ppermute | solution.py:48
  112.6 1.3 collective-permute-start.4
  114.2 5.6 %collective-permute-start.7 = (f32[1,1032,128]{2,1,0:T(8,128)S(1)}, f32[1,1032,128]{2,1,0:T(8,128)S(1)}, u32[]{:S(2)}, u32[]{:S(2)}) collective-permute-start(f32[1,1032,128]{2,1,0:T(8,128)S(1)} %select_maximum_fusion), channel_id=1, source_target_pairs={{8,0},{10,2},{12,4},{14,6},{9,1},{11,3},{13,5},{15,7},{24,16},{26,... | collective-permute-start | bytes 1585160 | tf_op jit(solution)/shard_map/ppermute | solution.py:48
  120.6 17.3 %collective-permute-done.4 = f32[1,1032,128]{2,1,0:T(8,128)S(1)} collective-permute-done((f32[1,1032,128]{2,1,0:T(8,128)S(1)}, f32[1,1032,128]{2,1,0:T(8,128)S(1)}, u32[]{:S(2)}, u32[]{:S(2)}) %collective-permute-start.4) | collective-permute-done | bytes 528416 | tf_op jit(solution)/shard_map/ppermute | solution.py:48
  140.1 3.5 %fusion.6 = f32[1,512,1024]{2,1,0:T(8,128)S(1)} fusion(f32[2,256,1024]{2,1,0:T(8,128)S(1)} %fusion.67, f32[2,256,1024]{2,1,0:T(8,128)S(1)} %copy-done.15, f32[1,520,2304]{2,1,0:T(8,128)} %convolution_bitcast_fusion.1.src_ref.halo_ref, f32[512,16]{1,0:T(8,128)S(1)} %bitcast.255, bf16[1,512,1280]{2,1,0:T(8,128)(2,1)S(1)} %copy-done.1, f32[1024]{0:T(1024)S(1)} %mul.475, ...), kind=kOutput, calls=%fused_computation.11 | convolution fusion | flops 105938944 | bytes 9483264 | tf_op jit(solution)/shard_map/grh,hk->grk/dot_general | solution.py:240
  147.3 3.5 %fusion.4 = f32[1,512,1024]{2,1,0:T(8,128)S(1)} fusion(f32[2,256,1024]{2,1,0:T(8,128)S(1)} %fusion.68, f32[2,256,1024]{2,1,0:T(8,128)S(1)} %copy-done.14, f32[1,520,2304]{2,1,0:T(8,128)} %convolution_bitcast_fusion.src_ref.halo_ref, f32[512,16]{1,0:T(8,128)S(1)} %bitcast.256, bf16[1,512,1280]{2,1,0:T(8,128)(2,1)S(1)} %copy-done.2, f32[1024]{0:T(1024)S(1)} %mul.475, ...), kind=kOutput, calls=%fused_computation.7 | convolution fusion | flops 105938944 | bytes 9483264 | tf_op jit(solution)/shard_map/grh,hk->grk/dot_general | solution.py:240
  150.8 1.4 copy-done.17
  152.8 6.4 %fusion.9 = f32[512,1024]{1,0:T(8,128)} fusion(bf16[1024,1024]{1,0:T(8,128)(2,1)S(1)} %copy-done, f32[1,512,1024]{2,1,0:T(8,128)} %copy-done.17, f32[512]{0:T(512)S(1)} %add_rsqrt_fusion, f32[1024]{0:T(1024)S(1)} %copy-done.30), kind=kOutput, calls=%fused_computation.17 | convolution fusion | flops 3226992640 | bytes 6297600 | tf_op jit(solution)/shard_map/grk,kd->grd/dot_general | solution.py:287
  159.2 4.5 %fusion.14 = bf16[1,512,1024]{2,1,0:T(8,128)(2,1)} fusion(f32[512,1024]{1,0:T(8,128)} %fusion.9, bf16[1024,1024]{1,0:T(8,128)(2,1)S(1)} %copy-done, f32[1,512,1024]{2,1,0:T(8,128)} %copy-done.16, f32[1024]{0:T(1024)S(1)} %copy-done.30, f32[512]{0:T(512)S(1)} %add_rsqrt_fusion.1), kind=kOutput, calls=%fused_computation.26 | convolution fusion | flops 1076363264 | bytes 7346176 | tf_op jit(solution)/shard_map/grk,kd->grd/dot_general | solution.py:285
  (155 shorter events, 32.7 us)
Async XLA Ops:
  0.0 152.4 %copy-start = (bf16[1024,1024]{1,0:T(8,128)(2,1)S(1)}, bf16[1024,1024]{1,0:T(8,128)(2,1)}, u32[]{:S(2)}) copy-start(bf16[1024,1024]{1,0:T(8,128)(2,1)} %param.35) | copy-start | bytes 6291460
  0.0 10.2 %copy-start.31 = (f32[16]{0:T(128)S(1)}, f32[16]{0:T(128)}, u32[]{:S(2)}) copy-start(f32[16]{0:T(128)} %param.32) | copy-start | bytes 196
  0.0 10.2 %copy-start.28 = (f32[16]{0:T(128)S(1)}, f32[16]{0:T(128)}, u32[]{:S(2)}) copy-start(f32[16]{0:T(128)} %param.31) | copy-start | bytes 196
  0.0 10.2 %copy-start.22 = (bf16[1024,16]{0,1:T(8,128)(2,1)S(1)}, bf16[1024,16]{0,1:T(8,128)(2,1)}, u32[]{:S(2)}) copy-start(bf16[1024,16]{0,1:T(8,128)(2,1)} %param.28) | copy-start | bytes 98308
  1.9 19.2 %copy-start.10 = (bf16[1,512,1024]{2,1,0:T(8,128)(2,1)}, bf16[1,512,1024]{2,1,0:T(8,128)(2,1)S(1)}, u32[]{:S(2)}) copy-start(bf16[1,512,1024]{2,1,0:T(8,128)(2,1)S(1)} %fusion.8) | copy-start | bytes 3145732
  2.6 38.3 %collective-permute-start.1 = (bf16[1,3,1024]{2,1,0:T(4,128)(2,1)S(1)}, bf16[1,3,1024]{2,1,0:T(4,128)(2,1)}, u32[]{:S(2)}, u32[]{:S(2)}) collective-permute-start(bf16[1,3,1024]{2,1,0:T(4,128)(2,1)S(1)} %get-tuple-element.97), channel_id=1, source_target_pairs={{2,0},{4,2},{6,4},{8,6},{10,8},{12,10},{14,12},{3,1},{5,3},{7,5},{... | collective-permute-start | bytes 18440 | tf_op jit(solution)/shard_map/ppermute | solution.py:264
  5.8 15.3 %collective-permute-start = (bf16[1,3,1024]{2,1,0:T(4,128)(2,1)}, bf16[1,3,1024]{2,1,0:T(4,128)(2,1)}, u32[]{:S(2)}, u32[]{:S(2)}) collective-permute-start(bf16[1,3,1024]{2,1,0:T(4,128)(2,1)} %get-tuple-element.98), channel_id=1, source_target_pairs={{0,2},{2,4},{4,6},{6,8},{8,10},{10,12},{12,14},{1,3},{3,5},{5,7},{... | collective-permute-start | bytes 18440 | tf_op jit(solution)/shard_map/ppermute | solution.py:263
  10.2 8.1 %copy-start.23 = (f32[1280]{0:T(1024)S(1)}, f32[1280]{0:T(1024)}, u32[]{:S(2)}) copy-start(f32[1280]{0:T(1024)} %param.30) | copy-start | bytes 15364
  10.8 4.0 %copy-start.13 = (f32[512,16]{1,0:T(8,128)}, f32[512,16]{1,0:T(8,128)S(1)}, u32[]{:S(2)}) copy-start(f32[512,16]{1,0:T(8,128)S(1)} %copy.21) | copy-start | bytes 98308
  16.5 11.7 %copy-start.11 = (f32[1,2,16,256]{2,3,1,0:T(8,128)}, f32[1,2,16,256]{2,3,1,0:T(8,128)S(1)}, u32[]{:S(2)}) copy-start(f32[1,2,16,256]{2,3,1,0:T(8,128)S(1)} %get-tuple-element.86) | copy-start | bytes 98308
  39.8 17.5 %copy-start.4 = (f32[1,16,64,128]{3,2,1,0:T(8,128)}, f32[1,16,64,128]{3,2,1,0:T(8,128)S(1)}, u32[]{:S(2)}) copy-start(f32[1,16,64,128]{3,2,1,0:T(8,128)S(1)} %fusion.36) | copy-start | bytes 1572868
  40.9 3.5 %copy-start.29 = (f32[16]{0:T(128)S(1)}, f32[16]{0:T(128)}, u32[]{:S(2)}) copy-start(f32[16]{0:T(128)} %param.31) | copy-start | bytes 196
  40.9 4.0 %copy-start.25 = (f32[16]{0:T(128)S(1)}, f32[16]{0:T(128)}, u32[]{:S(2)}) copy-start(f32[16]{0:T(128)} %copy-done.24) | copy-start | bytes 196
  47.3 9.3 %copy-start.12 = (f32[1,2,256,16]{3,2,1,0:T(8,128)}, f32[1,2,256,16]{3,2,1,0:T(8,128)S(1)}, u32[]{:S(2)}) copy-start(f32[1,2,256,16]{3,2,1,0:T(8,128)S(1)} %get-tuple-element.90) | copy-start | bytes 98308
  58.1 34.1 %collective-permute-start.2 = (f32[1,1032,128]{2,1,0:T(8,128)}, f32[1,1032,128]{2,1,0:T(8,128)}, u32[]{:S(2)}, u32[]{:S(2)}) collective-permute-start(f32[1,1032,128]{2,1,0:T(8,128)} %select_maximum_fusion.5), channel_id=1, source_target_pairs={{0,2},{2,4},{4,6},{6,8},{8,10},{10,12},{12,14},{1,3},{3,5},{5,7},{... | collective-permute-start | bytes 1585160 | tf_op jit(solution)/shard_map/ppermute | solution.py:48
  75.3 21.9 %collective-permute-start.5 = (f32[1,1032,128]{2,1,0:T(8,128)}, f32[1,1032,128]{2,1,0:T(8,128)}, u32[]{:S(2)}, u32[]{:S(2)}) collective-permute-start(f32[1,1032,128]{2,1,0:T(8,128)} %select_maximum_fusion.2), channel_id=1, source_target_pairs={{2,0},{4,2},{6,4},{8,6},{10,8},{12,10},{14,12},{3,1},{5,3},{7,5},{... | collective-permute-start | bytes 1585160 | tf_op jit(solution)/shard_map/ppermute | solution.py:48
  85.8 5.6 %copy-start.3 = (f32[2,16,64,128]{3,2,1,0:T(8,128)S(1)}, f32[2,16,64,128]{3,2,1,0:T(8,128)}, u32[]{:S(2)}) copy-start(f32[2,16,64,128]{3,2,1,0:T(8,128)} %shard_map.120) | copy-start | bytes 3145732
  91.3 2.7 %copy-start.5 = (f32[1,16,64,128]{3,2,1,0:T(8,128)S(1)}, f32[1,16,64,128]{3,2,1,0:T(8,128)}, u32[]{:S(2)}) copy-start(f32[1,16,64,128]{3,2,1,0:T(8,128)} %copy-done.4) | copy-start | bytes 1572868
  92.3 5.9 %copy-start.7 = (f32[1,1024,128]{2,1,0:T(8,128)S(1)}, f32[1,1024,128]{2,1,0:T(8,128)}, u32[]{:S(2)}) copy-start(f32[1,1024,128]{2,1,0:T(8,128)} %copy-done.6) | copy-start | bytes 1572868
  95.9 14.8 %collective-permute-start.3 = (f32[1,1032,128]{2,1,0:T(8,128)}, f32[1,1032,128]{2,1,0:T(8,128)}, u32[]{:S(2)}, u32[]{:S(2)}) collective-permute-start(f32[1,1032,128]{2,1,0:T(8,128)} %select_maximum_fusion.4), channel_id=1, source_target_pairs={{0,4},{2,6},{4,8},{6,10},{8,12},{10,14},{1,5},{3,7},{5,9},{7,11},{... | collective-permute-start | bytes 1585160 | tf_op jit(solution)/shard_map/ppermute | solution.py:48
  98.1 14.3 %copy-start.9 = (f32[1,16,64,128]{3,2,1,0:T(8,128)S(1)}, f32[1,16,64,128]{3,2,1,0:T(8,128)}, u32[]{:S(2)}) copy-start(f32[1,16,64,128]{3,2,1,0:T(8,128)} %copy-done.8) | copy-start | bytes 1572868
  99.5 14.4 %collective-permute-start.6 = (f32[1,1032,128]{2,1,0:T(8,128)S(1)}, f32[1,1032,128]{2,1,0:T(8,128)S(1)}, u32[]{:S(2)}, u32[]{:S(2)}) collective-permute-start(f32[1,1032,128]{2,1,0:T(8,128)S(1)} %select_maximum_fusion.1), channel_id=1, source_target_pairs={{4,0},{6,2},{8,4},{10,6},{12,8},{14,10},{5,1},{7,3},{9,5},{11,7},{... | collective-permute-start | bytes 1585160 | tf_op jit(solution)/shard_map/ppermute | solution.py:48
  112.6 25.2 %collective-permute-start.4 = (f32[1,1032,128]{2,1,0:T(8,128)S(1)}, f32[1,1032,128]{2,1,0:T(8,128)S(1)}, u32[]{:S(2)}, u32[]{:S(2)}) collective-permute-start(f32[1,1032,128]{2,1,0:T(8,128)S(1)} %select_maximum_fusion.3), channel_id=1, source_target_pairs={{0,8},{2,10},{4,12},{6,14},{1,9},{3,11},{5,13},{7,15},{16,24},{18,... | collective-permute-start | bytes 1585160 | tf_op jit(solution)/shard_map/ppermute | solution.py:48
  114.2 23.9 %copy-start.19 = (f32[1,1,16,64,128]{4,3,2,1,0:T(8,128)S(1)}, f32[1,1,16,64,128]{4,3,2,1,0:T(8,128)}, u32[]{:S(2)}) copy-start(f32[1,1,16,64,128]{4,3,2,1,0:T(8,128)} %slice_add_fusion) | copy-start | bytes 1572868
  114.2 29.6 %collective-permute-start.7 = (f32[1,1032,128]{2,1,0:T(8,128)S(1)}, f32[1,1032,128]{2,1,0:T(8,128)S(1)}, u32[]{:S(2)}, u32[]{:S(2)}) collective-permute-start(f32[1,1032,128]{2,1,0:T(8,128)S(1)} %select_maximum_fusion), channel_id=1, source_target_pairs={{8,0},{10,2},{12,4},{14,6},{9,1},{11,3},{13,5},{15,7},{24,16},{26,... | collective-permute-start | bytes 1585160 | tf_op jit(solution)/shard_map/ppermute | solution.py:48
  138.2 1.8 %copy-start.1 = (bf16[1,512,1280]{2,1,0:T(8,128)(2,1)S(1)}, bf16[1,512,1280]{2,1,0:T(8,128)(2,1)}, u32[]{:S(2)}) copy-start(bf16[1,512,1280]{2,1,0:T(8,128)(2,1)} %shard_map.118) | copy-start | bytes 3932164
  138.3 1.8 %copy-start.20 = (f32[1,2,256,16]{3,2,1,0:T(8,128)S(1)}, f32[1,2,256,16]{3,2,1,0:T(8,128)}, u32[]{:S(2)}) copy-start(f32[1,2,256,16]{3,2,1,0:T(8,128)} %get-tuple-element.85) | copy-start | bytes 98308
  138.3 1.8 %copy-start.26 = (s32[1024]{0:T(1024)S(1)}, s32[1024]{0:T(1024)}, u32[]{:S(2)}) copy-start(s32[1024]{0:T(1024)} %get-tuple-element.114) | copy-start | bytes 12292
  138.3 1.8 %copy-start.27 = (s32[1024]{0:T(1024)S(1)}, s32[1024]{0:T(1024)}, u32[]{:S(2)}) copy-start(s32[1024]{0:T(1024)} %get-tuple-element.115) | copy-start | bytes 12292
  138.3 1.8 %copy-start.33 = (pred[1024]{0:T(1024)(128)(4,1)S(1)}, pred[1024]{0:T(1024)(128)(4,1)}, u32[]{:S(2)}) copy-start(pred[1024]{0:T(1024)(128)(4,1)} %fusion.50) | copy-start | bytes 3076
  145.4 1.8 %copy-start.2 = (bf16[1,512,1280]{2,1,0:T(8,128)(2,1)S(1)}, bf16[1,512,1280]{2,1,0:T(8,128)(2,1)}, u32[]{:S(2)}) copy-start(bf16[1,512,1280]{2,1,0:T(8,128)(2,1)} %shard_map.121) | copy-start | bytes 3932164
  145.4 1.8 %copy-start.21 = (f32[1,2,256,16]{3,2,1,0:T(8,128)S(1)}, f32[1,2,256,16]{3,2,1,0:T(8,128)}, u32[]{:S(2)}) copy-start(f32[1,2,256,16]{3,2,1,0:T(8,128)} %get-tuple-element.89) | copy-start | bytes 98308
  (10 other events, 12.0 us)

commit v11 on v10

--- a/solution.py
+++ b/solution.py
@@ -34,7 +34,7 @@
     return (first_decay * next_decay, next_decay[..., None, None] * first_state + next_state)
 
 
-def exclusive_scans(fwd, rev, axis):
+def exclusive_scans(fwd, rev, axis, after_fwd):
     count = lax.axis_size(axis)
     place = lax.axis_index(axis)
     seen = [None, None]
@@ -49,14 +49,18 @@
             has = (place >= shift) if k == 0 else (place < count - shift)
             decay = jnp.where(has, decay, 1.0)
             got.append((decay, state))
+        last = 2 * shift >= count
         for k in range(2):
+            if k == 1 and last:
+                tail = after_fwd(seen[0][1])
+                got[1], tail = lax.optimization_barrier((got[1], tail))
             seen[k] = got[k] if seen[k] is None else chain(got[k], seen[k])
-            if 2 * shift < count:
+            if not last:
                 ahead[k] = chain(got[k], ahead[k])
         shift *= 2
     if seen[0] is None:
-        return fwd_identity(fwd), fwd_identity(rev)
-    return seen[0], seen[1]
+        return fwd_identity(rev), after_fwd(fwd_identity(fwd)[1])
+    return seen[1], tail
 
 
 def pack(decay, state):
@@ -278,13 +282,16 @@
         jnp.einsum("grd,dh->grh", mirrored, w_dt, preferred_element_type=jnp.float32) + dt_bias
     )
     sum_r, pend_r = strand_terms(proj_r, step_r, conv_w, conv_b, rates, True)
-    in_f, in_r = exclusive_scans(sum_f, sum_r, "seq")
-    normed_f = finish(pend_f, in_f[1], proj_f[:, :rows, :inner], d_skip, norm_gain)
+    def forward_out(incoming):
+        normed_f = finish(pend_f, incoming, proj_f[:, :rows, :inner], d_skip, norm_gain)
+        return jnp.einsum("grk,kd->grd", normed_f, w_out, preferred_element_type=jnp.float32)
+
+    in_r, out_f = exclusive_scans(sum_f, sum_r, "seq", forward_out)
     normed_r = finish(pend_r, in_r[1], proj_r[:, :rows, :inner], d_skip, norm_gain)
     w_out_mirrored = flip_lanes(w_out)
-    out = jnp.einsum(
-        "grk,kd->grd", normed_f, w_out, preferred_element_type=jnp.float32
-    ) + jnp.einsum("grk,kd->grd", normed_r, w_out_mirrored, preferred_element_type=jnp.float32)
+    out = out_f + jnp.einsum(
+        "grk,kd->grd", normed_r, w_out_mirrored, preferred_element_type=jnp.float32
+    )
     return out.astype(jnp.bfloat16)
 
 

time: 165 us -> 159 us (0.964)
  other arithmetic: 22.3 us -> 19.2 us
  matrix products: 39.8 us -> 38 us
    convert_element_type x0 -> x1, other arithmetic: none -> 3.51 us  [on_device(): return out.astype(jnp.bfloat16)]
    reshape x0 -> x6, local copies, waits for them, and re-layouts: none -> 3.4 us  [the longest x4 3.36 us: block_terms(): flat = lambda a: a.reshape((blocks,) + a.shape[2:])]
    reshape x2, other arithmetic: 2.54 us -> 0.16 us  [block_terms(): flat = lambda a: a.reshape((blocks,) + a.shape[2:])]
    exp x2, other arithmetic: 2.47 us -> 0.1 us  [block_terms(): return (inside, state, jnp.exp(end), jnp.exp(log_decay))]
    slice x3 -> x2, other arithmetic: 2.12 us -> 0.01 us  [strand_terms(): sofar = chain(sofar, (total[:, j], state[:, j]))]
    dot_general x1, matrix products: 4.49 us -> 2.66 us  [forward_out(): jnp.einsum('grk,kd->grd', normed_f, w_out, preferred_element_type=jnp.flo...]
    another operation x8 -> x10, local copies, waits for them, and re-layouts: 2.45 us -> 0.78 us
    unnamed x68 -> x52, local copies, waits for them, and re-layouts: 7.24 us -> 6.81 us
  transfers between devices with their start and end apart: 8 -> 8, of which waited for: 2 -> 2; matrix products, arithmetic and copies ran while one was open for 24% -> 23% of each run, Pallas kernels for 19% -> 20%
where the time goes in v11:
time: 159 us; the launch traced here: 158 us
  matrix products  38 us (24%)
  Pallas kernels  31.7 us (20%)
  starting transfers between devices  25.5 us (16%)
  waiting for transfers between devices  24.4 us (15%)
  other arithmetic  19.2 us (12%)
  local copies, waits for them, and re-layouts  18.2 us (11%)
    ppermute x6, waiting for transfers between devices, exclusive_scans(): decay, state = unpack(lax.ppermute(pack(*ahead[k]), axis, pairs))  24.4 us
    ppermute x6, starting transfers between devices, exclusive_scans(): decay, state = unpack(lax.ppermute(pack(*ahead[k]), axis, pairs))  19.7 us
    pallas_call x2, Pallas kernels, block_terms(): pl.pallas_call(partial(inside_kernel, reverse=reverse), grid=(blocks,), i...  11.2 us
    pallas_call x2, Pallas kernels, convolve(): pl.pallas_call(partial(conv_kernel, reverse=reverse), grid=(count, width...  10.3 us
    pallas_call x2, Pallas kernels, block_terms(): pl.pallas_call(state_kernel, grid=(blocks,), in_specs=[spec((Q, width)),...  10.2 us
    dot_general x1, matrix products, on_device(): jnp.einsum('grd,de->gre', ext_r, w_in, preferred_element_type=jnp.float32)  7.52 us
    dot_general x2, matrix products, finish(): jnp.einsum('grh,hk->grk', from_start.reshape(count, rows, H), spread, pre...  7.19 us
    dot_general x1, matrix products, on_device(): jnp.einsum('grd,de->gre', ext_f, w_in, preferred_element_type=jnp.float32)  7.14 us
  transfers between devices with their start and end apart: 8, of which 2 were waited for; matrix products, arithmetic and copies ran while one was open for 23% of the time, Pallas kernels for 20%

profile of v11, /device:TPU:24, one launch (start us, length us, event | category | flops | bytes accessed | tf_op | source)
XLA Modules:
  0.0 157.8 jit_solution(12094064123776156550)
XLA Ops:
  0.0 1.9 %fusion.9 = bf16[1,512,1024]{2,1,0:T(8,128)(2,1)S(1)} fusion(bf16[1,512,1024]{2,1,0:T(8,128)(2,1)} %param.25, bf16[4,1024]{1,0:T(4,128)(2,1)} %param.26, s32[512]{0:T(512)} %bitcast.285), kind=kOutput, calls=%fused_computation.17 | convolution fusion | flops 5769216 | bytes 2107392 | tf_op jit(solution)/shard_map/gtb,bd->gtd/dot_general | solution.py:263
  2.0 3.3 %collective-permute-start.1 = (bf16[1,3,1024]{2,1,0:T(4,128)(2,1)S(1)}, bf16[1,3,1024]{2,1,0:T(4,128)(2,1)S(1)}, u32[]{:S(2)}, u32[]{:S(2)}) collective-permute-start(bf16[1,3,1024]{2,1,0:T(4,128)(2,1)S(1)} %get-tuple-element.105), channel_id=1, source_target_pairs={{2,0},{4,2},{6,4},{8,6},{10,8},{12,10},{14,12},{3,1},{5,3},{7,5},{... | collective-permute-start | bytes 18440 | tf_op jit(solution)/shard_map/ppermute | solution.py:268
  5.2 2.6 %collective-permute-start = (bf16[1,3,1024]{2,1,0:T(4,128)(2,1)S(1)}, bf16[1,3,1024]{2,1,0:T(4,128)(2,1)S(1)}, u32[]{:S(2)}, u32[]{:S(2)}) collective-permute-start(bf16[1,3,1024]{2,1,0:T(4,128)(2,1)S(1)} %get-tuple-element.106), channel_id=1, source_target_pairs={{0,2},{2,4},{4,6},{6,8},{8,10},{10,12},{12,14},{1,3},{3,5},{5,7},{... | collective-permute-start | bytes 18440 | tf_op jit(solution)/shard_map/ppermute | solution.py:267
  8.4 1.1 reduce-window.14
  13.4 7.1 %convolution_bitcast_fusion.1.src_ref.halo_ref = f32[1,520,2304]{2,1,0:T(8,128)} fusion(bf16[1024,2304]{1,0:T(8,128)(2,1)} %param.27, bf16[1,3,1024]{2,1,0:T(4,128)(2,1)S(1)} %collective-permute-done, bf16[1,5,1024]{2,1,0:T(8,128)(2,1)S(1)} %broadcast_in_dim.12, bf16[1,512,1024]{2,1,0:T(8,128)(2,1)S(1)} %fusion.9), kind=kOutput, calls=%fused_computation.1 | convolution fusion | flops 2456862720 | bytes 10575872 | tf_op jit(solution)/shard_map/grd,de->gre/dot_general | solution.py:272
  20.6 5.2 %shard_map.118 = bf16[1,512,1280]{2,1,0:T(8,128)(2,1)} custom-call(f32[1,520,2304]{2,1,0:T(8,128)} %convolution_bitcast_fusion.1.src_ref.halo_ref, f32[1,520,2304]{2,1,0:T(8,128)} %convolution_bitcast_fusion.1.src_ref.halo_ref, f32[4,1280]{1,0:T(4,128)} %w_ref.3, f32[1,1280]{1,0:T(1,128)} %reshape.988.b_ref), custom_call_target="tpu_custom_call" | custom-call | tf_op jit(solution)/shard_map/pallas_call | solution.py:194
  25.7 5.1 %shard_map.119 = f32[2,16,64,128]{3,2,1,0:T(8,128)} custom-call(bf16[2,256,1280]{2,1,0:T(8,128)(2,1)} %bitcast.240, f32[2,256,16]{2,1,0:T(8,128)} %copy.28.to_end_ref), custom_call_target="tpu_custom_call" | custom-call | tf_op jit(solution)/shard_map/pallas_call | solution.py:132
  30.8 1.3 fusion.36
  33.2 2.5 %fusion.14 = bf16[520,1024]{1,0:T(8,128)(2,1)S(1)} fusion(bf16[1,5,1024]{2,1,0:T(8,128)(2,1)S(1)} %broadcast_in_dim.12, bf16[1,3,1024]{2,1,0:T(4,128)(2,1)S(1)} %collective-permute-done.1, bf16[1,512,1024]{2,1,0:T(8,128)(2,1)} %copy-done.10), kind=kOutput, calls=%fused_computation.27 | convolution fusion | flops 1096343552 | bytes 2129920 | tf_op jit(solution)/shard_map/...d,de->...e/dot_general | solution.py:28
  37.2 1.1 reduce-window.16
  39.2 7.5 %convolution_bitcast_fusion.src_ref.halo_ref = f32[1,520,2304]{2,1,0:T(8,128)} fusion(bf16[520,1024]{1,0:T(8,128)(2,1)} %copy-done.24, bf16[1024,2304]{1,0:T(8,128)(2,1)} %param.27), kind=kOutput, calls=%fused_computation | convolution fusion | flops 2453667840 | bytes 10575872 | tf_op jit(solution)/shard_map/grd,de->gre/dot_general | solution.py:280
  50.2 1.9 %collective-permute-start.5 = (f32[1,1032,128]{2,1,0:T(8,128)}, f32[1,1032,128]{2,1,0:T(8,128)}, u32[]{:S(2)}, u32[]{:S(2)}) collective-permute-start(f32[1,1032,128]{2,1,0:T(8,128)} %select_maximum_fusion.2), channel_id=1, source_target_pairs={{0,2},{2,4},{4,6},{6,8},{8,10},{10,12},{12,14},{1,3},{3,5},{5,7},{... | collective-permute-start | bytes 1585160 | tf_op jit(solution)/shard_map/ppermute | solution.py:48
  52.2 5.1 %shard_map.120 = bf16[1,512,1280]{2,1,0:T(8,128)(2,1)} custom-call(f32[1,520,2304]{2,1,0:T(8,128)} %convolution_bitcast_fusion.src_ref.halo_ref, f32[1,520,2304]{2,1,0:T(8,128)} %convolution_bitcast_fusion.src_ref.halo_ref, f32[4,1280]{1,0:T(4,128)} %w_ref.3, f32[1,1280]{1,0:T(1,128)} %reshape.988.b_ref), custom_call_target="tpu_custom_call" | custom-call | tf_op jit(solution)/shard_map/pallas_call | solution.py:194
  58.2 5.1 %shard_map.121 = f32[2,16,64,128]{3,2,1,0:T(8,128)} custom-call(bf16[2,256,1280]{2,1,0:T(8,128)(2,1)} %bitcast.242, f32[2,256,16]{2,1,0:T(8,128)} %copy.34.to_end_ref), custom_call_target="tpu_custom_call" | custom-call | tf_op jit(solution)/shard_map/pallas_call | solution.py:132
  63.3 2.1 %broadcast_add_fusion = (f32[1,1,16,64,128]{4,3,2,1,0:T(8,128)}, f32[1,1,16,64,128]{4,3,2,1,0:T(8,128)S(1)}, f32[1,1,16,64,128]{4,3,2,1,0:T(8,128)S(1)}) fusion(f32[16]{0:T(128)S(1)} %bitcast_multiply_fusion.7, f32[1,2,16,64,128]{4,3,2,1,0:T(8,128)} %bitcast.254), kind=kLoop, calls=%fused_computation.71 | loop fusion | flops 131072 | bytes 2621504 | tf_op jit(solution)/shard_map/add | solution.py:34
  67.4 5.0 %collective-permute-start.2 = (f32[1,1032,128]{2,1,0:T(8,128)}, f32[1,1032,128]{2,1,0:T(8,128)}, u32[]{:S(2)}, u32[]{:S(2)}) collective-permute-start(f32[1,1032,128]{2,1,0:T(8,128)} %select_maximum_fusion.5), channel_id=1, source_target_pairs={{2,0},{4,2},{6,4},{8,6},{10,8},{12,10},{14,12},{3,1},{5,3},{7,5},{... | collective-permute-start | bytes 1585160 | tf_op jit(solution)/shard_map/ppermute | solution.py:48
  72.4 5.6 %shard_map.122 = f32[2,256,1024]{2,1,0:T(8,128)} custom-call(bf16[2,256,1280]{2,1,0:T(8,128)(2,1)} %bitcast.241, f32[2,256,16]{2,1,0:T(8,128)} %copy.36.cum_ref, f32[2,16,256]{2,1,0:T(8,128)} %bitcast.262, f32[2,16,256]{2,1,0:T(8,128)} %bitcast.268), custom_call_target="tpu_custom_call" | custom-call | tf_op jit(solution)/shard_map/pallas_call | solution.py:139
  78.0 5.6 %shard_map.123 = f32[2,256,1024]{2,1,0:T(8,128)} custom-call(bf16[2,256,1280]{2,1,0:T(8,128)(2,1)} %bitcast.243, f32[2,256,16]{2,1,0:T(8,128)} %copy.39.cum_ref, f32[2,16,256]{2,1,0:T(8,128)} %bitcast.264, f32[2,16,256]{2,1,0:T(8,128)} %bitcast.269), custom_call_target="tpu_custom_call" | custom-call | tf_op jit(solution)/shard_map/pallas_call | solution.py:139
  85.2 1.1 slice.295
  88.1 1.3 collective-permute-start.6
  90.4 1.3 fusion.65
  91.7 4.6 %collective-permute-start.3 = (f32[1,1032,128]{2,1,0:T(8,128)S(1)}, f32[1,1032,128]{2,1,0:T(8,128)S(1)}, u32[]{:S(2)}, u32[]{:S(2)}) collective-permute-start(f32[1,1032,128]{2,1,0:T(8,128)S(1)} %select_maximum_fusion.4), channel_id=1, source_target_pairs={{4,0},{6,2},{8,4},{10,6},{12,8},{14,10},{5,1},{7,3},{9,5},{11,7},{... | collective-permute-start | bytes 1585160 | tf_op jit(solution)/shard_map/ppermute | solution.py:48
  96.3 6.6 %collective-permute-done.6 = f32[1,1032,128]{2,1,0:T(8,128)} collective-permute-done((f32[1,1032,128]{2,1,0:T(8,128)}, f32[1,1032,128]{2,1,0:T(8,128)}, u32[]{:S(2)}, u32[]{:S(2)}) %collective-permute-start.6) | collective-permute-done | bytes 528416 | tf_op jit(solution)/shard_map/ppermute | solution.py:48
  104.8 1.3 collective-permute-start.7
  106.4 5.6 %collective-permute-start.4 = (f32[1,1032,128]{2,1,0:T(8,128)S(1)}, f32[1,1032,128]{2,1,0:T(8,128)S(1)}, u32[]{:S(2)}, u32[]{:S(2)}) collective-permute-start(f32[1,1032,128]{2,1,0:T(8,128)S(1)} %select_maximum_fusion.3), channel_id=1, source_target_pairs={{8,0},{10,2},{12,4},{14,6},{9,1},{11,3},{13,5},{15,7},{24,16},{26,... | collective-permute-start | bytes 1585160 | tf_op jit(solution)/shard_map/ppermute | solution.py:48
  112.8 17.8 %collective-permute-done.7 = f32[1,1032,128]{2,1,0:T(8,128)S(1)} collective-permute-done((f32[1,1032,128]{2,1,0:T(8,128)S(1)}, f32[1,1032,128]{2,1,0:T(8,128)S(1)}, u32[]{:S(2)}, u32[]{:S(2)}) %collective-permute-start.7) | collective-permute-done | bytes 528416 | tf_op jit(solution)/shard_map/ppermute | solution.py:48
  132.8 3.6 %fusion.7 = f32[1,512,1024]{2,1,0:T(8,128)S(1)} fusion(f32[2,256,1024]{2,1,0:T(8,128)S(1)} %fusion.68, f32[2,256,1024]{2,1,0:T(8,128)S(1)} %copy-done.12, f32[1,520,2304]{2,1,0:T(8,128)} %convolution_bitcast_fusion.1.src_ref.halo_ref, f32[512,16]{0,1:T(8,128)S(1)} %bitcast.273, bf16[1,512,1280]{2,1,0:T(8,128)(2,1)S(1)} %copy-done.1, f32[1024]{0:T(1024)S(1)} %mul.500, ...), kind=kOutput, calls=%fused_computation.13 | convolution fusion | flops 105938944 | bytes 9483264 | tf_op jit(solution)/shard_map/grh,hk->grk/dot_general | solution.py:244
  137.1 2.7 %convolution_bitcast_fusion.2 = f32[1,512,1024]{2,1,0:T(8,128)} fusion(bf16[1024,1024]{1,0:T(8,128)(2,1)S(1)} %copy-done, f32[1,512,1024]{2,1,0:T(8,128)S(1)} %fusion.7, f32[1024]{0:T(1024)S(1)} %copy-done.22, f32[512]{0:T(512)S(1)} %add_rsqrt_fusion.1), kind=kOutput, calls=%fused_computation.26 | convolution fusion | flops 1075314688 | bytes 6297600 | tf_op jit(solution)/shard_map/grk,kd->grd/dot_general | solution.py:287
  142.7 3.6 %fusion.5 = f32[1,512,1024]{2,1,0:T(8,128)S(1)} fusion(f32[2,256,1024]{2,1,0:T(8,128)S(1)} %fusion.69, f32[2,256,1024]{2,1,0:T(8,128)S(1)} %copy-done.11, f32[1,520,2304]{2,1,0:T(8,128)} %convolution_bitcast_fusion.src_ref.halo_ref, f32[512,16]{0,1:T(8,128)S(1)} %bitcast.274, bf16[1,512,1280]{2,1,0:T(8,128)(2,1)S(1)} %copy-done.2, f32[1024]{0:T(1024)S(1)} %mul.500, ...), kind=kOutput, calls=%fused_computation.9 | convolution fusion | flops 105938944 | bytes 9483264 | tf_op jit(solution)/shard_map/grh,hk->grk/dot_general | solution.py:244
  146.4 1.3 copy-done.13
  147.9 6.4 %fusion.10 = f32[512,1024]{1,0:T(8,128)} fusion(bf16[1024,1024]{1,0:T(8,128)(2,1)S(1)} %copy-done, f32[1,512,1024]{2,1,0:T(8,128)} %copy-done.13, f32[512]{0:T(512)S(1)} %add_rsqrt_fusion, f32[1024]{0:T(1024)S(1)} %copy-done.22), kind=kOutput, calls=%fused_computation.18 | convolution fusion | flops 3226992640 | bytes 6297600 | tf_op jit(solution)/shard_map/grk,kd->grd/dot_general | solution.py:292
  154.3 3.5 %fusion.4 = bf16[1,512,1024]{2,1,0:T(8,128)(2,1)} fusion(f32[1,512,1024]{2,1,0:T(8,128)} %convolution_bitcast_fusion.2, f32[512,1024]{1,0:T(8,128)} %fusion.10), kind=kLoop, calls=%fused_computation.7 | loop fusion | flops 1048576 | bytes 5242880 | tf_op jit(solution)/shard_map/convert_element_type | solution.py:295
  (146 shorter events, 27.4 us)
Async XLA Ops:
  0.0 136.6 %copy-start = (bf16[1024,1024]{1,0:T(8,128)(2,1)S(1)}, bf16[1024,1024]{1,0:T(8,128)(2,1)}, u32[]{:S(2)}) copy-start(bf16[1024,1024]{1,0:T(8,128)(2,1)} %param.35) | copy-start | bytes 6291460
  0.0 7.8 %copy-start.23 = (f32[16]{0:T(128)S(1)}, f32[16]{0:T(128)}, u32[]{:S(2)}) copy-start(f32[16]{0:T(128)} %param.32) | copy-start | bytes 196
  0.0 7.9 %copy-start.20 = (f32[16]{0:T(128)S(1)}, f32[16]{0:T(128)}, u32[]{:S(2)}) copy-start(f32[16]{0:T(128)} %param.31) | copy-start | bytes 196
  0.0 7.9 %copy-start.18 = (bf16[1024,16]{0,1:T(8,128)(2,1)S(1)}, bf16[1024,16]{0,1:T(8,128)(2,1)}, u32[]{:S(2)}) copy-start(bf16[1024,16]{0,1:T(8,128)(2,1)} %param.28) | copy-start | bytes 98308
  0.0 10.3 %copy-start.19 = (f32[1280]{0:T(1024)S(1)}, f32[1280]{0:T(1024)}, u32[]{:S(2)}) copy-start(f32[1280]{0:T(1024)} %param.30) | copy-start | bytes 15364
  0.0 10.9 %copy-start.21 = (f32[16]{0:T(128)S(1)}, f32[16]{0:T(128)}, u32[]{:S(2)}) copy-start(f32[16]{0:T(128)} %param.33) | copy-start | bytes 196
  1.9 18.6 %copy-start.10 = (bf16[1,512,1024]{2,1,0:T(8,128)(2,1)}, bf16[1,512,1024]{2,1,0:T(8,128)(2,1)S(1)}, u32[]{:S(2)}) copy-start(bf16[1,512,1024]{2,1,0:T(8,128)(2,1)S(1)} %fusion.9) | copy-start | bytes 3145732
  2.0 31.3 %collective-permute-start.1 = (bf16[1,3,1024]{2,1,0:T(4,128)(2,1)S(1)}, bf16[1,3,1024]{2,1,0:T(4,128)(2,1)S(1)}, u32[]{:S(2)}, u32[]{:S(2)}) collective-permute-start(bf16[1,3,1024]{2,1,0:T(4,128)(2,1)S(1)} %get-tuple-element.105), channel_id=1, source_target_pairs={{2,0},{4,2},{6,4},{8,6},{10,8},{12,10},{14,12},{3,1},{5,3},{7,5},{... | collective-permute-start | bytes 18440 | tf_op jit(solution)/shard_map/ppermute | solution.py:268
  5.2 8.2 %collective-permute-start = (bf16[1,3,1024]{2,1,0:T(4,128)(2,1)S(1)}, bf16[1,3,1024]{2,1,0:T(4,128)(2,1)S(1)}, u32[]{:S(2)}, u32[]{:S(2)}) collective-permute-start(bf16[1,3,1024]{2,1,0:T(4,128)(2,1)S(1)} %get-tuple-element.106), channel_id=1, source_target_pairs={{0,2},{2,4},{4,6},{6,8},{8,10},{10,12},{12,14},{1,3},{3,5},{5,7},{... | collective-permute-start | bytes 18440 | tf_op jit(solution)/shard_map/ppermute | solution.py:267
  10.0 10.6 %copy-start.16 = (f32[1,2,16,256]{3,2,1,0:T(8,128)}, f32[1,2,16,256]{3,2,1,0:T(8,128)S(1)}, u32[]{:S(2)}) copy-start(f32[1,2,16,256]{3,2,1,0:T(8,128)S(1)} %get-tuple-element.96) | copy-start | bytes 98308
  32.1 17.2 %copy-start.4 = (f32[1,16,64,128]{3,2,1,0:T(8,128)}, f32[1,16,64,128]{3,2,1,0:T(8,128)S(1)}, u32[]{:S(2)}) copy-start(f32[1,16,64,128]{3,2,1,0:T(8,128)S(1)} %fusion.36) | copy-start | bytes 1572868
  35.7 1.0 copy-start.24
  39.1 9.5 %copy-start.17 = (f32[1,2,256,16]{2,3,1,0:T(8,128)}, f32[1,2,256,16]{2,3,1,0:T(8,128)S(1)}, u32[]{:S(2)}) copy-start(f32[1,2,256,16]{2,3,1,0:T(8,128)S(1)} %get-tuple-element.94) | copy-start | bytes 98308
  50.2 34.3 %collective-permute-start.5 = (f32[1,1032,128]{2,1,0:T(8,128)}, f32[1,1032,128]{2,1,0:T(8,128)}, u32[]{:S(2)}, u32[]{:S(2)}) collective-permute-start(f32[1,1032,128]{2,1,0:T(8,128)} %select_maximum_fusion.2), channel_id=1, source_target_pairs={{0,2},{2,4},{4,6},{6,8},{8,10},{10,12},{12,14},{1,3},{3,5},{5,7},{... | collective-permute-start | bytes 1585160 | tf_op jit(solution)/shard_map/ppermute | solution.py:48
  65.8 0.8 copy-start.6
  67.4 22.0 %collective-permute-start.2 = (f32[1,1032,128]{2,1,0:T(8,128)}, f32[1,1032,128]{2,1,0:T(8,128)}, u32[]{:S(2)}, u32[]{:S(2)}) collective-permute-start(f32[1,1032,128]{2,1,0:T(8,128)} %select_maximum_fusion.5), channel_id=1, source_target_pairs={{2,0},{4,2},{6,4},{8,6},{10,8},{12,10},{14,12},{3,1},{5,3},{7,5},{... | collective-permute-start | bytes 1585160 | tf_op jit(solution)/shard_map/ppermute | solution.py:48
  78.0 5.6 %copy-start.3 = (f32[2,16,64,128]{3,2,1,0:T(8,128)S(1)}, f32[2,16,64,128]{3,2,1,0:T(8,128)}, u32[]{:S(2)}) copy-start(f32[2,16,64,128]{3,2,1,0:T(8,128)} %shard_map.119) | copy-start | bytes 3145732
  83.6 2.7 %copy-start.5 = (f32[1,16,64,128]{3,2,1,0:T(8,128)S(1)}, f32[1,16,64,128]{3,2,1,0:T(8,128)}, u32[]{:S(2)}) copy-start(f32[1,16,64,128]{3,2,1,0:T(8,128)} %copy-done.4) | copy-start | bytes 1572868
  84.5 5.9 %copy-start.7 = (f32[1,1024,128]{2,1,0:T(8,128)S(1)}, f32[1,1024,128]{2,1,0:T(8,128)}, u32[]{:S(2)}) copy-start(f32[1,1024,128]{2,1,0:T(8,128)} %copy-done.6) | copy-start | bytes 1572868
  86.4 0.8 copy-start.8
  88.1 14.8 %collective-permute-start.6 = (f32[1,1032,128]{2,1,0:T(8,128)}, f32[1,1032,128]{2,1,0:T(8,128)}, u32[]{:S(2)}, u32[]{:S(2)}) collective-permute-start(f32[1,1032,128]{2,1,0:T(8,128)} %select_maximum_fusion.1), channel_id=1, source_target_pairs={{0,4},{2,6},{4,8},{6,10},{8,12},{10,14},{1,5},{3,7},{5,9},{7,11},{... | collective-permute-start | bytes 1585160 | tf_op jit(solution)/shard_map/ppermute | solution.py:48
  90.4 14.3 %copy-start.9 = (f32[1,16,64,128]{3,2,1,0:T(8,128)S(1)}, f32[1,16,64,128]{3,2,1,0:T(8,128)}, u32[]{:S(2)}) copy-start(f32[1,16,64,128]{3,2,1,0:T(8,128)} %copy-done.8) | copy-start | bytes 1572868
  91.7 14.4 %collective-permute-start.3 = (f32[1,1032,128]{2,1,0:T(8,128)S(1)}, f32[1,1032,128]{2,1,0:T(8,128)S(1)}, u32[]{:S(2)}, u32[]{:S(2)}) collective-permute-start(f32[1,1032,128]{2,1,0:T(8,128)S(1)} %select_maximum_fusion.4), channel_id=1, source_target_pairs={{4,0},{6,2},{8,4},{10,6},{12,8},{14,10},{5,1},{7,3},{9,5},{11,7},{... | collective-permute-start | bytes 1585160 | tf_op jit(solution)/shard_map/ppermute | solution.py:48
  104.8 25.7 %collective-permute-start.7 = (f32[1,1032,128]{2,1,0:T(8,128)S(1)}, f32[1,1032,128]{2,1,0:T(8,128)S(1)}, u32[]{:S(2)}, u32[]{:S(2)}) collective-permute-start(f32[1,1032,128]{2,1,0:T(8,128)S(1)} %select_maximum_fusion), channel_id=1, source_target_pairs={{0,8},{2,10},{4,12},{6,14},{1,9},{3,11},{5,13},{7,15},{16,24},{18,... | collective-permute-start | bytes 1585160 | tf_op jit(solution)/shard_map/ppermute | solution.py:48
  106.4 24.4 %copy-start.15 = (f32[1,1,16,64,128]{4,3,2,1,0:T(8,128)S(1)}, f32[1,1,16,64,128]{4,3,2,1,0:T(8,128)}, u32[]{:S(2)}) copy-start(f32[1,1,16,64,128]{4,3,2,1,0:T(8,128)} %slice_add_fusion) | copy-start | bytes 1572868
  106.4 33.3 %collective-permute-start.4 = (f32[1,1032,128]{2,1,0:T(8,128)S(1)}, f32[1,1032,128]{2,1,0:T(8,128)S(1)}, u32[]{:S(2)}, u32[]{:S(2)}) collective-permute-start(f32[1,1032,128]{2,1,0:T(8,128)S(1)} %select_maximum_fusion.3), channel_id=1, source_target_pairs={{8,0},{10,2},{12,4},{14,6},{9,1},{11,3},{13,5},{15,7},{24,16},{26,... | collective-permute-start | bytes 1585160 | tf_op jit(solution)/shard_map/ppermute | solution.py:48
  130.8 1.6 %copy-start.12 = (f32[2,256,1024]{2,1,0:T(8,128)S(1)}, f32[2,256,1024]{2,1,0:T(8,128)}, u32[]{:S(2)}) copy-start(f32[2,256,1024]{2,1,0:T(8,128)} %shard_map.122) | copy-start | bytes 6291460
  131.0 1.8 %copy-start.1 = (bf16[1,512,1280]{2,1,0:T(8,128)(2,1)S(1)}, bf16[1,512,1280]{2,1,0:T(8,128)(2,1)}, u32[]{:S(2)}) copy-start(bf16[1,512,1280]{2,1,0:T(8,128)(2,1)} %shard_map.118) | copy-start | bytes 3932164
  139.7 1.0 copy-start.14
  140.8 1.6 %copy-start.11 = (f32[2,256,1024]{2,1,0:T(8,128)S(1)}, f32[2,256,1024]{2,1,0:T(8,128)}, u32[]{:S(2)}) copy-start(f32[2,256,1024]{2,1,0:T(8,128)} %shard_map.123) | copy-start | bytes 6291460
  140.9 1.8 %copy-start.2 = (bf16[1,512,1280]{2,1,0:T(8,128)(2,1)S(1)}, bf16[1,512,1280]{2,1,0:T(8,128)(2,1)}, u32[]{:S(2)}) copy-start(bf16[1,512,1280]{2,1,0:T(8,128)(2,1)} %shard_map.120) | copy-start | bytes 3932164
  146.3 1.3 copy-start.13
  (1 other events, 0.7 us)

commit v12 on v11

--- a/solution.py
+++ b/solution.py
@@ -254,6 +254,27 @@
     ).astype(jnp.bfloat16)
 
 
+def project_kernel(a_ref, w_ref, add_ref, out_ref):
+    total = add_ref[...] + jnp.dot(a_ref[...], w_ref[...], preferred_element_type=jnp.float32)
+    out_ref[...] = total.astype(out_ref.dtype)
+
+
+def project_add(normed, w, addend, lanes=256):
+    count, rows, depth = normed.shape
+    width = w.shape[1]
+    return pl.pallas_call(
+        project_kernel,
+        grid=(count, width // lanes),
+        in_specs=[
+            pl.BlockSpec((None, rows, depth), lambda g, j: (g, 0, 0)),
+            pl.BlockSpec((depth, lanes), lambda g, j: (0, j)),
+            pl.BlockSpec((None, rows, lanes), lambda g, j: (g, 0, j)),
+        ],
+        out_specs=pl.BlockSpec((None, rows, lanes), lambda g, j: (g, 0, j)),
+        out_shape=jax.ShapeDtypeStruct((count, rows, width), jnp.bfloat16),
+    )(normed, w, addend)
+
+
 def on_device(
     tokens, hidden, base_table, w_in, w_dt, conv_w, conv_b, dt_bias, a_log, d_skip, norm_gain, w_out
 ):
@@ -289,10 +310,7 @@
     in_r, out_f = exclusive_scans(sum_f, sum_r, "seq", forward_out)
     normed_r = finish(pend_r, in_r[1], proj_r[:, :rows, :inner], d_skip, norm_gain)
     w_out_mirrored = flip_lanes(w_out)
-    out = out_f + jnp.einsum(
-        "grk,kd->grd", normed_r, w_out_mirrored, preferred_element_type=jnp.float32
-    )
-    return out.astype(jnp.bfloat16)
+    return project_add(normed_r, w_out_mirrored, out_f)
 
 
 def solution(mesh):

time: 159 us -> 161 us (1.013)
  Pallas kernels: 31.7 us -> 36.7 us
  matrix products: 38 us -> 35.2 us
    dot_general x1 -> x0, matrix products: 6.36 us -> none  [on_device(): jnp.einsum('grk,kd->grd', normed_r, w_out_mirrored, preferred_element_typ...]
    pallas_call x0 -> x1, Pallas kernels: none -> 5.13 us  [project_add(): pl.pallas_call(project_kernel, grid=(count, width // lanes), in_specs=[pl...]
    dot_general x1 -> x2, matrix products: 2.46 us -> 6.09 us  [flip_lanes(): jnp.einsum('...d,de->...e', a, j, preferred_element_type=jnp.float32)]
    slice x2 -> x3, other arithmetic: 0.01 us -> 2.7 us  [strand_terms(): sofar = chain(sofar, (total[:, j], state[:, j]))]
    convert_element_type x1, other arithmetic: 3.51 us -> 1.26 us  [finish(): return (gated * lax.rsqrt(jnp.mean(gated * gated, axis=-1, keepdims=True)...]
    reshape x4 -> x2, local copies, waits for them, and re-layouts: 3.36 us -> 1.66 us  [block_terms(): flat = lambda a: a.reshape((blocks,) + a.shape[2:])]
    add x7 -> x8, other arithmetic: 5.05 us -> 4.54 us  [chain(): next_decay[..., None, None] * first_state + next_state]
    unnamed x52 -> x69, local copies, waits for them, and re-layouts: 6.81 us -> 6.59 us
  transfers between devices with their start and end apart: 8 -> 8, of which waited for: 2 -> 2; matrix products, arithmetic and copies ran while one was open for 23% -> 26% of each run, Pallas kernels for 20% -> 20%
where the time goes in v12:
time: 161 us; the launch traced here: 159 us
  Pallas kernels  36.7 us (23%)
  matrix products  35.2 us (22%)
  starting transfers between devices  25.8 us (16%)
  waiting for transfers between devices  24.2 us (15%)
  other arithmetic  19.5 us (12%)
  local copies, waits for them, and re-layouts  17.4 us (11%)
    ppermute x6, waiting for transfers between devices, exclusive_scans(): decay, state = unpack(lax.ppermute(pack(*ahead[k]), axis, pairs))  24.2 us
    ppermute x6, starting transfers between devices, exclusive_scans(): decay, state = unpack(lax.ppermute(pack(*ahead[k]), axis, pairs))  19.9 us
    pallas_call x2, Pallas kernels, block_terms(): pl.pallas_call(partial(inside_kernel, reverse=reverse), grid=(blocks,), i...  11.1 us
    pallas_call x2, Pallas kernels, convolve(): pl.pallas_call(partial(conv_kernel, reverse=reverse), grid=(count, width...  10.3 us
    pallas_call x2, Pallas kernels, block_terms(): pl.pallas_call(state_kernel, grid=(blocks,), in_specs=[spec((Q, width)),...  10.2 us
    dot_general x1, matrix products, on_device(): jnp.einsum('grd,de->gre', ext_r, w_in, preferred_element_type=jnp.float32)  7.5 us
    dot_general x1, matrix products, on_device(): jnp.einsum('grd,de->gre', ext_f, w_in, preferred_element_type=jnp.float32)  7.21 us
    dot_general x2, matrix products, finish(): jnp.einsum('grh,hk->grk', from_start.reshape(count, rows, H), spread, pre...  7.03 us
  transfers between devices with their start and end apart: 8, of which 2 were waited for; matrix products, arithmetic and copies ran while one was open for 26% of the time, Pallas kernels for 20%

profile of v12, /device:TPU:24, one launch (start us, length us, event | category | flops | bytes accessed | tf_op | source)
XLA Modules:
  0.0 159.3 jit_solution(11090539489858894090)
XLA Ops:
  0.0 1.9 %fusion.6 = bf16[1,512,1024]{2,1,0:T(8,128)(2,1)S(1)} fusion(bf16[1,512,1024]{2,1,0:T(8,128)(2,1)} %param.25, bf16[4,1024]{1,0:T(4,128)(2,1)} %param.26, s32[512]{0:T(512)} %bitcast.278), kind=kOutput, calls=%fused_computation.14 | convolution fusion | flops 5769216 | bytes 2107392 | tf_op jit(solution)/shard_map/gtb,bd->gtd/dot_general | solution.py:284
  1.9 3.3 %collective-permute-start.1 = (bf16[1,3,1024]{2,1,0:T(4,128)(2,1)S(1)}, bf16[1,3,1024]{2,1,0:T(4,128)(2,1)S(1)}, u32[]{:S(2)}, u32[]{:S(2)}) collective-permute-start(bf16[1,3,1024]{2,1,0:T(4,128)(2,1)S(1)} %get-tuple-element.103), channel_id=1, source_target_pairs={{2,0},{4,2},{6,4},{8,6},{10,8},{12,10},{14,12},{3,1},{5,3},{7,5},{... | collective-permute-start | bytes 18440 | tf_op jit(solution)/shard_map/ppermute | solution.py:289
  5.2 2.6 %collective-permute-start = (bf16[1,3,1024]{2,1,0:T(4,128)(2,1)S(1)}, bf16[1,3,1024]{2,1,0:T(4,128)(2,1)S(1)}, u32[]{:S(2)}, u32[]{:S(2)}) collective-permute-start(bf16[1,3,1024]{2,1,0:T(4,128)(2,1)S(1)} %get-tuple-element.104), channel_id=1, source_target_pairs={{0,2},{2,4},{4,6},{6,8},{8,10},{10,12},{12,14},{1,3},{3,5},{5,7},{... | collective-permute-start | bytes 18440 | tf_op jit(solution)/shard_map/ppermute | solution.py:288
  8.9 1.1 reduce-window.14
  10.9 3.6 %convert_bitcast_fusion.w_ref = bf16[1024,1024]{1,0:T(8,128)(2,1)} fusion(bf16[1024,1024]{1,0:T(8,128)(2,1)S(1)} %copy-done), kind=kOutput, calls=%fused_computation.15 | convolution fusion | flops 2150629376 | bytes 4194304 | tf_op jit(solution)/shard_map/...d,de->...e/dot_general | solution.py:28
  18.7 7.2 %convolution_bitcast_fusion.1.src_ref.halo_ref = f32[1,520,2304]{2,1,0:T(8,128)} fusion(bf16[1024,2304]{1,0:T(8,128)(2,1)} %param.27, bf16[1,3,1024]{2,1,0:T(4,128)(2,1)S(1)} %collective-permute-done, bf16[1,5,1024]{2,1,0:T(8,128)(2,1)S(1)} %broadcast_in_dim.12, bf16[1,512,1024]{2,1,0:T(8,128)(2,1)S(1)} %fusion.6), kind=kOutput, calls=%fused_computation.1 | convolution fusion | flops 2456862720 | bytes 10575872 | tf_op jit(solution)/shard_map/grd,de->gre/dot_general | solution.py:293
  25.9 5.1 %shard_map.118 = bf16[1,512,1280]{2,1,0:T(8,128)(2,1)} custom-call(f32[1,520,2304]{2,1,0:T(8,128)} %convolution_bitcast_fusion.1.src_ref.halo_ref, f32[1,520,2304]{2,1,0:T(8,128)} %convolution_bitcast_fusion.1.src_ref.halo_ref, f32[4,1280]{1,0:T(4,128)} %w_ref.3, f32[1,1280]{1,0:T(1,128)} %reshape.984.b_ref), custom_call_target="tpu_custom_call" | custom-call | tf_op jit(solution)/shard_map/pallas_call | solution.py:194
  31.1 5.1 %shard_map.119 = f32[2,16,64,128]{3,2,1,0:T(8,128)} custom-call(bf16[2,256,1280]{2,1,0:T(8,128)(2,1)} %bitcast.227, f32[2,256,16]{2,1,0:T(8,128)} %copy.46.to_end_ref), custom_call_target="tpu_custom_call" | custom-call | tf_op jit(solution)/shard_map/pallas_call | solution.py:132
  36.2 1.3 fusion.23
  38.6 2.5 %fusion.9 = bf16[520,1024]{1,0:T(8,128)(2,1)S(1)} fusion(bf16[1,5,1024]{2,1,0:T(8,128)(2,1)S(1)} %broadcast_in_dim.12, bf16[1,3,1024]{2,1,0:T(4,128)(2,1)S(1)} %collective-permute-done.1, bf16[1,512,1024]{2,1,0:T(8,128)(2,1)} %copy-done.10), kind=kOutput, calls=%fused_computation.23 | convolution fusion | flops 1096343552 | bytes 2129920 | tf_op jit(solution)/shard_map/...d,de->...e/dot_general | solution.py:28
  43.2 1.1 reduce-window.16
  46.1 7.5 %convolution_bitcast_fusion.src_ref.halo_ref = f32[1,520,2304]{2,1,0:T(8,128)} fusion(bf16[520,1024]{1,0:T(8,128)(2,1)} %copy-done.33, bf16[1024,2304]{1,0:T(8,128)(2,1)} %param.27), kind=kOutput, calls=%fused_computation | convolution fusion | flops 2453667840 | bytes 10575872 | tf_op jit(solution)/shard_map/grd,de->gre/dot_general | solution.py:301
  56.8 2.1 %collective-permute-start.5 = (f32[1,1032,128]{2,1,0:T(8,128)}, f32[1,1032,128]{2,1,0:T(8,128)}, u32[]{:S(2)}, u32[]{:S(2)}) collective-permute-start(f32[1,1032,128]{2,1,0:T(8,128)} %select_maximum_fusion.2), channel_id=1, source_target_pairs={{0,2},{2,4},{4,6},{6,8},{8,10},{10,12},{12,14},{1,3},{3,5},{5,7},{... | collective-permute-start | bytes 1585160 | tf_op jit(solution)/shard_map/ppermute | solution.py:48
  58.9 5.1 %shard_map.120 = bf16[1,512,1280]{2,1,0:T(8,128)(2,1)} custom-call(f32[1,520,2304]{2,1,0:T(8,128)} %convolution_bitcast_fusion.src_ref.halo_ref, f32[1,520,2304]{2,1,0:T(8,128)} %convolution_bitcast_fusion.src_ref.halo_ref, f32[4,1280]{1,0:T(4,128)} %w_ref.3, f32[1,1280]{1,0:T(1,128)} %reshape.984.b_ref), custom_call_target="tpu_custom_call" | custom-call | tf_op jit(solution)/shard_map/pallas_call | solution.py:194
  64.9 5.1 %shard_map.122 = f32[2,16,64,128]{3,2,1,0:T(8,128)} custom-call(bf16[2,256,1280]{2,1,0:T(8,128)(2,1)} %bitcast.229, f32[2,256,16]{2,1,0:T(8,128)} %multiply_bitcast_fusion.to_end_ref), custom_call_target="tpu_custom_call" | custom-call | tf_op jit(solution)/shard_map/pallas_call | solution.py:132
  70.0 2.1 %fusion.47 = (f32[1,1,16,64,128]{4,3,2,1,0:T(8,128)S(1)}, f32[1,1,16,64,128]{4,3,2,1,0:T(8,128)}, f32[1,1,16,64,128]{4,3,2,1,0:T(8,128)S(1)}) fusion(f32[1,2,16,64,128]{4,3,2,1,0:T(8,128)} %bitcast.246, f32[16]{0:T(128)S(1)} %bitcast_multiply_fusion.7), kind=kLoop, calls=%fused_computation.131 | loop fusion | flops 131072 | bytes 2621504 | tf_op jit(solution)/shard_map/slice | solution.py:221
  74.1 4.8 %collective-permute-start.2 = (f32[1,1032,128]{2,1,0:T(8,128)}, f32[1,1032,128]{2,1,0:T(8,128)}, u32[]{:S(2)}, u32[]{:S(2)}) collective-permute-start(f32[1,1032,128]{2,1,0:T(8,128)} %select_maximum_fusion.5), channel_id=1, source_target_pairs={{2,0},{4,2},{6,4},{8,6},{10,8},{12,10},{14,12},{3,1},{5,3},{7,5},{... | collective-permute-start | bytes 1585160 | tf_op jit(solution)/shard_map/ppermute | solution.py:48
  78.9 5.5 %shard_map.123 = f32[2,256,1024]{2,1,0:T(8,128)} custom-call(bf16[2,256,1280]{2,1,0:T(8,128)(2,1)} %bitcast.228, f32[2,256,16]{2,1,0:T(8,128)} %copy.56.cum_ref, f32[2,16,256]{2,1,0:T(8,128)} %bitcast.256, f32[2,16,256]{2,1,0:T(8,128)} %bitcast.261), custom_call_target="tpu_custom_call" | custom-call | tf_op jit(solution)/shard_map/pallas_call | solution.py:139
  84.5 5.5 %shard_map.121 = f32[2,256,1024]{2,1,0:T(8,128)} custom-call(bf16[2,256,1280]{2,1,0:T(8,128)(2,1)} %bitcast.230, f32[2,256,16]{2,1,0:T(8,128)} %bitcast.240, f32[2,16,256]{2,1,0:T(8,128)} %copy.52.cum_t_ref, f32[2,16,256]{2,1,0:T(8,128)} %bitcast.262), custom_call_target="tpu_custom_call" | custom-call | tf_op jit(solution)/shard_map/pallas_call | solution.py:139
  91.7 1.1 slice.296
  94.6 1.3 collective-permute-start.6
  96.8 1.3 multiply_add_fusion.5
  98.2 4.6 %collective-permute-start.3 = (f32[1,1032,128]{2,1,0:T(8,128)S(1)}, f32[1,1032,128]{2,1,0:T(8,128)S(1)}, u32[]{:S(2)}, u32[]{:S(2)}) collective-permute-start(f32[1,1032,128]{2,1,0:T(8,128)S(1)} %select_maximum_fusion.4), channel_id=1, source_target_pairs={{4,0},{6,2},{8,4},{10,6},{12,8},{14,10},{5,1},{7,3},{9,5},{11,7},{... | collective-permute-start | bytes 1585160 | tf_op jit(solution)/shard_map/ppermute | solution.py:48
  102.8 6.6 %collective-permute-done.6 = f32[1,1032,128]{2,1,0:T(8,128)} collective-permute-done((f32[1,1032,128]{2,1,0:T(8,128)}, f32[1,1032,128]{2,1,0:T(8,128)}, u32[]{:S(2)}, u32[]{:S(2)}) %collective-permute-start.6) | collective-permute-done | bytes 528416 | tf_op jit(solution)/shard_map/ppermute | solution.py:48
  111.3 1.3 collective-permute-start.7
  112.9 5.9 %collective-permute-start.4 = (f32[1,1032,128]{2,1,0:T(8,128)S(1)}, f32[1,1032,128]{2,1,0:T(8,128)S(1)}, u32[]{:S(2)}, u32[]{:S(2)}) collective-permute-start(f32[1,1032,128]{2,1,0:T(8,128)S(1)} %select_maximum_fusion.3), channel_id=1, source_target_pairs={{8,0},{10,2},{12,4},{14,6},{9,1},{11,3},{13,5},{15,7},{24,16},{26,... | collective-permute-start | bytes 1585160 | tf_op jit(solution)/shard_map/ppermute | solution.py:48
  119.5 17.6 %collective-permute-done.7 = f32[1,1032,128]{2,1,0:T(8,128)S(1)} collective-permute-done((f32[1,1032,128]{2,1,0:T(8,128)S(1)}, f32[1,1032,128]{2,1,0:T(8,128)S(1)}, u32[]{:S(2)}, u32[]{:S(2)}) %collective-permute-start.7) | collective-permute-done | bytes 528416 | tf_op jit(solution)/shard_map/ppermute | solution.py:48
  139.3 3.5 %fusion.4 = f32[1,512,1024]{2,1,0:T(8,128)S(1)} fusion(f32[2,256,1024]{2,1,0:T(8,128)S(1)} %fusion.52, f32[2,256,1024]{2,1,0:T(8,128)S(1)} %copy-done.13, f32[1,520,2304]{2,1,0:T(8,128)} %convolution_bitcast_fusion.1.src_ref.halo_ref, f32[512,16]{0,1:T(8,128)S(1)} %bitcast.265, bf16[1,512,1280]{2,1,0:T(8,128)(2,1)S(1)} %copy-done.1, f32[1024]{0:T(1024)S(1)} %mul.502, ...), kind=kOutput, calls=%fused_computation.10 | convolution fusion | flops 105938944 | bytes 9483264 | tf_op jit(solution)/shard_map/grh,hk->grk/dot_general | solution.py:244
  143.5 2.6 %convolution_bitcast_fusion.2.add_ref = f32[1,512,1024]{2,1,0:T(8,128)} fusion(bf16[1024,1024]{1,0:T(8,128)(2,1)S(1)} %copy-done, f32[1,512,1024]{2,1,0:T(8,128)S(1)} %fusion.4, f32[1024]{0:T(1024)S(1)} %copy-done.23, f32[512]{0:T(512)S(1)} %add_rsqrt_fusion.1), kind=kOutput, calls=%fused_computation.22 | convolution fusion | flops 1075314688 | bytes 6297600 | tf_op jit(solution)/shard_map/grk,kd->grd/dot_general | solution.py:308
  149.2 3.5 %fusion.2 = f32[1,512,1024]{2,1,0:T(8,128)S(1)} fusion(f32[2,256,1024]{2,1,0:T(8,128)S(1)} %fusion.53, f32[2,256,1024]{2,1,0:T(8,128)S(1)} %copy-done.12, f32[1,520,2304]{2,1,0:T(8,128)} %convolution_bitcast_fusion.src_ref.halo_ref, f32[512,16]{1,0:T(8,128)S(1)} %bitcast.260, bf16[1,512,1280]{2,1,0:T(8,128)(2,1)S(1)} %copy-done.2, f32[1024]{0:T(1024)S(1)} %mul.502, ...), kind=kOutput, calls=%fused_computation.6 | convolution fusion | flops 105938944 | bytes 9483264 | tf_op jit(solution)/shard_map/grh,hk->grk/dot_general | solution.py:244
  152.9 1.3 multiply_convert_fusion.a_ref
  154.2 5.1 %shard_map.124 = bf16[1,512,1024]{2,1,0:T(8,128)(2,1)} custom-call(bf16[1,512,1024]{2,1,0:T(8,128)(2,1)} %multiply_convert_fusion.a_ref, bf16[1024,1024]{1,0:T(8,128)(2,1)} %convert_bitcast_fusion.w_ref, f32[1,512,1024]{2,1,0:T(8,128)} %convolution_bitcast_fusion.2.add_ref), custom_call_target="tpu_custom_call" | custom-call | tf_op jit(solution)/shard_map/pallas_call | solution.py:265
  (161 shorter events, 30.4 us)
Async XLA Ops:
  0.0 10.8 %copy-start = (bf16[1024,1024]{1,0:T(8,128)(2,1)S(1)}, bf16[1024,1024]{1,0:T(8,128)(2,1)}, u32[]{:S(2)}) copy-start(bf16[1024,1024]{1,0:T(8,128)(2,1)} %param.35) | copy-start | bytes 6291460
  0.0 8.4 %copy-start.32 = (f32[16]{0:T(128)S(1)}, f32[16]{0:T(128)}, u32[]{:S(2)}) copy-start(f32[16]{0:T(128)} %param.32) | copy-start | bytes 196
  0.0 8.4 %copy-start.29 = (f32[16]{0:T(128)S(1)}, f32[16]{0:T(128)}, u32[]{:S(2)}) copy-start(f32[16]{0:T(128)} %param.31) | copy-start | bytes 196
  0.0 8.4 %copy-start.20 = (bf16[1024,16]{0,1:T(8,128)(2,1)S(1)}, bf16[1024,16]{0,1:T(8,128)(2,1)}, u32[]{:S(2)}) copy-start(bf16[1024,16]{0,1:T(8,128)(2,1)} %param.28) | copy-start | bytes 98308
  1.9 16.8 %copy-start.10 = (bf16[1,512,1024]{2,1,0:T(8,128)(2,1)}, bf16[1,512,1024]{2,1,0:T(8,128)(2,1)S(1)}, u32[]{:S(2)}) copy-start(bf16[1,512,1024]{2,1,0:T(8,128)(2,1)S(1)} %fusion.6) | copy-start | bytes 3145732
  1.9 36.7 %collective-permute-start.1 = (bf16[1,3,1024]{2,1,0:T(4,128)(2,1)S(1)}, bf16[1,3,1024]{2,1,0:T(4,128)(2,1)S(1)}, u32[]{:S(2)}, u32[]{:S(2)}) collective-permute-start(bf16[1,3,1024]{2,1,0:T(4,128)(2,1)S(1)} %get-tuple-element.103), channel_id=1, source_target_pairs={{2,0},{4,2},{6,4},{8,6},{10,8},{12,10},{14,12},{3,1},{5,3},{7,5},{... | collective-permute-start | bytes 18440 | tf_op jit(solution)/shard_map/ppermute | solution.py:289
  5.2 13.5 %collective-permute-start = (bf16[1,3,1024]{2,1,0:T(4,128)(2,1)S(1)}, bf16[1,3,1024]{2,1,0:T(4,128)(2,1)S(1)}, u32[]{:S(2)}, u32[]{:S(2)}) collective-permute-start(bf16[1,3,1024]{2,1,0:T(4,128)(2,1)S(1)} %get-tuple-element.104), channel_id=1, source_target_pairs={{0,2},{2,4},{4,6},{6,8},{8,10},{10,12},{12,14},{1,3},{3,5},{5,7},{... | collective-permute-start | bytes 18440 | tf_op jit(solution)/shard_map/ppermute | solution.py:288
  10.5 7.3 %copy-start.16 = (f32[1,2,16,256]{3,2,1,0:T(8,128)}, f32[1,2,16,256]{3,2,1,0:T(8,128)S(1)}, u32[]{:S(2)}) copy-start(f32[1,2,16,256]{3,2,1,0:T(8,128)S(1)} %get-tuple-element.94) | copy-start | bytes 98308
  10.8 4.2 %copy-start.22 = (f32[1280]{0:T(1024)S(1)}, f32[1280]{0:T(1024)}, u32[]{:S(2)}) copy-start(f32[1280]{0:T(1024)} %param.30) | copy-start | bytes 15364
  10.8 4.8 %copy-start.30 = (f32[16]{0:T(128)S(1)}, f32[16]{0:T(128)}, u32[]{:S(2)}) copy-start(f32[16]{0:T(128)} %param.33) | copy-start | bytes 196
  37.5 18.4 %copy-start.4 = (f32[1,16,64,128]{3,2,1,0:T(8,128)}, f32[1,16,64,128]{3,2,1,0:T(8,128)S(1)}, u32[]{:S(2)}) copy-start(f32[1,16,64,128]{3,2,1,0:T(8,128)S(1)} %fusion.23) | copy-start | bytes 1572868
  45.5 9.8 %copy-start.11 = (f32[1,2,256,16]{3,2,1,0:T(8,128)}, f32[1,2,256,16]{3,2,1,0:T(8,128)S(1)}, u32[]{:S(2)}) copy-start(f32[1,2,256,16]{3,2,1,0:T(8,128)S(1)} %get-tuple-element.92) | copy-start | bytes 98308
  46.1 26.4 %copy-start.26 = (f32[1,1,16]{2,1,0:T(1,128)}, f32[1,1,16]{2,1,0:T(1,128)S(1)}, u32[]{:S(2)}) copy-start(f32[1,1,16]{2,1,0:T(1,128)S(1)} %get-tuple-element.112) | copy-start | bytes 196
  46.1 7.5 %copy-start.19 = (f32[512,16]{0,1:T(8,128)S(1)}, f32[512,16]{0,1:T(8,128)}, u32[]{:S(2)}) copy-start(f32[512,16]{0,1:T(8,128)} %copy-done.18) | copy-start | bytes 98308
  56.8 34.2 %collective-permute-start.5 = (f32[1,1032,128]{2,1,0:T(8,128)}, f32[1,1032,128]{2,1,0:T(8,128)}, u32[]{:S(2)}, u32[]{:S(2)}) collective-permute-start(f32[1,1032,128]{2,1,0:T(8,128)} %select_maximum_fusion.2), channel_id=1, source_target_pairs={{0,2},{2,4},{4,6},{6,8},{8,10},{10,12},{12,14},{1,3},{3,5},{5,7},{... | collective-permute-start | bytes 1585160 | tf_op jit(solution)/shard_map/ppermute | solution.py:48
  74.1 21.7 %collective-permute-start.2 = (f32[1,1032,128]{2,1,0:T(8,128)}, f32[1,1032,128]{2,1,0:T(8,128)}, u32[]{:S(2)}, u32[]{:S(2)}) collective-permute-start(f32[1,1032,128]{2,1,0:T(8,128)} %select_maximum_fusion.5), channel_id=1, source_target_pairs={{2,0},{4,2},{6,4},{8,6},{10,8},{12,10},{14,12},{3,1},{5,3},{7,5},{... | collective-permute-start | bytes 1585160 | tf_op jit(solution)/shard_map/ppermute | solution.py:48
  84.5 5.6 %copy-start.31 = (f32[1,1,16]{2,1,0:T(1,128)S(1)}, f32[1,1,16]{2,1,0:T(1,128)}, u32[]{:S(2)}) copy-start(f32[1,1,16]{2,1,0:T(1,128)} %get-tuple-element.111) | copy-start | bytes 196
  84.5 5.6 %copy-start.3 = (f32[2,16,64,128]{3,2,1,0:T(8,128)S(1)}, f32[2,16,64,128]{3,2,1,0:T(8,128)}, u32[]{:S(2)}) copy-start(f32[2,16,64,128]{3,2,1,0:T(8,128)} %shard_map.119) | copy-start | bytes 3145732
  90.0 2.8 %copy-start.5 = (f32[1,16,64,128]{3,2,1,0:T(8,128)S(1)}, f32[1,16,64,128]{3,2,1,0:T(8,128)}, u32[]{:S(2)}) copy-start(f32[1,16,64,128]{3,2,1,0:T(8,128)} %copy-done.4) | copy-start | bytes 1572868
  91.0 5.6 %copy-start.27 = (f32[1,1,16]{2,1,0:T(1,128)S(1)}, f32[1,1,16]{2,1,0:T(1,128)}, u32[]{:S(2)}) copy-start(f32[1,1,16]{2,1,0:T(1,128)} %copy-done.26) | copy-start | bytes 196
  91.0 5.9 %copy-start.7 = (f32[1,1024,128]{2,1,0:T(8,128)S(1)}, f32[1,1024,128]{2,1,0:T(8,128)}, u32[]{:S(2)}) copy-start(f32[1,1024,128]{2,1,0:T(8,128)} %copy-done.6) | copy-start | bytes 1572868
  94.6 14.8 %collective-permute-start.6 = (f32[1,1032,128]{2,1,0:T(8,128)}, f32[1,1032,128]{2,1,0:T(8,128)}, u32[]{:S(2)}, u32[]{:S(2)}) collective-permute-start(f32[1,1032,128]{2,1,0:T(8,128)} %select_maximum_fusion.1), channel_id=1, source_target_pairs={{0,4},{2,6},{4,8},{6,10},{8,12},{10,14},{1,5},{3,7},{5,9},{7,11},{... | collective-permute-start | bytes 1585160 | tf_op jit(solution)/shard_map/ppermute | solution.py:48
  96.8 14.3 %copy-start.9 = (f32[1,16,64,128]{3,2,1,0:T(8,128)S(1)}, f32[1,16,64,128]{3,2,1,0:T(8,128)}, u32[]{:S(2)}) copy-start(f32[1,16,64,128]{3,2,1,0:T(8,128)} %copy-done.8) | copy-start | bytes 1572868
  98.2 14.4 %collective-permute-start.3 = (f32[1,1032,128]{2,1,0:T(8,128)S(1)}, f32[1,1032,128]{2,1,0:T(8,128)S(1)}, u32[]{:S(2)}, u32[]{:S(2)}) collective-permute-start(f32[1,1032,128]{2,1,0:T(8,128)S(1)} %select_maximum_fusion.4), channel_id=1, source_target_pairs={{4,0},{6,2},{8,4},{10,6},{12,8},{14,10},{5,1},{7,3},{9,5},{11,7},{... | collective-permute-start | bytes 1585160 | tf_op jit(solution)/shard_map/ppermute | solution.py:48
  111.3 25.8 %collective-permute-start.7 = (f32[1,1032,128]{2,1,0:T(8,128)S(1)}, f32[1,1032,128]{2,1,0:T(8,128)S(1)}, u32[]{:S(2)}, u32[]{:S(2)}) collective-permute-start(f32[1,1032,128]{2,1,0:T(8,128)S(1)} %select_maximum_fusion), channel_id=1, source_target_pairs={{0,8},{2,10},{4,12},{6,14},{1,9},{3,11},{5,13},{7,15},{16,24},{18,... | collective-permute-start | bytes 1585160 | tf_op jit(solution)/shard_map/ppermute | solution.py:48
  112.9 24.5 %copy-start.15 = (f32[1,1,16,64,128]{4,3,2,1,0:T(8,128)S(1)}, f32[1,1,16,64,128]{4,3,2,1,0:T(8,128)}, u32[]{:S(2)}) copy-start(f32[1,1,16,64,128]{4,3,2,1,0:T(8,128)} %slice_add_fusion) | copy-start | bytes 1572868
  112.9 24.5 %copy-start.28 = (f32[2,16]{1,0:T(2,128)S(1)}, f32[2,16]{1,0:T(2,128)}, u32[]{:S(2)}) copy-start(f32[2,16]{1,0:T(2,128)} %pad_bitcast_fusion) | copy-start | bytes 388
  112.9 33.2 %collective-permute-start.4 = (f32[1,1032,128]{2,1,0:T(8,128)S(1)}, f32[1,1032,128]{2,1,0:T(8,128)S(1)}, u32[]{:S(2)}, u32[]{:S(2)}) collective-permute-start(f32[1,1032,128]{2,1,0:T(8,128)S(1)} %select_maximum_fusion.3), channel_id=1, source_target_pairs={{8,0},{10,2},{12,4},{14,6},{9,1},{11,3},{13,5},{15,7},{24,16},{26,... | collective-permute-start | bytes 1585160 | tf_op jit(solution)/shard_map/ppermute | solution.py:48
  137.5 1.8 %copy-start.1 = (bf16[1,512,1280]{2,1,0:T(8,128)(2,1)S(1)}, bf16[1,512,1280]{2,1,0:T(8,128)(2,1)}, u32[]{:S(2)}) copy-start(bf16[1,512,1280]{2,1,0:T(8,128)(2,1)} %shard_map.118) | copy-start | bytes 3932164
  137.5 1.8 %copy-start.21 = (f32[2,8,2,256]{3,1,2,0:T(8,128)S(1)}, f32[2,8,2,256]{3,1,2,0:T(8,128)}, u32[]{:S(2)}) copy-start(f32[2,8,2,256]{3,1,2,0:T(8,128)} %copy.66) | copy-start | bytes 98308
  147.3 1.8 %copy-start.2 = (bf16[1,512,1280]{2,1,0:T(8,128)(2,1)S(1)}, bf16[1,512,1280]{2,1,0:T(8,128)(2,1)}, u32[]{:S(2)}) copy-start(bf16[1,512,1280]{2,1,0:T(8,128)(2,1)} %shard_map.120) | copy-start | bytes 3932164
  147.4 1.8 %copy-start.17 = (f32[1,2,256,16]{3,2,1,0:T(8,128)S(1)}, f32[1,2,256,16]{3,2,1,0:T(8,128)}, u32[]{:S(2)}) copy-start(f32[1,2,256,16]{3,2,1,0:T(8,128)} %get-tuple-element.91) | copy-start | bytes 98308
  (10 other events, 11.7 us)

commit v13 on v11

--- a/solution.py
+++ b/solution.py
@@ -101,18 +101,19 @@
         )
 
 
-def state_kernel(xbc_ref, to_end_ref, state_ref):
+def state_kernel(xbc_ref, x_t_ref, to_end_ref, state_ref):
     inner = H * P_SIZE
     b_wide = xbc_ref[:, inner : inner + N].astype(jnp.float32)
     for h in range(H):
         state_weights = (b_wide * to_end_ref[:, h : h + 1]).astype(jnp.bfloat16)
-        x_h = xbc_ref[:, h * P_SIZE : (h + 1) * P_SIZE]
-        state_ref[h] = lax.dot_general(
-            x_h, state_weights, (((0,), (0,)), ((), ())), preferred_element_type=jnp.float32
+        state_ref[h] = jnp.dot(
+            x_t_ref[h * P_SIZE : (h + 1) * P_SIZE, :],
+            state_weights,
+            preferred_element_type=jnp.float32,
         )
 
 
-def block_terms(activated, step_size, rates, reverse):
+def block_terms(activated, activated_t, step_size, rates, reverse):
     count, rows, width = activated.shape
     spans = rows // Q
     blocks = count * spans
@@ -132,10 +133,14 @@
     state = pl.pallas_call(
         state_kernel,
         grid=(blocks,),
-        in_specs=[spec((Q, width)), spec((Q, H))],
+        in_specs=[
+            spec((Q, width)),
+            pl.BlockSpec((None, H * P_SIZE, Q), lambda i: (i // spans, 0, i % spans)),
+            spec((Q, H)),
+        ],
         out_specs=spec((H, P_SIZE, N)),
         out_shape=jax.ShapeDtypeStruct((blocks, H, P_SIZE, N), jnp.float32),
-    )(xbc, flat(to_end))
+    )(xbc, activated_t, flat(to_end))
     inside = pl.pallas_call(
         partial(inside_kernel, reverse=reverse),
         grid=(blocks,),
@@ -151,7 +156,7 @@
 CONV_LANES = 256
 
 
-def conv_kernel(src_ref, halo_ref, w_ref, b_ref, out_ref, *, reverse):
+def conv_kernel(src_ref, halo_ref, w_ref, b_ref, out_ref, out_t_ref, *, reverse):
     margin = KCONV - 1
     src = src_ref[...]
     rows = src.shape[0]
@@ -182,6 +187,7 @@
         out_ref[rows - edge :, :] = jax.nn.silu(side).astype(out_ref.dtype)
     else:
         out_ref[:edge, :] = jax.nn.silu(side).astype(out_ref.dtype)
+    out_t_ref[...] = jnp.transpose(out_ref[...].astype(jnp.float32)).astype(out_t_ref.dtype)
 
 
 def convolve(projected, rows, conv_w, conv_b, reverse):
@@ -200,17 +206,23 @@
             pl.BlockSpec((KCONV, lanes), lambda g, j: (0, j)),
             pl.BlockSpec((1, lanes), lambda g, j: (0, j)),
         ],
-        out_specs=pl.BlockSpec((None, rows, lanes), lambda g, j: (g, 0, j)),
-        out_shape=jax.ShapeDtypeStruct((count, rows, width), jnp.bfloat16),
+        out_specs=[
+            pl.BlockSpec((None, rows, lanes), lambda g, j: (g, 0, j)),
+            pl.BlockSpec((None, lanes, rows), lambda g, j: (g, j, 0)),
+        ],
+        out_shape=[
+            jax.ShapeDtypeStruct((count, rows, width), jnp.bfloat16),
+            jax.ShapeDtypeStruct((count, width, rows), jnp.bfloat16),
+        ],
     )(projected, projected, conv_w, conv_b.reshape(1, width))
 
 
 def strand_terms(projected, step_size, conv_w, conv_b, rates, reverse):
     inner = H * P_SIZE
     count, rows, _ = step_size.shape
-    activated = convolve(projected, rows, conv_w, conv_b, reverse)
+    activated, activated_t = convolve(projected, rows, conv_w, conv_b, reverse)
     spans = rows // Q
-    inside, state, total, from_start = block_terms(activated, step_size, rates, reverse)
+    inside, state, total, from_start = block_terms(activated, activated_t, step_size, rates, reverse)
     order = list(range(spans))
     if reverse:
         order = order[::-1]

time: 159 us -> 157 us (0.987)
  Pallas kernels: 31.7 us -> 29.6 us
    pallas_call x2, Pallas kernels: 10.2 us -> 7.55 us  [block_terms(): pl.pallas_call(state_kernel, grid=(blocks,), in_specs=[spec((Q, width)),...]
  transfers between devices with their start and end apart: 8 -> 8, of which waited for: 2 -> 2; matrix products, arithmetic and copies ran while one was open for 23% -> 23% of each run, Pallas kernels for 20% -> 19%
where the time goes in v13:
time: 157 us; the launch traced here: 156 us
  matrix products  38 us (24%)
  Pallas kernels  29.6 us (19%)
  starting transfers between devices  25.5 us (16%)
  waiting for transfers between devices  24.5 us (16%)
  other arithmetic  19.2 us (12%)
  local copies, waits for them, and re-layouts  18.2 us (12%)
    ppermute x6, waiting for transfers between devices, exclusive_scans(): decay, state = unpack(lax.ppermute(pack(*ahead[k]), axis, pairs))  24.5 us
    ppermute x6, starting transfers between devices, exclusive_scans(): decay, state = unpack(lax.ppermute(pack(*ahead[k]), axis, pairs))  19.7 us
    pallas_call x2, Pallas kernels, block_terms(): pl.pallas_call(partial(inside_kernel, reverse=reverse), grid=(blocks,), i...  11.2 us
    pallas_call x2, Pallas kernels, convolve(): pl.pallas_call(partial(conv_kernel, reverse=reverse), grid=(count, width...  10.8 us
    pallas_call x2, Pallas kernels, block_terms(): pl.pallas_call(state_kernel, grid=(blocks,), in_specs=[spec((Q, width)),...  7.55 us
    dot_general x1, matrix products, on_device(): jnp.einsum('grd,de->gre', ext_r, w_in, preferred_element_type=jnp.float32)  7.5 us
    dot_general x2, matrix products, finish(): jnp.einsum('grh,hk->grk', from_start.reshape(count, rows, H), spread, pre...  7.19 us
    dot_general x1, matrix products, on_device(): jnp.einsum('grd,de->gre', ext_f, w_in, preferred_element_type=jnp.float32)  7.13 us
  transfers between devices with their start and end apart: 8, of which 2 were waited for; matrix products, arithmetic and copies ran while one was open for 23% of the time, Pallas kernels for 19%

profile of v13, /device:TPU:24, one launch (start us, length us, event | category | flops | bytes accessed | tf_op | source)
XLA Modules:
  0.0 155.6 jit_solution(9678514435907889080)
XLA Ops:
  0.0 1.9 %fusion.9 = bf16[1,512,1024]{2,1,0:T(8,128)(2,1)S(1)} fusion(bf16[1,512,1024]{2,1,0:T(8,128)(2,1)} %param.25, bf16[4,1024]{1,0:T(4,128)(2,1)} %param.26, s32[512]{0:T(512)} %bitcast.285), kind=kOutput, calls=%fused_computation.17 | convolution fusion | flops 5769216 | bytes 2107392 | tf_op jit(solution)/shard_map/gtb,bd->gtd/dot_general | solution.py:275
  2.0 3.3 %collective-permute-start.1 = (bf16[1,3,1024]{2,1,0:T(4,128)(2,1)S(1)}, bf16[1,3,1024]{2,1,0:T(4,128)(2,1)S(1)}, u32[]{:S(2)}, u32[]{:S(2)}) collective-permute-start(bf16[1,3,1024]{2,1,0:T(4,128)(2,1)S(1)} %get-tuple-element.113), channel_id=1, source_target_pairs={{2,0},{4,2},{6,4},{8,6},{10,8},{12,10},{14,12},{3,1},{5,3},{7,5},{... | collective-permute-start | bytes 18440 | tf_op jit(solution)/shard_map/ppermute | solution.py:280
  5.2 2.6 %collective-permute-start = (bf16[1,3,1024]{2,1,0:T(4,128)(2,1)S(1)}, bf16[1,3,1024]{2,1,0:T(4,128)(2,1)S(1)}, u32[]{:S(2)}, u32[]{:S(2)}) collective-permute-start(bf16[1,3,1024]{2,1,0:T(4,128)(2,1)S(1)} %get-tuple-element.114), channel_id=1, source_target_pairs={{0,2},{2,4},{4,6},{6,8},{8,10},{10,12},{12,14},{1,3},{3,5},{5,7},{... | collective-permute-start | bytes 18440 | tf_op jit(solution)/shard_map/ppermute | solution.py:279
  8.4 1.1 reduce-window.14
  13.4 7.1 %convolution_bitcast_fusion.1.src_ref.halo_ref = f32[1,520,2304]{2,1,0:T(8,128)} fusion(bf16[1024,2304]{1,0:T(8,128)(2,1)} %param.27, bf16[1,3,1024]{2,1,0:T(4,128)(2,1)S(1)} %collective-permute-done, bf16[1,5,1024]{2,1,0:T(8,128)(2,1)S(1)} %broadcast_in_dim.12, bf16[1,512,1024]{2,1,0:T(8,128)(2,1)S(1)} %fusion.9), kind=kOutput, calls=%fused_computation.1 | convolution fusion | flops 2456862720 | bytes 10575872 | tf_op jit(solution)/shard_map/grd,de->gre/dot_general | solution.py:284
  20.5 5.4 %shard_map.118 = (bf16[1,512,1280]{2,1,0:T(8,128)(2,1)}, bf16[1,1280,512]{2,1,0:T(8,128)(2,1)}) custom-call(f32[1,520,2304]{2,1,0:T(8,128)} %convolution_bitcast_fusion.1.src_ref.halo_ref, f32[1,520,2304]{2,1,0:T(8,128)} %convolution_bitcast_fusion.1.src_ref.halo_ref, f32[4,1280]{1,0:T(4,128)} %w_ref.3, f32[1,1280]{1,0:T(1,128)} %reshape.988.b_ref), custom_call_target="tpu_custom_call" | custom-call | tf_op jit(solution)/shard_map/pallas_call | solution.py:200
  25.9 3.8 %shard_map.119 = f32[2,16,64,128]{3,2,1,0:T(8,128)} custom-call(bf16[2,256,1280]{2,1,0:T(8,128)(2,1)} %bitcast.242, bf16[1,1280,512]{2,1,0:T(8,128)(2,1)} %get-tuple-element.88.x_t_ref, f32[2,256,16]{2,1,0:T(8,128)} %copy.28.to_end_ref), custom_call_target="tpu_custom_call" | custom-call | tf_op jit(solution)/shard_map/pallas_call | solution.py:133
  29.7 1.3 fusion.36
  32.1 2.5 %fusion.14 = bf16[520,1024]{1,0:T(8,128)(2,1)S(1)} fusion(bf16[1,5,1024]{2,1,0:T(8,128)(2,1)S(1)} %broadcast_in_dim.12, bf16[1,3,1024]{2,1,0:T(4,128)(2,1)S(1)} %collective-permute-done.1, bf16[1,512,1024]{2,1,0:T(8,128)(2,1)} %copy-done.10), kind=kOutput, calls=%fused_computation.27 | convolution fusion | flops 1096343552 | bytes 2129920 | tf_op jit(solution)/shard_map/...d,de->...e/dot_general | solution.py:28
  36.1 1.1 reduce-window.16
  38.1 7.5 %convolution_bitcast_fusion.src_ref.halo_ref = f32[1,520,2304]{2,1,0:T(8,128)} fusion(bf16[520,1024]{1,0:T(8,128)(2,1)} %copy-done.24, bf16[1024,2304]{1,0:T(8,128)(2,1)} %param.27), kind=kOutput, calls=%fused_computation | convolution fusion | flops 2453667840 | bytes 10575872 | tf_op jit(solution)/shard_map/grd,de->gre/dot_general | solution.py:292
  49.1 1.9 %collective-permute-start.5 = (f32[1,1032,128]{2,1,0:T(8,128)}, f32[1,1032,128]{2,1,0:T(8,128)}, u32[]{:S(2)}, u32[]{:S(2)}) collective-permute-start(f32[1,1032,128]{2,1,0:T(8,128)} %select_maximum_fusion.2), channel_id=1, source_target_pairs={{0,2},{2,4},{4,6},{6,8},{8,10},{10,12},{12,14},{1,3},{3,5},{5,7},{... | collective-permute-start | bytes 1585160 | tf_op jit(solution)/shard_map/ppermute | solution.py:48
  51.0 5.4 %shard_map.120 = (bf16[1,512,1280]{2,1,0:T(8,128)(2,1)}, bf16[1,1280,512]{2,1,0:T(8,128)(2,1)}) custom-call(f32[1,520,2304]{2,1,0:T(8,128)} %convolution_bitcast_fusion.src_ref.halo_ref, f32[1,520,2304]{2,1,0:T(8,128)} %convolution_bitcast_fusion.src_ref.halo_ref, f32[4,1280]{1,0:T(4,128)} %w_ref.3, f32[1,1280]{1,0:T(1,128)} %reshape.988.b_ref), custom_call_target="tpu_custom_call" | custom-call | tf_op jit(solution)/shard_map/pallas_call | solution.py:200
  57.4 3.8 %shard_map.121 = f32[2,16,64,128]{3,2,1,0:T(8,128)} custom-call(bf16[2,256,1280]{2,1,0:T(8,128)(2,1)} %bitcast.244, bf16[1,1280,512]{2,1,0:T(8,128)(2,1)} %get-tuple-element.92.x_t_ref, f32[2,256,16]{2,1,0:T(8,128)} %copy.34.to_end_ref), custom_call_target="tpu_custom_call" | custom-call | tf_op jit(solution)/shard_map/pallas_call | solution.py:133
  61.2 2.1 %broadcast_add_fusion = (f32[1,1,16,64,128]{4,3,2,1,0:T(8,128)}, f32[1,1,16,64,128]{4,3,2,1,0:T(8,128)S(1)}, f32[1,1,16,64,128]{4,3,2,1,0:T(8,128)S(1)}) fusion(f32[16]{0:T(128)S(1)} %bitcast_multiply_fusion.7, f32[1,2,16,64,128]{4,3,2,1,0:T(8,128)} %bitcast.254), kind=kLoop, calls=%fused_computation.71 | loop fusion | flops 131072 | bytes 2621504 | tf_op jit(solution)/shard_map/add | solution.py:34
  65.2 5.0 %collective-permute-start.2 = (f32[1,1032,128]{2,1,0:T(8,128)}, f32[1,1032,128]{2,1,0:T(8,128)}, u32[]{:S(2)}, u32[]{:S(2)}) collective-permute-start(f32[1,1032,128]{2,1,0:T(8,128)} %select_maximum_fusion.5), channel_id=1, source_target_pairs={{2,0},{4,2},{6,4},{8,6},{10,8},{12,10},{14,12},{3,1},{5,3},{7,5},{... | collective-permute-start | bytes 1585160 | tf_op jit(solution)/shard_map/ppermute | solution.py:48
  70.2 5.6 %shard_map.122 = f32[2,256,1024]{2,1,0:T(8,128)} custom-call(bf16[2,256,1280]{2,1,0:T(8,128)(2,1)} %bitcast.243, f32[2,256,16]{2,1,0:T(8,128)} %copy.36.cum_ref, f32[2,16,256]{2,1,0:T(8,128)} %bitcast.262, f32[2,16,256]{2,1,0:T(8,128)} %bitcast.268), custom_call_target="tpu_custom_call" | custom-call | tf_op jit(solution)/shard_map/pallas_call | solution.py:144
  75.8 5.5 %shard_map.123 = f32[2,256,1024]{2,1,0:T(8,128)} custom-call(bf16[2,256,1280]{2,1,0:T(8,128)(2,1)} %bitcast.245, f32[2,256,16]{2,1,0:T(8,128)} %copy.39.cum_ref, f32[2,16,256]{2,1,0:T(8,128)} %bitcast.264, f32[2,16,256]{2,1,0:T(8,128)} %bitcast.269), custom_call_target="tpu_custom_call" | custom-call | tf_op jit(solution)/shard_map/pallas_call | solution.py:144
  83.0 1.1 slice.294
  85.9 1.3 collective-permute-start.6
  88.1 1.3 fusion.65
  89.5 4.6 %collective-permute-start.3 = (f32[1,1032,128]{2,1,0:T(8,128)S(1)}, f32[1,1032,128]{2,1,0:T(8,128)S(1)}, u32[]{:S(2)}, u32[]{:S(2)}) collective-permute-start(f32[1,1032,128]{2,1,0:T(8,128)S(1)} %select_maximum_fusion.4), channel_id=1, source_target_pairs={{4,0},{6,2},{8,4},{10,6},{12,8},{14,10},{5,1},{7,3},{9,5},{11,7},{... | collective-permute-start | bytes 1585160 | tf_op jit(solution)/shard_map/ppermute | solution.py:48
  94.1 6.6 %collective-permute-done.6 = f32[1,1032,128]{2,1,0:T(8,128)} collective-permute-done((f32[1,1032,128]{2,1,0:T(8,128)}, f32[1,1032,128]{2,1,0:T(8,128)}, u32[]{:S(2)}, u32[]{:S(2)}) %collective-permute-start.6) | collective-permute-done | bytes 528416 | tf_op jit(solution)/shard_map/ppermute | solution.py:48
  102.7 1.3 collective-permute-start.7
  104.3 5.6 %collective-permute-start.4 = (f32[1,1032,128]{2,1,0:T(8,128)S(1)}, f32[1,1032,128]{2,1,0:T(8,128)S(1)}, u32[]{:S(2)}, u32[]{:S(2)}) collective-permute-start(f32[1,1032,128]{2,1,0:T(8,128)S(1)} %select_maximum_fusion.3), channel_id=1, source_target_pairs={{8,0},{10,2},{12,4},{14,6},{9,1},{11,3},{13,5},{15,7},{24,16},{26,... | collective-permute-start | bytes 1585160 | tf_op jit(solution)/shard_map/ppermute | solution.py:48
  110.6 17.8 %collective-permute-done.7 = f32[1,1032,128]{2,1,0:T(8,128)S(1)} collective-permute-done((f32[1,1032,128]{2,1,0:T(8,128)S(1)}, f32[1,1032,128]{2,1,0:T(8,128)S(1)}, u32[]{:S(2)}, u32[]{:S(2)}) %collective-permute-start.7) | collective-permute-done | bytes 528416 | tf_op jit(solution)/shard_map/ppermute | solution.py:48
  130.6 3.6 %fusion.7 = f32[1,512,1024]{2,1,0:T(8,128)S(1)} fusion(f32[2,256,1024]{2,1,0:T(8,128)S(1)} %fusion.68, f32[2,256,1024]{2,1,0:T(8,128)S(1)} %copy-done.12, f32[1,520,2304]{2,1,0:T(8,128)} %convolution_bitcast_fusion.1.src_ref.halo_ref, f32[512,16]{0,1:T(8,128)S(1)} %bitcast.273, bf16[1,512,1280]{2,1,0:T(8,128)(2,1)S(1)} %copy-done.2, f32[1024]{0:T(1024)S(1)} %mul.500, ...), kind=kOutput, calls=%fused_computation.13 | convolution fusion | flops 105938944 | bytes 9483264 | tf_op jit(solution)/shard_map/grh,hk->grk/dot_general | solution.py:256
  134.9 2.7 %convolution_bitcast_fusion.2 = f32[1,512,1024]{2,1,0:T(8,128)} fusion(bf16[1024,1024]{1,0:T(8,128)(2,1)S(1)} %copy-done, f32[1,512,1024]{2,1,0:T(8,128)S(1)} %fusion.7, f32[1024]{0:T(1024)S(1)} %copy-done.22, f32[512]{0:T(512)S(1)} %add_rsqrt_fusion.1), kind=kOutput, calls=%fused_computation.26 | convolution fusion | flops 1075314688 | bytes 6297600 | tf_op jit(solution)/shard_map/grk,kd->grd/dot_general | solution.py:299
  140.6 3.6 %fusion.5 = f32[1,512,1024]{2,1,0:T(8,128)S(1)} fusion(f32[2,256,1024]{2,1,0:T(8,128)S(1)} %fusion.69, f32[2,256,1024]{2,1,0:T(8,128)S(1)} %copy-done.11, f32[1,520,2304]{2,1,0:T(8,128)} %convolution_bitcast_fusion.src_ref.halo_ref, f32[512,16]{0,1:T(8,128)S(1)} %bitcast.274, bf16[1,512,1280]{2,1,0:T(8,128)(2,1)S(1)} %copy-done.3, f32[1024]{0:T(1024)S(1)} %mul.500, ...), kind=kOutput, calls=%fused_computation.9 | convolution fusion | flops 105938944 | bytes 9483264 | tf_op jit(solution)/shard_map/grh,hk->grk/dot_general | solution.py:256
  144.2 1.3 copy-done.13
  145.8 6.4 %fusion.10 = f32[512,1024]{1,0:T(8,128)} fusion(bf16[1024,1024]{1,0:T(8,128)(2,1)S(1)} %copy-done, f32[1,512,1024]{2,1,0:T(8,128)} %copy-done.13, f32[512]{0:T(512)S(1)} %add_rsqrt_fusion, f32[1024]{0:T(1024)S(1)} %copy-done.22), kind=kOutput, calls=%fused_computation.18 | convolution fusion | flops 3226992640 | bytes 6297600 | tf_op jit(solution)/shard_map/grk,kd->grd/dot_general | solution.py:304
  152.1 3.5 %fusion.4 = bf16[1,512,1024]{2,1,0:T(8,128)(2,1)} fusion(f32[1,512,1024]{2,1,0:T(8,128)} %convolution_bitcast_fusion.2, f32[512,1024]{1,0:T(8,128)} %fusion.10), kind=kLoop, calls=%fused_computation.7 | loop fusion | flops 1048576 | bytes 5242880 | tf_op jit(solution)/shard_map/convert_element_type | solution.py:307
  (146 shorter events, 27.3 us)
Async XLA Ops:
  0.0 134.5 %copy-start = (bf16[1024,1024]{1,0:T(8,128)(2,1)S(1)}, bf16[1024,1024]{1,0:T(8,128)(2,1)}, u32[]{:S(2)}) copy-start(bf16[1024,1024]{1,0:T(8,128)(2,1)} %param.35) | copy-start | bytes 6291460
  0.0 7.8 %copy-start.23 = (f32[16]{0:T(128)S(1)}, f32[16]{0:T(128)}, u32[]{:S(2)}) copy-start(f32[16]{0:T(128)} %param.32) | copy-start | bytes 196
  0.0 7.9 %copy-start.20 = (f32[16]{0:T(128)S(1)}, f32[16]{0:T(128)}, u32[]{:S(2)}) copy-start(f32[16]{0:T(128)} %param.31) | copy-start | bytes 196
  0.0 7.9 %copy-start.18 = (bf16[1024,16]{0,1:T(8,128)(2,1)S(1)}, bf16[1024,16]{0,1:T(8,128)(2,1)}, u32[]{:S(2)}) copy-start(bf16[1024,16]{0,1:T(8,128)(2,1)} %param.28) | copy-start | bytes 98308
  0.0 10.3 %copy-start.19 = (f32[1280]{0:T(1024)S(1)}, f32[1280]{0:T(1024)}, u32[]{:S(2)}) copy-start(f32[1280]{0:T(1024)} %param.30) | copy-start | bytes 15364
  0.0 10.9 %copy-start.21 = (f32[16]{0:T(128)S(1)}, f32[16]{0:T(128)}, u32[]{:S(2)}) copy-start(f32[16]{0:T(128)} %param.33) | copy-start | bytes 196
  1.9 18.6 %copy-start.10 = (bf16[1,512,1024]{2,1,0:T(8,128)(2,1)}, bf16[1,512,1024]{2,1,0:T(8,128)(2,1)S(1)}, u32[]{:S(2)}) copy-start(bf16[1,512,1024]{2,1,0:T(8,128)(2,1)S(1)} %fusion.9) | copy-start | bytes 3145732
  2.0 30.2 %collective-permute-start.1 = (bf16[1,3,1024]{2,1,0:T(4,128)(2,1)S(1)}, bf16[1,3,1024]{2,1,0:T(4,128)(2,1)S(1)}, u32[]{:S(2)}, u32[]{:S(2)}) collective-permute-start(bf16[1,3,1024]{2,1,0:T(4,128)(2,1)S(1)} %get-tuple-element.113), channel_id=1, source_target_pairs={{2,0},{4,2},{6,4},{8,6},{10,8},{12,10},{14,12},{3,1},{5,3},{7,5},{... | collective-permute-start | bytes 18440 | tf_op jit(solution)/shard_map/ppermute | solution.py:280
  5.2 8.1 %collective-permute-start = (bf16[1,3,1024]{2,1,0:T(4,128)(2,1)S(1)}, bf16[1,3,1024]{2,1,0:T(4,128)(2,1)S(1)}, u32[]{:S(2)}, u32[]{:S(2)}) collective-permute-start(bf16[1,3,1024]{2,1,0:T(4,128)(2,1)S(1)} %get-tuple-element.114), channel_id=1, source_target_pairs={{0,2},{2,4},{4,6},{6,8},{8,10},{10,12},{12,14},{1,3},{3,5},{5,7},{... | collective-permute-start | bytes 18440 | tf_op jit(solution)/shard_map/ppermute | solution.py:279
  10.0 10.5 %copy-start.16 = (f32[1,2,16,256]{3,2,1,0:T(8,128)}, f32[1,2,16,256]{3,2,1,0:T(8,128)S(1)}, u32[]{:S(2)}) copy-start(f32[1,2,16,256]{3,2,1,0:T(8,128)S(1)} %get-tuple-element.104) | copy-start | bytes 98308
  31.1 17.2 %copy-start.4 = (f32[1,16,64,128]{3,2,1,0:T(8,128)}, f32[1,16,64,128]{3,2,1,0:T(8,128)S(1)}, u32[]{:S(2)}) copy-start(f32[1,16,64,128]{3,2,1,0:T(8,128)S(1)} %fusion.36) | copy-start | bytes 1572868
  34.6 1.0 copy-start.24
  38.0 9.5 %copy-start.17 = (f32[1,2,256,16]{2,3,1,0:T(8,128)}, f32[1,2,256,16]{2,3,1,0:T(8,128)S(1)}, u32[]{:S(2)}) copy-start(f32[1,2,256,16]{2,3,1,0:T(8,128)S(1)} %get-tuple-element.102) | copy-start | bytes 98308
  49.1 33.2 %collective-permute-start.5 = (f32[1,1032,128]{2,1,0:T(8,128)}, f32[1,1032,128]{2,1,0:T(8,128)}, u32[]{:S(2)}, u32[]{:S(2)}) collective-permute-start(f32[1,1032,128]{2,1,0:T(8,128)} %select_maximum_fusion.2), channel_id=1, source_target_pairs={{0,2},{2,4},{4,6},{6,8},{8,10},{10,12},{12,14},{1,3},{3,5},{5,7},{... | collective-permute-start | bytes 1585160 | tf_op jit(solution)/shard_map/ppermute | solution.py:48
  63.6 0.8 copy-start.6
  65.2 21.9 %collective-permute-start.2 = (f32[1,1032,128]{2,1,0:T(8,128)}, f32[1,1032,128]{2,1,0:T(8,128)}, u32[]{:S(2)}, u32[]{:S(2)}) collective-permute-start(f32[1,1032,128]{2,1,0:T(8,128)} %select_maximum_fusion.5), channel_id=1, source_target_pairs={{2,0},{4,2},{6,4},{8,6},{10,8},{12,10},{14,12},{3,1},{5,3},{7,5},{... | collective-permute-start | bytes 1585160 | tf_op jit(solution)/shard_map/ppermute | solution.py:48
  75.8 5.6 %copy-start.1 = (f32[2,16,64,128]{3,2,1,0:T(8,128)S(1)}, f32[2,16,64,128]{3,2,1,0:T(8,128)}, u32[]{:S(2)}) copy-start(f32[2,16,64,128]{3,2,1,0:T(8,128)} %shard_map.119) | copy-start | bytes 3145732
  81.4 2.7 %copy-start.5 = (f32[1,16,64,128]{3,2,1,0:T(8,128)S(1)}, f32[1,16,64,128]{3,2,1,0:T(8,128)}, u32[]{:S(2)}) copy-start(f32[1,16,64,128]{3,2,1,0:T(8,128)} %copy-done.4) | copy-start | bytes 1572868
  82.3 5.9 %copy-start.7 = (f32[1,1024,128]{2,1,0:T(8,128)S(1)}, f32[1,1024,128]{2,1,0:T(8,128)}, u32[]{:S(2)}) copy-start(f32[1,1024,128]{2,1,0:T(8,128)} %copy-done.6) | copy-start | bytes 1572868
  84.2 0.8 copy-start.8
  85.9 14.8 %collective-permute-start.6 = (f32[1,1032,128]{2,1,0:T(8,128)}, f32[1,1032,128]{2,1,0:T(8,128)}, u32[]{:S(2)}, u32[]{:S(2)}) collective-permute-start(f32[1,1032,128]{2,1,0:T(8,128)} %select_maximum_fusion.1), channel_id=1, source_target_pairs={{0,4},{2,6},{4,8},{6,10},{8,12},{10,14},{1,5},{3,7},{5,9},{7,11},{... | collective-permute-start | bytes 1585160 | tf_op jit(solution)/shard_map/ppermute | solution.py:48
  88.1 14.3 %copy-start.9 = (f32[1,16,64,128]{3,2,1,0:T(8,128)S(1)}, f32[1,16,64,128]{3,2,1,0:T(8,128)}, u32[]{:S(2)}) copy-start(f32[1,16,64,128]{3,2,1,0:T(8,128)} %copy-done.8) | copy-start | bytes 1572868
  89.5 14.5 %collective-permute-start.3 = (f32[1,1032,128]{2,1,0:T(8,128)S(1)}, f32[1,1032,128]{2,1,0:T(8,128)S(1)}, u32[]{:S(2)}, u32[]{:S(2)}) collective-permute-start(f32[1,1032,128]{2,1,0:T(8,128)S(1)} %select_maximum_fusion.4), channel_id=1, source_target_pairs={{4,0},{6,2},{8,4},{10,6},{12,8},{14,10},{5,1},{7,3},{9,5},{11,7},{... | collective-permute-start | bytes 1585160 | tf_op jit(solution)/shard_map/ppermute | solution.py:48
  102.7 25.8 %collective-permute-start.7 = (f32[1,1032,128]{2,1,0:T(8,128)S(1)}, f32[1,1032,128]{2,1,0:T(8,128)S(1)}, u32[]{:S(2)}, u32[]{:S(2)}) collective-permute-start(f32[1,1032,128]{2,1,0:T(8,128)S(1)} %select_maximum_fusion), channel_id=1, source_target_pairs={{0,8},{2,10},{4,12},{6,14},{1,9},{3,11},{5,13},{7,15},{16,24},{18,... | collective-permute-start | bytes 1585160 | tf_op jit(solution)/shard_map/ppermute | solution.py:48
  104.2 24.4 %copy-start.15 = (f32[1,1,16,64,128]{4,3,2,1,0:T(8,128)S(1)}, f32[1,1,16,64,128]{4,3,2,1,0:T(8,128)}, u32[]{:S(2)}) copy-start(f32[1,1,16,64,128]{4,3,2,1,0:T(8,128)} %slice_add_fusion) | copy-start | bytes 1572868
  104.3 33.3 %collective-permute-start.4 = (f32[1,1032,128]{2,1,0:T(8,128)S(1)}, f32[1,1032,128]{2,1,0:T(8,128)S(1)}, u32[]{:S(2)}, u32[]{:S(2)}) collective-permute-start(f32[1,1032,128]{2,1,0:T(8,128)S(1)} %select_maximum_fusion.3), channel_id=1, source_target_pairs={{8,0},{10,2},{12,4},{14,6},{9,1},{11,3},{13,5},{15,7},{24,16},{26,... | collective-permute-start | bytes 1585160 | tf_op jit(solution)/shard_map/ppermute | solution.py:48
  128.7 1.6 %copy-start.12 = (f32[2,256,1024]{2,1,0:T(8,128)S(1)}, f32[2,256,1024]{2,1,0:T(8,128)}, u32[]{:S(2)}) copy-start(f32[2,256,1024]{2,1,0:T(8,128)} %shard_map.122) | copy-start | bytes 6291460
  128.8 1.8 %copy-start.2 = (bf16[1,512,1280]{2,1,0:T(8,128)(2,1)S(1)}, bf16[1,512,1280]{2,1,0:T(8,128)(2,1)}, u32[]{:S(2)}) copy-start(bf16[1,512,1280]{2,1,0:T(8,128)(2,1)} %get-tuple-element.87) | copy-start | bytes 3932164
  137.6 1.0 copy-start.14
  138.6 1.6 %copy-start.11 = (f32[2,256,1024]{2,1,0:T(8,128)S(1)}, f32[2,256,1024]{2,1,0:T(8,128)}, u32[]{:S(2)}) copy-start(f32[2,256,1024]{2,1,0:T(8,128)} %shard_map.123) | copy-start | bytes 6291460
  138.8 1.8 %copy-start.3 = (bf16[1,512,1280]{2,1,0:T(8,128)(2,1)S(1)}, bf16[1,512,1280]{2,1,0:T(8,128)(2,1)}, u32[]{:S(2)}) copy-start(bf16[1,512,1280]{2,1,0:T(8,128)(2,1)} %get-tuple-element.91) | copy-start | bytes 3932164
  144.2 1.3 copy-start.13
  (1 other events, 0.7 us)

commit v14 on v13

--- a/solution.py
+++ b/solution.py
@@ -266,6 +266,27 @@
     ).astype(jnp.bfloat16)
 
 
+def project_kernel(a_ref, w_ref, add_ref, out_ref):
+    total = add_ref[...] + jnp.dot(a_ref[...], w_ref[...], preferred_element_type=jnp.float32)
+    out_ref[...] = total.astype(out_ref.dtype)
+
+
+def project_add(normed, w, addend, lanes=256):
+    count, rows, depth = normed.shape
+    width = w.shape[1]
+    return pl.pallas_call(
+        project_kernel,
+        grid=(count, width // lanes),
+        in_specs=[
+            pl.BlockSpec((None, rows, depth), lambda g, j: (g, 0, 0)),
+            pl.BlockSpec((depth, lanes), lambda g, j: (0, j)),
+            pl.BlockSpec((None, rows, lanes), lambda g, j: (g, 0, j)),
+        ],
+        out_specs=pl.BlockSpec((None, rows, lanes), lambda g, j: (g, 0, j)),
+        out_shape=jax.ShapeDtypeStruct((count, rows, width), jnp.bfloat16),
+    )(normed, w, addend)
+
+
 def on_device(
     tokens, hidden, base_table, w_in, w_dt, conv_w, conv_b, dt_bias, a_log, d_skip, norm_gain, w_out
 ):
@@ -301,10 +322,7 @@
     in_r, out_f = exclusive_scans(sum_f, sum_r, "seq", forward_out)
     normed_r = finish(pend_r, in_r[1], proj_r[:, :rows, :inner], d_skip, norm_gain)
     w_out_mirrored = flip_lanes(w_out)
-    out = out_f + jnp.einsum(
-        "grk,kd->grd", normed_r, w_out_mirrored, preferred_element_type=jnp.float32
-    )
-    return out.astype(jnp.bfloat16)
+    return project_add(normed_r, w_out_mirrored, out_f)
 
 
 def solution(mesh):

time: 157 us -> 159 us (1.013)
  Pallas kernels: 29.6 us -> 34.7 us
  matrix products: 38 us -> 35.1 us
    dot_general x1 -> x0, matrix products: 6.38 us -> none  [on_device(): jnp.einsum('grk,kd->grd', normed_r, w_out_mirrored, preferred_element_typ...]
    pallas_call x0 -> x1, Pallas kernels: none -> 5.13 us  [project_add(): pl.pallas_call(project_kernel, grid=(count, width // lanes), in_specs=[pl...]
    dot_general x1 -> x2, matrix products: 2.45 us -> 6.09 us  [flip_lanes(): jnp.einsum('...d,de->...e', a, j, preferred_element_type=jnp.float32)]
    slice x2 -> x3, other arithmetic: 0.01 us -> 2.67 us  [strand_terms(): sofar = chain(sofar, (total[:, j], state[:, j]))]
    convert_element_type x1, other arithmetic: 3.51 us -> 1.25 us  [finish(): return (gated * lax.rsqrt(jnp.mean(gated * gated, axis=-1, keepdims=True)...]
    reshape x4 -> x2, local copies, waits for them, and re-layouts: 3.33 us -> 1.68 us  [block_terms(): flat = lambda a: a.reshape((blocks,) + a.shape[2:])]
    add x7 -> x8, other arithmetic: 5.04 us -> 4.56 us  [chain(): next_decay[..., None, None] * first_state + next_state]
    unnamed x52 -> x69, local copies, waits for them, and re-layouts: 6.8 us -> 6.56 us
  transfers between devices with their start and end apart: 8 -> 8, of which waited for: 2 -> 2; matrix products, arithmetic and copies ran while one was open for 23% -> 26% of each run, Pallas kernels for 19% -> 19%
where the time goes in v14:
time: 159 us; the launch traced here: 157 us
  matrix products  35.1 us (22%)
  Pallas kernels  34.7 us (22%)
  starting transfers between devices  25.8 us (16%)
  waiting for transfers between devices  24.3 us (15%)
  other arithmetic  19.5 us (12%)
  local copies, waits for them, and re-layouts  17.3 us (11%)
    ppermute x6, waiting for transfers between devices, exclusive_scans(): decay, state = unpack(lax.ppermute(pack(*ahead[k]), axis, pairs))  24.3 us
    ppermute x6, starting transfers between devices, exclusive_scans(): decay, state = unpack(lax.ppermute(pack(*ahead[k]), axis, pairs))  19.9 us
    pallas_call x2, Pallas kernels, block_terms(): pl.pallas_call(partial(inside_kernel, reverse=reverse), grid=(blocks,), i...  11.1 us
    pallas_call x2, Pallas kernels, convolve(): pl.pallas_call(partial(conv_kernel, reverse=reverse), grid=(count, width...  10.9 us
    pallas_call x2, Pallas kernels, block_terms(): pl.pallas_call(state_kernel, grid=(blocks,), in_specs=[spec((Q, width)),...  7.57 us
    dot_general x1, matrix products, on_device(): jnp.einsum('grd,de->gre', ext_r, w_in, preferred_element_type=jnp.float32)  7.48 us
    dot_general x1, matrix products, on_device(): jnp.einsum('grd,de->gre', ext_f, w_in, preferred_element_type=jnp.float32)  7.18 us
    dot_general x2, matrix products, finish(): jnp.einsum('grh,hk->grk', from_start.reshape(count, rows, H), spread, pre...  7.03 us
  transfers between devices with their start and end apart: 8, of which 2 were waited for; matrix products, arithmetic and copies ran while one was open for 26% of the time, Pallas kernels for 19%

profile of v14, /device:TPU:24, one launch (start us, length us, event | category | flops | bytes accessed | tf_op | source)
XLA Modules:
  0.0 157.3 jit_solution(17753335536036701373)
XLA Ops:
  0.0 1.9 %fusion.6 = bf16[1,512,1024]{2,1,0:T(8,128)(2,1)S(1)} fusion(bf16[1,512,1024]{2,1,0:T(8,128)(2,1)} %param.25, bf16[4,1024]{1,0:T(4,128)(2,1)} %param.26, s32[512]{0:T(512)} %bitcast.278), kind=kOutput, calls=%fused_computation.14 | convolution fusion | flops 5769216 | bytes 2107392 | tf_op jit(solution)/shard_map/gtb,bd->gtd/dot_general | solution.py:296
  1.9 3.3 %collective-permute-start.1 = (bf16[1,3,1024]{2,1,0:T(4,128)(2,1)S(1)}, bf16[1,3,1024]{2,1,0:T(4,128)(2,1)S(1)}, u32[]{:S(2)}, u32[]{:S(2)}) collective-permute-start(bf16[1,3,1024]{2,1,0:T(4,128)(2,1)S(1)} %get-tuple-element.111), channel_id=1, source_target_pairs={{2,0},{4,2},{6,4},{8,6},{10,8},{12,10},{14,12},{3,1},{5,3},{7,5},{... | collective-permute-start | bytes 18440 | tf_op jit(solution)/shard_map/ppermute | solution.py:301
  5.2 2.6 %collective-permute-start = (bf16[1,3,1024]{2,1,0:T(4,128)(2,1)S(1)}, bf16[1,3,1024]{2,1,0:T(4,128)(2,1)S(1)}, u32[]{:S(2)}, u32[]{:S(2)}) collective-permute-start(bf16[1,3,1024]{2,1,0:T(4,128)(2,1)S(1)} %get-tuple-element.112), channel_id=1, source_target_pairs={{0,2},{2,4},{4,6},{6,8},{8,10},{10,12},{12,14},{1,3},{3,5},{5,7},{... | collective-permute-start | bytes 18440 | tf_op jit(solution)/shard_map/ppermute | solution.py:300
  8.9 1.1 reduce-window.14
  10.9 3.6 %convert_bitcast_fusion.w_ref = bf16[1024,1024]{1,0:T(8,128)(2,1)} fusion(bf16[1024,1024]{1,0:T(8,128)(2,1)S(1)} %copy-done), kind=kOutput, calls=%fused_computation.15 | convolution fusion | flops 2150629376 | bytes 4194304 | tf_op jit(solution)/shard_map/...d,de->...e/dot_general | solution.py:28
  18.7 7.2 %convolution_bitcast_fusion.1.src_ref.halo_ref = f32[1,520,2304]{2,1,0:T(8,128)} fusion(bf16[1024,2304]{1,0:T(8,128)(2,1)} %param.27, bf16[1,3,1024]{2,1,0:T(4,128)(2,1)S(1)} %collective-permute-done, bf16[1,5,1024]{2,1,0:T(8,128)(2,1)S(1)} %broadcast_in_dim.12, bf16[1,512,1024]{2,1,0:T(8,128)(2,1)S(1)} %fusion.6), kind=kOutput, calls=%fused_computation.1 | convolution fusion | flops 2456862720 | bytes 10575872 | tf_op jit(solution)/shard_map/grd,de->gre/dot_general | solution.py:305
  25.9 5.4 %shard_map.118 = (bf16[1,512,1280]{2,1,0:T(8,128)(2,1)}, bf16[1,1280,512]{2,1,0:T(8,128)(2,1)}) custom-call(f32[1,520,2304]{2,1,0:T(8,128)} %convolution_bitcast_fusion.1.src_ref.halo_ref, f32[1,520,2304]{2,1,0:T(8,128)} %convolution_bitcast_fusion.1.src_ref.halo_ref, f32[4,1280]{1,0:T(4,128)} %w_ref.3, f32[1,1280]{1,0:T(1,128)} %reshape.984.b_ref), custom_call_target="tpu_custom_call" | custom-call | tf_op jit(solution)/shard_map/pallas_call | solution.py:200
  31.3 3.8 %shard_map.119 = f32[2,16,64,128]{3,2,1,0:T(8,128)} custom-call(bf16[2,256,1280]{2,1,0:T(8,128)(2,1)} %bitcast.229, bf16[1,1280,512]{2,1,0:T(8,128)(2,1)} %get-tuple-element.88.x_t_ref, f32[2,256,16]{2,1,0:T(8,128)} %copy.46.to_end_ref), custom_call_target="tpu_custom_call" | custom-call | tf_op jit(solution)/shard_map/pallas_call | solution.py:133
  35.1 1.3 fusion.23
  37.5 2.5 %fusion.9 = bf16[520,1024]{1,0:T(8,128)(2,1)S(1)} fusion(bf16[1,5,1024]{2,1,0:T(8,128)(2,1)S(1)} %broadcast_in_dim.12, bf16[1,3,1024]{2,1,0:T(4,128)(2,1)S(1)} %collective-permute-done.1, bf16[1,512,1024]{2,1,0:T(8,128)(2,1)} %copy-done.10), kind=kOutput, calls=%fused_computation.23 | convolution fusion | flops 1096343552 | bytes 2129920 | tf_op jit(solution)/shard_map/...d,de->...e/dot_general | solution.py:28
  42.1 1.1 reduce-window.16
  45.0 7.5 %convolution_bitcast_fusion.src_ref.halo_ref = f32[1,520,2304]{2,1,0:T(8,128)} fusion(bf16[520,1024]{1,0:T(8,128)(2,1)} %copy-done.33, bf16[1024,2304]{1,0:T(8,128)(2,1)} %param.27), kind=kOutput, calls=%fused_computation | convolution fusion | flops 2453667840 | bytes 10575872 | tf_op jit(solution)/shard_map/grd,de->gre/dot_general | solution.py:313
  55.7 2.1 %collective-permute-start.5 = (f32[1,1032,128]{2,1,0:T(8,128)}, f32[1,1032,128]{2,1,0:T(8,128)}, u32[]{:S(2)}, u32[]{:S(2)}) collective-permute-start(f32[1,1032,128]{2,1,0:T(8,128)} %select_maximum_fusion.2), channel_id=1, source_target_pairs={{0,2},{2,4},{4,6},{6,8},{8,10},{10,12},{12,14},{1,3},{3,5},{5,7},{... | collective-permute-start | bytes 1585160 | tf_op jit(solution)/shard_map/ppermute | solution.py:48
  57.8 5.5 %shard_map.120 = (bf16[1,512,1280]{2,1,0:T(8,128)(2,1)}, bf16[1,1280,512]{2,1,0:T(8,128)(2,1)}) custom-call(f32[1,520,2304]{2,1,0:T(8,128)} %convolution_bitcast_fusion.src_ref.halo_ref, f32[1,520,2304]{2,1,0:T(8,128)} %convolution_bitcast_fusion.src_ref.halo_ref, f32[4,1280]{1,0:T(4,128)} %w_ref.3, f32[1,1280]{1,0:T(1,128)} %reshape.984.b_ref), custom_call_target="tpu_custom_call" | custom-call | tf_op jit(solution)/shard_map/pallas_call | solution.py:200
  64.2 3.8 %shard_map.122 = f32[2,16,64,128]{3,2,1,0:T(8,128)} custom-call(bf16[2,256,1280]{2,1,0:T(8,128)(2,1)} %bitcast.231, bf16[1,1280,512]{2,1,0:T(8,128)(2,1)} %get-tuple-element.92.x_t_ref, f32[2,256,16]{2,1,0:T(8,128)} %multiply_bitcast_fusion.to_end_ref), custom_call_target="tpu_custom_call" | custom-call | tf_op jit(solution)/shard_map/pallas_call | solution.py:133
  67.9 2.1 %fusion.47 = (f32[1,1,16,64,128]{4,3,2,1,0:T(8,128)S(1)}, f32[1,1,16,64,128]{4,3,2,1,0:T(8,128)}, f32[1,1,16,64,128]{4,3,2,1,0:T(8,128)S(1)}) fusion(f32[1,2,16,64,128]{4,3,2,1,0:T(8,128)} %bitcast.246, f32[16]{0:T(128)S(1)} %bitcast_multiply_fusion.7), kind=kLoop, calls=%fused_computation.131 | loop fusion | flops 131072 | bytes 2621504 | tf_op jit(solution)/shard_map/slice | solution.py:233
  72.0 4.8 %collective-permute-start.2 = (f32[1,1032,128]{2,1,0:T(8,128)}, f32[1,1032,128]{2,1,0:T(8,128)}, u32[]{:S(2)}, u32[]{:S(2)}) collective-permute-start(f32[1,1032,128]{2,1,0:T(8,128)} %select_maximum_fusion.5), channel_id=1, source_target_pairs={{2,0},{4,2},{6,4},{8,6},{10,8},{12,10},{14,12},{3,1},{5,3},{7,5},{... | collective-permute-start | bytes 1585160 | tf_op jit(solution)/shard_map/ppermute | solution.py:48
  76.8 5.5 %shard_map.123 = f32[2,256,1024]{2,1,0:T(8,128)} custom-call(bf16[2,256,1280]{2,1,0:T(8,128)(2,1)} %bitcast.230, f32[2,256,16]{2,1,0:T(8,128)} %copy.56.cum_ref, f32[2,16,256]{2,1,0:T(8,128)} %bitcast.256, f32[2,16,256]{2,1,0:T(8,128)} %bitcast.261), custom_call_target="tpu_custom_call" | custom-call | tf_op jit(solution)/shard_map/pallas_call | solution.py:144
  82.4 5.5 %shard_map.121 = f32[2,256,1024]{2,1,0:T(8,128)} custom-call(bf16[2,256,1280]{2,1,0:T(8,128)(2,1)} %bitcast.232, f32[2,256,16]{2,1,0:T(8,128)} %bitcast.240, f32[2,16,256]{2,1,0:T(8,128)} %copy.52.cum_t_ref, f32[2,16,256]{2,1,0:T(8,128)} %bitcast.262), custom_call_target="tpu_custom_call" | custom-call | tf_op jit(solution)/shard_map/pallas_call | solution.py:144
  92.5 1.3 collective-permute-start.6
  94.8 1.3 multiply_add_fusion.5
  96.2 4.6 %collective-permute-start.3 = (f32[1,1032,128]{2,1,0:T(8,128)S(1)}, f32[1,1032,128]{2,1,0:T(8,128)S(1)}, u32[]{:S(2)}, u32[]{:S(2)}) collective-permute-start(f32[1,1032,128]{2,1,0:T(8,128)S(1)} %select_maximum_fusion.4), channel_id=1, source_target_pairs={{4,0},{6,2},{8,4},{10,6},{12,8},{14,10},{5,1},{7,3},{9,5},{11,7},{... | collective-permute-start | bytes 1585160 | tf_op jit(solution)/shard_map/ppermute | solution.py:48
  100.8 6.6 %collective-permute-done.6 = f32[1,1032,128]{2,1,0:T(8,128)} collective-permute-done((f32[1,1032,128]{2,1,0:T(8,128)}, f32[1,1032,128]{2,1,0:T(8,128)}, u32[]{:S(2)}, u32[]{:S(2)}) %collective-permute-start.6) | collective-permute-done | bytes 528416 | tf_op jit(solution)/shard_map/ppermute | solution.py:48
  108.0 1.1 slice.297
  109.3 1.3 collective-permute-start.7
  110.9 5.9 %collective-permute-start.4 = (f32[1,1032,128]{2,1,0:T(8,128)S(1)}, f32[1,1032,128]{2,1,0:T(8,128)S(1)}, u32[]{:S(2)}, u32[]{:S(2)}) collective-permute-start(f32[1,1032,128]{2,1,0:T(8,128)S(1)} %select_maximum_fusion.3), channel_id=1, source_target_pairs={{8,0},{10,2},{12,4},{14,6},{9,1},{11,3},{13,5},{15,7},{24,16},{26,... | collective-permute-start | bytes 1585160 | tf_op jit(solution)/shard_map/ppermute | solution.py:48
  117.5 17.7 %collective-permute-done.7 = f32[1,1032,128]{2,1,0:T(8,128)S(1)} collective-permute-done((f32[1,1032,128]{2,1,0:T(8,128)S(1)}, f32[1,1032,128]{2,1,0:T(8,128)S(1)}, u32[]{:S(2)}, u32[]{:S(2)}) %collective-permute-start.7) | collective-permute-done | bytes 528416 | tf_op jit(solution)/shard_map/ppermute | solution.py:48
  137.4 3.5 %fusion.4 = f32[1,512,1024]{2,1,0:T(8,128)S(1)} fusion(f32[2,256,1024]{2,1,0:T(8,128)S(1)} %fusion.52, f32[2,256,1024]{2,1,0:T(8,128)S(1)} %copy-done.13, f32[1,520,2304]{2,1,0:T(8,128)} %convolution_bitcast_fusion.1.src_ref.halo_ref, f32[512,16]{0,1:T(8,128)S(1)} %bitcast.265, bf16[1,512,1280]{2,1,0:T(8,128)(2,1)S(1)} %copy-done.2, f32[1024]{0:T(1024)S(1)} %mul.502, ...), kind=kOutput, calls=%fused_computation.10 | convolution fusion | flops 105938944 | bytes 9483264 | tf_op jit(solution)/shard_map/grh,hk->grk/dot_general | solution.py:256
  141.6 2.6 %convolution_bitcast_fusion.2.add_ref = f32[1,512,1024]{2,1,0:T(8,128)} fusion(bf16[1024,1024]{1,0:T(8,128)(2,1)S(1)} %copy-done, f32[1,512,1024]{2,1,0:T(8,128)S(1)} %fusion.4, f32[1024]{0:T(1024)S(1)} %copy-done.23, f32[512]{0:T(512)S(1)} %add_rsqrt_fusion.1), kind=kOutput, calls=%fused_computation.22 | convolution fusion | flops 1075314688 | bytes 6297600 | tf_op jit(solution)/shard_map/grk,kd->grd/dot_general | solution.py:320
  147.2 3.5 %fusion.2 = f32[1,512,1024]{2,1,0:T(8,128)S(1)} fusion(f32[2,256,1024]{2,1,0:T(8,128)S(1)} %fusion.53, f32[2,256,1024]{2,1,0:T(8,128)S(1)} %copy-done.12, f32[1,520,2304]{2,1,0:T(8,128)} %convolution_bitcast_fusion.src_ref.halo_ref, f32[512,16]{1,0:T(8,128)S(1)} %bitcast.260, bf16[1,512,1280]{2,1,0:T(8,128)(2,1)S(1)} %copy-done.3, f32[1024]{0:T(1024)S(1)} %mul.502, ...), kind=kOutput, calls=%fused_computation.6 | convolution fusion | flops 105938944 | bytes 9483264 | tf_op jit(solution)/shard_map/grh,hk->grk/dot_general | solution.py:256
  151.0 1.2 multiply_convert_fusion.a_ref
  152.2 5.1 %shard_map.124 = bf16[1,512,1024]{2,1,0:T(8,128)(2,1)} custom-call(bf16[1,512,1024]{2,1,0:T(8,128)(2,1)} %multiply_convert_fusion.a_ref, bf16[1024,1024]{1,0:T(8,128)(2,1)} %convert_bitcast_fusion.w_ref, f32[1,512,1024]{2,1,0:T(8,128)} %convolution_bitcast_fusion.2.add_ref), custom_call_target="tpu_custom_call" | custom-call | tf_op jit(solution)/shard_map/pallas_call | solution.py:277
  (161 shorter events, 30.4 us)
Async XLA Ops:
  0.0 10.8 %copy-start = (bf16[1024,1024]{1,0:T(8,128)(2,1)S(1)}, bf16[1024,1024]{1,0:T(8,128)(2,1)}, u32[]{:S(2)}) copy-start(bf16[1024,1024]{1,0:T(8,128)(2,1)} %param.35) | copy-start | bytes 6291460
  0.0 8.4 %copy-start.32 = (f32[16]{0:T(128)S(1)}, f32[16]{0:T(128)}, u32[]{:S(2)}) copy-start(f32[16]{0:T(128)} %param.32) | copy-start | bytes 196
  0.0 8.4 %copy-start.29 = (f32[16]{0:T(128)S(1)}, f32[16]{0:T(128)}, u32[]{:S(2)}) copy-start(f32[16]{0:T(128)} %param.31) | copy-start | bytes 196
  0.0 8.4 %copy-start.20 = (bf16[1024,16]{0,1:T(8,128)(2,1)S(1)}, bf16[1024,16]{0,1:T(8,128)(2,1)}, u32[]{:S(2)}) copy-start(bf16[1024,16]{0,1:T(8,128)(2,1)} %param.28) | copy-start | bytes 98308
  1.9 16.8 %copy-start.10 = (bf16[1,512,1024]{2,1,0:T(8,128)(2,1)}, bf16[1,512,1024]{2,1,0:T(8,128)(2,1)S(1)}, u32[]{:S(2)}) copy-start(bf16[1,512,1024]{2,1,0:T(8,128)(2,1)S(1)} %fusion.6) | copy-start | bytes 3145732
  1.9 35.6 %collective-permute-start.1 = (bf16[1,3,1024]{2,1,0:T(4,128)(2,1)S(1)}, bf16[1,3,1024]{2,1,0:T(4,128)(2,1)S(1)}, u32[]{:S(2)}, u32[]{:S(2)}) collective-permute-start(bf16[1,3,1024]{2,1,0:T(4,128)(2,1)S(1)} %get-tuple-element.111), channel_id=1, source_target_pairs={{2,0},{4,2},{6,4},{8,6},{10,8},{12,10},{14,12},{3,1},{5,3},{7,5},{... | collective-permute-start | bytes 18440 | tf_op jit(solution)/shard_map/ppermute | solution.py:301
  5.2 13.5 %collective-permute-start = (bf16[1,3,1024]{2,1,0:T(4,128)(2,1)S(1)}, bf16[1,3,1024]{2,1,0:T(4,128)(2,1)S(1)}, u32[]{:S(2)}, u32[]{:S(2)}) collective-permute-start(bf16[1,3,1024]{2,1,0:T(4,128)(2,1)S(1)} %get-tuple-element.112), channel_id=1, source_target_pairs={{0,2},{2,4},{4,6},{6,8},{8,10},{10,12},{12,14},{1,3},{3,5},{5,7},{... | collective-permute-start | bytes 18440 | tf_op jit(solution)/shard_map/ppermute | solution.py:300
  10.6 7.3 %copy-start.16 = (f32[1,2,16,256]{3,2,1,0:T(8,128)}, f32[1,2,16,256]{3,2,1,0:T(8,128)S(1)}, u32[]{:S(2)}) copy-start(f32[1,2,16,256]{3,2,1,0:T(8,128)S(1)} %get-tuple-element.102) | copy-start | bytes 98308
  10.8 4.2 %copy-start.22 = (f32[1280]{0:T(1024)S(1)}, f32[1280]{0:T(1024)}, u32[]{:S(2)}) copy-start(f32[1280]{0:T(1024)} %param.30) | copy-start | bytes 15364
  10.9 4.8 %copy-start.30 = (f32[16]{0:T(128)S(1)}, f32[16]{0:T(128)}, u32[]{:S(2)}) copy-start(f32[16]{0:T(128)} %param.33) | copy-start | bytes 196
  36.5 18.4 %copy-start.4 = (f32[1,16,64,128]{3,2,1,0:T(8,128)}, f32[1,16,64,128]{3,2,1,0:T(8,128)S(1)}, u32[]{:S(2)}) copy-start(f32[1,16,64,128]{3,2,1,0:T(8,128)S(1)} %fusion.23) | copy-start | bytes 1572868
  44.4 9.7 %copy-start.11 = (f32[1,2,256,16]{3,2,1,0:T(8,128)}, f32[1,2,256,16]{3,2,1,0:T(8,128)S(1)}, u32[]{:S(2)}) copy-start(f32[1,2,256,16]{3,2,1,0:T(8,128)S(1)} %get-tuple-element.100) | copy-start | bytes 98308
  45.0 25.4 %copy-start.26 = (f32[1,1,16]{2,1,0:T(1,128)}, f32[1,1,16]{2,1,0:T(1,128)S(1)}, u32[]{:S(2)}) copy-start(f32[1,1,16]{2,1,0:T(1,128)S(1)} %get-tuple-element.120) | copy-start | bytes 196
  45.0 7.5 %copy-start.19 = (f32[512,16]{0,1:T(8,128)S(1)}, f32[512,16]{0,1:T(8,128)}, u32[]{:S(2)}) copy-start(f32[512,16]{0,1:T(8,128)} %copy-done.18) | copy-start | bytes 98308
  55.7 33.2 %collective-permute-start.5 = (f32[1,1032,128]{2,1,0:T(8,128)}, f32[1,1032,128]{2,1,0:T(8,128)}, u32[]{:S(2)}, u32[]{:S(2)}) collective-permute-start(f32[1,1032,128]{2,1,0:T(8,128)} %select_maximum_fusion.2), channel_id=1, source_target_pairs={{0,2},{2,4},{4,6},{6,8},{8,10},{10,12},{12,14},{1,3},{3,5},{5,7},{... | collective-permute-start | bytes 1585160 | tf_op jit(solution)/shard_map/ppermute | solution.py:48
  72.0 21.8 %collective-permute-start.2 = (f32[1,1032,128]{2,1,0:T(8,128)}, f32[1,1032,128]{2,1,0:T(8,128)}, u32[]{:S(2)}, u32[]{:S(2)}) collective-permute-start(f32[1,1032,128]{2,1,0:T(8,128)} %select_maximum_fusion.5), channel_id=1, source_target_pairs={{2,0},{4,2},{6,4},{8,6},{10,8},{12,10},{14,12},{3,1},{5,3},{7,5},{... | collective-permute-start | bytes 1585160 | tf_op jit(solution)/shard_map/ppermute | solution.py:48
  82.4 5.6 %copy-start.31 = (f32[1,1,16]{2,1,0:T(1,128)S(1)}, f32[1,1,16]{2,1,0:T(1,128)}, u32[]{:S(2)}) copy-start(f32[1,1,16]{2,1,0:T(1,128)} %get-tuple-element.119) | copy-start | bytes 196
  82.4 5.6 %copy-start.1 = (f32[2,16,64,128]{3,2,1,0:T(8,128)S(1)}, f32[2,16,64,128]{3,2,1,0:T(8,128)}, u32[]{:S(2)}) copy-start(f32[2,16,64,128]{3,2,1,0:T(8,128)} %shard_map.119) | copy-start | bytes 3145732
  87.9 2.8 %copy-start.5 = (f32[1,16,64,128]{3,2,1,0:T(8,128)S(1)}, f32[1,16,64,128]{3,2,1,0:T(8,128)}, u32[]{:S(2)}) copy-start(f32[1,16,64,128]{3,2,1,0:T(8,128)} %copy-done.4) | copy-start | bytes 1572868
  88.9 5.6 %copy-start.27 = (f32[1,1,16]{2,1,0:T(1,128)S(1)}, f32[1,1,16]{2,1,0:T(1,128)}, u32[]{:S(2)}) copy-start(f32[1,1,16]{2,1,0:T(1,128)} %copy-done.26) | copy-start | bytes 196
  88.9 5.9 %copy-start.7 = (f32[1,1024,128]{2,1,0:T(8,128)S(1)}, f32[1,1024,128]{2,1,0:T(8,128)}, u32[]{:S(2)}) copy-start(f32[1,1024,128]{2,1,0:T(8,128)} %copy-done.6) | copy-start | bytes 1572868
  92.5 14.8 %collective-permute-start.6 = (f32[1,1032,128]{2,1,0:T(8,128)}, f32[1,1032,128]{2,1,0:T(8,128)}, u32[]{:S(2)}, u32[]{:S(2)}) collective-permute-start(f32[1,1032,128]{2,1,0:T(8,128)} %select_maximum_fusion.1), channel_id=1, source_target_pairs={{0,4},{2,6},{4,8},{6,10},{8,12},{10,14},{1,5},{3,7},{5,9},{7,11},{... | collective-permute-start | bytes 1585160 | tf_op jit(solution)/shard_map/ppermute | solution.py:48
  94.8 14.3 %copy-start.9 = (f32[1,16,64,128]{3,2,1,0:T(8,128)S(1)}, f32[1,16,64,128]{3,2,1,0:T(8,128)}, u32[]{:S(2)}) copy-start(f32[1,16,64,128]{3,2,1,0:T(8,128)} %copy-done.8) | copy-start | bytes 1572868
  96.2 14.4 %collective-permute-start.3 = (f32[1,1032,128]{2,1,0:T(8,128)S(1)}, f32[1,1032,128]{2,1,0:T(8,128)S(1)}, u32[]{:S(2)}, u32[]{:S(2)}) collective-permute-start(f32[1,1032,128]{2,1,0:T(8,128)S(1)} %select_maximum_fusion.4), channel_id=1, source_target_pairs={{4,0},{6,2},{8,4},{10,6},{12,8},{14,10},{5,1},{7,3},{9,5},{11,7},{... | collective-permute-start | bytes 1585160 | tf_op jit(solution)/shard_map/ppermute | solution.py:48
  109.3 25.8 %collective-permute-start.7 = (f32[1,1032,128]{2,1,0:T(8,128)S(1)}, f32[1,1032,128]{2,1,0:T(8,128)S(1)}, u32[]{:S(2)}, u32[]{:S(2)}) collective-permute-start(f32[1,1032,128]{2,1,0:T(8,128)S(1)} %select_maximum_fusion), channel_id=1, source_target_pairs={{0,8},{2,10},{4,12},{6,14},{1,9},{3,11},{5,13},{7,15},{16,24},{18,... | collective-permute-start | bytes 1585160 | tf_op jit(solution)/shard_map/ppermute | solution.py:48
  110.9 24.5 %copy-start.15 = (f32[1,1,16,64,128]{4,3,2,1,0:T(8,128)S(1)}, f32[1,1,16,64,128]{4,3,2,1,0:T(8,128)}, u32[]{:S(2)}) copy-start(f32[1,1,16,64,128]{4,3,2,1,0:T(8,128)} %slice_add_fusion) | copy-start | bytes 1572868
  110.9 24.5 %copy-start.28 = (f32[2,16]{1,0:T(2,128)S(1)}, f32[2,16]{1,0:T(2,128)}, u32[]{:S(2)}) copy-start(f32[2,16]{1,0:T(2,128)} %pad_bitcast_fusion) | copy-start | bytes 388
  110.9 33.3 %collective-permute-start.4 = (f32[1,1032,128]{2,1,0:T(8,128)S(1)}, f32[1,1032,128]{2,1,0:T(8,128)S(1)}, u32[]{:S(2)}, u32[]{:S(2)}) collective-permute-start(f32[1,1032,128]{2,1,0:T(8,128)S(1)} %select_maximum_fusion.3), channel_id=1, source_target_pairs={{8,0},{10,2},{12,4},{14,6},{9,1},{11,3},{13,5},{15,7},{24,16},{26,... | collective-permute-start | bytes 1585160 | tf_op jit(solution)/shard_map/ppermute | solution.py:48
  135.6 1.8 %copy-start.2 = (bf16[1,512,1280]{2,1,0:T(8,128)(2,1)S(1)}, bf16[1,512,1280]{2,1,0:T(8,128)(2,1)}, u32[]{:S(2)}) copy-start(bf16[1,512,1280]{2,1,0:T(8,128)(2,1)} %get-tuple-element.87) | copy-start | bytes 3932164
  135.6 1.8 %copy-start.21 = (f32[2,8,2,256]{3,1,2,0:T(8,128)S(1)}, f32[2,8,2,256]{3,1,2,0:T(8,128)}, u32[]{:S(2)}) copy-start(f32[2,8,2,256]{3,1,2,0:T(8,128)} %copy.66) | copy-start | bytes 98308
  145.4 1.8 %copy-start.3 = (bf16[1,512,1280]{2,1,0:T(8,128)(2,1)S(1)}, bf16[1,512,1280]{2,1,0:T(8,128)(2,1)}, u32[]{:S(2)}) copy-start(bf16[1,512,1280]{2,1,0:T(8,128)(2,1)} %get-tuple-element.91) | copy-start | bytes 3932164
  145.4 1.8 %copy-start.17 = (f32[1,2,256,16]{3,2,1,0:T(8,128)S(1)}, f32[1,2,256,16]{3,2,1,0:T(8,128)}, u32[]{:S(2)}) copy-start(f32[1,2,256,16]{3,2,1,0:T(8,128)} %get-tuple-element.99) | copy-start | bytes 98308
  (10 other events, 11.7 us)

commit v15 on v13

--- a/solution.py
+++ b/solution.py
@@ -196,7 +196,7 @@
     width = conv_w.shape[1]
     edge = 8
     lanes = CONV_LANES
-    skip = inner // lanes
+    skip = (projected.shape[2] - width) // lanes
     return pl.pallas_call(
         partial(conv_kernel, reverse=reverse),
         grid=(count, width // lanes),
@@ -281,7 +281,9 @@
     rates = -jnp.exp(a_log)
     gap = jnp.zeros((strand.shape[0], 8 - margin, strand.shape[2]), strand.dtype)
     ext_f = jnp.concatenate([strand, gap, low], axis=1)
-    proj_f = jnp.einsum("grd,de->gre", ext_f, w_in, preferred_element_type=jnp.float32)
+    w_source = w_in[:, inner:]
+    w_gate = w_in[:, :inner]
+    proj_f = jnp.einsum("grd,de->gre", ext_f, w_source, preferred_element_type=jnp.float32)
     step_f = jax.nn.softplus(
         jnp.einsum("grd,dh->grh", strand, w_dt, preferred_element_type=jnp.float32) + dt_bias
     )
@@ -289,17 +291,19 @@
     sum_f, (strand_late, high) = lax.optimization_barrier((sum_f, (strand, high)))
     ext_r = flip_lanes(jnp.concatenate([strand_late, high, gap], axis=1))
     mirrored = ext_r[:, :rows]
-    proj_r = jnp.einsum("grd,de->gre", ext_r, w_in, preferred_element_type=jnp.float32)
+    proj_r = jnp.einsum("grd,de->gre", ext_r, w_source, preferred_element_type=jnp.float32)
     step_r = jax.nn.softplus(
         jnp.einsum("grd,dh->grh", mirrored, w_dt, preferred_element_type=jnp.float32) + dt_bias
     )
     sum_r, pend_r = strand_terms(proj_r, step_r, conv_w, conv_b, rates, True)
     def forward_out(incoming):
-        normed_f = finish(pend_f, incoming, proj_f[:, :rows, :inner], d_skip, norm_gain)
+        gate_f = jnp.einsum("grd,de->gre", strand, w_gate, preferred_element_type=jnp.float32)
+        normed_f = finish(pend_f, incoming, gate_f, d_skip, norm_gain)
         return jnp.einsum("grk,kd->grd", normed_f, w_out, preferred_element_type=jnp.float32)
 
     in_r, out_f = exclusive_scans(sum_f, sum_r, "seq", forward_out)
-    normed_r = finish(pend_r, in_r[1], proj_r[:, :rows, :inner], d_skip, norm_gain)
+    gate_r = jnp.einsum("grd,de->gre", mirrored, w_gate, preferred_element_type=jnp.float32)
+    normed_r = finish(pend_r, in_r[1], gate_r, d_skip, norm_gain)
     w_out_mirrored = flip_lanes(w_out)
     out = out_f + jnp.einsum(
         "grk,kd->grd", normed_r, w_out_mirrored, preferred_element_type=jnp.float32

time: 157 us -> 159 us (1.013)
  other arithmetic: 19.2 us -> 21.2 us
    dot_general x2 -> x4, matrix products: 14.6 us -> 18.7 us  [the longest x1 5.13 us: on_device(): jnp.einsum('grd,de->gre', ext_r, w_source, preferred_element_type=jnp.flo...]
    dot_general x2, matrix products: 7.19 us -> 3.55 us  [finish(): jnp.einsum('grh,hk->grk', from_start.reshape(count, rows, H), spread, pre...]
    unnamed x52 -> x66, local copies, waits for them, and re-layouts: 6.8 us -> 7.43 us
  transfers between devices with their start and end apart: 8 -> 8, of which waited for: 2 -> 3; matrix products, arithmetic and copies ran while one was open for 23% -> 29% of each run, Pallas kernels for 19% -> 19%
where the time goes in v15:
time: 159 us; the launch traced here: 158 us
  matrix products  37.2 us (23%)
  Pallas kernels  29.5 us (19%)
  starting transfers between devices  25.4 us (16%)
  waiting for transfers between devices  24.4 us (15%)
  other arithmetic  21.2 us (13%)
  local copies, waits for them, and re-layouts  19.7 us (12%)
    ppermute x6, waiting for transfers between devices, exclusive_scans(): decay, state = unpack(lax.ppermute(pack(*ahead[k]), axis, pairs))  24.4 us
    ppermute x6, starting transfers between devices, exclusive_scans(): decay, state = unpack(lax.ppermute(pack(*ahead[k]), axis, pairs))  19.6 us
    pallas_call x2, Pallas kernels, block_terms(): pl.pallas_call(partial(inside_kernel, reverse=reverse), grid=(blocks,), i...  11.1 us
    pallas_call x2, Pallas kernels, convolve(): pl.pallas_call(partial(conv_kernel, reverse=reverse), grid=(count, width...  10.9 us
    pallas_call x2, Pallas kernels, block_terms(): pl.pallas_call(state_kernel, grid=(blocks,), in_specs=[spec((Q, width)),...  7.55 us
    unnamed x66, local copies, waits for them, and re-layouts  7.43 us
    dot_general x1, matrix products, on_device(): jnp.einsum('grk,kd->grd', normed_r, w_out_mirrored, preferred_element_typ...  6.38 us
    add x7, other arithmetic, chain(): next_decay[..., None, None] * first_state + next_state  6.2 us
  transfers between devices with their start and end apart: 8, of which 3 were waited for; matrix products, arithmetic and copies ran while one was open for 29% of the time, Pallas kernels for 19%

profile of v15, /device:TPU:24, one launch (start us, length us, event | category | flops | bytes accessed | tf_op | source)
XLA Modules:
  0.0 158.2 jit_solution(5422777478414531023)
XLA Ops:
  0.0 1.9 %fusion.9 = bf16[1,512,1024]{2,1,0:T(8,128)(2,1)S(1)} fusion(bf16[1,512,1024]{2,1,0:T(8,128)(2,1)} %param.25, bf16[4,1024]{1,0:T(4,128)(2,1)} %param.26, s32[512]{0:T(512)} %bitcast.290), kind=kOutput, calls=%fused_computation.19 | convolution fusion | flops 5769216 | bytes 2107392 | tf_op jit(solution)/shard_map/gtb,bd->gtd/dot_general | solution.py:275
  1.9 3.3 %collective-permute-start.1 = (bf16[1,3,1024]{2,1,0:T(4,128)(2,1)S(1)}, bf16[1,3,1024]{2,1,0:T(4,128)(2,1)S(1)}, u32[]{:S(2)}, u32[]{:S(2)}) collective-permute-start(bf16[1,3,1024]{2,1,0:T(4,128)(2,1)S(1)} %get-tuple-element.113), channel_id=1, source_target_pairs={{2,0},{4,2},{6,4},{8,6},{10,8},{12,10},{14,12},{3,1},{5,3},{7,5},{... | collective-permute-start | bytes 18440 | tf_op jit(solution)/shard_map/ppermute | solution.py:280
  5.2 2.6 %collective-permute-start = (bf16[1,3,1024]{2,1,0:T(4,128)(2,1)S(1)}, bf16[1,3,1024]{2,1,0:T(4,128)(2,1)S(1)}, u32[]{:S(2)}, u32[]{:S(2)}) collective-permute-start(bf16[1,3,1024]{2,1,0:T(4,128)(2,1)S(1)} %get-tuple-element.114), channel_id=1, source_target_pairs={{0,2},{2,4},{4,6},{6,8},{8,10},{10,12},{12,14},{1,3},{3,5},{5,7},{... | collective-permute-start | bytes 18440 | tf_op jit(solution)/shard_map/ppermute | solution.py:279
  11.4 4.2 %fusion.16 = f32[512,1024]{1,0:T(8,128)} fusion(bf16[1024,2304]{1,0:T(8,128)(2,1)} %param.27, bf16[1,512,1024]{2,1,0:T(8,128)(2,1)S(1)} %fusion.9), kind=kOutput, calls=%fused_computation.30 | convolution fusion | flops 1073741824 | bytes 5242880 | tf_op jit(solution)/shard_map/grd,de->gre/dot_general | solution.py:300
  19.2 4.8 %convolution_bitcast_fusion.1.src_ref.halo_ref = f32[1,520,1280]{2,1,0:T(8,128)} fusion(bf16[1024,2304]{1,0:T(8,128)(2,1)} %param.27, bf16[1,3,1024]{2,1,0:T(4,128)(2,1)S(1)} %collective-permute-done, bf16[1,5,1024]{2,1,0:T(8,128)(2,1)S(1)} %broadcast_in_dim.12, bf16[1,512,1024]{2,1,0:T(8,128)(2,1)S(1)} %fusion.9), kind=kOutput, calls=%fused_computation.4 | convolution fusion | flops 1366343680 | bytes 6348800 | tf_op jit(solution)/shard_map/grd,de->gre/dot_general | solution.py:286
  24.0 5.4 %shard_map.118 = (bf16[1,512,1280]{2,1,0:T(8,128)(2,1)}, bf16[1,1280,512]{2,1,0:T(8,128)(2,1)}) custom-call(f32[1,520,1280]{2,1,0:T(8,128)} %convolution_bitcast_fusion.1.src_ref.halo_ref, f32[1,520,1280]{2,1,0:T(8,128)} %convolution_bitcast_fusion.1.src_ref.halo_ref, f32[4,1280]{1,0:T(4,128)} %w_ref.3, f32[1,1280]{1,0:T(1,128)} %reshape.1002.b_ref), custom_call_target="tpu_custom_call" | custom-call | tf_op jit(solution)/shard_map/pallas_call | solution.py:200
  29.4 3.8 %shard_map.119 = f32[2,16,64,128]{3,2,1,0:T(8,128)} custom-call(bf16[2,256,1280]{2,1,0:T(8,128)(2,1)} %bitcast.247, bf16[1,1280,512]{2,1,0:T(8,128)(2,1)} %get-tuple-element.88.x_t_ref, f32[2,256,16]{2,1,0:T(8,128)} %copy.28.to_end_ref), custom_call_target="tpu_custom_call" | custom-call | tf_op jit(solution)/shard_map/pallas_call | solution.py:133
  33.2 1.4 fusion.41
  34.6 1.9 %slice_add_fusion = f32[1,1,16,64,128]{4,3,2,1,0:T(8,128)} fusion(f32[1,2,16,64,128]{4,3,2,1,0:T(8,128)} %bitcast.246, f32[16]{0:T(128)S(1)} %get-tuple-element.123), kind=kLoop, calls=%fused_computation.77 | loop fusion | flops 131072 | bytes 1048640 | tf_op jit(solution)/shard_map/add | solution.py:34
  36.6 1.2 fusion.18
  41.8 5.1 %convolution_bitcast_fusion.src_ref.halo_ref = f32[1,520,1280]{2,1,0:T(8,128)} fusion(bf16[520,1024]{1,0:T(8,128)(2,1)} %copy-done.28, bf16[1024,2304]{1,0:T(8,128)(2,1)} %param.27), kind=kOutput, calls=%fused_computation.3 | convolution fusion | flops 1363148800 | bytes 6348800 | tf_op jit(solution)/shard_map/grd,de->gre/dot_general | solution.py:294
  48.2 1.9 %collective-permute-start.5 = (f32[1,1032,128]{2,1,0:T(8,128)S(1)}, f32[1,1032,128]{2,1,0:T(8,128)}, u32[]{:S(2)}, u32[]{:S(2)}) collective-permute-start(f32[1,1032,128]{2,1,0:T(8,128)S(1)} %select_maximum_fusion.2), channel_id=1, source_target_pairs={{0,2},{2,4},{4,6},{6,8},{8,10},{10,12},{12,14},{1,3},{3,5},{5,7},{... | collective-permute-start | bytes 1585160 | tf_op jit(solution)/shard_map/ppermute | solution.py:48
  50.1 5.4 %shard_map.120 = (bf16[1,512,1280]{2,1,0:T(8,128)(2,1)}, bf16[1,1280,512]{2,1,0:T(8,128)(2,1)}) custom-call(f32[1,520,1280]{2,1,0:T(8,128)} %convolution_bitcast_fusion.src_ref.halo_ref, f32[1,520,1280]{2,1,0:T(8,128)} %convolution_bitcast_fusion.src_ref.halo_ref, f32[4,1280]{1,0:T(4,128)} %w_ref.3, f32[1,1280]{1,0:T(1,128)} %reshape.1002.b_ref), custom_call_target="tpu_custom_call" | custom-call | tf_op jit(solution)/shard_map/pallas_call | solution.py:200
  55.5 3.8 %shard_map.121 = f32[2,16,64,128]{3,2,1,0:T(8,128)} custom-call(bf16[2,256,1280]{2,1,0:T(8,128)(2,1)} %bitcast.249, bf16[1,1280,512]{2,1,0:T(8,128)(2,1)} %get-tuple-element.92.x_t_ref, f32[2,256,16]{2,1,0:T(8,128)} %copy.34.to_end_ref), custom_call_target="tpu_custom_call" | custom-call | tf_op jit(solution)/shard_map/pallas_call | solution.py:133
  59.3 2.1 %broadcast_add_fusion = (f32[1,1,16,64,128]{4,3,2,1,0:T(8,128)}, f32[1,1,16,64,128]{4,3,2,1,0:T(8,128)S(1)}, f32[1,1,16,64,128]{4,3,2,1,0:T(8,128)S(1)}) fusion(f32[16]{0:T(128)S(1)} %bitcast_multiply_fusion.9, f32[1,2,16,64,128]{4,3,2,1,0:T(8,128)} %bitcast.259), kind=kLoop, calls=%fused_computation.78 | loop fusion | flops 131072 | bytes 2621504 | tf_op jit(solution)/shard_map/add | solution.py:34
  66.7 5.0 %collective-permute-start.2 = (f32[1,1032,128]{2,1,0:T(8,128)}, f32[1,1032,128]{2,1,0:T(8,128)}, u32[]{:S(2)}, u32[]{:S(2)}) collective-permute-start(f32[1,1032,128]{2,1,0:T(8,128)} %select_maximum_fusion.5), channel_id=1, source_target_pairs={{2,0},{4,2},{6,4},{8,6},{10,8},{12,10},{14,12},{3,1},{5,3},{7,5},{... | collective-permute-start | bytes 1585160 | tf_op jit(solution)/shard_map/ppermute | solution.py:48
  71.7 5.6 %shard_map.122 = f32[2,256,1024]{2,1,0:T(8,128)} custom-call(bf16[2,256,1280]{2,1,0:T(8,128)(2,1)} %bitcast.248, f32[2,256,16]{2,1,0:T(8,128)} %copy.36.cum_ref, f32[2,16,256]{2,1,0:T(8,128)} %bitcast.267, f32[2,16,256]{2,1,0:T(8,128)} %bitcast.273), custom_call_target="tpu_custom_call" | custom-call | tf_op jit(solution)/shard_map/pallas_call | solution.py:144
  77.3 5.5 %shard_map.123 = f32[2,256,1024]{2,1,0:T(8,128)} custom-call(bf16[2,256,1280]{2,1,0:T(8,128)(2,1)} %bitcast.250, f32[2,256,16]{2,1,0:T(8,128)} %copy.39.cum_ref, f32[2,16,256]{2,1,0:T(8,128)} %bitcast.269, f32[2,16,256]{2,1,0:T(8,128)} %bitcast.274), custom_call_target="tpu_custom_call" | custom-call | tf_op jit(solution)/shard_map/pallas_call | solution.py:144
  83.3 4.6 %fusion.14 = f32[512,1024]{1,0:T(8,128)} fusion(bf16[1024,2304]{1,0:T(8,128)(2,1)} %param.27, bf16[1,520,1024]{2,1,0:T(8,128)(2,1)} %bitcast.292), kind=kOutput, calls=%fused_computation.28 | convolution fusion | flops 1073741824 | bytes 5242880 | tf_op jit(solution)/shard_map/grd,de->gre/dot_general | solution.py:305
  91.4 1.3 collective-permute-start.6
  93.7 1.5 fusion.70
  95.2 4.6 %collective-permute-start.3 = (f32[1,1032,128]{2,1,0:T(8,128)S(1)}, f32[1,1032,128]{2,1,0:T(8,128)S(1)}, u32[]{:S(2)}, u32[]{:S(2)}) collective-permute-start(f32[1,1032,128]{2,1,0:T(8,128)S(1)} %select_maximum_fusion.4), channel_id=1, source_target_pairs={{4,0},{6,2},{8,4},{10,6},{12,8},{14,10},{5,1},{7,3},{9,5},{11,7},{... | collective-permute-start | bytes 1585160 | tf_op jit(solution)/shard_map/ppermute | solution.py:48
  99.8 6.5 %collective-permute-done.6 = f32[1,1032,128]{2,1,0:T(8,128)} collective-permute-done((f32[1,1032,128]{2,1,0:T(8,128)}, f32[1,1032,128]{2,1,0:T(8,128)}, u32[]{:S(2)}, u32[]{:S(2)}) %collective-permute-start.6) | collective-permute-done | bytes 528416 | tf_op jit(solution)/shard_map/ppermute | solution.py:48
  108.2 1.3 collective-permute-start.7
  109.9 5.5 %collective-permute-start.4 = (f32[1,1032,128]{2,1,0:T(8,128)S(1)}, f32[1,1032,128]{2,1,0:T(8,128)S(1)}, u32[]{:S(2)}, u32[]{:S(2)}) collective-permute-start(f32[1,1032,128]{2,1,0:T(8,128)S(1)} %select_maximum_fusion.3), channel_id=1, source_target_pairs={{8,0},{10,2},{12,4},{14,6},{9,1},{11,3},{13,5},{15,7},{24,16},{26,... | collective-permute-start | bytes 1585160 | tf_op jit(solution)/shard_map/ppermute | solution.py:48
  116.2 17.8 %collective-permute-done.7 = f32[1,1032,128]{2,1,0:T(8,128)S(1)} collective-permute-done((f32[1,1032,128]{2,1,0:T(8,128)S(1)}, f32[1,1032,128]{2,1,0:T(8,128)S(1)}, u32[]{:S(2)}, u32[]{:S(2)}) %collective-permute-start.7) | collective-permute-done | bytes 528416 | tf_op jit(solution)/shard_map/ppermute | solution.py:48
  136.7 1.8 %bitcast_multiply_fusion.2 = f32[1,512,1024]{2,1,0:T(8,128)S(1)} fusion(f32[2,256,1024]{2,1,0:T(8,128)S(1)} %fusion.73, f32[2,256,1024]{2,1,0:T(8,128)S(1)} %copy-done.9, f32[512,1024]{1,0:T(8,128)S(1)} %copy-done.30, f32[512,16]{0,1:T(8,128)S(1)} %bitcast.278, bf16[1,512,1280]{2,1,0:T(8,128)(2,1)S(1)} %copy-done.1, f32[1024]{0:T(1024)S(1)} %mul.506, ...), kind=kOutput, calls=%fused_computation.14 | convolution fusion | flops 105938944 | bytes 9483264 | tf_op jit(solution)/shard_map/grh,hk->grk/dot_general | solution.py:256
  139.2 2.6 %convolution_bitcast_fusion.2 = f32[1,512,1024]{2,1,0:T(8,128)} fusion(bf16[1024,1024]{1,0:T(8,128)(2,1)S(1)} %copy-done, f32[1,512,1024]{2,1,0:T(8,128)S(1)} %bitcast_multiply_fusion.2, f32[1024]{0:T(1024)S(1)} %copy-done.26, f32[512]{0:T(512)S(1)} %add_rsqrt_fusion.1), kind=kOutput, calls=%fused_computation.32 | convolution fusion | flops 1075314688 | bytes 6297600 | tf_op jit(solution)/shard_map/grk,kd->grd/dot_general | solution.py:302
  144.9 1.7 %bitcast_multiply_fusion = f32[1,512,1024]{2,1,0:T(8,128)S(1)} fusion(f32[2,256,1024]{2,1,0:T(8,128)S(1)} %fusion.74, f32[2,256,1024]{2,1,0:T(8,128)S(1)} %copy-done.8, f32[512,1024]{1,0:T(8,128)S(1)} %copy-done.31, f32[512,16]{0,1:T(8,128)S(1)} %bitcast.279, bf16[1,512,1280]{2,1,0:T(8,128)(2,1)S(1)} %copy-done.2, f32[1024]{0:T(1024)S(1)} %mul.506, ...), kind=kOutput, calls=%fused_computation.10 | convolution fusion | flops 105938944 | bytes 9483264 | tf_op jit(solution)/shard_map/grh,hk->grk/dot_general | solution.py:256
  146.7 1.3 copy-done.10
  148.3 6.4 %fusion.10 = f32[512,1024]{1,0:T(8,128)} fusion(bf16[1024,1024]{1,0:T(8,128)(2,1)S(1)} %copy-done, f32[1,512,1024]{2,1,0:T(8,128)} %copy-done.10, f32[512]{0:T(512)S(1)} %add_rsqrt_fusion, f32[1024]{0:T(1024)S(1)} %copy-done.26), kind=kOutput, calls=%fused_computation.20 | convolution fusion | flops 3226992640 | bytes 6297600 | tf_op jit(solution)/shard_map/grk,kd->grd/dot_general | solution.py:308
  154.7 3.5 %fusion.6 = bf16[1,512,1024]{2,1,0:T(8,128)(2,1)} fusion(f32[1,512,1024]{2,1,0:T(8,128)} %convolution_bitcast_fusion.2, f32[512,1024]{1,0:T(8,128)} %fusion.10), kind=kLoop, calls=%fused_computation.9 | loop fusion | flops 1048576 | bytes 5242880 | tf_op jit(solution)/shard_map/convert_element_type | solution.py:311
  (162 shorter events, 32.1 us)
Async XLA Ops:
  0.0 138.7 %copy-start = (bf16[1024,1024]{1,0:T(8,128)(2,1)S(1)}, bf16[1024,1024]{1,0:T(8,128)(2,1)}, u32[]{:S(2)}) copy-start(bf16[1024,1024]{1,0:T(8,128)(2,1)} %param.35) | copy-start | bytes 6291460
  0.0 8.9 %copy-start.27 = (f32[16]{0:T(128)S(1)}, f32[16]{0:T(128)}, u32[]{:S(2)}) copy-start(f32[16]{0:T(128)} %param.32) | copy-start | bytes 196
  0.0 8.9 %copy-start.23 = (f32[16]{0:T(128)S(1)}, f32[16]{0:T(128)}, u32[]{:S(2)}) copy-start(f32[16]{0:T(128)} %param.31) | copy-start | bytes 196
  0.0 8.9 %copy-start.15 = (bf16[1024,16]{0,1:T(8,128)(2,1)S(1)}, bf16[1024,16]{0,1:T(8,128)(2,1)}, u32[]{:S(2)}) copy-start(bf16[1024,16]{0,1:T(8,128)(2,1)} %param.28) | copy-start | bytes 98308
  1.9 17.3 %copy-start.6 = (bf16[1,512,1024]{2,1,0:T(8,128)(2,1)}, bf16[1,512,1024]{2,1,0:T(8,128)(2,1)S(1)}, u32[]{:S(2)}) copy-start(bf16[1,512,1024]{2,1,0:T(8,128)(2,1)S(1)} %fusion.9) | copy-start | bytes 3145732
  1.9 34.6 %collective-permute-start.1 = (bf16[1,3,1024]{2,1,0:T(4,128)(2,1)S(1)}, bf16[1,3,1024]{2,1,0:T(4,128)(2,1)S(1)}, u32[]{:S(2)}, u32[]{:S(2)}) collective-permute-start(bf16[1,3,1024]{2,1,0:T(4,128)(2,1)S(1)} %get-tuple-element.113), channel_id=1, source_target_pairs={{2,0},{4,2},{6,4},{8,6},{10,8},{12,10},{14,12},{3,1},{5,3},{7,5},{... | collective-permute-start | bytes 18440 | tf_op jit(solution)/shard_map/ppermute | solution.py:280
  5.2 13.9 %collective-permute-start = (bf16[1,3,1024]{2,1,0:T(4,128)(2,1)S(1)}, bf16[1,3,1024]{2,1,0:T(4,128)(2,1)S(1)}, u32[]{:S(2)}, u32[]{:S(2)}) collective-permute-start(bf16[1,3,1024]{2,1,0:T(4,128)(2,1)S(1)} %get-tuple-element.114), channel_id=1, source_target_pairs={{0,2},{2,4},{4,6},{6,8},{8,10},{10,12},{12,14},{1,3},{3,5},{5,7},{... | collective-permute-start | bytes 18440 | tf_op jit(solution)/shard_map/ppermute | solution.py:279
  11.1 7.3 %copy-start.13 = (f32[1,2,16,256]{3,2,1,0:T(8,128)}, f32[1,2,16,256]{3,2,1,0:T(8,128)S(1)}, u32[]{:S(2)}) copy-start(f32[1,2,16,256]{3,2,1,0:T(8,128)S(1)} %get-tuple-element.104) | copy-start | bytes 98308
  11.3 4.7 %copy-start.16 = (f32[1280]{0:T(1024)S(1)}, f32[1280]{0:T(1024)}, u32[]{:S(2)}) copy-start(f32[1280]{0:T(1024)} %param.30) | copy-start | bytes 15364
  11.4 5.3 %copy-start.24 = (f32[16]{0:T(128)S(1)}, f32[16]{0:T(128)}, u32[]{:S(2)}) copy-start(f32[16]{0:T(128)} %param.33) | copy-start | bytes 196
  33.2 3.4 %copy-start.7 = (bf16[1,512,1024]{2,1,0:T(8,128)(2,1)S(1)}, bf16[1,512,1024]{2,1,0:T(8,128)(2,1)}, u32[]{:S(2)}) copy-start(bf16[1,512,1024]{2,1,0:T(8,128)(2,1)} %copy-done.6) | copy-start | bytes 3145732
  41.2 24.7 %copy-start.14 = (f32[1,2,256,16]{2,3,1,0:T(8,128)}, f32[1,2,256,16]{2,3,1,0:T(8,128)S(1)}, u32[]{:S(2)}) copy-start(f32[1,2,256,16]{2,3,1,0:T(8,128)S(1)} %get-tuple-element.102) | copy-start | bytes 98308
  41.8 20.0 %copy-start.19 = (f32[1,1,16]{2,1,0:T(1,128)}, f32[1,1,16]{2,1,0:T(1,128)S(1)}, u32[]{:S(2)}) copy-start(f32[1,1,16]{2,1,0:T(1,128)S(1)} %get-tuple-element.120) | copy-start | bytes 196
  48.2 39.7 %collective-permute-start.5 = (f32[1,1032,128]{2,1,0:T(8,128)S(1)}, f32[1,1032,128]{2,1,0:T(8,128)}, u32[]{:S(2)}, u32[]{:S(2)}) collective-permute-start(f32[1,1032,128]{2,1,0:T(8,128)S(1)} %select_maximum_fusion.2), channel_id=1, source_target_pairs={{0,2},{2,4},{4,6},{6,8},{8,10},{10,12},{12,14},{1,3},{3,5},{5,7},{... | collective-permute-start | bytes 1585160 | tf_op jit(solution)/shard_map/ppermute | solution.py:48
  66.7 26.0 %collective-permute-start.2 = (f32[1,1032,128]{2,1,0:T(8,128)}, f32[1,1032,128]{2,1,0:T(8,128)}, u32[]{:S(2)}, u32[]{:S(2)}) collective-permute-start(f32[1,1032,128]{2,1,0:T(8,128)} %select_maximum_fusion.5), channel_id=1, source_target_pairs={{2,0},{4,2},{6,4},{8,6},{10,8},{12,10},{14,12},{3,1},{5,3},{7,5},{... | collective-permute-start | bytes 1585160 | tf_op jit(solution)/shard_map/ppermute | solution.py:48
  77.3 5.5 %copy-start.25 = (f32[1,1,16]{2,1,0:T(1,128)S(1)}, f32[1,1,16]{2,1,0:T(1,128)}, u32[]{:S(2)}) copy-start(f32[1,1,16]{2,1,0:T(1,128)} %get-tuple-element.119) | copy-start | bytes 196
  87.9 5.5 %copy-start.20 = (f32[1,1,16]{2,1,0:T(1,128)S(1)}, f32[1,1,16]{2,1,0:T(1,128)}, u32[]{:S(2)}) copy-start(f32[1,1,16]{2,1,0:T(1,128)} %copy-done.19) | copy-start | bytes 196
  91.4 14.9 %collective-permute-start.6 = (f32[1,1032,128]{2,1,0:T(8,128)}, f32[1,1032,128]{2,1,0:T(8,128)}, u32[]{:S(2)}, u32[]{:S(2)}) collective-permute-start(f32[1,1032,128]{2,1,0:T(8,128)} %select_maximum_fusion.1), channel_id=1, source_target_pairs={{0,4},{2,6},{4,8},{6,10},{8,12},{10,14},{1,5},{3,7},{5,9},{7,11},{... | collective-permute-start | bytes 1585160 | tf_op jit(solution)/shard_map/ppermute | solution.py:48
  93.7 14.3 %copy-start.5 = (f32[1,16,64,128]{3,2,1,0:T(8,128)S(1)}, f32[1,16,64,128]{3,2,1,0:T(8,128)}, u32[]{:S(2)}) copy-start(f32[1,16,64,128]{3,2,1,0:T(8,128)} %copy-done.4) | copy-start | bytes 1572868
  95.2 14.4 %collective-permute-start.3 = (f32[1,1032,128]{2,1,0:T(8,128)S(1)}, f32[1,1032,128]{2,1,0:T(8,128)S(1)}, u32[]{:S(2)}, u32[]{:S(2)}) collective-permute-start(f32[1,1032,128]{2,1,0:T(8,128)S(1)} %select_maximum_fusion.4), channel_id=1, source_target_pairs={{4,0},{6,2},{8,4},{10,6},{12,8},{14,10},{5,1},{7,3},{9,5},{11,7},{... | collective-permute-start | bytes 1585160 | tf_op jit(solution)/shard_map/ppermute | solution.py:48
  108.2 25.7 %collective-permute-start.7 = (f32[1,1032,128]{2,1,0:T(8,128)S(1)}, f32[1,1032,128]{2,1,0:T(8,128)S(1)}, u32[]{:S(2)}, u32[]{:S(2)}) collective-permute-start(f32[1,1032,128]{2,1,0:T(8,128)S(1)} %select_maximum_fusion), channel_id=1, source_target_pairs={{0,8},{2,10},{4,12},{6,14},{1,9},{3,11},{5,13},{7,15},{16,24},{18,... | collective-permute-start | bytes 1585160 | tf_op jit(solution)/shard_map/ppermute | solution.py:48
  109.9 24.3 %copy-start.11 = (f32[1,1,16,64,128]{4,3,2,1,0:T(8,128)S(1)}, f32[1,1,16,64,128]{4,3,2,1,0:T(8,128)}, u32[]{:S(2)}) copy-start(f32[1,1,16,64,128]{4,3,2,1,0:T(8,128)} %slice_add_fusion) | copy-start | bytes 1572868
  109.9 24.3 %copy-start.21 = (f32[2,16]{1,0:T(2,128)S(1)}, f32[2,16]{1,0:T(2,128)}, u32[]{:S(2)}) copy-start(f32[2,16]{1,0:T(2,128)} %pad_bitcast_fusion.1) | copy-start | bytes 388
  109.9 31.9 %collective-permute-start.4 = (f32[1,1032,128]{2,1,0:T(8,128)S(1)}, f32[1,1032,128]{2,1,0:T(8,128)S(1)}, u32[]{:S(2)}, u32[]{:S(2)}) collective-permute-start(f32[1,1032,128]{2,1,0:T(8,128)S(1)} %select_maximum_fusion.3), channel_id=1, source_target_pairs={{8,0},{10,2},{12,4},{14,6},{9,1},{11,3},{13,5},{15,7},{24,16},{26,... | collective-permute-start | bytes 1585160 | tf_op jit(solution)/shard_map/ppermute | solution.py:48
  134.2 2.1 %copy-start.9 = (f32[2,256,1024]{2,1,0:T(8,128)S(1)}, f32[2,256,1024]{2,1,0:T(8,128)}, u32[]{:S(2)}) copy-start(f32[2,256,1024]{2,1,0:T(8,128)} %shard_map.122) | copy-start | bytes 6291460
  134.4 2.3 %copy-start.1 = (bf16[1,512,1280]{2,1,0:T(8,128)(2,1)S(1)}, bf16[1,512,1280]{2,1,0:T(8,128)(2,1)}, u32[]{:S(2)}) copy-start(bf16[1,512,1280]{2,1,0:T(8,128)(2,1)} %get-tuple-element.87) | copy-start | bytes 3932164
  134.4 2.3 %copy-start.17 = (s32[1024]{0:T(1024)S(1)}, s32[1024]{0:T(1024)}, u32[]{:S(2)}) copy-start(s32[1024]{0:T(1024)} %get-tuple-element.126) | copy-start | bytes 12292
  134.4 2.3 %copy-start.18 = (s32[1024]{0:T(1024)S(1)}, s32[1024]{0:T(1024)}, u32[]{:S(2)}) copy-start(s32[1024]{0:T(1024)} %get-tuple-element.127) | copy-start | bytes 12292
  134.4 2.3 %copy-start.29 = (pred[1024]{0:T(1024)(128)(4,1)S(1)}, pred[1024]{0:T(1024)(128)(4,1)}, u32[]{:S(2)}) copy-start(pred[1024]{0:T(1024)(128)(4,1)} %fusion.57) | copy-start | bytes 3076
  141.9 2.2 %copy-start.31 = (f32[512,1024]{1,0:T(8,128)S(1)}, f32[512,1024]{1,0:T(8,128)}, u32[]{:S(2)}) copy-start(f32[512,1024]{1,0:T(8,128)} %fusion.14) | copy-start | bytes 6291460
  142.9 1.7 %copy-start.8 = (f32[2,256,1024]{2,1,0:T(8,128)S(1)}, f32[2,256,1024]{2,1,0:T(8,128)}, u32[]{:S(2)}) copy-start(f32[2,256,1024]{2,1,0:T(8,128)} %shard_map.123) | copy-start | bytes 6291460
  143.0 1.9 %copy-start.2 = (bf16[1,512,1280]{2,1,0:T(8,128)(2,1)S(1)}, bf16[1,512,1280]{2,1,0:T(8,128)(2,1)}, u32[]{:S(2)}) copy-start(bf16[1,512,1280]{2,1,0:T(8,128)(2,1)} %get-tuple-element.91) | copy-start | bytes 3932164
  (8 other events, 8.3 us)

commit v16 on v15

--- a/solution.py
+++ b/solution.py
@@ -266,6 +266,25 @@
     ).astype(jnp.bfloat16)
 
 
+def matmul_kernel(x_ref, w_ref, out_ref):
+    out_ref[...] = jnp.dot(x_ref[...], w_ref[...], preferred_element_type=jnp.float32)
+
+
+def column_matmul(x, w, start, width, lanes=256):
+    count, rows, depth = x.shape
+    first = start // lanes
+    return pl.pallas_call(
+        matmul_kernel,
+        grid=(count, width // lanes),
+        in_specs=[
+            pl.BlockSpec((None, rows, depth), lambda g, j: (g, 0, 0)),
+            pl.BlockSpec((depth, lanes), lambda g, j: (0, j + first)),
+        ],
+        out_specs=pl.BlockSpec((None, rows, lanes), lambda g, j: (g, 0, j)),
+        out_shape=jax.ShapeDtypeStruct((count, rows, width), jnp.float32),
+    )(x, w)
+
+
 def on_device(
     tokens, hidden, base_table, w_in, w_dt, conv_w, conv_b, dt_bias, a_log, d_skip, norm_gain, w_out
 ):
@@ -281,9 +300,8 @@
     rates = -jnp.exp(a_log)
     gap = jnp.zeros((strand.shape[0], 8 - margin, strand.shape[2]), strand.dtype)
     ext_f = jnp.concatenate([strand, gap, low], axis=1)
-    w_source = w_in[:, inner:]
-    w_gate = w_in[:, :inner]
-    proj_f = jnp.einsum("grd,de->gre", ext_f, w_source, preferred_element_type=jnp.float32)
+    source_width = w_in.shape[1] - inner
+    proj_f = column_matmul(ext_f, w_in, inner, source_width)
     step_f = jax.nn.softplus(
         jnp.einsum("grd,dh->grh", strand, w_dt, preferred_element_type=jnp.float32) + dt_bias
     )
@@ -291,18 +309,18 @@
     sum_f, (strand_late, high) = lax.optimization_barrier((sum_f, (strand, high)))
     ext_r = flip_lanes(jnp.concatenate([strand_late, high, gap], axis=1))
     mirrored = ext_r[:, :rows]
-    proj_r = jnp.einsum("grd,de->gre", ext_r, w_source, preferred_element_type=jnp.float32)
+    proj_r = column_matmul(ext_r, w_in, inner, source_width)
     step_r = jax.nn.softplus(
         jnp.einsum("grd,dh->grh", mirrored, w_dt, preferred_element_type=jnp.float32) + dt_bias
     )
     sum_r, pend_r = strand_terms(proj_r, step_r, conv_w, conv_b, rates, True)
     def forward_out(incoming):
-        gate_f = jnp.einsum("grd,de->gre", strand, w_gate, preferred_element_type=jnp.float32)
+        gate_f = column_matmul(strand, w_in, 0, inner)
         normed_f = finish(pend_f, incoming, gate_f, d_skip, norm_gain)
         return jnp.einsum("grk,kd->grd", normed_f, w_out, preferred_element_type=jnp.float32)
 
     in_r, out_f = exclusive_scans(sum_f, sum_r, "seq", forward_out)
-    gate_r = jnp.einsum("grd,de->gre", mirrored, w_gate, preferred_element_type=jnp.float32)
+    gate_r = column_matmul(mirrored, w_in, 0, inner)
     normed_r = finish(pend_r, in_r[1], gate_r, d_skip, norm_gain)
     w_out_mirrored = flip_lanes(w_out)
     out = out_f + jnp.einsum(

time: 159 us -> 174 us (1.094); the launches traced: 158 us -> 170 us
  Pallas kernels: 29.5 us -> 52.3 us
  matrix products: 37.2 us -> 18.4 us
  other arithmetic: 21.2 us -> 31 us
  waiting for transfers between devices: 24.4 us -> 20.2 us
  local copies, waits for them, and re-layouts: 19.7 us -> 21.7 us
    pallas_call x0 -> x4, Pallas kernels: none -> 22.6 us  [column_matmul(): pl.pallas_call(matmul_kernel, grid=(count, width // lanes), in_specs=[pl....]
    dot_general x4 -> x0, matrix products: 18.7 us -> none  [the longest x1 5.13 us: on_device(): jnp.einsum('grd,de->gre', ext_r, w_source, preferred_element_type=jnp.flo...]
    ppermute x6, waiting for transfers between devices: 24.4 us -> 20.2 us  [exclusive_scans(): decay, state = unpack(lax.ppermute(pack(*ahead[k]), axis, pairs))]
    concatenate x0 -> x1, other arithmetic: none -> 2.32 us  [on_device(): ext_f = jnp.concatenate([strand, gap, low], axis=1)]
    concatenate x6, other arithmetic: 1.81 us -> 4.07 us  [pack(): return jnp.concatenate([flat, extra], axis=1)]
    unnamed x66 -> x96, local copies, waits for them, and re-layouts: 7.43 us -> 8.26 us
  transfers between devices with their start and end apart: 8 -> 8, of which waited for: 3 -> 3; matrix products, arithmetic and copies ran while one was open for 29% -> 21% of each run, Pallas kernels for 19% -> 22%
where the time goes in v16:
time: 174 us; the launch traced here: 170 us
  Pallas kernels  52.3 us (30%)
  other arithmetic  31 us (18%)
  starting transfers between devices  25.8 us (15%)
  local copies, waits for them, and re-layouts  21.7 us (12%)
  waiting for transfers between devices  20.2 us (12%)
  matrix products  18.4 us (11%)
    pallas_call x4, Pallas kernels, column_matmul(): pl.pallas_call(matmul_kernel, grid=(count, width // lanes), in_specs=[pl....  22.6 us
    ppermute x6, waiting for transfers between devices, exclusive_scans(): decay, state = unpack(lax.ppermute(pack(*ahead[k]), axis, pairs))  20.2 us
    ppermute x6, starting transfers between devices, exclusive_scans(): decay, state = unpack(lax.ppermute(pack(*ahead[k]), axis, pairs))  19.1 us
    pallas_call x2, Pallas kernels, block_terms(): pl.pallas_call(partial(inside_kernel, reverse=reverse), grid=(blocks,), i...  11.2 us
    pallas_call x2, Pallas kernels, convolve(): pl.pallas_call(partial(conv_kernel, reverse=reverse), grid=(count, width...  10.8 us
    unnamed x96, local copies, waits for them, and re-layouts  8.26 us
    pallas_call x2, Pallas kernels, block_terms(): pl.pallas_call(state_kernel, grid=(blocks,), in_specs=[spec((Q, width)),...  7.67 us
    add x7, other arithmetic, chain(): next_decay[..., None, None] * first_state + next_state  7.16 us
  transfers between devices with their start and end apart: 8, of which 3 were waited for; matrix products, arithmetic and copies ran while one was open for 21% of the time, Pallas kernels for 22%

profile of v16, /device:TPU:24, one launch (start us, length us, event | category | flops | bytes accessed | tf_op | source)
XLA Modules:
  0.0 170.3 jit_solution(14315888000640425366)
XLA Ops:
  0.0 1.9 %fusion.9.x_ref = bf16[1,512,1024]{2,1,0:T(8,128)(2,1)S(1)} fusion(bf16[1,512,1024]{2,1,0:T(8,128)(2,1)} %param.25, bf16[4,1024]{1,0:T(4,128)(2,1)} %param.26, s32[512]{0:T(512)} %bitcast.276), kind=kOutput, calls=%fused_computation.15 | convolution fusion | flops 5769216 | bytes 2107392 | tf_op jit(solution)/shard_map/gtb,bd->gtd/dot_general | solution.py:294
  1.9 3.4 %collective-permute-start = (bf16[1,3,1024]{2,1,0:T(4,128)(2,1)S(1)}, bf16[1,3,1024]{2,1,0:T(4,128)(2,1)S(1)}, u32[]{:S(2)}, u32[]{:S(2)}) collective-permute-start(bf16[1,3,1024]{2,1,0:T(4,128)(2,1)S(1)} %get-tuple-element.114), channel_id=1, source_target_pairs={{0,2},{2,4},{4,6},{6,8},{8,10},{10,12},{12,14},{1,3},{3,5},{5,7},{... | collective-permute-start | bytes 18440 | tf_op jit(solution)/shard_map/ppermute | solution.py:298
  5.4 3.3 %collective-permute-start.1 = (bf16[1,3,1024]{2,1,0:T(4,128)(2,1)S(1)}, bf16[1,3,1024]{2,1,0:T(4,128)(2,1)S(1)}, u32[]{:S(2)}, u32[]{:S(2)}) collective-permute-start(bf16[1,3,1024]{2,1,0:T(4,128)(2,1)S(1)} %get-tuple-element.113), channel_id=1, source_target_pairs={{2,0},{4,2},{6,4},{8,6},{10,8},{12,10},{14,12},{3,1},{5,3},{7,5},{... | collective-permute-start | bytes 18440 | tf_op jit(solution)/shard_map/ppermute | solution.py:299
  16.3 5.1 %shard_map.125 = f32[1,512,1024]{2,1,0:T(8,128)} custom-call(bf16[1,512,1024]{2,1,0:T(8,128)(2,1)} %copy-done.1, bf16[1024,2304]{1,0:T(8,128)(2,1)} %w_ref.11), custom_call_target="tpu_custom_call" | custom-call | tf_op jit(solution)/shard_map/pallas_call | solution.py:276
  22.2 2.3 %pad_maximum_fusion.x_ref = bf16[1,520,1024]{2,1,0:T(8,128)(2,1)} fusion(bf16[1,3,1024]{2,1,0:T(4,128)(2,1)S(1)} %collective-permute-done, bf16[1,5,1024]{2,1,0:T(8,128)(2,1)S(1)} %broadcast_in_dim.12, bf16[1,512,1024]{2,1,0:T(8,128)(2,1)} %copy-done.1), kind=kLoop, calls=%fused_computation.29 | loop fusion | flops 3194880 | bytes 2129920 | tf_op jit(solution)/shard_map/concatenate | solution.py:302
  24.5 6.2 %shard_map.118.src_ref.halo_ref = f32[1,520,1280]{2,1,0:T(8,128)} custom-call(bf16[1,520,1024]{2,1,0:T(8,128)(2,1)} %pad_maximum_fusion.x_ref, bf16[1024,2304]{1,0:T(8,128)(2,1)} %w_ref.11), custom_call_target="tpu_custom_call" | custom-call | tf_op jit(solution)/shard_map/pallas_call | solution.py:276
  30.7 5.4 %shard_map.119 = (bf16[1,512,1280]{2,1,0:T(8,128)(2,1)}, bf16[1,1280,512]{2,1,0:T(8,128)(2,1)}) custom-call(f32[1,520,1280]{2,1,0:T(8,128)} %shard_map.118.src_ref.halo_ref, f32[1,520,1280]{2,1,0:T(8,128)} %shard_map.118.src_ref.halo_ref, f32[4,1280]{1,0:T(4,128)} %w_ref.9, f32[1,1280]{1,0:T(1,128)} %reshape.980.b_ref), custom_call_target="tpu_custom_call" | custom-call | tf_op jit(solution)/shard_map/pallas_call | solution.py:200
  36.1 3.9 %shard_map.120 = f32[2,16,64,128]{3,2,1,0:T(8,128)} custom-call(bf16[2,256,1280]{2,1,0:T(8,128)(2,1)} %bitcast.233, bf16[1,1280,512]{2,1,0:T(8,128)(2,1)} %get-tuple-element.88.x_t_ref, f32[2,256,16]{2,1,0:T(8,128)} %copy.28.to_end_ref), custom_call_target="tpu_custom_call" | custom-call | tf_op jit(solution)/shard_map/pallas_call | solution.py:133
  40.0 2.2 %fusion.34 = f32[1,16,64,128]{3,2,1,0:T(8,128)} fusion(f32[1,2,16,64,128]{4,3,2,1,0:T(8,128)} %bitcast.231, f32[16]{0:T(128)S(1)} %get-tuple-element.123, f32[16]{0:T(128)S(1)} %get-tuple-element.124), kind=kLoop, calls=%fused_computation.53 | loop fusion | flops 393216 | bytes 1572992 | tf_op jit(solution)/shard_map/add | solution.py:34
  48.0 6.3 %shard_map.121.src_ref.halo_ref = f32[1,520,1280]{2,1,0:T(8,128)} custom-call(bf16[1,520,1024]{2,1,0:T(8,128)(2,1)} %copy-done.14, bf16[1024,2304]{1,0:T(8,128)(2,1)} %w_ref.11), custom_call_target="tpu_custom_call" | custom-call | tf_op jit(solution)/shard_map/pallas_call | solution.py:276
  56.3 5.4 %shard_map.122 = (bf16[1,512,1280]{2,1,0:T(8,128)(2,1)}, bf16[1,1280,512]{2,1,0:T(8,128)(2,1)}) custom-call(f32[1,520,1280]{2,1,0:T(8,128)} %shard_map.121.src_ref.halo_ref, f32[1,520,1280]{2,1,0:T(8,128)} %shard_map.121.src_ref.halo_ref, f32[4,1280]{1,0:T(4,128)} %w_ref.9, f32[1,1280]{1,0:T(1,128)} %reshape.980.b_ref), custom_call_target="tpu_custom_call" | custom-call | tf_op jit(solution)/shard_map/pallas_call | solution.py:200
  63.6 3.8 %shard_map.123 = f32[2,16,64,128]{3,2,1,0:T(8,128)} custom-call(bf16[2,256,1280]{2,1,0:T(8,128)(2,1)} %bitcast.235, bf16[1,1280,512]{2,1,0:T(8,128)(2,1)} %get-tuple-element.92.x_t_ref, f32[2,256,16]{2,1,0:T(8,128)} %copy.34.to_end_ref), custom_call_target="tpu_custom_call" | custom-call | tf_op jit(solution)/shard_map/pallas_call | solution.py:133
  67.4 2.3 %broadcast_add_fusion = (f32[1,1,16,64,128]{4,3,2,1,0:T(8,128)}, f32[1,1,16,64,128]{4,3,2,1,0:T(8,128)S(1)}, f32[1,1,16,64,128]{4,3,2,1,0:T(8,128)}) fusion(f32[16]{0:T(128)S(1)} %copy-done.39, f32[1,2,16,64,128]{4,3,2,1,0:T(8,128)} %bitcast.245), kind=kLoop, calls=%fused_computation.66 | loop fusion | flops 131072 | bytes 2621504 | tf_op jit(solution)/shard_map/add | solution.py:34
  69.9 1.4 select_maximum_fusion.2
  71.4 2.5 %collective-permute-start.5 = (f32[1,1032,128]{2,1,0:T(8,128)}, f32[1,1032,128]{2,1,0:T(8,128)}, u32[]{:S(2)}, u32[]{:S(2)}) collective-permute-start(f32[1,1032,128]{2,1,0:T(8,128)} %select_maximum_fusion.2), channel_id=1, source_target_pairs={{0,2},{2,4},{4,6},{6,8},{8,10},{10,12},{12,14},{1,3},{3,5},{5,7},{... | collective-permute-start | bytes 1585160 | tf_op jit(solution)/shard_map/ppermute | solution.py:48
  73.9 1.4 bitcast_add_fusion.4
  77.0 4.2 %collective-permute-start.2 = (f32[1,1032,128]{2,1,0:T(8,128)}, f32[1,1032,128]{2,1,0:T(8,128)}, u32[]{:S(2)}, u32[]{:S(2)}) collective-permute-start(f32[1,1032,128]{2,1,0:T(8,128)} %select_maximum_fusion.5), channel_id=1, source_target_pairs={{2,0},{4,2},{6,4},{8,6},{10,8},{12,10},{14,12},{3,1},{5,3},{7,5},{... | collective-permute-start | bytes 1585160 | tf_op jit(solution)/shard_map/ppermute | solution.py:48
  82.7 5.1 %shard_map.127 = f32[1,512,1024]{2,1,0:T(8,128)} custom-call(bf16[1,512,1024]{2,1,0:T(8,128)(2,1)} %slice.274.x_ref, bf16[1024,2304]{1,0:T(8,128)(2,1)} %w_ref.11), custom_call_target="tpu_custom_call" | custom-call | tf_op jit(solution)/shard_map/pallas_call | solution.py:276
  87.8 5.6 %shard_map.124 = f32[2,256,1024]{2,1,0:T(8,128)} custom-call(bf16[2,256,1280]{2,1,0:T(8,128)(2,1)} %bitcast.234, f32[2,256,16]{2,1,0:T(8,128)} %copy.36.cum_ref, f32[2,16,256]{2,1,0:T(8,128)} %bitcast.253, f32[2,16,256]{2,1,0:T(8,128)} %bitcast.259), custom_call_target="tpu_custom_call" | custom-call | tf_op jit(solution)/shard_map/pallas_call | solution.py:144
  93.4 5.6 %shard_map.126 = f32[2,256,1024]{2,1,0:T(8,128)} custom-call(bf16[2,256,1280]{2,1,0:T(8,128)(2,1)} %bitcast.236, f32[2,256,16]{2,1,0:T(8,128)} %copy.39.cum_ref, f32[2,16,256]{2,1,0:T(8,128)} %bitcast.255, f32[2,16,256]{2,1,0:T(8,128)} %bitcast.260), custom_call_target="tpu_custom_call" | custom-call | tf_op jit(solution)/shard_map/pallas_call | solution.py:144
  105.7 2.0 %fusion.65 = (f32[1,1024,128]{2,1,0:T(8,128)}, f32[1,1024,128]{2,1,0:T(8,128)S(1)}) fusion(f32[1,1032,128]{2,1,0:T(8,128)} %collective-permute-done.2, f32[1,1024,128]{2,1,0:T(8,128)S(1)} %copy-done.9, f32[1024]{0:T(1024)S(1)} %mul.475), kind=kLoop, calls=%fused_computation.140 | loop fusion | flops 262144 | bytes 2101248 | tf_op jit(solution)/shard_map/slice | solution.py:76
  109.4 5.4 %collective-permute-start.3 = (f32[1,1032,128]{2,1,0:T(8,128)}, f32[1,1032,128]{2,1,0:T(8,128)}, u32[]{:S(2)}, u32[]{:S(2)}) collective-permute-start(f32[1,1032,128]{2,1,0:T(8,128)} %select_maximum_fusion.4), channel_id=1, source_target_pairs={{4,0},{6,2},{8,4},{10,6},{12,8},{14,10},{5,1},{7,3},{9,5},{11,7},{... | collective-permute-start | bytes 1585160 | tf_op jit(solution)/shard_map/ppermute | solution.py:48
  114.9 3.5 %collective-permute-done.6 = f32[1,1032,128]{2,1,0:T(8,128)} collective-permute-done((f32[1,1032,128]{2,1,0:T(8,128)}, f32[1,1032,128]{2,1,0:T(8,128)}, u32[]{:S(2)}, u32[]{:S(2)}) %collective-permute-start.6) | collective-permute-done | bytes 528416 | tf_op jit(solution)/shard_map/ppermute | solution.py:48
  121.6 2.5 %collective-permute-done.3 = f32[1,1032,128]{2,1,0:T(8,128)} collective-permute-done((f32[1,1032,128]{2,1,0:T(8,128)}, f32[1,1032,128]{2,1,0:T(8,128)}, u32[]{:S(2)}, u32[]{:S(2)}) %collective-permute-start.3) | collective-permute-done | bytes 528416 | tf_op jit(solution)/shard_map/ppermute | solution.py:48
  126.1 4.4 %collective-permute-start.4 = (f32[1,1032,128]{2,1,0:T(8,128)S(1)}, f32[1,1032,128]{2,1,0:T(8,128)S(1)}, u32[]{:S(2)}, u32[]{:S(2)}) collective-permute-start(f32[1,1032,128]{2,1,0:T(8,128)S(1)} %select_maximum_fusion.3), channel_id=1, source_target_pairs={{8,0},{10,2},{12,4},{14,6},{9,1},{11,3},{13,5},{15,7},{24,16},{26,... | collective-permute-start | bytes 1585160 | tf_op jit(solution)/shard_map/ppermute | solution.py:48
  131.9 14.2 %collective-permute-done.7 = f32[1,1032,128]{2,1,0:T(8,128)S(1)} collective-permute-done((f32[1,1032,128]{2,1,0:T(8,128)S(1)}, f32[1,1032,128]{2,1,0:T(8,128)S(1)}, u32[]{:S(2)}, u32[]{:S(2)}) %collective-permute-start.7) | collective-permute-done | bytes 528416 | tf_op jit(solution)/shard_map/ppermute | solution.py:48
  148.8 1.7 %fusion.7 = f32[1,512,1024]{2,1,0:T(8,128)S(1)} fusion(f32[2,256,1024]{2,1,0:T(8,128)S(1)} %fusion.68, f32[2,256,1024]{2,1,0:T(8,128)S(1)} %copy-done.17, f32[1,512,1024]{2,1,0:T(8,128)S(1)} %copy-done.19, f32[512,16]{0,1:T(8,128)S(1)} %bitcast.264, bf16[1,512,1280]{2,1,0:T(8,128)(2,1)S(1)} %copy-done.4, f32[1024]{0:T(1024)S(1)} %copy-done.33, ...), kind=kOutput, calls=%fused_computation.11 | convolution fusion | flops 105938944 | bytes 9483264 | tf_op jit(solution)/shard_map/grh,hk->grk/dot_general | solution.py:256
  151.3 2.6 %convolution_bitcast_fusion = f32[1,512,1024]{2,1,0:T(8,128)} fusion(bf16[1024,1024]{1,0:T(8,128)(2,1)S(1)} %copy-done, f32[1,512,1024]{2,1,0:T(8,128)S(1)} %fusion.7, f32[1024]{0:T(1024)S(1)} %copy-done.44, f32[512]{0:T(512)S(1)} %add_rsqrt_fusion.1), kind=kOutput, calls=%fused_computation.24 | convolution fusion | flops 1075314688 | bytes 6297600 | tf_op jit(solution)/shard_map/grk,kd->grd/dot_general | solution.py:320
  157.0 1.7 %fusion.5 = f32[1,512,1024]{2,1,0:T(8,128)S(1)} fusion(f32[2,256,1024]{2,1,0:T(8,128)S(1)} %fusion.69, f32[2,256,1024]{2,1,0:T(8,128)S(1)} %copy-done.16, f32[1,512,1024]{2,1,0:T(8,128)S(1)} %copy-done.20, f32[512,16]{0,1:T(8,128)S(1)} %bitcast.265, bf16[1,512,1280]{2,1,0:T(8,128)(2,1)S(1)} %copy-done.5, f32[1024]{0:T(1024)S(1)} %copy-done.33, ...), kind=kOutput, calls=%fused_computation.7 | convolution fusion | flops 105938944 | bytes 9483264 | tf_op jit(solution)/shard_map/grh,hk->grk/dot_general | solution.py:256
  158.8 1.4 copy-done.18
  160.3 6.4 %fusion.10 = f32[512,1024]{1,0:T(8,128)} fusion(bf16[1024,1024]{1,0:T(8,128)(2,1)S(1)} %copy-done, f32[1,512,1024]{2,1,0:T(8,128)} %copy-done.18, f32[512]{0:T(512)S(1)} %add_rsqrt_fusion, f32[1024]{0:T(1024)S(1)} %copy-done.44), kind=kOutput, calls=%fused_computation.16 | convolution fusion | flops 3226992640 | bytes 6297600 | tf_op jit(solution)/shard_map/grk,kd->grd/dot_general | solution.py:326
  166.7 3.5 %fusion.4 = bf16[1,512,1024]{2,1,0:T(8,128)(2,1)} fusion(f32[1,512,1024]{2,1,0:T(8,128)} %convolution_bitcast_fusion, f32[512,1024]{1,0:T(8,128)} %fusion.10), kind=kLoop, calls=%fused_computation.5 | loop fusion | flops 1048576 | bytes 5242880 | tf_op jit(solution)/shard_map/convert_element_type | solution.py:329
  (194 shorter events, 42.9 us)
Async XLA Ops:
  0.0 150.8 %copy-start = (bf16[1024,1024]{1,0:T(8,128)(2,1)S(1)}, bf16[1024,1024]{1,0:T(8,128)(2,1)}, u32[]{:S(2)}) copy-start(bf16[1024,1024]{1,0:T(8,128)(2,1)} %param.35) | copy-start | bytes 6291460
  0.0 9.9 %copy-start.45 = (f32[16]{0:T(128)S(1)}, f32[16]{0:T(128)}, u32[]{:S(2)}) copy-start(f32[16]{0:T(128)} %param.32) | copy-start | bytes 196
  0.0 9.9 %copy-start.26 = (bf16[1024,16]{0,1:T(8,128)(2,1)S(1)}, bf16[1024,16]{0,1:T(8,128)(2,1)}, u32[]{:S(2)}) copy-start(bf16[1024,16]{0,1:T(8,128)(2,1)} %param.28) | copy-start | bytes 98308
  0.0 9.9 %copy-start.41 = (f32[16]{0:T(128)S(1)}, f32[16]{0:T(128)}, u32[]{:S(2)}) copy-start(f32[16]{0:T(128)} %param.31) | copy-start | bytes 196
  0.0 13.4 %copy-start.30 = (f32[1280]{0:T(1024)S(1)}, f32[1280]{0:T(1024)}, u32[]{:S(2)}) copy-start(f32[1280]{0:T(1024)} %param.30) | copy-start | bytes 15364
  1.9 14.4 %copy-start.1 = (bf16[1,512,1024]{2,1,0:T(8,128)(2,1)}, bf16[1,512,1024]{2,1,0:T(8,128)(2,1)S(1)}, u32[]{:S(2)}) copy-start(bf16[1,512,1024]{2,1,0:T(8,128)(2,1)S(1)} %fusion.9.x_ref) | copy-start | bytes 3145732
  1.9 20.2 %collective-permute-start = (bf16[1,3,1024]{2,1,0:T(4,128)(2,1)S(1)}, bf16[1,3,1024]{2,1,0:T(4,128)(2,1)S(1)}, u32[]{:S(2)}, u32[]{:S(2)}) collective-permute-start(bf16[1,3,1024]{2,1,0:T(4,128)(2,1)S(1)} %get-tuple-element.114), channel_id=1, source_target_pairs={{0,2},{2,4},{4,6},{6,8},{8,10},{10,12},{12,14},{1,3},{3,5},{5,7},{... | collective-permute-start | bytes 18440 | tf_op jit(solution)/shard_map/ppermute | solution.py:298
  5.4 36.8 %collective-permute-start.1 = (bf16[1,3,1024]{2,1,0:T(4,128)(2,1)S(1)}, bf16[1,3,1024]{2,1,0:T(4,128)(2,1)S(1)}, u32[]{:S(2)}, u32[]{:S(2)}) collective-permute-start(bf16[1,3,1024]{2,1,0:T(4,128)(2,1)S(1)} %get-tuple-element.113), channel_id=1, source_target_pairs={{2,0},{4,2},{6,4},{8,6},{10,8},{12,10},{14,12},{3,1},{5,3},{7,5},{... | collective-permute-start | bytes 18440 | tf_op jit(solution)/shard_map/ppermute | solution.py:299
  12.0 9.3 %copy-start.24 = (f32[1,2,16,256]{3,2,1,0:T(8,128)}, f32[1,2,16,256]{3,2,1,0:T(8,128)S(1)}, u32[]{:S(2)}) copy-start(f32[1,2,16,256]{3,2,1,0:T(8,128)S(1)} %get-tuple-element.104) | copy-start | bytes 98308
  12.7 27.2 %copy-start.31 = (f32[16]{0:T(128)}, f32[16]{0:T(128)S(1)}, u32[]{:S(2)}) copy-start(f32[16]{0:T(128)S(1)} %get-tuple-element.123) | copy-start | bytes 196
  16.3 5.1 %copy-start.42 = (f32[16]{0:T(128)S(1)}, f32[16]{0:T(128)}, u32[]{:S(2)}) copy-start(f32[16]{0:T(128)} %param.33) | copy-start | bytes 196
  36.1 6.0 %copy-start.2 = (bf16[1,512,1024]{2,1,0:T(8,128)(2,1)S(1)}, bf16[1,512,1024]{2,1,0:T(8,128)(2,1)}, u32[]{:S(2)}) copy-start(bf16[1,512,1024]{2,1,0:T(8,128)(2,1)} %copy-done.1) | copy-start | bytes 3145732
  46.8 34.5 %copy-start.25 = (f32[1,2,256,16]{2,3,1,0:T(8,128)}, f32[1,2,256,16]{2,3,1,0:T(8,128)S(1)}, u32[]{:S(2)}) copy-start(f32[1,2,256,16]{2,3,1,0:T(8,128)S(1)} %get-tuple-element.102) | copy-start | bytes 98308
  46.9 7.4 %copy-start.28 = (f32[2,16]{1,0:T(2,128)}, f32[2,16]{1,0:T(2,128)S(1)}, u32[]{:S(2)}) copy-start(f32[2,16]{1,0:T(2,128)S(1)} %get-tuple-element.98) | copy-start | bytes 388
  48.0 7.2 %copy-start.15 = (bf16[1,520,1024]{2,1,0:T(8,128)(2,1)S(1)}, bf16[1,520,1024]{2,1,0:T(8,128)(2,1)}, u32[]{:S(2)}) copy-start(bf16[1,520,1024]{2,1,0:T(8,128)(2,1)} %copy-done.14) | copy-start | bytes 3194884
  69.9 6.2 %copy-start.36 = (f32[1,1,16]{2,1,0:T(1,128)S(1)}, f32[1,1,16]{2,1,0:T(1,128)}, u32[]{:S(2)}) copy-start(f32[1,1,16]{2,1,0:T(1,128)} %get-tuple-element.120) | copy-start | bytes 196
  71.4 28.6 %collective-permute-start.5 = (f32[1,1032,128]{2,1,0:T(8,128)}, f32[1,1032,128]{2,1,0:T(8,128)}, u32[]{:S(2)}, u32[]{:S(2)}) collective-permute-start(f32[1,1032,128]{2,1,0:T(8,128)} %select_maximum_fusion.2), channel_id=1, source_target_pairs={{0,2},{2,4},{4,6},{6,8},{8,10},{10,12},{12,14},{1,3},{3,5},{5,7},{... | collective-permute-start | bytes 1585160 | tf_op jit(solution)/shard_map/ppermute | solution.py:48
  77.0 27.9 %collective-permute-start.2 = (f32[1,1032,128]{2,1,0:T(8,128)}, f32[1,1032,128]{2,1,0:T(8,128)}, u32[]{:S(2)}, u32[]{:S(2)}) collective-permute-start(f32[1,1032,128]{2,1,0:T(8,128)} %select_maximum_fusion.5), channel_id=1, source_target_pairs={{2,0},{4,2},{6,4},{8,6},{10,8},{12,10},{14,12},{3,1},{5,3},{7,5},{... | collective-permute-start | bytes 1585160 | tf_op jit(solution)/shard_map/ppermute | solution.py:48
  93.4 5.6 %copy-start.43 = (f32[1,1,16]{2,1,0:T(1,128)S(1)}, f32[1,1,16]{2,1,0:T(1,128)}, u32[]{:S(2)}) copy-start(f32[1,1,16]{2,1,0:T(1,128)} %get-tuple-element.119) | copy-start | bytes 196
  93.4 5.6 %copy-start.3 = (f32[2,16,64,128]{3,2,1,0:T(8,128)S(1)}, f32[2,16,64,128]{3,2,1,0:T(8,128)}, u32[]{:S(2)}) copy-start(f32[2,16,64,128]{3,2,1,0:T(8,128)} %shard_map.120) | copy-start | bytes 3145732
  93.4 5.6 %copy-start.32 = (f32[16]{0:T(128)S(1)}, f32[16]{0:T(128)}, u32[]{:S(2)}) copy-start(f32[16]{0:T(128)} %copy-done.31) | copy-start | bytes 196
  93.4 6.6 %copy-start.27 = (f32[1,16]{1,0:T(1,128)S(1)}, f32[1,16]{1,0:T(1,128)}, u32[]{:S(2)}) copy-start(f32[1,16]{1,0:T(1,128)} %get-tuple-element.93) | copy-start | bytes 196
  100.0 5.6 %copy-start.37 = (f32[1,1,16]{2,1,0:T(1,128)S(1)}, f32[1,1,16]{2,1,0:T(1,128)}, u32[]{:S(2)}) copy-start(f32[1,1,16]{2,1,0:T(1,128)} %get-tuple-element.120) | copy-start | bytes 196
  100.0 5.7 %copy-start.9 = (f32[1,1024,128]{2,1,0:T(8,128)S(1)}, f32[1,1024,128]{2,1,0:T(8,128)}, u32[]{:S(2)}) copy-start(f32[1,1024,128]{2,1,0:T(8,128)} %copy-done.8) | copy-start | bytes 1572868
  103.6 14.8 %collective-permute-start.6 = (f32[1,1032,128]{2,1,0:T(8,128)}, f32[1,1032,128]{2,1,0:T(8,128)}, u32[]{:S(2)}, u32[]{:S(2)}) collective-permute-start(f32[1,1032,128]{2,1,0:T(8,128)} %select_maximum_fusion.1), channel_id=1, source_target_pairs={{0,4},{2,6},{4,8},{6,10},{8,12},{10,14},{1,5},{3,7},{5,9},{7,11},{... | collective-permute-start | bytes 1585160 | tf_op jit(solution)/shard_map/ppermute | solution.py:48
  107.7 12.4 %copy-start.11 = (f32[1,16,64,128]{3,2,1,0:T(8,128)S(1)}, f32[1,16,64,128]{3,2,1,0:T(8,128)}, u32[]{:S(2)}) copy-start(f32[1,16,64,128]{3,2,1,0:T(8,128)} %copy-done.10) | copy-start | bytes 1572868
  109.4 14.7 %collective-permute-start.3 = (f32[1,1032,128]{2,1,0:T(8,128)}, f32[1,1032,128]{2,1,0:T(8,128)}, u32[]{:S(2)}, u32[]{:S(2)}) collective-permute-start(f32[1,1032,128]{2,1,0:T(8,128)} %select_maximum_fusion.4), channel_id=1, source_target_pairs={{4,0},{6,2},{8,4},{10,6},{12,8},{14,10},{5,1},{7,3},{9,5},{11,7},{... | collective-permute-start | bytes 1585160 | tf_op jit(solution)/shard_map/ppermute | solution.py:48
  114.9 9.9 %copy-start.13 = (f32[1,1024,128]{2,1,0:T(8,128)S(1)}, f32[1,1024,128]{2,1,0:T(8,128)}, u32[]{:S(2)}) copy-start(f32[1,1024,128]{2,1,0:T(8,128)} %copy-done.12) | copy-start | bytes 1572868
  120.3 25.8 %collective-permute-start.7 = (f32[1,1032,128]{2,1,0:T(8,128)S(1)}, f32[1,1032,128]{2,1,0:T(8,128)S(1)}, u32[]{:S(2)}, u32[]{:S(2)}) collective-permute-start(f32[1,1032,128]{2,1,0:T(8,128)S(1)} %select_maximum_fusion), channel_id=1, source_target_pairs={{0,8},{2,10},{4,12},{6,14},{1,9},{3,11},{5,13},{7,15},{16,24},{18,... | collective-permute-start | bytes 1585160 | tf_op jit(solution)/shard_map/ppermute | solution.py:48
  126.0 20.3 %copy-start.22 = (f32[1,1,16,64,128]{4,3,2,1,0:T(8,128)S(1)}, f32[1,1,16,64,128]{4,3,2,1,0:T(8,128)}, u32[]{:S(2)}) copy-start(f32[1,1,16,64,128]{4,3,2,1,0:T(8,128)} %slice_add_fusion) | copy-start | bytes 1572868
  126.0 20.3 %copy-start.40 = (f32[2,16]{1,0:T(2,128)S(1)}, f32[2,16]{1,0:T(2,128)}, u32[]{:S(2)}) copy-start(f32[2,16]{1,0:T(2,128)} %pad_bitcast_fusion.1) | copy-start | bytes 388
  126.1 27.8 %collective-permute-start.4 = (f32[1,1032,128]{2,1,0:T(8,128)S(1)}, f32[1,1032,128]{2,1,0:T(8,128)S(1)}, u32[]{:S(2)}, u32[]{:S(2)}) collective-permute-start(f32[1,1032,128]{2,1,0:T(8,128)S(1)} %select_maximum_fusion.3), channel_id=1, source_target_pairs={{8,0},{10,2},{12,4},{14,6},{9,1},{11,3},{13,5},{15,7},{24,16},{26,... | collective-permute-start | bytes 1585160 | tf_op jit(solution)/shard_map/ppermute | solution.py:48
  (23 other events, 47.6 us)

commit v17 on v15

--- a/solution.py
+++ b/solution.py
@@ -297,12 +297,18 @@
     )
     sum_r, pend_r = strand_terms(proj_r, step_r, conv_w, conv_b, rates, True)
     def forward_out(incoming):
-        gate_f = jnp.einsum("grd,de->gre", strand, w_gate, preferred_element_type=jnp.float32)
+        incoming, (strand_gate, mirrored_gate) = lax.optimization_barrier(
+            (incoming, (strand, mirrored))
+        )
+        gate_f = jnp.einsum("grd,de->gre", strand_gate, w_gate, preferred_element_type=jnp.float32)
+        gate_r = jnp.einsum(
+            "grd,de->gre", mirrored_gate, w_gate, preferred_element_type=jnp.float32
+        )
         normed_f = finish(pend_f, incoming, gate_f, d_skip, norm_gain)
-        return jnp.einsum("grk,kd->grd", normed_f, w_out, preferred_element_type=jnp.float32)
-
-    in_r, out_f = exclusive_scans(sum_f, sum_r, "seq", forward_out)
-    gate_r = jnp.einsum("grd,de->gre", mirrored, w_gate, preferred_element_type=jnp.float32)
+        out_f = jnp.einsum("grk,kd->grd", normed_f, w_out, preferred_element_type=jnp.float32)
+        return out_f, gate_r
+
+    in_r, (out_f, gate_r) = exclusive_scans(sum_f, sum_r, "seq", forward_out)
     normed_r = finish(pend_r, in_r[1], gate_r, d_skip, norm_gain)
     w_out_mirrored = flip_lanes(w_out)
     out = out_f + jnp.einsum(

time: 159 us -> 161 us (1.013)
  other arithmetic: 21.2 us -> 28.2 us
  waiting for transfers between devices: 24.4 us -> 20 us
  matrix products: 37.2 us -> 34.1 us
    ppermute x6, waiting for transfers between devices: 24.4 us -> 20 us  [exclusive_scans(): decay, state = unpack(lax.ppermute(pack(*ahead[k]), axis, pairs))]
    dot_general x2, matrix products: 8.75 us -> 5.79 us  [the longest x1 2.92 us: forward_out(): jnp.einsum('grd,de->gre', strand_gate, w_gate, preferred_element_type=jnp...]
    concatenate x6, other arithmetic: 1.81 us -> 4.08 us  [pack(): return jnp.concatenate([flat, extra], axis=1)]
    dot_general x1, matrix products: 5.13 us -> 3.08 us  [on_device(): jnp.einsum('grd,de->gre', ext_r, w_source, preferred_element_type=jnp.flo...]
    unnamed x66 -> x94, local copies, waits for them, and re-layouts: 7.43 us -> 7.39 us
  transfers between devices with their start and end apart: 8 -> 8, of which waited for: 3 -> 3; matrix products, arithmetic and copies ran while one was open for 29% -> 31% of each run, Pallas kernels for 19% -> 18%
where the time goes in v17:
time: 161 us; the launch traced here: 160 us
  matrix products  34.1 us (21%)
  Pallas kernels  29.5 us (18%)
  other arithmetic  28.2 us (18%)
  starting transfers between devices  26.2 us (16%)
  local copies, waits for them, and re-layouts  21.1 us (13%)
  waiting for transfers between devices  20 us (12%)
    ppermute x6, waiting for transfers between devices, exclusive_scans(): decay, state = unpack(lax.ppermute(pack(*ahead[k]), axis, pairs))  20 us
    ppermute x6, starting transfers between devices, exclusive_scans(): decay, state = unpack(lax.ppermute(pack(*ahead[k]), axis, pairs))  19.5 us
    pallas_call x2, Pallas kernels, block_terms(): pl.pallas_call(partial(inside_kernel, reverse=reverse), grid=(blocks,), i...  11.1 us
    pallas_call x2, Pallas kernels, convolve(): pl.pallas_call(partial(conv_kernel, reverse=reverse), grid=(count, width...  10.8 us
    pallas_call x2, Pallas kernels, block_terms(): pl.pallas_call(state_kernel, grid=(blocks,), in_specs=[spec((Q, width)),...  7.57 us
    unnamed x94, local copies, waits for them, and re-layouts  7.39 us
    dot_general x1, matrix products, on_device(): jnp.einsum('grk,kd->grd', normed_r, w_out_mirrored, preferred_element_typ...  6.41 us
    add x7, other arithmetic, chain(): next_decay[..., None, None] * first_state + next_state  5.89 us
  transfers between devices with their start and end apart: 8, of which 3 were waited for; matrix products, arithmetic and copies ran while one was open for 31% of the time, Pallas kernels for 18%

profile of v17, /device:TPU:24, one launch (start us, length us, event | category | flops | bytes accessed | tf_op | source)
XLA Modules:
  0.0 159.9 jit_solution(16581206030123086170)
XLA Ops:
  0.0 1.9 %fusion.10 = bf16[1,512,1024]{2,1,0:T(8,128)(2,1)S(1)} fusion(bf16[1,512,1024]{2,1,0:T(8,128)(2,1)} %param.25, bf16[4,1024]{1,0:T(4,128)(2,1)} %param.26, s32[512]{0:T(512)} %bitcast.295), kind=kOutput, calls=%fused_computation.19 | convolution fusion | flops 5769216 | bytes 2107392 | tf_op jit(solution)/shard_map/gtb,bd->gtd/dot_general | solution.py:275
  2.0 3.4 %collective-permute-start = (bf16[1,3,1024]{2,1,0:T(4,128)(2,1)S(1)}, bf16[1,3,1024]{2,1,0:T(4,128)(2,1)S(1)}, u32[]{:S(2)}, u32[]{:S(2)}) collective-permute-start(bf16[1,3,1024]{2,1,0:T(4,128)(2,1)S(1)} %get-tuple-element.122), channel_id=1, source_target_pairs={{0,2},{2,4},{4,6},{6,8},{8,10},{10,12},{12,14},{1,3},{3,5},{5,7},{... | collective-permute-start | bytes 18440 | tf_op jit(solution)/shard_map/ppermute | solution.py:279
  5.4 3.3 %collective-permute-start.1 = (bf16[1,3,1024]{2,1,0:T(4,128)(2,1)S(1)}, bf16[1,3,1024]{2,1,0:T(4,128)(2,1)S(1)}, u32[]{:S(2)}, u32[]{:S(2)}) collective-permute-start(bf16[1,3,1024]{2,1,0:T(4,128)(2,1)S(1)} %get-tuple-element.121), channel_id=1, source_target_pairs={{2,0},{4,2},{6,4},{8,6},{10,8},{12,10},{14,12},{3,1},{5,3},{7,5},{... | collective-permute-start | bytes 18440 | tf_op jit(solution)/shard_map/ppermute | solution.py:280
  16.0 4.8 %convolution_bitcast_fusion.1.src_ref.halo_ref = f32[1,520,1280]{2,1,0:T(8,128)} fusion(bf16[1024,2304]{1,0:T(8,128)(2,1)} %param.27, bf16[1,3,1024]{2,1,0:T(4,128)(2,1)S(1)} %collective-permute-done, bf16[1,5,1024]{2,1,0:T(8,128)(2,1)S(1)} %broadcast_in_dim.12, bf16[1,512,1024]{2,1,0:T(8,128)(2,1)S(1)} %fusion.10), kind=kOutput, calls=%fused_computation.4 | convolution fusion | flops 1366343680 | bytes 6348800 | tf_op jit(solution)/shard_map/grd,de->gre/dot_general | solution.py:286
  20.8 5.4 %shard_map.118 = (bf16[1,512,1280]{2,1,0:T(8,128)(2,1)}, bf16[1,1280,512]{2,1,0:T(8,128)(2,1)}) custom-call(f32[1,520,1280]{2,1,0:T(8,128)} %convolution_bitcast_fusion.1.src_ref.halo_ref, f32[1,520,1280]{2,1,0:T(8,128)} %convolution_bitcast_fusion.1.src_ref.halo_ref, f32[4,1280]{1,0:T(4,128)} %w_ref.3, f32[1,1280]{1,0:T(1,128)} %reshape.1012.b_ref), custom_call_target="tpu_custom_call" | custom-call | tf_op jit(solution)/shard_map/pallas_call | solution.py:200
  26.3 3.8 %shard_map.119 = f32[2,16,64,128]{3,2,1,0:T(8,128)} custom-call(bf16[2,256,1280]{2,1,0:T(8,128)(2,1)} %bitcast.251, bf16[1,1280,512]{2,1,0:T(8,128)(2,1)} %get-tuple-element.92.x_t_ref, f32[2,256,16]{2,1,0:T(8,128)} %copy.28.to_end_ref), custom_call_target="tpu_custom_call" | custom-call | tf_op jit(solution)/shard_map/pallas_call | solution.py:133
  30.0 1.5 fusion.47
  32.7 2.5 %fusion.22 = bf16[520,1024]{1,0:T(8,128)(2,1)S(1)} fusion(bf16[1,5,1024]{2,1,0:T(8,128)(2,1)S(1)} %broadcast_in_dim.12, bf16[1,3,1024]{2,1,0:T(4,128)(2,1)S(1)} %collective-permute-done.1, bf16[1,512,1024]{2,1,0:T(8,128)(2,1)} %copy-done.15), kind=kOutput, calls=%fused_computation.34 | convolution fusion | flops 1096343552 | bytes 2129920 | tf_op jit(solution)/shard_map/...d,de->...e/dot_general | solution.py:28
  36.7 3.1 %convolution_bitcast_fusion.src_ref.halo_ref = f32[1,520,1280]{2,1,0:T(8,128)} fusion(bf16[520,1024]{1,0:T(8,128)(2,1)S(1)} %fusion.22, bf16[1024,2304]{1,0:T(8,128)(2,1)S(1)} %bitcast.297), kind=kOutput, calls=%fused_computation.3 | convolution fusion | flops 1363148800 | bytes 6348800 | tf_op jit(solution)/shard_map/grd,de->gre/dot_general | solution.py:294
  43.9 2.5 %collective-permute-start.5 = (f32[1,1032,128]{2,1,0:T(8,128)}, f32[1,1032,128]{2,1,0:T(8,128)}, u32[]{:S(2)}, u32[]{:S(2)}) collective-permute-start(f32[1,1032,128]{2,1,0:T(8,128)} %select_maximum_fusion.2), channel_id=1, source_target_pairs={{0,2},{2,4},{4,6},{6,8},{8,10},{10,12},{12,14},{1,3},{3,5},{5,7},{... | collective-permute-start | bytes 1585160 | tf_op jit(solution)/shard_map/ppermute | solution.py:48
  47.3 5.4 %shard_map.120 = (bf16[1,512,1280]{2,1,0:T(8,128)(2,1)}, bf16[1,1280,512]{2,1,0:T(8,128)(2,1)}) custom-call(f32[1,520,1280]{2,1,0:T(8,128)} %convolution_bitcast_fusion.src_ref.halo_ref, f32[1,520,1280]{2,1,0:T(8,128)} %convolution_bitcast_fusion.src_ref.halo_ref, f32[4,1280]{1,0:T(4,128)} %w_ref.3, f32[1,1280]{1,0:T(1,128)} %reshape.1012.b_ref), custom_call_target="tpu_custom_call" | custom-call | tf_op jit(solution)/shard_map/pallas_call | solution.py:200
  53.8 3.8 %shard_map.121 = f32[2,16,64,128]{3,2,1,0:T(8,128)} custom-call(bf16[2,256,1280]{2,1,0:T(8,128)(2,1)} %bitcast.247, bf16[1,1280,512]{2,1,0:T(8,128)(2,1)} %get-tuple-element.96.x_t_ref, f32[2,256,16]{2,1,0:T(8,128)} %copy.34.to_end_ref), custom_call_target="tpu_custom_call" | custom-call | tf_op jit(solution)/shard_map/pallas_call | solution.py:133
  57.5 2.1 %broadcast_add_fusion = (f32[1,1,16,64,128]{4,3,2,1,0:T(8,128)}, f32[1,1,16,64,128]{4,3,2,1,0:T(8,128)S(1)}, f32[1,1,16,64,128]{4,3,2,1,0:T(8,128)S(1)}) fusion(f32[16]{0:T(128)S(1)} %copy-done.35, f32[1,2,16,64,128]{4,3,2,1,0:T(8,128)} %bitcast.261), kind=kLoop, calls=%fused_computation.80 | loop fusion | flops 131072 | bytes 2621504 | tf_op jit(solution)/shard_map/add | solution.py:34
  62.2 1.5 select_maximum_fusion.5
  63.7 4.4 %collective-permute-start.2 = (f32[1,1032,128]{2,1,0:T(8,128)}, f32[1,1032,128]{2,1,0:T(8,128)}, u32[]{:S(2)}, u32[]{:S(2)}) collective-permute-start(f32[1,1032,128]{2,1,0:T(8,128)} %select_maximum_fusion.5), channel_id=1, source_target_pairs={{2,0},{4,2},{6,4},{8,6},{10,8},{12,10},{14,12},{3,1},{5,3},{7,5},{... | collective-permute-start | bytes 1585160 | tf_op jit(solution)/shard_map/ppermute | solution.py:48
  69.6 5.5 %shard_map.122 = f32[2,256,1024]{2,1,0:T(8,128)} custom-call(bf16[2,256,1280]{2,1,0:T(8,128)(2,1)} %bitcast.252, f32[2,256,16]{2,1,0:T(8,128)} %copy.36.cum_ref, f32[2,16,256]{2,1,0:T(8,128)} %bitcast.272, f32[2,16,256]{2,1,0:T(8,128)} %bitcast.278), custom_call_target="tpu_custom_call" | custom-call | tf_op jit(solution)/shard_map/pallas_call | solution.py:144
  75.2 5.6 %shard_map.123 = f32[2,256,1024]{2,1,0:T(8,128)} custom-call(bf16[2,256,1280]{2,1,0:T(8,128)(2,1)} %bitcast.248, f32[2,256,16]{2,1,0:T(8,128)} %copy.39.cum_ref, f32[2,16,256]{2,1,0:T(8,128)} %bitcast.274, f32[2,16,256]{2,1,0:T(8,128)} %bitcast.280), custom_call_target="tpu_custom_call" | custom-call | tf_op jit(solution)/shard_map/pallas_call | solution.py:144
  81.7 2.4 %fusion.51 = f32[512,1024]{1,0:T(8,128)} fusion(f32[512,16]{0,1:T(8,128)S(1)} %bitcast.279, s32[1024]{0:T(1024)S(1)} %copy-done.25, s32[1024]{0:T(1024)S(1)} %copy-done.26, pred[1024]{0:T(1024)(128)(4,1)S(1)} %copy-done.37), kind=kOutput, calls=%fused_computation.86 | convolution fusion | flops 100696064 | bytes 2139136 | tf_op jit(solution)/shard_map/grh,hk->grk/dot_general | solution.py:256
  89.9 2.0 %fusion.80 = (f32[1,1024,128]{2,1,0:T(8,128)}, f32[1,1024,128]{2,1,0:T(8,128)S(1)}) fusion(f32[1,1032,128]{2,1,0:T(8,128)} %collective-permute-done.2, f32[1,1024,128]{2,1,0:T(8,128)S(1)} %copy-done.10, f32[1024]{0:T(1024)S(1)} %mul.484), kind=kLoop, calls=%fused_computation.156 | loop fusion | flops 262144 | bytes 2101248 | tf_op jit(solution)/shard_map/slice | solution.py:76
  93.6 5.3 %collective-permute-start.3 = (f32[1,1032,128]{2,1,0:T(8,128)}, f32[1,1032,128]{2,1,0:T(8,128)}, u32[]{:S(2)}, u32[]{:S(2)}) collective-permute-start(f32[1,1032,128]{2,1,0:T(8,128)} %select_maximum_fusion.4), channel_id=1, source_target_pairs={{4,0},{6,2},{8,4},{10,6},{12,8},{14,10},{5,1},{7,3},{9,5},{11,7},{... | collective-permute-start | bytes 1585160 | tf_op jit(solution)/shard_map/ppermute | solution.py:48
  99.1 3.5 %collective-permute-done.6 = f32[1,1032,128]{2,1,0:T(8,128)} collective-permute-done((f32[1,1032,128]{2,1,0:T(8,128)}, f32[1,1032,128]{2,1,0:T(8,128)}, u32[]{:S(2)}, u32[]{:S(2)}) %collective-permute-start.6) | collective-permute-done | bytes 528416 | tf_op jit(solution)/shard_map/ppermute | solution.py:48
  104.5 1.3 collective-permute-start.7
  105.8 2.5 %collective-permute-done.3 = f32[1,1032,128]{2,1,0:T(8,128)} collective-permute-done((f32[1,1032,128]{2,1,0:T(8,128)}, f32[1,1032,128]{2,1,0:T(8,128)}, u32[]{:S(2)}, u32[]{:S(2)}) %collective-permute-start.3) | collective-permute-done | bytes 528416 | tf_op jit(solution)/shard_map/ppermute | solution.py:48
  110.3 4.6 %collective-permute-start.4 = (f32[1,1032,128]{2,1,0:T(8,128)S(1)}, f32[1,1032,128]{2,1,0:T(8,128)S(1)}, u32[]{:S(2)}, u32[]{:S(2)}) collective-permute-start(f32[1,1032,128]{2,1,0:T(8,128)S(1)} %select_maximum_fusion.3), channel_id=1, source_target_pairs={{8,0},{10,2},{12,4},{14,6},{9,1},{11,3},{13,5},{15,7},{24,16},{26,... | collective-permute-start | bytes 1585160 | tf_op jit(solution)/shard_map/ppermute | solution.py:48
  116.3 14.0 %collective-permute-done.7 = f32[1,1032,128]{2,1,0:T(8,128)S(1)} collective-permute-done((f32[1,1032,128]{2,1,0:T(8,128)S(1)}, f32[1,1032,128]{2,1,0:T(8,128)S(1)}, u32[]{:S(2)}, u32[]{:S(2)}) %collective-permute-start.7) | collective-permute-done | bytes 528416 | tf_op jit(solution)/shard_map/ppermute | solution.py:48
  130.6 2.9 %fusion.17 = f32[512,1024]{1,0:T(8,128)S(1)} fusion(bf16[1024,2304]{1,0:T(8,128)(2,1)} %param.27, bf16[1,512,1024]{2,1,0:T(8,128)(2,1)S(1)} %copy-done.16), kind=kOutput, calls=%fused_computation.30 | convolution fusion | flops 1073741824 | bytes 5242880 | tf_op jit(solution)/shard_map/grd,de->gre/dot_general | solution.py:303
  135.5 1.7 %bitcast_multiply_fusion.1 = f32[1,512,1024]{2,1,0:T(8,128)S(1)} fusion(f32[2,256,1024]{2,1,0:T(8,128)S(1)} %fusion.83, f32[2,256,1024]{2,1,0:T(8,128)S(1)} %copy-done.17, f32[512,1024]{1,0:T(8,128)S(1)} %fusion.17, f32[512,16]{0,1:T(8,128)S(1)} %bitcast.284, bf16[1,512,1280]{2,1,0:T(8,128)(2,1)S(1)} %copy-done.6, f32[1024]{0:T(1024)S(1)} %mul.510, ...), kind=kOutput, calls=%fused_computation.14 | convolution fusion | flops 105938944 | bytes 9483264 | tf_op jit(solution)/shard_map/grh,hk->grk/dot_general | solution.py:256
  138.5 2.9 %fusion.19 = f32[1,512,1024]{2,1,0:T(8,128)S(1)} fusion(bf16[1024,2304]{1,0:T(8,128)(2,1)} %param.27, bf16[1,512,1024]{2,1,0:T(8,128)(2,1)S(1)} %copy-done.21), kind=kOutput, calls=%fused_computation.32 | convolution fusion | flops 1073741824 | bytes 5242880 | tf_op jit(solution)/shard_map/grd,de->gre/dot_general | solution.py:304
  141.4 2.6 %convolution_bitcast_fusion.2 = f32[1,512,1024]{2,1,0:T(8,128)} fusion(bf16[1024,1024]{1,0:T(8,128)(2,1)S(1)} %copy-done, f32[1,512,1024]{2,1,0:T(8,128)S(1)} %bitcast_multiply_fusion.1, f32[1024]{0:T(1024)S(1)} %copy-done.42, f32[512]{0:T(512)S(1)} %add_rsqrt_fusion.1), kind=kOutput, calls=%fused_computation.33 | convolution fusion | flops 1075314688 | bytes 6297600 | tf_op jit(solution)/shard_map/grk,kd->grd/dot_general | solution.py:308
  148.4 1.4 copy-done.4
  150.0 6.4 %fusion.11 = f32[512,1024]{1,0:T(8,128)} fusion(bf16[1024,1024]{1,0:T(8,128)(2,1)S(1)} %copy-done, f32[1,512,1024]{2,1,0:T(8,128)} %copy-done.4, f32[512]{0:T(512)S(1)} %add_rsqrt_fusion, f32[1024]{0:T(1024)S(1)} %copy-done.42), kind=kOutput, calls=%fused_computation.20 | convolution fusion | flops 3226992640 | bytes 6297600 | tf_op jit(solution)/shard_map/grk,kd->grd/dot_general | solution.py:314
  156.4 3.5 %fusion.6 = bf16[1,512,1024]{2,1,0:T(8,128)(2,1)} fusion(f32[1,512,1024]{2,1,0:T(8,128)} %convolution_bitcast_fusion.2, f32[512,1024]{1,0:T(8,128)} %fusion.11), kind=kLoop, calls=%fused_computation.9 | loop fusion | flops 1048576 | bytes 5242880 | tf_op jit(solution)/shard_map/convert_element_type | solution.py:317
  (193 shorter events, 41.5 us)
Async XLA Ops:
  0.0 141.3 %copy-start = (bf16[1024,1024]{1,0:T(8,128)(2,1)S(1)}, bf16[1024,1024]{1,0:T(8,128)(2,1)}, u32[]{:S(2)}) copy-start(bf16[1024,1024]{1,0:T(8,128)(2,1)} %param.35) | copy-start | bytes 6291460
  0.0 9.9 %copy-start.24 = (bf16[1024,16]{0,1:T(8,128)(2,1)S(1)}, bf16[1024,16]{0,1:T(8,128)(2,1)}, u32[]{:S(2)}) copy-start(bf16[1024,16]{0,1:T(8,128)(2,1)} %param.28) | copy-start | bytes 98308
  0.0 9.9 %copy-start.39 = (f32[16]{0:T(128)S(1)}, f32[16]{0:T(128)}, u32[]{:S(2)}) copy-start(f32[16]{0:T(128)} %param.31) | copy-start | bytes 196
  0.0 10.3 %copy-start.43 = (f32[16]{0:T(128)S(1)}, f32[16]{0:T(128)}, u32[]{:S(2)}) copy-start(f32[16]{0:T(128)} %param.32) | copy-start | bytes 196
  0.0 13.7 %copy-start.31 = (f32[1280]{0:T(1024)S(1)}, f32[1280]{0:T(1024)}, u32[]{:S(2)}) copy-start(f32[1280]{0:T(1024)} %param.30) | copy-start | bytes 15364
  0.0 15.8 %copy-start.40 = (f32[16]{0:T(128)S(1)}, f32[16]{0:T(128)}, u32[]{:S(2)}) copy-start(f32[16]{0:T(128)} %param.33) | copy-start | bytes 196
  1.9 18.9 %copy-start.15 = (bf16[1,512,1024]{2,1,0:T(8,128)(2,1)}, bf16[1,512,1024]{2,1,0:T(8,128)(2,1)S(1)}, u32[]{:S(2)}) copy-start(bf16[1,512,1024]{2,1,0:T(8,128)(2,1)S(1)} %fusion.10) | copy-start | bytes 3145732
  2.0 14.1 %collective-permute-start = (bf16[1,3,1024]{2,1,0:T(4,128)(2,1)S(1)}, bf16[1,3,1024]{2,1,0:T(4,128)(2,1)S(1)}, u32[]{:S(2)}, u32[]{:S(2)}) collective-permute-start(bf16[1,3,1024]{2,1,0:T(4,128)(2,1)S(1)} %get-tuple-element.122), channel_id=1, source_target_pairs={{0,2},{2,4},{4,6},{6,8},{8,10},{10,12},{12,14},{1,3},{3,5},{5,7},{... | collective-permute-start | bytes 18440 | tf_op jit(solution)/shard_map/ppermute | solution.py:279
  5.4 27.4 %collective-permute-start.1 = (bf16[1,3,1024]{2,1,0:T(4,128)(2,1)S(1)}, bf16[1,3,1024]{2,1,0:T(4,128)(2,1)S(1)}, u32[]{:S(2)}, u32[]{:S(2)}) collective-permute-start(bf16[1,3,1024]{2,1,0:T(4,128)(2,1)S(1)} %get-tuple-element.121), channel_id=1, source_target_pairs={{2,0},{4,2},{6,4},{8,6},{10,8},{12,10},{14,12},{3,1},{5,3},{7,5},{... | collective-permute-start | bytes 18440 | tf_op jit(solution)/shard_map/ppermute | solution.py:280
  12.0 8.8 %copy-start.22 = (f32[1,2,16,256]{3,2,1,0:T(8,128)}, f32[1,2,16,256]{3,2,1,0:T(8,128)S(1)}, u32[]{:S(2)}) copy-start(f32[1,2,16,256]{3,2,1,0:T(8,128)S(1)} %get-tuple-element.112) | copy-start | bytes 98308
  12.3 17.7 %copy-start.32 = (f32[16]{0:T(128)}, f32[16]{0:T(128)S(1)}, u32[]{:S(2)}) copy-start(f32[16]{0:T(128)S(1)} %get-tuple-element.131) | copy-start | bytes 196
  12.3 30.7 %copy-start.27 = (f32[1,16]{1,0:T(1,128)}, f32[1,16]{1,0:T(1,128)S(1)}, u32[]{:S(2)}) copy-start(f32[1,16]{1,0:T(1,128)S(1)} %get-tuple-element.97) | copy-start | bytes 196
  30.0 6.7 %slice-start = ((s8[4718592]{0:T(1024)(128)(4,1)}), s8[4194304]{0:T(1024)(128)(4,1)S(1)}, s32[]{:S(2)}) async-start(s8[4718592]{0:T(1024)(128)(4,1)} %bitcast.296), calls=%async_computation | async-start | bytes 8388608
  31.5 11.5 %copy-start.7 = (f32[1,16,64,128]{3,2,1,0:T(8,128)}, f32[1,16,64,128]{3,2,1,0:T(8,128)S(1)}, u32[]{:S(2)}) copy-start(f32[1,16,64,128]{3,2,1,0:T(8,128)S(1)} %fusion.47) | copy-start | bytes 1572868
  41.8 26.4 %copy-start.23 = (f32[1,2,256,16]{2,3,1,0:T(8,128)}, f32[1,2,256,16]{2,3,1,0:T(8,128)S(1)}, u32[]{:S(2)}) copy-start(f32[1,2,256,16]{2,3,1,0:T(8,128)S(1)} %get-tuple-element.110) | copy-start | bytes 98308
  41.9 10.8 %copy-start.29 = (f32[2,16]{1,0:T(2,128)}, f32[2,16]{1,0:T(2,128)S(1)}, u32[]{:S(2)}) copy-start(f32[2,16]{1,0:T(2,128)S(1)} %get-tuple-element.106) | copy-start | bytes 388
  43.9 40.3 %collective-permute-start.5 = (f32[1,1032,128]{2,1,0:T(8,128)}, f32[1,1032,128]{2,1,0:T(8,128)}, u32[]{:S(2)}, u32[]{:S(2)}) collective-permute-start(f32[1,1032,128]{2,1,0:T(8,128)} %select_maximum_fusion.2), channel_id=1, source_target_pairs={{0,2},{2,4},{4,6},{6,8},{8,10},{10,12},{12,14},{1,3},{3,5},{5,7},{... | collective-permute-start | bytes 1585160 | tf_op jit(solution)/shard_map/ppermute | solution.py:48
  60.4 7.7 %copy-start.41 = (f32[1,1,16]{2,1,0:T(1,128)S(1)}, f32[1,1,16]{2,1,0:T(1,128)}, u32[]{:S(2)}) copy-start(f32[1,1,16]{2,1,0:T(1,128)} %get-tuple-element.127) | copy-start | bytes 196
  63.7 25.3 %collective-permute-start.2 = (f32[1,1032,128]{2,1,0:T(8,128)}, f32[1,1032,128]{2,1,0:T(8,128)}, u32[]{:S(2)}, u32[]{:S(2)}) collective-permute-start(f32[1,1032,128]{2,1,0:T(8,128)} %select_maximum_fusion.5), channel_id=1, source_target_pairs={{2,0},{4,2},{6,4},{8,6},{10,8},{12,10},{14,12},{3,1},{5,3},{7,5},{... | collective-permute-start | bytes 1585160 | tf_op jit(solution)/shard_map/ppermute | solution.py:48
  75.2 5.6 %copy-start.33 = (f32[16]{0:T(128)S(1)}, f32[16]{0:T(128)}, u32[]{:S(2)}) copy-start(f32[16]{0:T(128)} %copy-done.32) | copy-start | bytes 196
  75.2 6.5 %copy-start.25 = (s32[1024]{0:T(1024)S(1)}, s32[1024]{0:T(1024)}, u32[]{:S(2)}) copy-start(s32[1024]{0:T(1024)} %get-tuple-element.134) | copy-start | bytes 12292
  75.2 6.5 %copy-start.26 = (s32[1024]{0:T(1024)S(1)}, s32[1024]{0:T(1024)}, u32[]{:S(2)}) copy-start(s32[1024]{0:T(1024)} %get-tuple-element.135) | copy-start | bytes 12292
  75.2 6.5 %copy-start.37 = (pred[1024]{0:T(1024)(128)(4,1)S(1)}, pred[1024]{0:T(1024)(128)(4,1)}, u32[]{:S(2)}) copy-start(pred[1024]{0:T(1024)(128)(4,1)} %fusion.66) | copy-start | bytes 3076
  84.1 5.7 %copy-start.34 = (f32[1,1,16]{2,1,0:T(1,128)S(1)}, f32[1,1,16]{2,1,0:T(1,128)}, u32[]{:S(2)}) copy-start(f32[1,1,16]{2,1,0:T(1,128)} %get-tuple-element.128) | copy-start | bytes 196
  84.1 5.8 %copy-start.10 = (f32[1,1024,128]{2,1,0:T(8,128)S(1)}, f32[1,1024,128]{2,1,0:T(8,128)}, u32[]{:S(2)}) copy-start(f32[1,1024,128]{2,1,0:T(8,128)} %copy-done.9) | copy-start | bytes 1572868
  87.7 14.9 %collective-permute-start.6 = (f32[1,1032,128]{2,1,0:T(8,128)}, f32[1,1032,128]{2,1,0:T(8,128)}, u32[]{:S(2)}, u32[]{:S(2)}) collective-permute-start(f32[1,1032,128]{2,1,0:T(8,128)} %select_maximum_fusion.1), channel_id=1, source_target_pairs={{0,4},{2,6},{4,8},{6,10},{8,12},{10,14},{1,5},{3,7},{5,9},{7,11},{... | collective-permute-start | bytes 1585160 | tf_op jit(solution)/shard_map/ppermute | solution.py:48
  91.9 12.5 %copy-start.12 = (f32[1,16,64,128]{3,2,1,0:T(8,128)S(1)}, f32[1,16,64,128]{3,2,1,0:T(8,128)}, u32[]{:S(2)}) copy-start(f32[1,16,64,128]{3,2,1,0:T(8,128)} %copy-done.11) | copy-start | bytes 1572868
  93.6 14.7 %collective-permute-start.3 = (f32[1,1032,128]{2,1,0:T(8,128)}, f32[1,1032,128]{2,1,0:T(8,128)}, u32[]{:S(2)}, u32[]{:S(2)}) collective-permute-start(f32[1,1032,128]{2,1,0:T(8,128)} %select_maximum_fusion.4), channel_id=1, source_target_pairs={{4,0},{6,2},{8,4},{10,6},{12,8},{14,10},{5,1},{7,3},{9,5},{11,7},{... | collective-permute-start | bytes 1585160 | tf_op jit(solution)/shard_map/ppermute | solution.py:48
  99.1 9.2 %copy-start.14 = (f32[1,1024,128]{2,1,0:T(8,128)S(1)}, f32[1,1024,128]{2,1,0:T(8,128)}, u32[]{:S(2)}) copy-start(f32[1,1024,128]{2,1,0:T(8,128)} %copy-done.13) | copy-start | bytes 1572868
  104.5 25.8 %collective-permute-start.7 = (f32[1,1032,128]{2,1,0:T(8,128)S(1)}, f32[1,1032,128]{2,1,0:T(8,128)S(1)}, u32[]{:S(2)}, u32[]{:S(2)}) collective-permute-start(f32[1,1032,128]{2,1,0:T(8,128)S(1)} %select_maximum_fusion), channel_id=1, source_target_pairs={{0,8},{2,10},{4,12},{6,14},{1,9},{3,11},{5,13},{7,15},{16,24},{18,... | collective-permute-start | bytes 1585160 | tf_op jit(solution)/shard_map/ppermute | solution.py:48
  110.2 20.3 %copy-start.16 = (bf16[1,512,1024]{2,1,0:T(8,128)(2,1)S(1)}, bf16[1,512,1024]{2,1,0:T(8,128)(2,1)}, u32[]{:S(2)}) copy-start(bf16[1,512,1024]{2,1,0:T(8,128)(2,1)} %copy-done.15) | copy-start | bytes 3145732
  110.3 33.7 %collective-permute-start.4 = (f32[1,1032,128]{2,1,0:T(8,128)S(1)}, f32[1,1032,128]{2,1,0:T(8,128)S(1)}, u32[]{:S(2)}, u32[]{:S(2)}) collective-permute-start(f32[1,1032,128]{2,1,0:T(8,128)S(1)} %select_maximum_fusion.3), channel_id=1, source_target_pairs={{8,0},{10,2},{12,4},{14,6},{9,1},{11,3},{13,5},{15,7},{24,16},{26,... | collective-permute-start | bytes 1585160 | tf_op jit(solution)/shard_map/ppermute | solution.py:48
  (22 other events, 56.7 us)

commit v18 on v15

--- a/solution.py
+++ b/solution.py
@@ -34,7 +34,7 @@
     return (first_decay * next_decay, next_decay[..., None, None] * first_state + next_state)
 
 
-def exclusive_scans(fwd, rev, axis, after_fwd):
+def exclusive_scans(fwd, rev, axis, after_fwd, middle=None):
     count = lax.axis_size(axis)
     place = lax.axis_index(axis)
     seen = [None, None]
@@ -44,23 +44,35 @@
         up = [(i, i + shift) for i in range(count - shift)]
         down = [(i + shift, i) for i in range(count - shift)]
         got = []
+        fill = middle if shift == 2 and fill_pending(middle) else None
+        if fill is not None:
+            ahead, fill_args = lax.optimization_barrier((ahead, fill[1]))
         for k, pairs in ((0, up), (1, down)):
             decay, state = unpack(lax.ppermute(pack(*ahead[k]), axis, pairs))
             has = (place >= shift) if k == 0 else (place < count - shift)
             decay = jnp.where(has, decay, 1.0)
             got.append((decay, state))
+        if fill is not None:
+            got, middle = lax.optimization_barrier((got, fill[0](*fill_args)))
         last = 2 * shift >= count
         for k in range(2):
             if k == 1 and last:
-                tail = after_fwd(seen[0][1])
+                if fill_pending(middle):
+                    middle = middle[0](*middle[1])
+                tail = after_fwd(seen[0][1], middle)
                 got[1], tail = lax.optimization_barrier((got[1], tail))
             seen[k] = got[k] if seen[k] is None else chain(got[k], seen[k])
             if not last:
                 ahead[k] = chain(got[k], ahead[k])
         shift *= 2
     if seen[0] is None:
-        return fwd_identity(rev), after_fwd(fwd_identity(fwd)[1])
-    return seen[1], tail
+        middle = middle[0](*middle[1])
+        return fwd_identity(rev), after_fwd(fwd_identity(fwd)[1], middle), middle
+    return seen[1], tail, middle
+
+
+def fill_pending(item):
+    return isinstance(item, tuple) and callable(item[0])
 
 
 def pack(decay, state):
@@ -296,13 +308,20 @@
         jnp.einsum("grd,dh->grh", mirrored, w_dt, preferred_element_type=jnp.float32) + dt_bias
     )
     sum_r, pend_r = strand_terms(proj_r, step_r, conv_w, conv_b, rates, True)
-    def forward_out(incoming):
-        gate_f = jnp.einsum("grd,de->gre", strand, w_gate, preferred_element_type=jnp.float32)
-        normed_f = finish(pend_f, incoming, gate_f, d_skip, norm_gain)
+    def forward_out(incoming, gates):
+        normed_f = finish(pend_f, incoming, gates[0], d_skip, norm_gain)
         return jnp.einsum("grk,kd->grd", normed_f, w_out, preferred_element_type=jnp.float32)
 
-    in_r, out_f = exclusive_scans(sum_f, sum_r, "seq", forward_out)
-    gate_r = jnp.einsum("grd,de->gre", mirrored, w_gate, preferred_element_type=jnp.float32)
+    def gate_pair(a, b):
+        return (
+            jnp.einsum("grd,de->gre", a, w_gate, preferred_element_type=jnp.float32),
+            jnp.einsum("grd,de->gre", b, w_gate, preferred_element_type=jnp.float32),
+        )
+
+    in_r, out_f, gates = exclusive_scans(
+        sum_f, sum_r, "seq", forward_out, (gate_pair, (strand, mirrored))
+    )
+    gate_r = gates[1]
     normed_r = finish(pend_r, in_r[1], gate_r, d_skip, norm_gain)
     w_out_mirrored = flip_lanes(w_out)
     out = out_f + jnp.einsum(

time: 159 us -> 154 us (0.969)
  waiting for transfers between devices: 24.4 us -> 21.2 us
  local copies, waits for them, and re-layouts: 19.7 us -> 18 us
    ppermute x6, waiting for transfers between devices: 24.4 us -> 21.2 us  [exclusive_scans(): decay, state = unpack(lax.ppermute(pack(*ahead[k]), axis, pairs))]
    dot_general x2, matrix products: 8.75 us -> 5.71 us  [the longest x1 2.86 us: gate_pair(): jnp.einsum('grd,de->gre', a, w_gate, preferred_element_type=jnp.float32)]
    mul x0 -> x2, other arithmetic: none -> 2.53 us  [finish(): gated = scanned * jax.nn.silu(gate_part)]
    add x7, other arithmetic: 6.2 us -> 4.36 us  [chain(): next_decay[..., None, None] * first_state + next_state]
    slice x2 -> x0, other arithmetic: 1.66 us -> none  [unpack(): return (packed[:, rows, :H], packed[:, :rows].reshape(count, H, P_SIZE, N))]
    unnamed x66 -> x54, local copies, waits for them, and re-layouts: 7.43 us -> 5.82 us
    another operation x9 -> x7, other arithmetic: 3.19 us -> 2.5 us
  transfers between devices with their start and end apart: 8 -> 8, of which waited for: 3 -> 3; matrix products, arithmetic and copies ran while one was open for 29% -> 26% of each run, Pallas kernels for 19% -> 19%
where the time goes in v18:
time: 154 us; the launch traced here: 153 us
  matrix products  36.8 us (24%)
  Pallas kernels  29.7 us (19%)
  starting transfers between devices  26.7 us (17%)
  waiting for transfers between devices  21.2 us (14%)
  other arithmetic  19.7 us (13%)
  local copies, waits for them, and re-layouts  18 us (12%)
    ppermute x6, waiting for transfers between devices, exclusive_scans(): decay, state = unpack(lax.ppermute(pack(*ahead[k]), axis, pairs))  21.2 us
    ppermute x6, starting transfers between devices, exclusive_scans(): decay, state = unpack(lax.ppermute(pack(*ahead[k]), axis, pairs))  19.9 us
    pallas_call x2, Pallas kernels, block_terms(): pl.pallas_call(partial(inside_kernel, reverse=reverse), grid=(blocks,), i...  11.2 us
    pallas_call x2, Pallas kernels, convolve(): pl.pallas_call(partial(conv_kernel, reverse=reverse), grid=(count, width...  10.9 us
    pallas_call x2, Pallas kernels, block_terms(): pl.pallas_call(state_kernel, grid=(blocks,), in_specs=[spec((Q, width)),...  7.57 us
    dot_general x1, matrix products, on_device(): jnp.einsum('grk,kd->grd', normed_r, w_out_mirrored, preferred_element_typ...  6.4 us
    unnamed x54, local copies, waits for them, and re-layouts  5.82 us
    dot_general x1, matrix products, on_device(): jnp.einsum('grd,de->gre', ext_r, w_source, preferred_element_type=jnp.flo...  5.16 us
  transfers between devices with their start and end apart: 8, of which 3 were waited for; matrix products, arithmetic and copies ran while one was open for 26% of the time, Pallas kernels for 19%

profile of v18, /device:TPU:24, one launch (start us, length us, event | category | flops | bytes accessed | tf_op | source)
XLA Modules:
  0.0 152.7 jit_solution(4802015247757330846)
XLA Ops:
  0.0 1.9 %fusion.11 = bf16[1,512,1024]{2,1,0:T(8,128)(2,1)S(1)} fusion(bf16[1,512,1024]{2,1,0:T(8,128)(2,1)} %param.25, bf16[4,1024]{1,0:T(4,128)(2,1)} %param.26, s32[512]{0:T(512)} %bitcast.316), kind=kOutput, calls=%fused_computation.19 | convolution fusion | flops 5769216 | bytes 2107392 | tf_op jit(solution)/shard_map/gtb,bd->gtd/dot_general | solution.py:287
  1.9 3.4 %collective-permute-start = (bf16[1,3,1024]{2,1,0:T(4,128)(2,1)S(1)}, bf16[1,3,1024]{2,1,0:T(4,128)(2,1)S(1)}, u32[]{:S(2)}, u32[]{:S(2)}) collective-permute-start(bf16[1,3,1024]{2,1,0:T(4,128)(2,1)S(1)} %get-tuple-element.133), channel_id=1, source_target_pairs={{0,2},{2,4},{4,6},{6,8},{8,10},{10,12},{12,14},{1,3},{3,5},{5,7},{... | collective-permute-start | bytes 18440 | tf_op jit(solution)/shard_map/ppermute | solution.py:291
  5.4 3.3 %collective-permute-start.1 = (bf16[1,3,1024]{2,1,0:T(4,128)(2,1)S(1)}, bf16[1,3,1024]{2,1,0:T(4,128)(2,1)S(1)}, u32[]{:S(2)}, u32[]{:S(2)}) collective-permute-start(bf16[1,3,1024]{2,1,0:T(4,128)(2,1)S(1)} %get-tuple-element.132), channel_id=1, source_target_pairs={{2,0},{4,2},{6,4},{8,6},{10,8},{12,10},{14,12},{3,1},{5,3},{7,5},{... | collective-permute-start | bytes 18440 | tf_op jit(solution)/shard_map/ppermute | solution.py:292
  11.2 2.3 %fusion.58 = f32[512,1024]{1,0:T(8,128)} fusion(f32[512,16]{0,1:T(8,128)S(1)} %bitcast.301, s32[1024]{0:T(1024)S(1)} %get-tuple-element.151, s32[1024]{0:T(1024)S(1)} %get-tuple-element.152, pred[1024]{0:T(1024)(128)(4,1)S(1)} %fusion.73), kind=kOutput, calls=%fused_computation.91 | convolution fusion | flops 100696064 | bytes 2139136 | tf_op jit(solution)/shard_map/grh,hk->grk/dot_general | solution.py:268
  16.6 4.8 %convolution_bitcast_fusion.1.src_ref.halo_ref = f32[1,520,1280]{2,1,0:T(8,128)} fusion(bf16[1024,2304]{1,0:T(8,128)(2,1)} %param.27, bf16[1,3,1024]{2,1,0:T(4,128)(2,1)S(1)} %collective-permute-done, bf16[1,5,1024]{2,1,0:T(8,128)(2,1)S(1)} %broadcast_in_dim.12, bf16[1,512,1024]{2,1,0:T(8,128)(2,1)S(1)} %fusion.11), kind=kOutput, calls=%fused_computation.4 | convolution fusion | flops 1366343680 | bytes 6348800 | tf_op jit(solution)/shard_map/grd,de->gre/dot_general | solution.py:298
  21.5 5.5 %shard_map.118 = (bf16[1,512,1280]{2,1,0:T(8,128)(2,1)}, bf16[1,1280,512]{2,1,0:T(8,128)(2,1)}) custom-call(f32[1,520,1280]{2,1,0:T(8,128)} %convolution_bitcast_fusion.1.src_ref.halo_ref, f32[1,520,1280]{2,1,0:T(8,128)} %convolution_bitcast_fusion.1.src_ref.halo_ref, f32[4,1280]{1,0:T(4,128)} %w_ref.3, f32[1,1280]{1,0:T(1,128)} %reshape.955.b_ref), custom_call_target="tpu_custom_call" | custom-call | tf_op jit(solution)/shard_map/pallas_call | solution.py:212
  27.0 3.8 %shard_map.119 = f32[2,16,64,128]{3,2,1,0:T(8,128)} custom-call(bf16[2,256,1280]{2,1,0:T(8,128)(2,1)} %bitcast.263, bf16[1,1280,512]{2,1,0:T(8,128)(2,1)} %get-tuple-element.100.x_t_ref, f32[2,256,16]{2,1,0:T(8,128)} %copy.28.to_end_ref), custom_call_target="tpu_custom_call" | custom-call | tf_op jit(solution)/shard_map/pallas_call | solution.py:145
  30.7 1.3 fusion.51
  32.1 2.6 %fusion.26 = bf16[520,1024]{1,0:T(8,128)(2,1)S(1)} fusion(bf16[1,5,1024]{2,1,0:T(8,128)(2,1)S(1)} %broadcast_in_dim.12, bf16[1,3,1024]{2,1,0:T(4,128)(2,1)S(1)} %collective-permute-done.1, bf16[1,512,1024]{2,1,0:T(8,128)(2,1)} %copy-done.12), kind=kOutput, calls=%fused_computation.35 | convolution fusion | flops 1096343552 | bytes 2129920 | tf_op jit(solution)/shard_map/...d,de->...e/dot_general | solution.py:28
  38.2 5.2 %convolution_bitcast_fusion.src_ref.halo_ref = f32[1,520,1280]{2,1,0:T(8,128)} fusion(bf16[520,1024]{1,0:T(8,128)(2,1)} %copy-done.16, bf16[1024,2304]{1,0:T(8,128)(2,1)} %param.27), kind=kOutput, calls=%fused_computation.3 | convolution fusion | flops 1363148800 | bytes 6348800 | tf_op jit(solution)/shard_map/grd,de->gre/dot_general | solution.py:306
  44.2 2.5 %collective-permute-start.2 = (f32[1,1032,128]{2,1,0:T(8,128)}, f32[1,1032,128]{2,1,0:T(8,128)}, u32[]{:S(2)}, u32[]{:S(2)}) collective-permute-start(f32[1,1032,128]{2,1,0:T(8,128)} %select_maximum_fusion.5), channel_id=1, source_target_pairs={{0,2},{2,4},{4,6},{6,8},{8,10},{10,12},{12,14},{1,3},{3,5},{5,7},{... | collective-permute-start | bytes 1585160 | tf_op jit(solution)/shard_map/ppermute | solution.py:51
  46.7 5.4 %shard_map.120 = (bf16[1,512,1280]{2,1,0:T(8,128)(2,1)}, bf16[1,1280,512]{2,1,0:T(8,128)(2,1)}) custom-call(f32[1,520,1280]{2,1,0:T(8,128)} %convolution_bitcast_fusion.src_ref.halo_ref, f32[1,520,1280]{2,1,0:T(8,128)} %convolution_bitcast_fusion.src_ref.halo_ref, f32[4,1280]{1,0:T(4,128)} %w_ref.3, f32[1,1280]{1,0:T(1,128)} %reshape.955.b_ref), custom_call_target="tpu_custom_call" | custom-call | tf_op jit(solution)/shard_map/pallas_call | solution.py:212
  53.1 3.8 %shard_map.121 = f32[2,16,64,128]{3,2,1,0:T(8,128)} custom-call(bf16[2,256,1280]{2,1,0:T(8,128)(2,1)} %bitcast.265, bf16[1,1280,512]{2,1,0:T(8,128)(2,1)} %get-tuple-element.106.x_t_ref, f32[2,256,16]{2,1,0:T(8,128)} %copy.34.to_end_ref), custom_call_target="tpu_custom_call" | custom-call | tf_op jit(solution)/shard_map/pallas_call | solution.py:145
  56.8 2.1 %broadcast_add_fusion = (f32[1,1,16,64,128]{4,3,2,1,0:T(8,128)}, f32[1,1,16,64,128]{4,3,2,1,0:T(8,128)S(1)}, f32[1,1,16,64,128]{4,3,2,1,0:T(8,128)S(1)}) fusion(f32[16]{0:T(128)S(1)} %get-tuple-element.142, f32[1,2,16,64,128]{4,3,2,1,0:T(8,128)} %bitcast.267), kind=kLoop, calls=%fused_computation.84 | loop fusion | flops 131072 | bytes 2621504 | tf_op jit(solution)/shard_map/add | solution.py:34
  60.4 4.4 %collective-permute-start.3 = (f32[1,1032,128]{2,1,0:T(8,128)}, f32[1,1032,128]{2,1,0:T(8,128)}, u32[]{:S(2)}, u32[]{:S(2)}) collective-permute-start(f32[1,1032,128]{2,1,0:T(8,128)} %select_maximum_fusion.4), channel_id=1, source_target_pairs={{2,0},{4,2},{6,4},{8,6},{10,8},{12,10},{14,12},{3,1},{5,3},{7,5},{... | collective-permute-start | bytes 1585160 | tf_op jit(solution)/shard_map/ppermute | solution.py:51
  64.9 2.4 %fusion.57 = f32[512,1024]{1,0:T(8,128)} fusion(f32[512,16]{0,1:T(8,128)S(1)} %bitcast.300, s32[1024]{0:T(1024)S(1)} %get-tuple-element.151, s32[1024]{0:T(1024)S(1)} %get-tuple-element.152, pred[1024]{0:T(1024)(128)(4,1)S(1)} %fusion.73), kind=kOutput, calls=%fused_computation.90 | convolution fusion | flops 100696064 | bytes 2139136 | tf_op jit(solution)/shard_map/grh,hk->grk/dot_general | solution.py:268
  71.7 5.6 %shard_map.122 = f32[2,256,1024]{2,1,0:T(8,128)} custom-call(bf16[2,256,1280]{2,1,0:T(8,128)(2,1)} %bitcast.264, f32[2,256,16]{2,1,0:T(8,128)} %copy.36.cum_ref, f32[2,16,256]{2,1,0:T(8,128)} %bitcast.292, f32[2,16,256]{2,1,0:T(8,128)} %bitcast.298), custom_call_target="tpu_custom_call" | custom-call | tf_op jit(solution)/shard_map/pallas_call | solution.py:156
  77.3 5.6 %shard_map.123 = f32[2,256,1024]{2,1,0:T(8,128)} custom-call(bf16[2,256,1280]{2,1,0:T(8,128)(2,1)} %bitcast.266, f32[2,256,16]{2,1,0:T(8,128)} %copy.39.cum_ref, f32[2,16,256]{2,1,0:T(8,128)} %bitcast.294, f32[2,16,256]{2,1,0:T(8,128)} %bitcast.299), custom_call_target="tpu_custom_call" | custom-call | tf_op jit(solution)/shard_map/pallas_call | solution.py:156
  87.1 1.3 collective-permute-start.4
  88.5 4.7 %collective-permute-start.5 = (f32[1,1032,128]{2,1,0:T(8,128)S(1)}, f32[1,1032,128]{2,1,0:T(8,128)S(1)}, u32[]{:S(2)}, u32[]{:S(2)}) collective-permute-start(f32[1,1032,128]{2,1,0:T(8,128)S(1)} %select_maximum_fusion.2), channel_id=1, source_target_pairs={{4,0},{6,2},{8,4},{10,6},{12,8},{14,10},{5,1},{7,3},{9,5},{11,7},{... | collective-permute-start | bytes 1585160 | tf_op jit(solution)/shard_map/ppermute | solution.py:51
  93.2 2.9 %fusion.20 = f32[1,512,1024]{2,1,0:T(8,128)S(1)} fusion(bf16[1024,2304]{1,0:T(8,128)(2,1)} %param.27, bf16[1,512,1024]{2,1,0:T(8,128)(2,1)S(1)} %copy-done.13), kind=kOutput, calls=%fused_computation.32 | convolution fusion | flops 1073741824 | bytes 5242880 | tf_op jit(solution)/shard_map/grd,de->gre/dot_general | solution.py:317
  96.1 2.8 %fusion.23 = f32[1,512,1024]{2,1,0:T(8,128)S(1)} fusion(bf16[1024,2304]{1,0:T(8,128)(2,1)} %param.27, bf16[1,512,1024]{2,1,0:T(8,128)(2,1)S(1)} %copy-done.15), kind=kOutput, calls=%fused_computation.33 | convolution fusion | flops 1073741824 | bytes 5242880 | tf_op jit(solution)/shard_map/grd,de->gre/dot_general | solution.py:318
  99.0 2.7 %collective-permute-done.4 = f32[1,1032,128]{2,1,0:T(8,128)S(1)} collective-permute-done((f32[1,1032,128]{2,1,0:T(8,128)S(1)}, f32[1,1032,128]{2,1,0:T(8,128)S(1)}, u32[]{:S(2)}, u32[]{:S(2)}) %collective-permute-start.4) | collective-permute-done | bytes 528416 | tf_op jit(solution)/shard_map/ppermute | solution.py:51
  101.7 1.3 collective-permute-done.5
  104.0 1.3 collective-permute-start.7
  106.7 5.7 %collective-permute-start.6 = (f32[1,1032,128]{2,1,0:T(8,128)S(1)}, f32[1,1032,128]{2,1,0:T(8,128)S(1)}, u32[]{:S(2)}, u32[]{:S(2)}) collective-permute-start(f32[1,1032,128]{2,1,0:T(8,128)S(1)} %select_maximum_fusion.1), channel_id=1, source_target_pairs={{8,0},{10,2},{12,4},{14,6},{9,1},{11,3},{13,5},{15,7},{24,16},{26,... | collective-permute-start | bytes 1585160 | tf_op jit(solution)/shard_map/ppermute | solution.py:51
  112.4 17.2 %collective-permute-done.7 = f32[1,1032,128]{2,1,0:T(8,128)S(1)} collective-permute-done((f32[1,1032,128]{2,1,0:T(8,128)S(1)}, f32[1,1032,128]{2,1,0:T(8,128)S(1)}, u32[]{:S(2)}, u32[]{:S(2)}) %collective-permute-start.7) | collective-permute-done | bytes 528416 | tf_op jit(solution)/shard_map/ppermute | solution.py:51
  132.3 1.3 fusion.9
  134.3 2.6 %convolution_bitcast_fusion.2 = f32[1,512,1024]{2,1,0:T(8,128)} fusion(bf16[1024,1024]{1,0:T(8,128)(2,1)S(1)} %copy-done, f32[1,512,1024]{2,1,0:T(8,128)S(1)} %fusion.9, f32[1024]{0:T(1024)S(1)} %copy-done.24, f32[512]{0:T(512)S(1)} %add_rsqrt_fusion.1), kind=kOutput, calls=%fused_computation.34 | convolution fusion | flops 1075314688 | bytes 6297600 | tf_op jit(solution)/shard_map/grk,kd->grd/dot_general | solution.py:313
  141.3 1.3 copy-done.8
  142.8 6.4 %fusion.12 = f32[512,1024]{1,0:T(8,128)} fusion(bf16[1024,1024]{1,0:T(8,128)(2,1)S(1)} %copy-done, f32[1,512,1024]{2,1,0:T(8,128)} %copy-done.8, f32[512]{0:T(512)S(1)} %add_rsqrt_fusion, f32[1024]{0:T(1024)S(1)} %copy-done.24), kind=kOutput, calls=%fused_computation.20 | convolution fusion | flops 3226992640 | bytes 6297600 | tf_op jit(solution)/shard_map/grk,kd->grd/dot_general | solution.py:327
  149.2 3.5 %fusion.6 = bf16[1,512,1024]{2,1,0:T(8,128)(2,1)} fusion(f32[1,512,1024]{2,1,0:T(8,128)} %convolution_bitcast_fusion.2, f32[512,1024]{1,0:T(8,128)} %fusion.12), kind=kLoop, calls=%fused_computation.9 | loop fusion | flops 1048576 | bytes 5242880 | tf_op jit(solution)/shard_map/convert_element_type | solution.py:330
  (149 shorter events, 31.0 us)
Async XLA Ops:
  0.0 133.8 %copy-start = (bf16[1024,1024]{1,0:T(8,128)(2,1)S(1)}, bf16[1024,1024]{1,0:T(8,128)(2,1)}, u32[]{:S(2)}) copy-start(bf16[1024,1024]{1,0:T(8,128)(2,1)} %param.35) | copy-start | bytes 6291460
  0.0 8.7 %copy-start.20 = (bf16[1024,16]{0,1:T(8,128)(2,1)S(1)}, bf16[1024,16]{0,1:T(8,128)(2,1)}, u32[]{:S(2)}) copy-start(bf16[1024,16]{0,1:T(8,128)(2,1)} %param.28) | copy-start | bytes 98308
  0.0 8.7 %copy-start.22 = (f32[16]{0:T(128)S(1)}, f32[16]{0:T(128)}, u32[]{:S(2)}) copy-start(f32[16]{0:T(128)} %param.31) | copy-start | bytes 196
  0.0 9.2 %copy-start.25 = (f32[16]{0:T(128)S(1)}, f32[16]{0:T(128)}, u32[]{:S(2)}) copy-start(f32[16]{0:T(128)} %param.32) | copy-start | bytes 196
  1.9 14.7 %copy-start.12 = (bf16[1,512,1024]{2,1,0:T(8,128)(2,1)}, bf16[1,512,1024]{2,1,0:T(8,128)(2,1)S(1)}, u32[]{:S(2)}) copy-start(bf16[1,512,1024]{2,1,0:T(8,128)(2,1)S(1)} %fusion.11) | copy-start | bytes 3145732
  1.9 11.7 %copy-start.21 = (f32[1280]{0:T(1024)S(1)}, f32[1280]{0:T(1024)}, u32[]{:S(2)}) copy-start(f32[1280]{0:T(1024)} %param.30) | copy-start | bytes 15364
  1.9 14.7 %collective-permute-start = (bf16[1,3,1024]{2,1,0:T(4,128)(2,1)S(1)}, bf16[1,3,1024]{2,1,0:T(4,128)(2,1)S(1)}, u32[]{:S(2)}, u32[]{:S(2)}) collective-permute-start(bf16[1,3,1024]{2,1,0:T(4,128)(2,1)S(1)} %get-tuple-element.133), channel_id=1, source_target_pairs={{0,2},{2,4},{4,6},{6,8},{8,10},{10,12},{12,14},{1,3},{3,5},{5,7},{... | collective-permute-start | bytes 18440 | tf_op jit(solution)/shard_map/ppermute | solution.py:291
  5.4 26.7 %collective-permute-start.1 = (bf16[1,3,1024]{2,1,0:T(4,128)(2,1)S(1)}, bf16[1,3,1024]{2,1,0:T(4,128)(2,1)S(1)}, u32[]{:S(2)}, u32[]{:S(2)}) collective-permute-start(bf16[1,3,1024]{2,1,0:T(4,128)(2,1)S(1)} %get-tuple-element.132), channel_id=1, source_target_pairs={{2,0},{4,2},{6,4},{8,6},{10,8},{12,10},{14,12},{3,1},{5,3},{7,5},{... | collective-permute-start | bytes 18440 | tf_op jit(solution)/shard_map/ppermute | solution.py:292
  8.8 7.7 %copy-start.23 = (f32[16]{0:T(128)S(1)}, f32[16]{0:T(128)}, u32[]{:S(2)}) copy-start(f32[16]{0:T(128)} %param.33) | copy-start | bytes 196
  10.9 10.6 %copy-start.18 = (f32[1,2,16,256]{3,2,1,0:T(8,128)}, f32[1,2,16,256]{3,2,1,0:T(8,128)S(1)}, u32[]{:S(2)}) copy-start(f32[1,2,16,256]{3,2,1,0:T(8,128)S(1)} %get-tuple-element.128) | copy-start | bytes 98308
  32.1 11.3 %copy-start.10 = (f32[1,16,64,128]{3,2,1,0:T(8,128)}, f32[1,16,64,128]{3,2,1,0:T(8,128)S(1)}, u32[]{:S(2)}) copy-start(f32[1,16,64,128]{3,2,1,0:T(8,128)S(1)} %fusion.51) | copy-start | bytes 1572868
  38.1 32.1 %copy-start.19 = (f32[1,2,256,16]{2,3,1,0:T(8,128)}, f32[1,2,256,16]{2,3,1,0:T(8,128)S(1)}, u32[]{:S(2)}) copy-start(f32[1,2,256,16]{2,3,1,0:T(8,128)S(1)} %get-tuple-element.126) | copy-start | bytes 98308
  44.2 38.8 %collective-permute-start.2 = (f32[1,1032,128]{2,1,0:T(8,128)}, f32[1,1032,128]{2,1,0:T(8,128)}, u32[]{:S(2)}, u32[]{:S(2)}) collective-permute-start(f32[1,1032,128]{2,1,0:T(8,128)} %select_maximum_fusion.5), channel_id=1, source_target_pairs={{0,2},{2,4},{4,6},{6,8},{8,10},{10,12},{12,14},{1,3},{3,5},{5,7},{... | collective-permute-start | bytes 1585160 | tf_op jit(solution)/shard_map/ppermute | solution.py:51
  59.2 8.1 %copy-start.17 = (bf16[520,1024]{1,0:T(8,128)(2,1)S(1)}, bf16[520,1024]{1,0:T(8,128)(2,1)}, u32[]{:S(2)}) copy-start(bf16[520,1024]{1,0:T(8,128)(2,1)} %copy-done.16) | copy-start | bytes 3194884
  60.4 23.9 %collective-permute-start.3 = (f32[1,1032,128]{2,1,0:T(8,128)}, f32[1,1032,128]{2,1,0:T(8,128)}, u32[]{:S(2)}, u32[]{:S(2)}) collective-permute-start(f32[1,1032,128]{2,1,0:T(8,128)} %select_maximum_fusion.4), channel_id=1, source_target_pairs={{2,0},{4,2},{6,4},{8,6},{10,8},{12,10},{14,12},{3,1},{5,3},{7,5},{... | collective-permute-start | bytes 1585160 | tf_op jit(solution)/shard_map/ppermute | solution.py:51
  77.3 5.6 %copy-start.9 = (f32[2,16,64,128]{3,2,1,0:T(8,128)S(1)}, f32[2,16,64,128]{3,2,1,0:T(8,128)}, u32[]{:S(2)}) copy-start(f32[2,16,64,128]{3,2,1,0:T(8,128)} %shard_map.119) | copy-start | bytes 3145732
  82.9 1.3 copy-start.11
  83.0 2.4 %copy-start.3 = (f32[2,16,64,128]{3,2,1,0:T(8,128)S(1)}, f32[2,16,64,128]{3,2,1,0:T(8,128)}, u32[]{:S(2)}) copy-start(f32[2,16,64,128]{3,2,1,0:T(8,128)} %shard_map.121) | copy-start | bytes 3145732
  85.4 7.8 %copy-start.13 = (bf16[1,512,1024]{2,1,0:T(8,128)(2,1)S(1)}, bf16[1,512,1024]{2,1,0:T(8,128)(2,1)}, u32[]{:S(2)}) copy-start(bf16[1,512,1024]{2,1,0:T(8,128)(2,1)} %copy-done.12) | copy-start | bytes 3145732
  87.1 14.5 %collective-permute-start.4 = (f32[1,1032,128]{2,1,0:T(8,128)S(1)}, f32[1,1032,128]{2,1,0:T(8,128)S(1)}, u32[]{:S(2)}, u32[]{:S(2)}) collective-permute-start(f32[1,1032,128]{2,1,0:T(8,128)S(1)} %select_maximum_fusion.3), channel_id=1, source_target_pairs={{0,4},{2,6},{4,8},{6,10},{8,12},{10,14},{1,5},{3,7},{5,9},{7,11},{... | collective-permute-start | bytes 1585160 | tf_op jit(solution)/shard_map/ppermute | solution.py:51
  88.5 7.6 %copy-start.15 = (bf16[1,512,1024]{2,1,0:T(8,128)(2,1)S(1)}, bf16[1,512,1024]{2,1,0:T(8,128)(2,1)}, u32[]{:S(2)}) copy-start(bf16[1,512,1024]{2,1,0:T(8,128)(2,1)} %slice.284) | copy-start | bytes 3145732
  88.5 14.5 %collective-permute-start.5 = (f32[1,1032,128]{2,1,0:T(8,128)S(1)}, f32[1,1032,128]{2,1,0:T(8,128)S(1)}, u32[]{:S(2)}, u32[]{:S(2)}) collective-permute-start(f32[1,1032,128]{2,1,0:T(8,128)S(1)} %select_maximum_fusion.2), channel_id=1, source_target_pairs={{4,0},{6,2},{8,4},{10,6},{12,8},{14,10},{5,1},{7,3},{9,5},{11,7},{... | collective-permute-start | bytes 1585160 | tf_op jit(solution)/shard_map/ppermute | solution.py:51
  104.0 25.6 %collective-permute-start.7 = (f32[1,1032,128]{2,1,0:T(8,128)S(1)}, f32[1,1032,128]{2,1,0:T(8,128)S(1)}, u32[]{:S(2)}, u32[]{:S(2)}) collective-permute-start(f32[1,1032,128]{2,1,0:T(8,128)S(1)} %select_maximum_fusion), channel_id=1, source_target_pairs={{0,8},{2,10},{4,12},{6,14},{1,9},{3,11},{5,13},{7,15},{16,24},{18,... | collective-permute-start | bytes 1585160 | tf_op jit(solution)/shard_map/ppermute | solution.py:51
  106.7 30.2 %collective-permute-start.6 = (f32[1,1032,128]{2,1,0:T(8,128)S(1)}, f32[1,1032,128]{2,1,0:T(8,128)S(1)}, u32[]{:S(2)}, u32[]{:S(2)}) collective-permute-start(f32[1,1032,128]{2,1,0:T(8,128)S(1)} %select_maximum_fusion.1), channel_id=1, source_target_pairs={{8,0},{10,2},{12,4},{14,6},{9,1},{11,3},{13,5},{15,7},{24,16},{26,... | collective-permute-start | bytes 1585160 | tf_op jit(solution)/shard_map/ppermute | solution.py:51
  129.6 1.6 %copy-start.6 = (f32[512,1024]{1,0:T(8,128)S(1)}, f32[512,1024]{1,0:T(8,128)}, u32[]{:S(2)}) copy-start(f32[512,1024]{1,0:T(8,128)} %fusion.58) | copy-start | bytes 6291460
  129.8 2.1 %copy-start.5 = (f32[2,256,1024]{2,1,0:T(8,128)S(1)}, f32[2,256,1024]{2,1,0:T(8,128)}, u32[]{:S(2)}) copy-start(f32[2,256,1024]{2,1,0:T(8,128)} %shard_map.122) | copy-start | bytes 6291460
  130.0 2.3 %copy-start.1 = (bf16[1,512,1280]{2,1,0:T(8,128)(2,1)S(1)}, bf16[1,512,1280]{2,1,0:T(8,128)(2,1)}, u32[]{:S(2)}) copy-start(bf16[1,512,1280]{2,1,0:T(8,128)(2,1)} %get-tuple-element.99) | copy-start | bytes 3932164
  136.9 1.0 copy-start.14
  136.9 2.2 %copy-start.7 = (f32[512,1024]{1,0:T(8,128)S(1)}, f32[512,1024]{1,0:T(8,128)}, u32[]{:S(2)}) copy-start(f32[512,1024]{1,0:T(8,128)} %fusion.57) | copy-start | bytes 6291460
  137.9 1.7 %copy-start.4 = (f32[2,256,1024]{2,1,0:T(8,128)S(1)}, f32[2,256,1024]{2,1,0:T(8,128)}, u32[]{:S(2)}) copy-start(f32[2,256,1024]{2,1,0:T(8,128)} %shard_map.123) | copy-start | bytes 6291460
  138.1 1.9 %copy-start.2 = (bf16[1,512,1280]{2,1,0:T(8,128)(2,1)S(1)}, bf16[1,512,1280]{2,1,0:T(8,128)(2,1)}, u32[]{:S(2)}) copy-start(bf16[1,512,1280]{2,1,0:T(8,128)(2,1)} %get-tuple-element.105) | copy-start | bytes 3932164
  141.3 1.3 copy-start.8
  (2 other events, 1.7 us)
